TPU v7x, 256 devices: a whole 4x4x8 slice. The times are simulated.
256 devices in a mesh: dp: 16 (over z, core), tensor: 16 (over y, x).
Axes of the slice: x: 4, y: 4, z: 8, core: 2. Of those that a mesh axis runs over, the one named last changes fastest.
Arguments:
- tokens: bfloat16 [8192, 2048], P(('dp', 'tensor')), may hold values from -6 to 6
- lengths: int32 [16, 8], P('dp'), may hold values from 1 to 128, 512 in all within a row
- group_prefix: int32 [16], replicated, may hold values from 0 to 15, as said below
- prefix_cache: bfloat16 [65536, 512], P(('dp', 'tensor')), may hold values from -340 to 340
- query_weight: bfloat16 [2048, 1024], P(None, 'tensor'), may hold values from -0.125 to 0.125
- key_weight: bfloat16 [2048, 256], replicated, may hold values from -0.375 to 0.375
- value_weight: bfloat16 [2048, 256], replicated, may hold values from -0.125 to 0.125
- out_weight: bfloat16 [1024, 2048], P('tensor'), may hold values from -0.1875 to 0.1875
- gate_up_weight: bfloat16 [2, 2048, 5120], P(None, None, 'tensor'), may hold values from -0.125 to 0.125
- down_weight: bfloat16 [5120, 2048], P('tensor'), may hold values from -0.078125 to 0.078125
Outputs:
- layer_out: bfloat16 [8192, 2048], P(('dp', 'tensor'))
Inputs may be any that keep to these rules, and one draw needn't show every extreme that they name: The 8 lengths of a group sum to 512, and one of them is exactly 128. `group_prefix`: several groups may continue the same slot.
All inputs are finite; a program needn't handle non-finite values.
Results may differ from a plain program's by a relative error of at most 0.023.
Values may be sent and summed in bfloat16 or wider, within the bound.
No kernel may reach another device: no remote copies, remote signals or barrier semaphores. Data moves between devices by JAX's collectives and lax.ppermute only.
A program may use at most 64 MiB of HBM per device.

v0:
```python
import math

import jax
import jax.numpy as jnp
from jax import lax
from jax.sharding import PartitionSpec as P

QH = 16
KVH = 4
HD = 64
PLEN = 4096


NEG_FILL = -1e30


def token_layout(lengths, total_rows):
    ends_at = jnp.cumsum(lengths)
    starts_at = ends_at - lengths
    indices = jnp.arange(total_rows, dtype=jnp.int32)
    request = jnp.sum((indices[:, None] >= ends_at[None, :]).astype(jnp.int32), axis=1)
    begins = jnp.max(
        jnp.where(starts_at[None, :] <= indices[:, None], starts_at[None, :], 0), axis=1
    )
    return ((PLEN + indices - begins).astype(jnp.float32), request)


def rope_tables(positions):
    halves = HD // 2
    steps_float = jnp.arange(halves, dtype=jnp.float32)
    inverse = jnp.exp(steps_float * (-2.0 * math.log(10000.0) / HD))
    angles = positions[:, None] * inverse[None, :]
    return (jnp.cos(angles), jnp.sin(angles))


def rotate(values, cos_table, sin_table):
    halves = values.shape[-1] // 2
    former = values[..., :halves]
    latter = values[..., halves:]
    cos_rows = cos_table[:, None, :]
    sin_rows = sin_table[:, None, :]
    return jnp.concatenate(
        [former * cos_rows - latter * sin_rows, latter * cos_rows + former * sin_rows], axis=-1
    )


def norm_rows(inputs):
    floats = inputs.astype(jnp.float32)
    return (floats * lax.rsqrt(jnp.mean(floats * floats, axis=-1, keepdims=True) + 1e-05)).astype(
        jnp.bfloat16
    )


def softmax_block(queries, keys_block, values_block, scaling, allowed):
    scores = (
        jnp.einsum("thd,nhd->thn", queries, keys_block, preferred_element_type=jnp.float32)
        * scaling
    )
    if allowed is not None:
        scores = jnp.where(allowed, scores, NEG_FILL)
    top_score = jnp.max(scores, axis=2)
    exponent = jnp.exp(scores - top_score[:, :, None])
    weight = jnp.sum(exponent, axis=2)
    blended = jnp.einsum(
        "thn,nhd->thd",
        exponent.astype(jnp.bfloat16),
        values_block,
        preferred_element_type=jnp.float32,
    )
    return (top_score, weight, blended)


def merge_states(former, latter):
    top_one, weight_one, blend_one = former
    top_two, weight_two, blend_two = latter
    overall = jnp.maximum(top_one, top_two)
    factor_one = jnp.exp(top_one - overall)
    factor_two = jnp.exp(top_two - overall)
    return (
        overall,
        weight_one * factor_one + weight_two * factor_two,
        blend_one * factor_one[:, :, None] + blend_two * factor_two[:, :, None],
    )


def on_device(
    tokens,
    lengths,
    group_prefix,
    prefix_cache,
    query_weight,
    key_weight,
    value_weight,
    out_weight,
    gate_up_weight,
    down_weight,
):
    tensor_count = lax.axis_size("tensor")
    tensor_rank = lax.axis_index("tensor")
    group_rank = lax.axis_index("dp")
    row_count = tokens.shape[0]
    group_tokens = row_count * tensor_count
    local_heads = query_weight.shape[1] // HD
    head_ratio = QH // KVH
    local_kv = max(1, local_heads // head_ratio)
    repeat_by = local_heads // local_kv
    kv_first = tensor_rank * local_heads // head_ratio
    kv_total = KVH * HD
    query_width = local_heads * HD
    kv_width = local_kv * HD
    scaling = 1.0 / math.sqrt(HD)
    positions, request = token_layout(lengths[0], group_tokens)
    cos_table, sin_table = rope_tables(positions)
    key_cols = lax.dynamic_slice_in_dim(key_weight, kv_first * HD, kv_width, 1)
    value_cols = lax.dynamic_slice_in_dim(value_weight, kv_first * HD, kv_width, 1)
    projection = jnp.concatenate([query_weight, key_cols, value_cols], axis=1)
    normed = norm_rows(tokens)
    segment = lax.all_gather(normed, "tensor", axis=0, tiled=True)
    seg_rows = segment.shape[0]
    mapped = jnp.dot(segment, projection, preferred_element_type=jnp.float32)
    query_part = rotate(
        mapped[:, :query_width].reshape(seg_rows, local_heads, HD), cos_table, sin_table
    )
    key_part = rotate(
        mapped[:, query_width : query_width + kv_width].reshape(seg_rows, local_kv, HD),
        cos_table,
        sin_table,
    )
    projected = jnp.concatenate(
        [
            query_part.reshape(seg_rows, query_width),
            key_part.reshape(seg_rows, kv_width),
            mapped[:, query_width + kv_width :],
        ],
        axis=1,
    ).astype(jnp.bfloat16)
    queries = projected[:, :query_width].reshape(group_tokens, local_heads, HD)
    own_keys = jnp.repeat(
        projected[:, query_width : query_width + kv_width].reshape(group_tokens, local_kv, HD),
        repeat_by,
        axis=1,
    )
    own_values = jnp.repeat(
        projected[:, query_width + kv_width :].reshape(group_tokens, local_kv, HD),
        repeat_by,
        axis=1,
    )
    slot_wanted = group_prefix[group_rank]
    shard_rows = prefix_cache.shape[0]
    segment = lax.all_gather(prefix_cache, "dp", axis=0, tiled=True)
    seg_rows = segment.shape[0]
    indices = jnp.arange(seg_rows, dtype=jnp.int32)
    matches = indices // shard_rows == slot_wanted
    places = indices % shard_rows
    chosen = (
        jnp.zeros_like(prefix_cache)
        .at[places]
        .add(jnp.where(matches[:, None], segment, jnp.zeros_like(segment)))
    )
    start_state = (
        jnp.full((group_tokens, local_heads), NEG_FILL, jnp.float32),
        jnp.zeros((group_tokens, local_heads), jnp.float32),
        jnp.zeros((group_tokens, local_heads, HD), jnp.float32),
    )
    segment = lax.all_gather(chosen, "tensor", axis=0, tiled=True)
    seg_rows = segment.shape[0]
    keys_block = lax.dynamic_slice_in_dim(segment, kv_first * HD, kv_width, 1).reshape(
        seg_rows, local_kv, HD
    )
    values_block = lax.dynamic_slice_in_dim(segment, kv_total + kv_first * HD, kv_width, 1).reshape(
        seg_rows, local_kv, HD
    )
    keys_block = jnp.repeat(keys_block, repeat_by, axis=1)
    values_block = jnp.repeat(values_block, repeat_by, axis=1)
    prefix_state = merge_states(
        start_state, softmax_block(queries, keys_block, values_block, scaling, None)
    )
    indices = jnp.arange(group_tokens, dtype=jnp.int32)
    allowed = (request[:, None] == request[None, :]) & (indices[None, :] <= indices[:, None])
    suffix_state = softmax_block(queries, own_keys, own_values, scaling, allowed[:, None, :])
    top_score, weight, blended = merge_states(prefix_state, suffix_state)
    attended = (
        (blended / weight[:, :, None]).astype(jnp.bfloat16).reshape(group_tokens, query_width)
    )
    attn_sum = lax.psum_scatter(
        jnp.dot(attended, out_weight, preferred_element_type=jnp.float32).astype(jnp.bfloat16),
        "tensor",
        scatter_dimension=0,
        tiled=True,
    ).astype(jnp.float32)
    middle = (tokens.astype(jnp.float32) + attn_sum).astype(jnp.bfloat16)
    segment = lax.all_gather(norm_rows(middle), "tensor", axis=0, tiled=True)
    gate_value = jnp.dot(segment, gate_up_weight[0], preferred_element_type=jnp.float32)
    upward = jnp.dot(segment, gate_up_weight[1], preferred_element_type=jnp.float32)
    hidden = (jax.nn.silu(gate_value) * upward).astype(jnp.bfloat16)
    ffn_sum = lax.psum_scatter(
        jnp.dot(hidden, down_weight, preferred_element_type=jnp.float32).astype(jnp.bfloat16),
        "tensor",
        scatter_dimension=0,
        tiled=True,
    ).astype(jnp.float32)
    return (middle.astype(jnp.float32) + ffn_sum).astype(jnp.bfloat16)


def solution(mesh):
    return jax.shard_map(
        on_device,
        mesh=mesh,
        in_specs=(
            P(("dp", "tensor"), None),
            P("dp", None),
            P(),
            P(("dp", "tensor"), None),
            P(None, "tensor"),
            P(),
            P(),
            P("tensor", None),
            P(None, None, "tensor"),
            P("tensor", None),
        ),
        out_specs=P(("dp", "tensor"), None),
        check_vma=False,
    )
```

profile of v0, /device:TPU:0, one launch (start us, length us, event | category | flops | bytes accessed | tf_op | source)
XLA Modules:
  0.0 398.8 jit_solution(4943395580398315689)
XLA Ops:
  6.5 0.7 all-gather.5.cloned.1.call-update
  7.3 1.0 fusion.66
  8.4 1.7 fusion.67
  10.1 1.2 dynamic_slice.15
  11.4 0.6 fusion.93
  12.0 40.6 %all-gather.5.cloned.1.call-done = bf16[4096,512]{1,0:T(8,128)(2,1)} async-done(((bf16[256,512]{1,0:T(8,128)(2,1)}), bf16[4096,512]{1,0:T(8,128)(2,1)}) %all-gather.5.cloned.1.call-update) | async-done | bytes 4194320 | tf_op jit(solution)/shard_map/all_gather | solution.py:150
  52.6 28.1 %scatter_custom_fusion = bf16[256,512]{1,0:T(8,128)(2,1)} fusion(s32[4096]{0:T(1024)S(1)} %bitcast.114, bf16[4096,512]{1,0:T(8,128)(2,1)} %all-gather.5.cloned.1.call-done, pred[4096]{0:T(1024)(128)(4,1)S(1)} %fusion.93, bf16[]{:T(256)} %constant.71.clone.1), kind=kCustom, calls=%fused_computation.7 | custom fusion | flops 4194304 | bytes 4461568 | tf_op jit(solution)/shard_map/scatter-add | solution.py:158
  81.5 1.6 constant_dynamic-slice_fusion
  83.0 20.5 %all-gather.9.cloned.1.call-done = bf16[512,2048]{1,0:T(8,128)(2,1)} async-done(((bf16[32,2048]{1,0:T(8,128)(2,1)}), bf16[512,2048]{1,0:T(8,128)(2,1)}) %all-gather.9.cloned.1.call-update) | async-done | bytes 2097168 | tf_op jit(solution)/shard_map/all_gather | solution.py:118
  103.5 2.7 fusion.41
  106.6 0.4 fusion.112
  107.2 54.8 %all-gather.7.cloned.1.call-done = bf16[4096,512]{1,0:T(8,128)(2,1)} async-done(((bf16[256,512]{1,0:T(8,128)(2,1)}), bf16[4096,512]{1,0:T(8,128)(2,1)}) %all-gather.7.cloned.1.call-update) | async-done | bytes 4194320 | tf_op jit(solution)/shard_map/all_gather | solution.py:165
  162.0 2.5 multiply_reduce_fusion
  164.5 1.4 fusion.1
  166.0 3.1 fusion.36
  169.1 2.3 convolution_convert_fusion.1
  171.5 79.3 %reduce-scatter.3.cloned.1.call-done = bf16[32,2048]{1,0:T(8,128)(2,1)} async-done(((bf16[512,2048]{1,0:T(8,128)(2,1)}), bf16[32,2048]{1,0:T(8,128)(2,1)}) %reduce-scatter.3.cloned.1.call-update) | async-done | bytes 131088 | tf_op jit(solution)/shard_map/reduce_scatter | solution.py:185
  250.9 1.1 fusion.69
  251.9 1.7 fusion.70
  253.8 49.2 %all-gather.11.cloned.1.call-done = bf16[512,2048]{1,0:T(8,128)(2,1)} async-done(((bf16[32,2048]{1,0:T(8,128)(2,1)}), bf16[512,2048]{1,0:T(8,128)(2,1)}) %all-gather.11.cloned.1.call-update) | async-done | bytes 2097168 | tf_op jit(solution)/shard_map/all_gather | solution.py:192
  303.0 2.8 fusion.13
  305.9 5.5 %convolution_convert_fusion = bf16[512,2048]{1,0:T(8,128)(2,1)} fusion(bf16[320,2048]{1,0:T(8,128)(2,1)S(1)} %copy-done, bf16[512,2048]{1,0:T(8,128)(2,1)} %all-gather.11.cloned.1.call-done, bf16[2,2048,320]{1,2,0:T(8,128)(2,1)} %param.18, f32[512,320]{0,1:T(8,128)S(1)} %fusion.13), kind=kOutput, calls=%fused_computation.11 | convolution fusion | flops 1344208896 | bytes 7471104 | tf_op jit(solution)/shard_map/dot_general | solution.py:197
  311.4 79.0 %reduce-scatter.5.cloned.1.call-done = bf16[32,2048]{1,0:T(8,128)(2,1)} async-done(((bf16[512,2048]{1,0:T(8,128)(2,1)}), bf16[32,2048]{1,0:T(8,128)(2,1)}) %reduce-scatter.5.cloned.1.call-update) | async-done | bytes 131088 | tf_op jit(solution)/shard_map/reduce_scatter | solution.py:196
  390.4 1.6 fusion.71
  (37 shorter events, 1.7 us)
Async XLA Ops:
  6.5 299.3 %copy-start = (bf16[320,2048]{1,0:T(8,128)(2,1)S(1)}, bf16[320,2048]{1,0:T(8,128)(2,1)}, u32[]{:S(2)}) copy-start(bf16[320,2048]{1,0:T(8,128)(2,1)} %param.19) | copy-start | bytes 3932164
  6.5 46.0 %all-gather.5.cloned.1.call-start = ((), (), s32[]{:S(2)}) async-start(), calls=%async_computation.2 | async-start | bytes 4456448 | tf_op jit(solution)/shard_map/all_gather | solution.py:150
  7.3 96.3 %all-gather.9.cloned.1.call-start = ((), (), s32[]{:S(2)}) async-start(), calls=%async_computation.4 | async-start | bytes 2228224 | tf_op jit(solution)/shard_map/all_gather | solution.py:118
  8.3 72.5 %copy-start.5 = (s32[1,8]{1,0:T(1,128)S(1)}, s32[1,8]{1,0:T(1,128)}, u32[]{:S(2)}) copy-start(s32[1,8]{1,0:T(1,128)} %param.11) | copy-start | bytes 100
  8.4 72.6 %copy-start.3 = (bf16[2048,64]{0,1:T(8,128)(2,1)S(1)}, bf16[2048,64]{0,1:T(8,128)(2,1)}, u32[]{:S(2)}) copy-start(bf16[2048,64]{0,1:T(8,128)(2,1)} %param.14) | copy-start | bytes 786436
  10.1 151.9 %all-gather.7.cloned.1.call-start = ((), (), s32[]{:S(2)}) async-start(), calls=%async_computation.3 | async-start | bytes 4456448 | tf_op jit(solution)/shard_map/all_gather | solution.py:165
  80.7 170.2 %reduce-scatter.3.cloned.1.call-start = ((), (), s32[]{:S(2)}) async-start(), calls=%async_computation.5 | async-start | bytes 2228224 | tf_op jit(solution)/shard_map/reduce_scatter | solution.py:185
  166.0 3.1 copy-start.4
  169.1 81.7 %copy-start.1 = (bf16[32,2048]{1,0:T(8,128)(2,1)S(1)}, bf16[32,2048]{1,0:T(8,128)(2,1)}, u32[]{:S(2)}) copy-start(bf16[32,2048]{1,0:T(8,128)(2,1)} %param.10) | copy-start | bytes 393220
  171.5 131.5 %all-gather.11.cloned.1.call-start = ((), (), s32[]{:S(2)}) async-start(), calls=%async_computation.6 | async-start | bytes 2228224 | tf_op jit(solution)/shard_map/all_gather | solution.py:192
  253.6 136.7 %reduce-scatter.5.cloned.1.call-start = ((), (), s32[]{:S(2)}) async-start(), calls=%async_computation.7 | async-start | bytes 2228224 | tf_op jit(solution)/shard_map/reduce_scatter | solution.py:196
  305.9 84.5 %copy-start.2 = (bf16[32,2048]{1,0:T(8,128)(2,1)S(1)}, bf16[32,2048]{1,0:T(8,128)(2,1)}, u32[]{:S(2)}) copy-start(bf16[32,2048]{1,0:T(8,128)(2,1)} %reduce-scatter.3.cloned.1.call-done) | copy-start | bytes 393220
Sparse Core Ops, SparseCore 0:
  9.2 43.3 all-gather.4
  55.0 48.5 all-gather.8
  106.0 55.9 all-gather.6
  171.6 79.2 reduce-scatter.2
  253.7 49.2 all-gather.10
  311.5 78.8 reduce-scatter.4
where the time goes:
time: 401 us; the launch traced here: 399 us
  waiting for transfers between devices  324 us (81%)
  other arithmetic  38.2 us (10%)
  matrix products  19.4 us (5%)
  between operations  13.7 us (3%)
    reduce_scatter x1, waiting for transfers between devices, on_device(): lax.psum_scatter(jnp.dot(attended, out_weight, preferred_element_type=jnp...  79.3 us
    reduce_scatter x1, waiting for transfers between devices, on_device(): lax.psum_scatter(jnp.dot(hidden, down_weight, preferred_element_type=jnp....  79 us
    all_gather x1, waiting for transfers between devices, on_device(): segment = lax.all_gather(chosen, 'tensor', axis=0, tiled=True)  54.8 us
    all_gather x1, waiting for transfers between devices, on_device(): segment = lax.all_gather(norm_rows(middle), 'tensor', axis=0, tiled=True)  49.2 us
    all_gather x1, waiting for transfers between devices, on_device(): segment = lax.all_gather(prefix_cache, 'dp', axis=0, tiled=True)  40.6 us
    scatter-add x1, other arithmetic, on_device(): chosen = jnp.zeros_like(prefix_cache).at[places].add(jnp.where(matches[:,...  28.1 us
    all_gather x1, waiting for transfers between devices, on_device(): segment = lax.all_gather(normed, 'tensor', axis=0, tiled=True)  20.5 us
  transfers between devices with their start and end apart: 6, of which 6 were waited for; matrix products, arithmetic and copies ran while one was open for 10% of the time, Pallas kernels for 0%

commit v1 on v0

--- a/solution.py
+++ b/solution.py
@@ -81,6 +81,20 @@
         weight_one * factor_one + weight_two * factor_two,
         blend_one * factor_one[:, :, None] + blend_two * factor_two[:, :, None],
     )
+
+
+def gather_rows(values, axis):
+    count = lax.axis_size(axis)
+    copies = jnp.broadcast_to(values[None], (count,) + values.shape)
+    received = lax.all_to_all(copies, axis, 0, 0, tiled=True)
+    return received.reshape((count * values.shape[0],) + values.shape[1:])
+
+
+def sum_scatter_rows(values, axis):
+    count = lax.axis_size(axis)
+    parts = values.reshape((count, values.shape[0] // count) + values.shape[1:])
+    received = lax.all_to_all(parts, axis, 0, 0, tiled=True)
+    return jnp.sum(received.astype(jnp.float32), axis=0)
 
 
 def on_device(
@@ -114,8 +128,23 @@
     key_cols = lax.dynamic_slice_in_dim(key_weight, kv_first * HD, kv_width, 1)
     value_cols = lax.dynamic_slice_in_dim(value_weight, kv_first * HD, kv_width, 1)
     projection = jnp.concatenate([query_weight, key_cols, value_cols], axis=1)
+
+    slot_wanted = group_prefix[group_rank]
+    shard_rows = prefix_cache.shape[0]
+    every_slot = lax.all_gather(prefix_cache, "dp", axis=0, tiled=True)
+    chosen = lax.dynamic_slice_in_dim(every_slot, slot_wanted * shard_rows, shard_rows, 0)
+    by_head = chosen.reshape(shard_rows, 2, KVH // local_kv, kv_width)
+    by_head = jnp.transpose(by_head, (2, 0, 1, 3)).reshape(KVH // local_kv, shard_rows, 2 * kv_width)
+    wanted_by = (jnp.arange(tensor_count) * local_heads // head_ratio) // local_kv
+    outgoing = jnp.take(by_head, wanted_by, axis=0)
+    incoming = lax.all_to_all(outgoing, "tensor", 0, 0, tiled=True)
+    seg_rows = tensor_count * shard_rows
+    incoming = incoming.reshape(seg_rows, 2 * kv_width)
+    keys_block = jnp.repeat(incoming[:, :kv_width].reshape(seg_rows, local_kv, HD), repeat_by, axis=1)
+    values_block = jnp.repeat(incoming[:, kv_width:].reshape(seg_rows, local_kv, HD), repeat_by, axis=1)
+
     normed = norm_rows(tokens)
-    segment = lax.all_gather(normed, "tensor", axis=0, tiled=True)
+    segment = gather_rows(normed, "tensor")
     seg_rows = segment.shape[0]
     mapped = jnp.dot(segment, projection, preferred_element_type=jnp.float32)
     query_part = rotate(
@@ -145,33 +174,11 @@
         repeat_by,
         axis=1,
     )
-    slot_wanted = group_prefix[group_rank]
-    shard_rows = prefix_cache.shape[0]
-    segment = lax.all_gather(prefix_cache, "dp", axis=0, tiled=True)
-    seg_rows = segment.shape[0]
-    indices = jnp.arange(seg_rows, dtype=jnp.int32)
-    matches = indices // shard_rows == slot_wanted
-    places = indices % shard_rows
-    chosen = (
-        jnp.zeros_like(prefix_cache)
-        .at[places]
-        .add(jnp.where(matches[:, None], segment, jnp.zeros_like(segment)))
-    )
     start_state = (
         jnp.full((group_tokens, local_heads), NEG_FILL, jnp.float32),
         jnp.zeros((group_tokens, local_heads), jnp.float32),
         jnp.zeros((group_tokens, local_heads, HD), jnp.float32),
     )
-    segment = lax.all_gather(chosen, "tensor", axis=0, tiled=True)
-    seg_rows = segment.shape[0]
-    keys_block = lax.dynamic_slice_in_dim(segment, kv_first * HD, kv_width, 1).reshape(
-        seg_rows, local_kv, HD
-    )
-    values_block = lax.dynamic_slice_in_dim(segment, kv_total + kv_first * HD, kv_width, 1).reshape(
-        seg_rows, local_kv, HD
-    )
-    keys_block = jnp.repeat(keys_block, repeat_by, axis=1)
-    values_block = jnp.repeat(values_block, repeat_by, axis=1)
     prefix_state = merge_states(
         start_state, softmax_block(queries, keys_block, values_block, scaling, None)
     )
@@ -182,23 +189,19 @@
     attended = (
         (blended / weight[:, :, None]).astype(jnp.bfloat16).reshape(group_tokens, query_width)
     )
-    attn_sum = lax.psum_scatter(
+    attn_sum = sum_scatter_rows(
         jnp.dot(attended, out_weight, preferred_element_type=jnp.float32).astype(jnp.bfloat16),
         "tensor",
-        scatter_dimension=0,
-        tiled=True,
-    ).astype(jnp.float32)
+    )
     middle = (tokens.astype(jnp.float32) + attn_sum).astype(jnp.bfloat16)
-    segment = lax.all_gather(norm_rows(middle), "tensor", axis=0, tiled=True)
+    segment = gather_rows(norm_rows(middle), "tensor")
     gate_value = jnp.dot(segment, gate_up_weight[0], preferred_element_type=jnp.float32)
     upward = jnp.dot(segment, gate_up_weight[1], preferred_element_type=jnp.float32)
     hidden = (jax.nn.silu(gate_value) * upward).astype(jnp.bfloat16)
-    ffn_sum = lax.psum_scatter(
+    ffn_sum = sum_scatter_rows(
         jnp.dot(hidden, down_weight, preferred_element_type=jnp.float32).astype(jnp.bfloat16),
         "tensor",
-        scatter_dimension=0,
-        tiled=True,
-    ).astype(jnp.float32)
+    )
     return (middle.astype(jnp.float32) + ffn_sum).astype(jnp.bfloat16)
 
 

time: 401 us -> 206 us (0.51)
  waiting for transfers between devices: 324 us -> 49.8 us
  blocking collectives: 0 us -> 94.5 us
  other arithmetic: 38.2 us -> 7.28 us
  starting transfers between devices: 0.39 us -> 11.5 us
  local copies, waits for them, and re-layouts: 3.13 us -> 11.5 us
    reduce_scatter x2 -> x0, waiting for transfers between devices: 158 us -> none  [the longest x1 79.3 us: on_device(): lax.psum_scatter(jnp.dot(attended, out_weight, preferred_element_type=jnp...]
    all_gather x4 -> x1, waiting for transfers between devices: 165 us -> 36.9 us  [on_device(): every_slot = lax.all_gather(prefix_cache, 'dp', axis=0, tiled=True)]
    all_to_all x0 -> x3, blocking collectives: none -> 94.5 us  [the longest x2 63.4 us: sum_scatter_rows(): received = lax.all_to_all(parts, axis, 0, 0, tiled=True)]
    scatter-add x1 -> x0, other arithmetic: 28.1 us -> none  [on_device(): chosen = jnp.zeros_like(prefix_cache).at[places].add(jnp.where(matches[:,...]
    all_to_all x0 -> x2, waiting for transfers between devices: none -> 12.9 us  [the longest x1 12.9 us: on_device(): incoming = lax.all_to_all(outgoing, 'tensor', 0, 0, tiled=True)]
    all_to_all x0 -> x2, starting transfers between devices: none -> 11.5 us  [the longest x1 5.97 us: on_device(): incoming = lax.all_to_all(outgoing, 'tensor', 0, 0, tiled=True)]
    unnamed x13 -> x20, local copies, waits for them, and re-layouts: 0.3 us -> 4.55 us
  transfers between devices with their start and end apart: 6 -> 3, of which waited for: 6 -> 2; matrix products, arithmetic and copies ran while one was open for 10% -> 7% of each run, Pallas kernels for 0% -> 0%
where the time goes in v1:
time: 206 us; the launch traced here: 204 us
  blocking collectives  94.5 us (46%)
  waiting for transfers between devices  49.8 us (24%)
  matrix products  15.4 us (7%)
  between operations  14.3 us (7%)
  local copies, waits for them, and re-layouts  11.5 us (6%)
  starting transfers between devices  11.5 us (6%)
  other arithmetic  7.28 us (4%)
    all_to_all x2, blocking collectives, sum_scatter_rows(): received = lax.all_to_all(parts, axis, 0, 0, tiled=True)  63.4 us
    all_gather x1, waiting for transfers between devices, on_device(): every_slot = lax.all_gather(prefix_cache, 'dp', axis=0, tiled=True)  36.9 us
    all_to_all x1, blocking collectives, gather_rows(): received = lax.all_to_all(copies, axis, 0, 0, tiled=True)  31.1 us
    all_to_all x1, waiting for transfers between devices, on_device(): incoming = lax.all_to_all(outgoing, 'tensor', 0, 0, tiled=True)  12.9 us
    all_to_all x1, starting transfers between devices, on_device(): incoming = lax.all_to_all(outgoing, 'tensor', 0, 0, tiled=True)  5.97 us
    all_to_all x1, starting transfers between devices, gather_rows(): received = lax.all_to_all(copies, axis, 0, 0, tiled=True)  5.49 us
    dot_general x1, matrix products, on_device(): jnp.dot(hidden, down_weight, preferred_element_type=jnp.float32)  4.97 us
    unnamed x20, local copies, waits for them, and re-layouts  4.55 us
  transfers between devices with their start and end apart: 3, of which 2 were waited for; matrix products, arithmetic and copies ran while one was open for 7% of the time, Pallas kernels for 0%

profile of v1, /device:TPU:0, one launch (start us, length us, event | category | flops | bytes accessed | tf_op | source)
XLA Modules:
  0.0 204.2 jit_solution(2618785324650212779)
XLA Ops:
  6.5 1.9 copy.19
  8.5 1.0 fusion.62
  9.5 1.0 fusion.63
  10.5 1.6 broadcast_in_dim.34
  12.1 5.5 %all-to-all-start.1 = ((bf16[16,32,2048]{2,1,0:T(8,128)(2,1)}), bf16[16,32,2048]{2,1,0:T(8,128)(2,1)}, u32[]{:S(2)}, u32[]{:S(2)}) async-start(bf16[16,32,2048]{2,1,0:T(8,128)(2,1)} %broadcast_in_dim.34), calls=%async_computation.1 | async-start | bytes 4194304 | tf_op jit(solution)/shard_map/all_to_all | solution.py:89
  19.1 1.1 copy.22
  20.4 2.2 %constant_dynamic-slice_fusion = (bf16[2048,64]{1,0:T(8,128)(2,1)S(1)}, bf16[2048,64]{1,0:T(8,128)(2,1)}) fusion(bf16[2048,256]{1,0:T(8,128)(2,1)S(1)} %copy-done.4, s32[]{:T(128)S(6)} %select_n.70, bf16[2048,256]{1,0:T(8,128)(2,1)} %param.15), kind=kLoop, calls=%fused_computation.122 | loop fusion | bytes 1048580 | tf_op jit(solution)/shard_map/dynamic_slice | solution.py:129
  22.7 36.9 %all-gather.2.cloned.1.call-done = bf16[4096,512]{0,1:T(8,128)(2,1)} async-done(((bf16[256,512]{0,1:T(8,128)(2,1)}), bf16[4096,512]{0,1:T(8,128)(2,1)}) %all-gather.2.cloned.1.call-update) | async-done | bytes 4194320 | tf_op jit(solution)/shard_map/all_gather | solution.py:134
  59.5 1.0 constant_dynamic-slice_fusion.2
  61.2 1.2 broadcast_select_fusion
  62.3 6.0 %all-to-all-start = ((bf16[16,256,128]{1,2,0:T(8,128)(2,1)}), bf16[16,256,128]{1,2,0:T(8,128)(2,1)S(1)}, u32[]{:S(2)}, u32[]{:S(2)}) async-start(bf16[16,256,128]{1,2,0:T(8,128)(2,1)} %broadcast_select_fusion), calls=%async_computation | async-start | bytes 2097152 | tf_op jit(solution)/shard_map/all_to_all | solution.py:140
  68.3 3.0 %fusion.40 = f32[512,192]{0,1:T(8,128)S(1)} fusion(bf16[512,2048]{1,0:T(8,128)(2,1)} %bitcast.6, bf16[2048,64]{1,0:T(8,128)(2,1)S(1)} %get-tuple-element.24, bf16[2048,64]{1,0:T(8,128)(2,1)} %get-tuple-element.25, bf16[2048,64]{1,0:T(8,128)(2,1)} %copy.22), kind=kOutput, calls=%fused_computation.36 | convolution fusion | flops 405012480 | bytes 3276800 | tf_op jit(solution)/shard_map/dot_general | solution.py:149
  72.1 1.0 copy-done.1
  73.3 12.9 %all-to-all-done = bf16[16,256,128]{1,2,0:T(8,128)(2,1)S(1)} async-done(((bf16[16,256,128]{1,2,0:T(8,128)(2,1)}), bf16[16,256,128]{1,2,0:T(8,128)(2,1)S(1)}, u32[]{:S(2)}, u32[]{:S(2)}) %all-to-all-start) | async-done | bytes 1048608 | tf_op jit(solution)/shard_map/all_to_all | solution.py:140
  86.8 1.2 multiply_reduce_fusion
  88.1 1.4 fusion.1
  89.5 1.8 fusion.32
  91.4 2.3 %convolution_convert_fusion.1 = bf16[512,2048]{1,0:T(8,128)(2,1)S(1)} fusion(bf16[64,2048]{1,0:T(8,128)(2,1)} %param.17, f32[1,64,512]{2,1,0:T(8,128)S(1)} %fusion.32, f32[512,1,512]{0,2,1:T(8,128)} %copy-done.1, f32[512]{0:T(512)S(1)} %get-tuple-element.22, f32[512,192]{0,1:T(8,128)} %copy-done.3, f32[512]{0:T(512)S(1)} %get-tuple-element.7, ...), kind=kOutput, calls=%fused_computation.11 | convolution fusion | flops 169476096 | bytes 3610624 | tf_op jit(solution)/shard_map/dot_general | solution.py:193
  93.6 31.7 %all_to_all.25 = bf16[16,32,2048]{2,1,0:T(8,128)(2,1)S(1)} all-to-all(bf16[16,32,2048]{2,1,0:T(8,128)(2,1)S(1)} %bitcast.126), channel_id=1, replica_groups=mesh['dp'=16,'tensor'=16] {'tensor'}, dimensions={0} | all-to-all | bytes 4194304 | tf_op jit(solution)/shard_map/all_to_all | solution.py:96
  126.8 31.1 %all_to_all.26 = bf16[16,32,2048]{2,1,0:T(8,128)(2,1)S(1)} all-to-all(bf16[16,32,2048]{2,1,0:T(8,128)(2,1)S(1)} %broadcast_in_dim.38), channel_id=1, replica_groups=mesh['dp'=16,'tensor'=16] {'tensor'}, dimensions={0} | all-to-all | bytes 4194304 | tf_op jit(solution)/shard_map/all_to_all | solution.py:89
  157.9 1.7 fusion.9
  159.6 5.0 %convolution_convert_fusion = bf16[512,2048]{1,0:T(8,128)(2,1)} fusion(bf16[320,2048]{1,0:T(8,128)(2,1)S(1)} %copy-done, bf16[512,2048]{1,0:T(8,128)(2,1)S(1)} %bitcast.129, bf16[2,2048,320]{1,2,0:T(8,128)(2,1)} %param.18, f32[512,320]{0,1:T(8,128)} %fusion.9), kind=kOutput, calls=%fused_computation.10 | convolution fusion | flops 1344208896 | bytes 7471104 | tf_op jit(solution)/shard_map/dot_general | solution.py:202
  164.6 31.7 %all_to_all.27 = bf16[16,32,2048]{2,1,0:T(8,128)(2,1)S(1)} all-to-all(bf16[16,32,2048]{2,1,0:T(8,128)(2,1)} %bitcast.130), channel_id=1, replica_groups=mesh['dp'=16,'tensor'=16] {'tensor'}, dimensions={0} | all-to-all | bytes 4194304 | tf_op jit(solution)/shard_map/all_to_all | solution.py:96
  196.6 0.7 fusion.67
  (45 shorter events, 5.0 us)
Async XLA Ops:
  6.5 153.1 %copy-start = (bf16[320,2048]{1,0:T(8,128)(2,1)S(1)}, bf16[320,2048]{1,0:T(8,128)(2,1)}, u32[]{:S(2)}) copy-start(bf16[320,2048]{1,0:T(8,128)(2,1)} %param.19) | copy-start | bytes 3932164
  6.5 53.0 %all-gather.2.cloned.1.call-start = ((), (), s32[]{:S(2)}) async-start(), calls=%async_computation.5 | async-start | bytes 4456448 | tf_op jit(solution)/shard_map/all_gather | solution.py:134
  12.1 5.5 %copy-start.7 = (s32[16]{0:T(128)S(1)}, s32[16]{0:T(128)}, u32[]{:S(2)}) copy-start(s32[16]{0:T(128)} %param.12) | copy-start | bytes 196
  12.1 6.8 %copy-start.8 = (s32[1,8]{1,0:T(1,128)S(1)}, s32[1,8]{1,0:T(1,128)}, u32[]{:S(2)}) copy-start(s32[1,8]{1,0:T(1,128)} %param.11) | copy-start | bytes 100
  12.1 7.0 %copy-start.5 = (bf16[2048,64]{0,1:T(8,128)(2,1)S(1)}, bf16[2048,64]{0,1:T(8,128)(2,1)}, u32[]{:S(2)}) copy-start(bf16[2048,64]{0,1:T(8,128)(2,1)} %param.14) | copy-start | bytes 786436
  12.1 8.3 %copy-start.4 = (bf16[2048,256]{1,0:T(8,128)(2,1)S(1)}, bf16[2048,256]{1,0:T(8,128)(2,1)}, u32[]{:S(2)}) copy-start(bf16[2048,256]{1,0:T(8,128)(2,1)} %param.16) | copy-start | bytes 3145732
  12.1 50.2 %all-to-all-start.1 = ((bf16[16,32,2048]{2,1,0:T(8,128)(2,1)}), bf16[16,32,2048]{2,1,0:T(8,128)(2,1)}, u32[]{:S(2)}, u32[]{:S(2)}) async-start(bf16[16,32,2048]{2,1,0:T(8,128)(2,1)} %broadcast_in_dim.34), calls=%async_computation.1 | async-start | bytes 4194304 | tf_op jit(solution)/shard_map/all_to_all | solution.py:89
  62.3 23.8 %all-to-all-start = ((bf16[16,256,128]{1,2,0:T(8,128)(2,1)}), bf16[16,256,128]{1,2,0:T(8,128)(2,1)S(1)}, u32[]{:S(2)}, u32[]{:S(2)}) async-start(bf16[16,256,128]{1,2,0:T(8,128)(2,1)} %broadcast_select_fusion), calls=%async_computation | async-start | bytes 2097152 | tf_op jit(solution)/shard_map/all_to_all | solution.py:140
  71.3 0.8 copy-start.3
  72.0 1.0 copy-start.1
  125.3 0.9 copy-start.2
  126.7 31.1 %copy-start.6 = (bf16[2,2048,320]{1,2,0:T(8,128)(2,1)S(1)}, bf16[2,2048,320]{1,2,0:T(8,128)(2,1)}, u32[]{:S(2)}) copy-start(bf16[2,2048,320]{1,2,0:T(8,128)(2,1)} %param.18) | copy-start | bytes 7864324
Sparse Core Ops, SparseCore 0:
  9.1 50.3 all-gather.1

commit v2 on v1

--- a/solution.py
+++ b/solution.py
@@ -132,6 +132,8 @@
     slot_wanted = group_prefix[group_rank]
     shard_rows = prefix_cache.shape[0]
     every_slot = lax.all_gather(prefix_cache, "dp", axis=0, tiled=True)
+    every_slot, out_rows = lax.optimization_barrier((every_slot, out_weight))
+    out_full = lax.all_gather(out_rows, "tensor", axis=0, tiled=True)
     chosen = lax.dynamic_slice_in_dim(every_slot, slot_wanted * shard_rows, shard_rows, 0)
     by_head = chosen.reshape(shard_rows, 2, KVH // local_kv, kv_width)
     by_head = jnp.transpose(by_head, (2, 0, 1, 3)).reshape(KVH // local_kv, shard_rows, 2 * kv_width)
@@ -186,13 +188,18 @@
     allowed = (request[:, None] == request[None, :]) & (indices[None, :] <= indices[:, None])
     suffix_state = softmax_block(queries, own_keys, own_values, scaling, allowed[:, None, :])
     top_score, weight, blended = merge_states(prefix_state, suffix_state)
-    attended = (
-        (blended / weight[:, :, None]).astype(jnp.bfloat16).reshape(group_tokens, query_width)
-    )
-    attn_sum = sum_scatter_rows(
-        jnp.dot(attended, out_weight, preferred_element_type=jnp.float32).astype(jnp.bfloat16),
-        "tensor",
-    )
+    attended = (blended / weight[:, :, None]).astype(jnp.bfloat16)
+    attended = lax.all_to_all(
+        attended.reshape(tensor_count, row_count, query_width), "tensor", 0, 0, tiled=True
+    )
+    feature_groups = out_full.shape[0] // query_width
+    partials = jnp.einsum(
+        "grk,gkd->grd",
+        attended,
+        out_full.reshape(feature_groups, query_width, out_full.shape[1]),
+        preferred_element_type=jnp.float32,
+    ).astype(jnp.bfloat16)
+    attn_sum = jnp.sum(partials.astype(jnp.float32), axis=0)
     middle = (tokens.astype(jnp.float32) + attn_sum).astype(jnp.bfloat16)
     segment = gather_rows(norm_rows(middle), "tensor")
     gate_value = jnp.dot(segment, gate_up_weight[0], preferred_element_type=jnp.float32)

time: 206 us -> 232 us (1.13)
  waiting for transfers between devices: 49.8 us -> 102 us
  blocking collectives: 94.5 us -> 67.1 us
    all_to_all x2 -> x1, blocking collectives: 63.4 us -> 27.3 us  [sum_scatter_rows(): received = lax.all_to_all(parts, axis, 0, 0, tiled=True)]
    all_to_all x1, waiting for transfers between devices: 0.01 us -> 29.1 us  [gather_rows(): received = lax.all_to_all(copies, axis, 0, 0, tiled=True)]
    all_gather x1, waiting for transfers between devices: 36.9 us -> 51.3 us  [on_device(): every_slot = lax.all_gather(prefix_cache, 'dp', axis=0, tiled=True)]
    all_to_all x0 -> x1, blocking collectives: none -> 11.4 us  [on_device(): lax.all_to_all(attended.reshape(tensor_count, row_count, query_width), 't...]
    all_to_all x1, waiting for transfers between devices: 12.9 us -> 22 us  [on_device(): incoming = lax.all_to_all(outgoing, 'tensor', 0, 0, tiled=True)]
    all_to_all x1, blocking collectives: 31.1 us -> 28.5 us  [gather_rows(): received = lax.all_to_all(copies, axis, 0, 0, tiled=True)]
  transfers between devices with their start and end apart: 3 -> 4, of which waited for: 2 -> 3; matrix products, arithmetic and copies ran while one was open for 7% -> 9% of each run, Pallas kernels for 0% -> 0%
where the time goes in v2:
time: 232 us; the launch traced here: 230 us
  waiting for transfers between devices  102 us (44%)
  blocking collectives  67.1 us (29%)
  matrix products  17.6 us (8%)
  between operations  14.3 us (6%)
  local copies, waits for them, and re-layouts  11.3 us (5%)
  starting transfers between devices  9.94 us (4%)
  other arithmetic  6.89 us (3%)
    all_gather x1, waiting for transfers between devices, on_device(): every_slot = lax.all_gather(prefix_cache, 'dp', axis=0, tiled=True)  51.3 us
    all_to_all x1, waiting for transfers between devices, gather_rows(): received = lax.all_to_all(copies, axis, 0, 0, tiled=True)  29.1 us
    all_to_all x1, blocking collectives, gather_rows(): received = lax.all_to_all(copies, axis, 0, 0, tiled=True)  28.5 us
    all_to_all x1, blocking collectives, sum_scatter_rows(): received = lax.all_to_all(parts, axis, 0, 0, tiled=True)  27.3 us
    all_to_all x1, waiting for transfers between devices, on_device(): incoming = lax.all_to_all(outgoing, 'tensor', 0, 0, tiled=True)  22 us
    all_to_all x1, blocking collectives, on_device(): lax.all_to_all(attended.reshape(tensor_count, row_count, query_width), 't...  11.4 us
    all_to_all x1, starting transfers between devices, gather_rows(): received = lax.all_to_all(copies, axis, 0, 0, tiled=True)  6.24 us
    dot_general x1, matrix products, on_device(): jnp.dot(hidden, down_weight, preferred_element_type=jnp.float32)  4.97 us
  transfers between devices with their start and end apart: 4, of which 3 were waited for; matrix products, arithmetic and copies ran while one was open for 9% of the time, Pallas kernels for 0%

profile of v2, /device:TPU:0, one launch (start us, length us, event | category | flops | bytes accessed | tf_op | source)
XLA Modules:
  0.0 229.5 jit_solution(2884264637171825472)
XLA Ops:
  6.5 1.9 copy.22
  8.5 51.3 %all-gather.3.cloned.1.call-done = bf16[4096,512]{0,1:T(8,128)(2,1)} async-done(((bf16[256,512]{0,1:T(8,128)(2,1)}), bf16[4096,512]{0,1:T(8,128)(2,1)}) %all-gather.3.cloned.1.call-update) | async-done | bytes 4194320 | tf_op jit(solution)/shard_map/all_gather | solution.py:134
  59.8 1.0 fusion.60
  60.8 1.0 fusion.61
  61.8 1.6 broadcast_in_dim.34
  63.4 6.2 %all-to-all-start.1 = ((bf16[16,32,2048]{2,1,0:T(8,128)(2,1)}), bf16[16,32,2048]{2,1,0:T(8,128)(2,1)}, u32[]{:S(2)}, u32[]{:S(2)}) async-start(bf16[16,32,2048]{2,1,0:T(8,128)(2,1)} %broadcast_in_dim.34), calls=%async_computation.1 | async-start | bytes 4194304 | tf_op jit(solution)/shard_map/all_to_all | solution.py:89
  69.7 1.1 copy.25
  72.4 2.2 constant_dynamic-slice_fusion
  76.3 1.1 broadcast_select_fusion
  77.4 29.1 %all-to-all-done.1 = bf16[16,32,2048]{2,1,0:T(8,128)(2,1)} async-done(((bf16[16,32,2048]{2,1,0:T(8,128)(2,1)}), bf16[16,32,2048]{2,1,0:T(8,128)(2,1)}, u32[]{:S(2)}, u32[]{:S(2)}) %all-to-all-start.1) | async-done | bytes 2097184 | tf_op jit(solution)/shard_map/all_to_all | solution.py:89
  106.5 3.7 %all-to-all-start = ((bf16[16,256,128]{1,2,0:T(8,128)(2,1)}), bf16[16,256,128]{1,2,0:T(8,128)(2,1)S(1)}, u32[]{:S(2)}, u32[]{:S(2)}) async-start(bf16[16,256,128]{1,2,0:T(8,128)(2,1)} %broadcast_select_fusion), calls=%async_computation | async-start | bytes 2097152 | tf_op jit(solution)/shard_map/all_to_all | solution.py:142
  110.2 3.3 %fusion.40 = f32[512,192]{0,1:T(8,128)S(1)} fusion(bf16[512,2048]{1,0:T(8,128)(2,1)} %bitcast.6, bf16[2048,64]{1,0:T(8,128)(2,1)S(1)} %get-tuple-element.28, bf16[2048,64]{1,0:T(8,128)(2,1)} %get-tuple-element.29, bf16[2048,64]{1,0:T(8,128)(2,1)} %copy.25), kind=kOutput, calls=%fused_computation.36 | convolution fusion | flops 405012480 | bytes 3276800 | tf_op jit(solution)/shard_map/dot_general | solution.py:151
  114.3 1.0 copy-done.1
  115.5 22.0 %all-to-all-done = bf16[16,256,128]{1,2,0:T(8,128)(2,1)S(1)} async-done(((bf16[16,256,128]{1,2,0:T(8,128)(2,1)}), bf16[16,256,128]{1,2,0:T(8,128)(2,1)S(1)}, u32[]{:S(2)}, u32[]{:S(2)}) %all-to-all-start) | async-done | bytes 1048608 | tf_op jit(solution)/shard_map/all_to_all | solution.py:142
  138.1 1.2 multiply_reduce_fusion
  139.4 1.4 fusion.1
  140.9 1.8 fusion.32
  142.7 1.2 fusion.36
  144.2 11.4 %all_to_all.25 = bf16[16,2,1024]{2,1,0:T(2,128)(2,1)S(1)} all-to-all(bf16[16,2,1024]{2,1,0:T(2,128)(2,1)S(1)} %reshape.413), channel_id=1, replica_groups=mesh['dp'=16,'tensor'=16] {'tensor'}, dimensions={0} | all-to-all | bytes 131072 | tf_op jit(solution)/shard_map/all_to_all | solution.py:192
  155.7 2.9 %convert_reduce_fusion.1 = f32[32,2048]{1,0:T(8,128)S(1)} fusion(bf16[16,32,64]{2,1,0:T(8,128)(2,1)S(1)} %reshape.414, bf16[16,64,2048]{2,1,0:T(8,128)(2,1)} %bitcast.122), kind=kOutput, calls=%fused_computation.8 | convolution fusion | flops 137297920 | bytes 4521984 | tf_op jit(solution)/shard_map/grk,gkd->grd/dot_general | solution.py:196
  159.1 28.5 %all_to_all.26 = bf16[16,32,2048]{2,1,0:T(8,128)(2,1)S(1)} all-to-all(bf16[16,32,2048]{2,1,0:T(8,128)(2,1)S(1)} %broadcast_in_dim.38), channel_id=1, replica_groups=mesh['dp'=16,'tensor'=16] {'tensor'}, dimensions={0} | all-to-all | bytes 4194304 | tf_op jit(solution)/shard_map/all_to_all | solution.py:89
  187.7 1.7 fusion.9
  189.4 5.0 %convolution_convert_fusion = bf16[512,2048]{1,0:T(8,128)(2,1)} fusion(bf16[320,2048]{1,0:T(8,128)(2,1)S(1)} %copy-done, bf16[512,2048]{1,0:T(8,128)(2,1)S(1)} %bitcast.124, bf16[2,2048,320]{1,2,0:T(8,128)(2,1)} %param.18, f32[512,320]{0,1:T(8,128)} %fusion.9), kind=kOutput, calls=%fused_computation.10 | convolution fusion | flops 1344208896 | bytes 7471104 | tf_op jit(solution)/shard_map/dot_general | solution.py:209
  194.3 27.3 %all_to_all.27 = bf16[16,32,2048]{2,1,0:T(8,128)(2,1)S(1)} all-to-all(bf16[16,32,2048]{2,1,0:T(8,128)(2,1)} %bitcast.125), channel_id=1, replica_groups=mesh['dp'=16,'tensor'=16] {'tensor'}, dimensions={0} | all-to-all | bytes 4194304 | tf_op jit(solution)/shard_map/all_to_all | solution.py:96
  (53 shorter events, 6.3 us)
Async XLA Ops:
  6.5 182.8 %copy-start = (bf16[320,2048]{1,0:T(8,128)(2,1)S(1)}, bf16[320,2048]{1,0:T(8,128)(2,1)}, u32[]{:S(2)}) copy-start(bf16[320,2048]{1,0:T(8,128)(2,1)} %param.19) | copy-start | bytes 3932164
  6.5 53.2 %all-gather.3.cloned.1.call-start = ((), (), s32[]{:S(2)}) async-start(), calls=%async_computation.5 | async-start | bytes 4456448 | tf_op jit(solution)/shard_map/all_gather | solution.py:134
  8.4 147.2 %all-gather.5.cloned.1.call-start = ((), (), s32[]{:S(2)}) async-start(), calls=%async_computation.6 | async-start | bytes 4456448 | tf_op jit(solution)/shard_map/all_gather | solution.py:136
  63.4 6.3 %copy-start.6 = (bf16[2048,64]{0,1:T(8,128)(2,1)S(1)}, bf16[2048,64]{0,1:T(8,128)(2,1)}, u32[]{:S(2)}) copy-start(bf16[2048,64]{0,1:T(8,128)(2,1)} %param.14) | copy-start | bytes 786436
  63.4 7.3 %copy-start.9 = (s32[1,8]{1,0:T(1,128)S(1)}, s32[1,8]{1,0:T(1,128)}, u32[]{:S(2)}) copy-start(s32[1,8]{1,0:T(1,128)} %param.11) | copy-start | bytes 100
  63.4 7.5 %copy-start.8 = (s32[16]{0:T(128)S(1)}, s32[16]{0:T(128)}, u32[]{:S(2)}) copy-start(s32[16]{0:T(128)} %param.12) | copy-start | bytes 196
  63.4 9.0 %copy-start.5 = (bf16[2048,256]{1,0:T(8,128)(2,1)S(1)}, bf16[2048,256]{1,0:T(8,128)(2,1)}, u32[]{:S(2)}) copy-start(bf16[2048,256]{1,0:T(8,128)(2,1)} %param.16) | copy-start | bytes 3145732
  63.4 43.1 %all-to-all-start.1 = ((bf16[16,32,2048]{2,1,0:T(8,128)(2,1)}), bf16[16,32,2048]{2,1,0:T(8,128)(2,1)}, u32[]{:S(2)}, u32[]{:S(2)}) async-start(bf16[16,32,2048]{2,1,0:T(8,128)(2,1)} %broadcast_in_dim.34), calls=%async_computation.1 | async-start | bytes 4194304 | tf_op jit(solution)/shard_map/all_to_all | solution.py:89
  106.5 31.0 %all-to-all-start = ((bf16[16,256,128]{1,2,0:T(8,128)(2,1)}), bf16[16,256,128]{1,2,0:T(8,128)(2,1)S(1)}, u32[]{:S(2)}, u32[]{:S(2)}) async-start(bf16[16,256,128]{1,2,0:T(8,128)(2,1)} %broadcast_select_fusion), calls=%async_computation | async-start | bytes 2097152 | tf_op jit(solution)/shard_map/all_to_all | solution.py:142
  113.5 0.8 copy-start.4
  114.3 1.0 copy-start.1
  140.8 1.8 copy-start.2
  143.9 14.7 %copy-start.3 = (bf16[32,2048]{1,0:T(8,128)(2,1)S(1)}, bf16[32,2048]{1,0:T(8,128)(2,1)}, u32[]{:S(2)}) copy-start(bf16[32,2048]{1,0:T(8,128)(2,1)} %param.10) | copy-start | bytes 393220
  159.1 28.5 %copy-start.7 = (bf16[2,2048,320]{1,2,0:T(8,128)(2,1)S(1)}, bf16[2,2048,320]{1,2,0:T(8,128)(2,1)}, u32[]{:S(2)}) copy-start(bf16[2,2048,320]{1,2,0:T(8,128)(2,1)} %param.18) | copy-start | bytes 7864324
Sparse Core Ops, SparseCore 0:
  9.1 50.5 all-gather.2
  62.2 79.5 all-gather.4

commit v3 on v2

--- a/solution.py
+++ b/solution.py
@@ -95,6 +95,35 @@
     parts = values.reshape((count, values.shape[0] // count) + values.shape[1:])
     received = lax.all_to_all(parts, axis, 0, 0, tiled=True)
     return jnp.sum(received.astype(jnp.float32), axis=0)
+
+
+CORES = 2
+
+
+def fetch_slot(prefix_cache, group_prefix, group_rank):
+    group_count = lax.axis_size("dp")
+    chips = group_count // CORES
+    chip = group_rank // CORES
+    core = group_rank % CORES
+    onward = [(i, (i + CORES) % group_count) for i in range(group_count)]
+    backward = [(i, (i - CORES) % group_count) for i in range(group_count)]
+    held = [None] * chips
+    held[0] = prefix_cache
+    ahead = prefix_cache
+    behind = prefix_cache
+    for step in range(1, chips // 2 + 1):
+        ahead = lax.ppermute(ahead, "dp", onward)
+        held[(chips - step) % chips] = ahead
+        if step < chips - step:
+            behind = lax.ppermute(behind, "dp", backward)
+            held[step] = behind
+    held = jnp.stack(held)
+    slot_wanted = group_prefix[group_rank]
+    partner_slot = group_prefix[group_rank ^ 1]
+    mine = lax.dynamic_index_in_dim(held, (slot_wanted // CORES - chip) % chips, 0, keepdims=False)
+    theirs = lax.dynamic_index_in_dim(held, (partner_slot // CORES - chip) % chips, 0, keepdims=False)
+    swapped = lax.ppermute(theirs, "dp", [(i, i ^ 1) for i in range(group_count)])
+    return jnp.where(slot_wanted % CORES == core, mine, swapped)
 
 
 def on_device(
@@ -129,12 +158,9 @@
     value_cols = lax.dynamic_slice_in_dim(value_weight, kv_first * HD, kv_width, 1)
     projection = jnp.concatenate([query_weight, key_cols, value_cols], axis=1)
 
-    slot_wanted = group_prefix[group_rank]
     shard_rows = prefix_cache.shape[0]
-    every_slot = lax.all_gather(prefix_cache, "dp", axis=0, tiled=True)
-    every_slot, out_rows = lax.optimization_barrier((every_slot, out_weight))
-    out_full = lax.all_gather(out_rows, "tensor", axis=0, tiled=True)
-    chosen = lax.dynamic_slice_in_dim(every_slot, slot_wanted * shard_rows, shard_rows, 0)
+    chosen = fetch_slot(prefix_cache, group_prefix, group_rank)
+    out_full = lax.all_gather(out_weight, "tensor", axis=0, tiled=True)
     by_head = chosen.reshape(shard_rows, 2, KVH // local_kv, kv_width)
     by_head = jnp.transpose(by_head, (2, 0, 1, 3)).reshape(KVH // local_kv, shard_rows, 2 * kv_width)
     wanted_by = (jnp.arange(tensor_count) * local_heads // head_ratio) // local_kv

time: 232 us -> 193 us (0.83)
  waiting for transfers between devices: 102 us -> 34.5 us
  starting transfers between devices: 9.94 us -> 25 us
  blocking collectives: 67.1 us -> 72.8 us
  between operations: 14.3 us -> 19.1 us
  local copies, waits for them, and re-layouts: 11.3 us -> 15.7 us
    all_gather x2 -> x1, waiting for transfers between devices: 51.3 us -> 0.02 us  [on_device(): out_full = lax.all_gather(out_weight, 'tensor', axis=0, tiled=True)]
    all_to_all x1, waiting for transfers between devices: 29.1 us -> 0.01 us  [gather_rows(): received = lax.all_to_all(copies, axis, 0, 0, tiled=True)]
    ppermute x0 -> x8, waiting for transfers between devices: none -> 11.4 us  [the longest x4 8.93 us: fetch_slot(): ahead = lax.ppermute(ahead, 'dp', onward)]
    ppermute x0 -> x8, starting transfers between devices: none -> 10.9 us  [the longest x3 10.7 us: fetch_slot(): behind = lax.ppermute(behind, 'dp', backward)]
    all_to_all x1, starting transfers between devices: 3.65 us -> 6.89 us  [on_device(): incoming = lax.all_to_all(outgoing, 'tensor', 0, 0, tiled=True)]
    unnamed x24 -> x30, local copies, waits for them, and re-layouts: 4.26 us -> 7.37 us
    all_to_all x1, blocking collectives: 28.5 us -> 31.5 us  [gather_rows(): received = lax.all_to_all(copies, axis, 0, 0, tiled=True)]
    all_to_all x1, blocking collectives: 27.3 us -> 30 us  [sum_scatter_rows(): received = lax.all_to_all(parts, axis, 0, 0, tiled=True)]
  transfers between devices with their start and end apart: 4 -> 11, of which waited for: 3 -> 4; matrix products, arithmetic and copies ran while one was open for 9% -> 15% of each run, Pallas kernels for 0% -> 0%
where the time goes in v3:
time: 193 us; the launch traced here: 191 us
  blocking collectives  72.8 us (38%)
  waiting for transfers between devices  34.5 us (18%)
  starting transfers between devices  25 us (13%)
  between operations  19.1 us (10%)
  matrix products  17.3 us (9%)
  local copies, waits for them, and re-layouts  15.7 us (8%)
  other arithmetic  7 us (4%)
    all_to_all x1, blocking collectives, gather_rows(): received = lax.all_to_all(copies, axis, 0, 0, tiled=True)  31.5 us
    all_to_all x1, blocking collectives, sum_scatter_rows(): received = lax.all_to_all(parts, axis, 0, 0, tiled=True)  30 us
    all_to_all x1, waiting for transfers between devices, on_device(): incoming = lax.all_to_all(outgoing, 'tensor', 0, 0, tiled=True)  23.1 us
    all_to_all x1, blocking collectives, on_device(): lax.all_to_all(attended.reshape(tensor_count, row_count, query_width), 't...  11.3 us
    ppermute x3, starting transfers between devices, fetch_slot(): behind = lax.ppermute(behind, 'dp', backward)  10.7 us
    ppermute x4, waiting for transfers between devices, fetch_slot(): ahead = lax.ppermute(ahead, 'dp', onward)  8.93 us
    unnamed x30, local copies, waits for them, and re-layouts  7.37 us
    all_to_all x1, starting transfers between devices, gather_rows(): received = lax.all_to_all(copies, axis, 0, 0, tiled=True)  7.22 us
  transfers between devices with their start and end apart: 11, of which 4 were waited for; matrix products, arithmetic and copies ran while one was open for 15% of the time, Pallas kernels for 0%

profile of v3, /device:TPU:0, one launch (start us, length us, event | category | flops | bytes accessed | tf_op | source)
XLA Modules:
  0.0 191.4 jit_solution(5153805070379291747)
XLA Ops:
  6.5 4.1 %collective-permute-start = (bf16[256,512]{1,0:T(8,128)(2,1)}, bf16[256,512]{1,0:T(8,128)(2,1)S(1)}, u32[]{:S(2)}, u32[]{:S(2)}) collective-permute-start(bf16[256,512]{1,0:T(8,128)(2,1)} %param.13), channel_id=1, source_target_pairs={{0,224},{16,240},{32,0},{48,16},{64,32},{80,48},{96,64},{112,80},{... | collective-permute-start | bytes 786440 | tf_op jit(solution)/shard_map/ppermute | solution.py:118
  12.7 1.6 broadcast_in_dim.34
  14.3 7.2 %all-to-all-start.1 = ((bf16[16,32,2048]{2,1,0:T(8,128)(2,1)}), bf16[16,32,2048]{2,1,0:T(8,128)(2,1)}, u32[]{:S(2)}, u32[]{:S(2)}) async-start(bf16[16,32,2048]{2,1,0:T(8,128)(2,1)} %broadcast_in_dim.34), calls=%async_computation.1 | async-start | bytes 4194304 | tf_op jit(solution)/shard_map/all_to_all | solution.py:89
  22.7 3.3 %collective-permute-start.1 = (bf16[256,512]{1,0:T(8,128)(2,1)S(1)}, bf16[256,512]{1,0:T(8,128)(2,1)S(1)}, u32[]{:S(2)}, u32[]{:S(2)}) collective-permute-start(bf16[256,512]{1,0:T(8,128)(2,1)S(1)} %collective-permute-done), channel_id=1, source_target_pairs={{0,224},{16,240},{32,0},{48,16},{64,32},{80,48},{96,64},{112,80},{... | collective-permute-start | bytes 786440 | tf_op jit(solution)/shard_map/ppermute | solution.py:118
  26.1 5.3 %collective-permute-done.4 = bf16[256,512]{1,0:T(8,128)(2,1)S(1)} collective-permute-done((bf16[256,512]{1,0:T(8,128)(2,1)S(1)}, bf16[256,512]{1,0:T(8,128)(2,1)S(1)}, u32[]{:S(2)}, u32[]{:S(2)}) %collective-permute-start.4) | collective-permute-done | bytes 262176 | tf_op jit(solution)/shard_map/ppermute | solution.py:115
  37.4 3.3 %collective-permute-start.2 = (bf16[256,512]{1,0:T(8,128)(2,1)S(1)}, bf16[256,512]{1,0:T(8,128)(2,1)S(1)}, u32[]{:S(2)}, u32[]{:S(2)}) collective-permute-start(bf16[256,512]{1,0:T(8,128)(2,1)S(1)} %collective-permute-done.1), channel_id=1, source_target_pairs={{0,224},{16,240},{32,0},{48,16},{64,32},{80,48},{96,64},{112,80},{... | collective-permute-start | bytes 786440 | tf_op jit(solution)/shard_map/ppermute | solution.py:118
  42.2 2.4 %collective-permute-done.2 = bf16[256,512]{1,0:T(8,128)(2,1)S(1)} collective-permute-done((bf16[256,512]{1,0:T(8,128)(2,1)S(1)}, bf16[256,512]{1,0:T(8,128)(2,1)S(1)}, u32[]{:S(2)}, u32[]{:S(2)}) %collective-permute-start.2) | collective-permute-done | bytes 262176 | tf_op jit(solution)/shard_map/ppermute | solution.py:118
  45.4 3.7 %collective-permute-done.6 = bf16[256,512]{1,0:T(8,128)(2,1)S(1)} collective-permute-done((bf16[256,512]{1,0:T(8,128)(2,1)S(1)}, bf16[256,512]{1,0:T(8,128)(2,1)S(1)}, u32[]{:S(2)}, u32[]{:S(2)}) %collective-permute-start.6) | collective-permute-done | bytes 262176 | tf_op jit(solution)/shard_map/ppermute | solution.py:115
  51.9 1.1 constant_dynamic-slice_fusion.3
  54.3 2.3 %constant_dynamic-slice_fusion = (bf16[2048,64]{1,0:T(8,128)(2,1)S(1)}, bf16[2048,64]{1,0:T(8,128)(2,1)}) fusion(bf16[2048,256]{1,0:T(8,128)(2,1)} %param.16, s32[]{:T(128)S(6)} %select_n.123, bf16[2048,256]{1,0:T(8,128)(2,1)} %param.15), kind=kLoop, calls=%fused_computation.126 | loop fusion | bytes 1048580 | tf_op jit(solution)/shard_map/dynamic_slice | solution.py:158
  57.5 1.2 broadcast_select_fusion
  58.7 6.9 %all-to-all-start = ((bf16[16,256,128]{1,2,0:T(8,128)(2,1)}), bf16[16,256,128]{1,2,0:T(8,128)(2,1)S(1)}, u32[]{:S(2)}, u32[]{:S(2)}) async-start(bf16[16,256,128]{1,2,0:T(8,128)(2,1)} %broadcast_select_fusion), calls=%async_computation | async-start | bytes 2097152 | tf_op jit(solution)/shard_map/all_to_all | solution.py:168
  65.6 3.0 %fusion.40 = f32[512,192]{0,1:T(8,128)S(1)} fusion(bf16[512,2048]{1,0:T(8,128)(2,1)} %bitcast.17, bf16[2048,64]{1,0:T(8,128)(2,1)S(1)} %get-tuple-element.28, bf16[2048,64]{1,0:T(8,128)(2,1)} %get-tuple-element.29, bf16[2048,64]{1,0:T(8,128)(2,1)} %copy.28), kind=kOutput, calls=%fused_computation.36 | convolution fusion | flops 405012480 | bytes 3276800 | tf_op jit(solution)/shard_map/dot_general | solution.py:177
  70.5 23.1 %all-to-all-done = bf16[16,256,128]{1,2,0:T(8,128)(2,1)S(1)} async-done(((bf16[16,256,128]{1,2,0:T(8,128)(2,1)}), bf16[16,256,128]{1,2,0:T(8,128)(2,1)S(1)}, u32[]{:S(2)}, u32[]{:S(2)}) %all-to-all-start) | async-done | bytes 1048608 | tf_op jit(solution)/shard_map/all_to_all | solution.py:168
  94.3 1.2 multiply_reduce_fusion
  95.5 1.4 fusion.1
  97.0 1.8 fusion.32
  98.8 1.2 fusion.36
  100.3 11.3 %all_to_all.25 = bf16[16,2,1024]{2,1,0:T(2,128)(2,1)S(1)} all-to-all(bf16[16,2,1024]{2,1,0:T(2,128)(2,1)S(1)} %reshape.411), channel_id=1, replica_groups=mesh['dp'=16,'tensor'=16] {'tensor'}, dimensions={0} | all-to-all | bytes 131072 | tf_op jit(solution)/shard_map/all_to_all | solution.py:218
  111.8 2.9 %convert_reduce_fusion.1 = f32[32,2048]{1,0:T(8,128)S(1)} fusion(bf16[16,32,64]{2,1,0:T(8,128)(2,1)S(1)} %reshape.412, bf16[16,64,2048]{2,1,0:T(8,128)(2,1)} %bitcast.142), kind=kOutput, calls=%fused_computation.8 | convolution fusion | flops 137297920 | bytes 4521984 | tf_op jit(solution)/shard_map/grk,gkd->grd/dot_general | solution.py:222
  115.3 31.5 %all_to_all.26 = bf16[16,32,2048]{2,1,0:T(8,128)(2,1)S(1)} all-to-all(bf16[16,32,2048]{2,1,0:T(8,128)(2,1)S(1)} %broadcast_in_dim.38), channel_id=1, replica_groups=mesh['dp'=16,'tensor'=16] {'tensor'}, dimensions={0} | all-to-all | bytes 4194304 | tf_op jit(solution)/shard_map/all_to_all | solution.py:89
  146.8 1.7 fusion.9
  148.5 5.0 %convolution_convert_fusion = bf16[512,2048]{1,0:T(8,128)(2,1)} fusion(bf16[320,2048]{1,0:T(8,128)(2,1)S(1)} %copy-done, bf16[512,2048]{1,0:T(8,128)(2,1)S(1)} %bitcast.144, bf16[2,2048,320]{1,2,0:T(8,128)(2,1)} %param.18, f32[512,320]{0,1:T(8,128)} %fusion.9), kind=kOutput, calls=%fused_computation.10 | convolution fusion | flops 1344208896 | bytes 7471104 | tf_op jit(solution)/shard_map/dot_general | solution.py:235
  153.5 30.0 %all_to_all.27 = bf16[16,32,2048]{2,1,0:T(8,128)(2,1)S(1)} all-to-all(bf16[16,32,2048]{2,1,0:T(8,128)(2,1)} %bitcast.145), channel_id=1, replica_groups=mesh['dp'=16,'tensor'=16] {'tensor'}, dimensions={0} | all-to-all | bytes 4194304 | tf_op jit(solution)/shard_map/all_to_all | solution.py:96
  (76 shorter events, 15.7 us)
Async XLA Ops:
  6.5 142.0 %copy-start = (bf16[320,2048]{1,0:T(8,128)(2,1)S(1)}, bf16[320,2048]{1,0:T(8,128)(2,1)}, u32[]{:S(2)}) copy-start(bf16[320,2048]{1,0:T(8,128)(2,1)} %param.19) | copy-start | bytes 3932164
  6.5 105.2 %all-gather.2.cloned.1.call-start = ((), (), s32[]{:S(2)}) async-start(), calls=%async_computation.5 | async-start | bytes 4456448 | tf_op jit(solution)/shard_map/all_gather | solution.py:163
  6.5 16.2 %collective-permute-start = (bf16[256,512]{1,0:T(8,128)(2,1)}, bf16[256,512]{1,0:T(8,128)(2,1)S(1)}, u32[]{:S(2)}, u32[]{:S(2)}) collective-permute-start(bf16[256,512]{1,0:T(8,128)(2,1)} %param.13), channel_id=1, source_target_pairs={{0,224},{16,240},{32,0},{48,16},{64,32},{80,48},{96,64},{112,80},{... | collective-permute-start | bytes 786440 | tf_op jit(solution)/shard_map/ppermute | solution.py:118
  10.7 11.9 %collective-permute-start.3 = (bf16[256,512]{1,0:T(8,128)(2,1)}, bf16[256,512]{1,0:T(8,128)(2,1)S(1)}, u32[]{:S(2)}, u32[]{:S(2)}) collective-permute-start(bf16[256,512]{1,0:T(8,128)(2,1)} %param.13), channel_id=1, source_target_pairs={{0,32},{16,48},{32,64},{48,80},{64,96},{80,112},{96,128},{112,144}... | collective-permute-start | bytes 786440 | tf_op jit(solution)/shard_map/ppermute | solution.py:115
  14.3 7.2 %copy-start.9 = (s32[1,8]{1,0:T(1,128)S(1)}, s32[1,8]{1,0:T(1,128)}, u32[]{:S(2)}) copy-start(s32[1,8]{1,0:T(1,128)} %param.11) | copy-start | bytes 100
  14.3 7.4 %copy-start.6 = (bf16[256,512]{1,0:T(8,128)(2,1)S(1)}, bf16[256,512]{1,0:T(8,128)(2,1)}, u32[]{:S(2)}) copy-start(bf16[256,512]{1,0:T(8,128)(2,1)} %param.13) | copy-start | bytes 786436
  14.3 17.1 %copy-start.7 = (s32[16]{0:T(128)S(1)}, s32[16]{0:T(128)}, u32[]{:S(2)}) copy-start(s32[16]{0:T(128)} %param.12) | copy-start | bytes 196
  14.3 44.3 %all-to-all-start.1 = ((bf16[16,32,2048]{2,1,0:T(8,128)(2,1)}), bf16[16,32,2048]{2,1,0:T(8,128)(2,1)}, u32[]{:S(2)}, u32[]{:S(2)}) async-start(bf16[16,32,2048]{2,1,0:T(8,128)(2,1)} %broadcast_in_dim.34), calls=%async_computation.1 | async-start | bytes 4194304 | tf_op jit(solution)/shard_map/all_to_all | solution.py:89
  22.6 8.8 %collective-permute-start.4 = (bf16[256,512]{1,0:T(8,128)(2,1)S(1)}, bf16[256,512]{1,0:T(8,128)(2,1)S(1)}, u32[]{:S(2)}, u32[]{:S(2)}) collective-permute-start(bf16[256,512]{1,0:T(8,128)(2,1)S(1)} %collective-permute-done.3), channel_id=1, source_target_pairs={{0,32},{16,48},{32,64},{48,80},{64,96},{80,112},{96,128},{112,144}... | collective-permute-start | bytes 786440 | tf_op jit(solution)/shard_map/ppermute | solution.py:115
  22.7 14.7 %collective-permute-start.1 = (bf16[256,512]{1,0:T(8,128)(2,1)S(1)}, bf16[256,512]{1,0:T(8,128)(2,1)S(1)}, u32[]{:S(2)}, u32[]{:S(2)}) collective-permute-start(bf16[256,512]{1,0:T(8,128)(2,1)S(1)} %collective-permute-done), channel_id=1, source_target_pairs={{0,224},{16,240},{32,0},{48,16},{64,32},{80,48},{96,64},{112,80},{... | collective-permute-start | bytes 786440 | tf_op jit(solution)/shard_map/ppermute | solution.py:118
  31.4 10.1 %collective-permute-start.5 = (bf16[256,512]{1,0:T(8,128)(2,1)S(1)}, bf16[256,512]{1,0:T(8,128)(2,1)S(1)}, u32[]{:S(2)}, u32[]{:S(2)}) collective-permute-start(bf16[256,512]{1,0:T(8,128)(2,1)S(1)} %collective-permute-done.4), channel_id=1, source_target_pairs={{0,32},{16,48},{32,64},{48,80},{64,96},{80,112},{96,128},{112,144}... | collective-permute-start | bytes 786440 | tf_op jit(solution)/shard_map/ppermute | solution.py:115
  37.4 7.2 %collective-permute-start.2 = (bf16[256,512]{1,0:T(8,128)(2,1)S(1)}, bf16[256,512]{1,0:T(8,128)(2,1)S(1)}, u32[]{:S(2)}, u32[]{:S(2)}) collective-permute-start(bf16[256,512]{1,0:T(8,128)(2,1)S(1)} %collective-permute-done.1), channel_id=1, source_target_pairs={{0,224},{16,240},{32,0},{48,16},{64,32},{80,48},{96,64},{112,80},{... | collective-permute-start | bytes 786440 | tf_op jit(solution)/shard_map/ppermute | solution.py:118
  41.4 7.6 %collective-permute-start.6 = (bf16[256,512]{1,0:T(8,128)(2,1)S(1)}, bf16[256,512]{1,0:T(8,128)(2,1)S(1)}, u32[]{:S(2)}, u32[]{:S(2)}) collective-permute-start(bf16[256,512]{1,0:T(8,128)(2,1)S(1)} %collective-permute-done.5), channel_id=1, source_target_pairs={{0,32},{16,48},{32,64},{48,80},{64,96},{80,112},{96,128},{112,144}... | collective-permute-start | bytes 786440 | tf_op jit(solution)/shard_map/ppermute | solution.py:115
  42.2 11.1 %copy-start.5 = (bf16[2048,64]{0,1:T(8,128)(2,1)S(1)}, bf16[2048,64]{0,1:T(8,128)(2,1)}, u32[]{:S(2)}) copy-start(bf16[2048,64]{0,1:T(8,128)(2,1)} %param.14) | copy-start | bytes 786436
  53.1 3.6 %collective-permute-start.7 = (bf16[256,512]{0,1:T(8,128)(2,1)S(1)}, bf16[256,512]{0,1:T(8,128)(2,1)S(1)}, u32[]{:S(2)}, u32[]{:S(2)}) collective-permute-start(bf16[256,512]{0,1:T(8,128)(2,1)S(1)} %bitcast.148), channel_id=1, source_target_pairs={{0,16},{16,0},{32,48},{48,32},{64,80},{80,64},{96,112},{112,96},{1... | collective-permute-start | bytes 786440 | tf_op jit(solution)/shard_map/ppermute | solution.py:125
  58.7 35.0 %all-to-all-start = ((bf16[16,256,128]{1,2,0:T(8,128)(2,1)}), bf16[16,256,128]{1,2,0:T(8,128)(2,1)S(1)}, u32[]{:S(2)}, u32[]{:S(2)}) async-start(bf16[16,256,128]{1,2,0:T(8,128)(2,1)} %broadcast_select_fusion), calls=%async_computation | async-start | bytes 2097152 | tf_op jit(solution)/shard_map/all_to_all | solution.py:168
  68.6 0.8 copy-start.4
  69.4 1.0 copy-start.1
  97.0 1.8 copy-start.2
  111.8 3.0 %copy-start.3 = (bf16[32,2048]{1,0:T(8,128)(2,1)S(1)}, bf16[32,2048]{1,0:T(8,128)(2,1)}, u32[]{:S(2)}) copy-start(bf16[32,2048]{1,0:T(8,128)(2,1)} %param.10) | copy-start | bytes 393220
  115.3 31.5 %copy-start.8 = (bf16[2,2048,320]{1,2,0:T(8,128)(2,1)S(1)}, bf16[2,2048,320]{1,2,0:T(8,128)(2,1)}, u32[]{:S(2)}) copy-start(bf16[2,2048,320]{1,2,0:T(8,128)(2,1)} %param.18) | copy-start | bytes 7864324
Sparse Core Ops, SparseCore 0:
  10.8 81.7 all-gather.1

commit v4 on v3

--- a/solution.py
+++ b/solution.py
@@ -158,18 +158,11 @@
     value_cols = lax.dynamic_slice_in_dim(value_weight, kv_first * HD, kv_width, 1)
     projection = jnp.concatenate([query_weight, key_cols, value_cols], axis=1)
 
-    shard_rows = prefix_cache.shape[0]
     chosen = fetch_slot(prefix_cache, group_prefix, group_rank)
     out_full = lax.all_gather(out_weight, "tensor", axis=0, tiled=True)
-    by_head = chosen.reshape(shard_rows, 2, KVH // local_kv, kv_width)
-    by_head = jnp.transpose(by_head, (2, 0, 1, 3)).reshape(KVH // local_kv, shard_rows, 2 * kv_width)
-    wanted_by = (jnp.arange(tensor_count) * local_heads // head_ratio) // local_kv
-    outgoing = jnp.take(by_head, wanted_by, axis=0)
-    incoming = lax.all_to_all(outgoing, "tensor", 0, 0, tiled=True)
-    seg_rows = tensor_count * shard_rows
-    incoming = incoming.reshape(seg_rows, 2 * kv_width)
-    keys_block = jnp.repeat(incoming[:, :kv_width].reshape(seg_rows, local_kv, HD), repeat_by, axis=1)
-    values_block = jnp.repeat(incoming[:, kv_width:].reshape(seg_rows, local_kv, HD), repeat_by, axis=1)
+    chunk_rows = chosen.shape[0]
+    chunk_keys = jnp.repeat(chosen[:, :kv_total].reshape(chunk_rows, KVH, HD), head_ratio, axis=1)
+    chunk_values = jnp.repeat(chosen[:, kv_total:].reshape(chunk_rows, KVH, HD), head_ratio, axis=1)
 
     normed = norm_rows(tokens)
     segment = gather_rows(normed, "tensor")
@@ -202,22 +195,43 @@
         repeat_by,
         axis=1,
     )
-    start_state = (
-        jnp.full((group_tokens, local_heads), NEG_FILL, jnp.float32),
-        jnp.zeros((group_tokens, local_heads), jnp.float32),
-        jnp.zeros((group_tokens, local_heads, HD), jnp.float32),
-    )
-    prefix_state = merge_states(
-        start_state, softmax_block(queries, keys_block, values_block, scaling, None)
-    )
+    every_query = lax.all_to_all(
+        jnp.broadcast_to(queries[None], (tensor_count,) + queries.shape), "tensor", 0, 0, tiled=True
+    )
+    every_query = jnp.transpose(every_query, (1, 0, 2, 3)).reshape(group_tokens, QH, HD)
+    chunk_state = softmax_block(every_query, chunk_keys, chunk_values, scaling, None)
+
     indices = jnp.arange(group_tokens, dtype=jnp.int32)
     allowed = (request[:, None] == request[None, :]) & (indices[None, :] <= indices[:, None])
-    suffix_state = softmax_block(queries, own_keys, own_values, scaling, allowed[:, None, :])
-    top_score, weight, blended = merge_states(prefix_state, suffix_state)
+    suffix_top, suffix_weight, suffix_blend = softmax_block(
+        queries, own_keys, own_values, scaling, allowed[:, None, :]
+    )
+    head_first = tensor_rank * local_heads
+    suffix_state = (
+        lax.dynamic_update_slice_in_dim(
+            jnp.full((group_tokens, QH), NEG_FILL, jnp.float32), suffix_top, head_first, 1
+        ),
+        lax.dynamic_update_slice_in_dim(
+            jnp.zeros((group_tokens, QH), jnp.float32), suffix_weight, head_first, 1
+        ),
+        lax.dynamic_update_slice_in_dim(
+            jnp.zeros((group_tokens, QH, HD), jnp.float32), suffix_blend, head_first, 1
+        ),
+    )
+    top_score, weight, blended = merge_states(chunk_state, suffix_state)
+    packed = jnp.concatenate([blended, top_score[:, :, None], weight[:, :, None]], axis=2)
+    packed = lax.all_to_all(
+        packed.reshape((tensor_count, row_count) + packed.shape[1:]), "tensor", 0, 0, tiled=True
+    )
+    part_blend = packed[..., :HD]
+    part_top = packed[..., HD]
+    part_weight = packed[..., HD + 1]
+    overall = jnp.max(part_top, axis=0)
+    factor = jnp.exp(part_top - overall[None])
+    weight = jnp.sum(part_weight * factor, axis=0)
+    blended = jnp.sum(part_blend * factor[..., None], axis=0)
     attended = (blended / weight[:, :, None]).astype(jnp.bfloat16)
-    attended = lax.all_to_all(
-        attended.reshape(tensor_count, row_count, query_width), "tensor", 0, 0, tiled=True
-    )
+    attended = attended.reshape(row_count, tensor_count, query_width).transpose(1, 0, 2)
     feature_groups = out_full.shape[0] // query_width
     partials = jnp.einsum(
         "grk,gkd->grd",

time: 193 us -> 279 us (1.45)
  blocking collectives: 72.8 us -> 117 us
  local copies, waits for them, and re-layouts: 15.7 us -> 49.7 us
  other arithmetic: 7 us -> 22.4 us
  waiting for transfers between devices: 34.5 us -> 23.6 us
    all_to_all x1, blocking collectives: 11.3 us -> 53.9 us  [on_device(): lax.all_to_all(packed.reshape((tensor_count, row_count) + packed.shape[1:...]
    all_to_all x1, waiting for transfers between devices: 23.1 us -> 9.15 us  [on_device(): lax.all_to_all(jnp.broadcast_to(queries[None], (tensor_count,) + queries....]
    unnamed x30 -> x39, local copies, waits for them, and re-layouts: 7.37 us -> 19 us
    concatenate x0 -> x1, other arithmetic: none -> 6.88 us  [on_device(): jnp.concatenate([blended, top_score[:, :, None], weight[:, :, None]], axi...]
    concatenate x0 -> x4, local copies, waits for them, and re-layouts: none -> 6.23 us  [on_device(): jnp.concatenate([blended, top_score[:, :, None], weight[:, :, None]], axi...]
    slice x0 -> x1, other arithmetic: none -> 5.44 us  [on_device(): part_weight = packed[..., HD + 1]]
    broadcast_in_dim x0 -> x6, local copies, waits for them, and re-layouts: none -> 4.9 us  [the longest x1 1.59 us: on_device(): jnp.zeros((group_tokens, QH, HD), jnp.float32)]
    ppermute x4, waiting for transfers between devices: 8.93 us -> 12.9 us  [fetch_slot(): ahead = lax.ppermute(ahead, 'dp', onward)]
  transfers between devices with their start and end apart: 11 -> 11, of which waited for: 4 -> 4; matrix products, arithmetic and copies ran while one was open for 15% -> 29% of each run, Pallas kernels for 0% -> 0%
where the time goes in v4:
time: 279 us; the launch traced here: 276 us
  blocking collectives  117 us (42%)
  local copies, waits for them, and re-layouts  49.7 us (18%)
  starting transfers between devices  24.9 us (9%)
  waiting for transfers between devices  23.6 us (8%)
  other arithmetic  22.4 us (8%)
  matrix products  19.8 us (7%)
  between operations  18.9 us (7%)
    all_to_all x1, blocking collectives, on_device(): lax.all_to_all(packed.reshape((tensor_count, row_count) + packed.shape[1:...  53.9 us
    all_to_all x1, blocking collectives, sum_scatter_rows(): received = lax.all_to_all(parts, axis, 0, 0, tiled=True)  31.7 us
    all_to_all x1, blocking collectives, gather_rows(): received = lax.all_to_all(copies, axis, 0, 0, tiled=True)  31.1 us
    unnamed x39, local copies, waits for them, and re-layouts  19 us
    ppermute x4, waiting for transfers between devices, fetch_slot(): ahead = lax.ppermute(ahead, 'dp', onward)  12.9 us
    ppermute x3, starting transfers between devices, fetch_slot(): behind = lax.ppermute(behind, 'dp', backward)  10.6 us
    all_to_all x1, waiting for transfers between devices, on_device(): lax.all_to_all(jnp.broadcast_to(queries[None], (tensor_count,) + queries....  9.15 us
    all_to_all x1, starting transfers between devices, gather_rows(): received = lax.all_to_all(copies, axis, 0, 0, tiled=True)  7.17 us
  transfers between devices with their start and end apart: 11, of which 4 were waited for; matrix products, arithmetic and copies ran while one was open for 29% of the time, Pallas kernels for 0%

profile of v4, /device:TPU:0, one launch (start us, length us, event | category | flops | bytes accessed | tf_op | source)
XLA Modules:
  0.0 276.2 jit_solution(11447726396289523098)
XLA Ops:
  6.5 4.1 %collective-permute-start = (bf16[256,512]{1,0:T(8,128)(2,1)}, bf16[256,512]{1,0:T(8,128)(2,1)}, u32[]{:S(2)}, u32[]{:S(2)}) collective-permute-start(bf16[256,512]{1,0:T(8,128)(2,1)} %param.13), channel_id=1, source_target_pairs={{0,224},{16,240},{32,0},{48,16},{64,32},{80,48},{96,64},{112,80},{... | collective-permute-start | bytes 786440 | tf_op jit(solution)/shard_map/ppermute | solution.py:118
  14.3 7.2 %all-to-all-start = ((bf16[16,32,2048]{2,1,0:T(8,128)(2,1)}), bf16[16,32,2048]{2,1,0:T(8,128)(2,1)S(1)}, u32[]{:S(2)}, u32[]{:S(2)}) async-start(bf16[16,32,2048]{2,1,0:T(8,128)(2,1)} %broadcast_in_dim.31), calls=%async_computation | async-start | bytes 4194304 | tf_op jit(solution)/shard_map/all_to_all | solution.py:89
  24.2 2.6 constant_dynamic-slice_fusion
  26.8 3.2 %collective-permute-start.1 = (bf16[256,512]{1,0:T(8,128)(2,1)}, bf16[256,512]{1,0:T(8,128)(2,1)}, u32[]{:S(2)}, u32[]{:S(2)}) collective-permute-start(bf16[256,512]{1,0:T(8,128)(2,1)} %collective-permute-done), channel_id=1, source_target_pairs={{0,224},{16,240},{32,0},{48,16},{64,32},{80,48},{96,64},{112,80},{... | collective-permute-start | bytes 786440 | tf_op jit(solution)/shard_map/ppermute | solution.py:118
  30.1 8.4 %collective-permute-done.4 = bf16[256,512]{1,0:T(8,128)(2,1)} collective-permute-done((bf16[256,512]{1,0:T(8,128)(2,1)}, bf16[256,512]{1,0:T(8,128)(2,1)}, u32[]{:S(2)}, u32[]{:S(2)}) %collective-permute-start.4) | collective-permute-done | bytes 262176 | tf_op jit(solution)/shard_map/ppermute | solution.py:115
  46.3 3.2 %collective-permute-start.2 = (bf16[256,512]{1,0:T(8,128)(2,1)}, bf16[256,512]{1,0:T(8,128)(2,1)S(1)}, u32[]{:S(2)}, u32[]{:S(2)}) collective-permute-start(bf16[256,512]{1,0:T(8,128)(2,1)} %collective-permute-done.1), channel_id=1, source_target_pairs={{0,224},{16,240},{32,0},{48,16},{64,32},{80,48},{96,64},{112,80},{... | collective-permute-start | bytes 786440 | tf_op jit(solution)/shard_map/ppermute | solution.py:118
  54.5 4.5 %collective-permute-done.6 = bf16[256,512]{1,0:T(8,128)(2,1)S(1)} collective-permute-done((bf16[256,512]{1,0:T(8,128)(2,1)}, bf16[256,512]{1,0:T(8,128)(2,1)S(1)}, u32[]{:S(2)}, u32[]{:S(2)}) %collective-permute-start.6) | collective-permute-done | bytes 262176 | tf_op jit(solution)/shard_map/ppermute | solution.py:115
  70.2 2.5 fusion.26
  75.5 7.1 %all-to-all-start.1 = ((bf16[16,512,1,64]{1,3,2,0:T(8,128)(2,1)}), bf16[16,512,1,64]{1,3,2,0:T(8,128)(2,1)S(1)}, u32[]{:S(2)}, u32[]{:S(2)}) async-start(bf16[16,512,1,64]{1,3,2,0:T(8,128)(2,1)} %broadcast_in_dim.33), calls=%async_computation.1 | async-start | bytes 2097152 | tf_op jit(solution)/shard_map/all_to_all | solution.py:198
  92.0 9.1 %all-to-all-done.1 = bf16[16,512,1,64]{1,3,2,0:T(8,128)(2,1)S(1)} async-done(((bf16[16,512,1,64]{1,3,2,0:T(8,128)(2,1)}), bf16[16,512,1,64]{1,3,2,0:T(8,128)(2,1)S(1)}, u32[]{:S(2)}, u32[]{:S(2)}) %all-to-all-start.1) | async-done | bytes 1048608 | tf_op jit(solution)/shard_map/all_to_all | solution.py:198
  105.6 3.3 %fusion.8 = f32[512,16,64]{0,2,1:T(8,128)S(1)} fusion(f32[512,16,64]{0,2,1:T(8,128)} %fusion.25, bf16[256,16,64]{0,2,1:T(8,128)(2,1)S(1)} %bitcast.136, f32[16,256,512]{2,1,0:T(8,128)S(1)} %get-tuple-element.31, f32[512,16]{0,1:T(8,128)S(1)} %get-tuple-element.30, f32[512,16]{0,1:T(8,128)S(1)} %get-tuple-element.9, f32[512,16]{0,1:T(8,128)S(1)} %get-tuple-element.8), kind=kOutput, calls=%fused_computation.16 | convolution fusion | flops 276299776 | bytes 13205504 | tf_op jit(solution)/shard_map/thn,nhd->thd/dot_general | solution.py:64
  108.9 3.8 %copy.106 = f32[512,16,64]{2,1,0:T(8,128)} copy(f32[512,16,64]{0,2,1:T(8,128)S(1)} %fusion.8) | data formatting | bytes 4194304 | tf_op jit(solution)/shard_map/add | solution.py:82
  112.9 3.0 %copy.107 = f32[16,32,16,1]{3,2,1,0:T(8,128)} copy(f32[16,32,16,1]{1,0,2,3:T(8,128)S(1)} %concatenate.27) | data formatting | bytes 65536 | tf_op jit(solution)/shard_map/concatenate | solution.py:222
  116.0 3.0 %copy.108 = f32[16,32,16,1]{3,2,1,0:T(8,128)} copy(f32[16,32,16,1]{1,0,2,3:T(8,128)S(1)} %concatenate.28) | data formatting | bytes 65536 | tf_op jit(solution)/shard_map/concatenate | solution.py:222
  119.0 6.9 %pad_maximum_fusion = f32[16,32,16,66]{3,2,1,0:T(8,128)S(1)} fusion(f32[16,32,16,1]{3,2,1,0:T(8,128)} %copy.108, f32[16,32,16,1]{3,2,1,0:T(8,128)} %copy.107, f32[16,32,16,64]{3,2,1,0:T(8,128)} %bitcast.134), kind=kLoop, calls=%fused_computation.8 | loop fusion | flops 1081344 | bytes 4325376 | tf_op jit(solution)/shard_map/concatenate | solution.py:222
  125.9 53.9 %all_to_all.25 = f32[16,32,16,66]{3,2,1,0:T(8,128)S(1)} all-to-all(f32[16,32,16,66]{3,2,1,0:T(8,128)S(1)} %pad_maximum_fusion), channel_id=1, replica_groups=mesh['dp'=16,'tensor'=16] {'tensor'}, dimensions={0} | all-to-all | bytes 4325376 | tf_op jit(solution)/shard_map/all_to_all | solution.py:223
  179.8 5.4 %fusion.83 = (f32[16,32,16,1]{3,2,1,0:T(8,128)}, f32[32,16]{1,0:T(8,128)S(1)}, f32[16,32,16,1]{3,2,1,0:T(8,128)}) fusion(f32[16,32,16,66]{3,2,1,0:T(8,128)S(1)} %all_to_all.25), kind=kLoop, calls=%fused_computation.127 | loop fusion | flops 7680 | bytes 133120 | tf_op jit(solution)/shard_map/slice | solution.py:228
  185.3 3.3 %copy.115 = f32[16,32,16,1]{1,2,3,0:T(8,128)S(1)} copy(f32[16,32,16,1]{3,2,1,0:T(8,128)} %get-tuple-element.13) | data formatting | bytes 65536
  188.5 3.3 %copy.116 = f32[16,32,16,1]{1,2,3,0:T(8,128)S(1)} copy(f32[16,32,16,1]{3,2,1,0:T(8,128)} %get-tuple-element.11) | data formatting | bytes 65536
  192.1 2.9 %fusion.5 = f32[32,16,64]{2,1,0:T(8,128)S(1)} fusion(f32[16,32,16,66]{3,2,1,0:T(8,128)} %copy-done.1, f32[16,32,16]{2,1,0:T(8,128)S(1)} %copy.110), kind=kLoop, calls=%fused_computation.7 | loop fusion | flops 1015808 | bytes 2260992 | tf_op jit(solution)/shard_map/reduce_sum | solution.py:232
  195.2 2.9 %convert_reduce_fusion.1 = f32[32,2048]{1,0:T(8,128)S(1)} fusion(bf16[16,64,2048]{2,1,0:T(8,128)(2,1)} %bitcast.135, bf16[16,32,64]{2,0,1:T(8,128)(2,1)S(1)} %fusion.54), kind=kOutput, calls=%fused_computation.10 | convolution fusion | flops 137297920 | bytes 4521984 | tf_op jit(solution)/shard_map/grk,gkd->grd/dot_general | solution.py:236
  198.7 31.1 %all_to_all.26 = bf16[16,32,2048]{2,1,0:T(8,128)(2,1)S(1)} all-to-all(bf16[16,32,2048]{2,1,0:T(8,128)(2,1)S(1)} %broadcast_in_dim.38), channel_id=1, replica_groups=mesh['dp'=16,'tensor'=16] {'tensor'}, dimensions={0} | all-to-all | bytes 4194304 | tf_op jit(solution)/shard_map/all_to_all | solution.py:89
  231.6 5.0 %convolution_convert_fusion = bf16[512,2048]{1,0:T(8,128)(2,1)} fusion(bf16[320,2048]{1,0:T(8,128)(2,1)S(1)} %copy-done, bf16[512,2048]{1,0:T(8,128)(2,1)S(1)} %bitcast.140, bf16[2,2048,320]{1,2,0:T(8,128)(2,1)} %param.18, f32[512,320]{0,1:T(8,128)} %fusion.14), kind=kOutput, calls=%fused_computation.13 | convolution fusion | flops 1344208896 | bytes 7471104 | tf_op jit(solution)/shard_map/dot_general | solution.py:249
  236.6 31.7 %all_to_all.27 = bf16[16,32,2048]{2,1,0:T(8,128)(2,1)S(1)} all-to-all(bf16[16,32,2048]{2,1,0:T(8,128)(2,1)} %bitcast.141), channel_id=1, replica_groups=mesh['dp'=16,'tensor'=16] {'tensor'}, dimensions={0} | all-to-all | bytes 4194304 | tf_op jit(solution)/shard_map/all_to_all | solution.py:96
  (100 shorter events, 45.6 us)
Async XLA Ops:
  6.5 225.1 %copy-start = (bf16[320,2048]{1,0:T(8,128)(2,1)S(1)}, bf16[320,2048]{1,0:T(8,128)(2,1)}, u32[]{:S(2)}) copy-start(bf16[320,2048]{1,0:T(8,128)(2,1)} %param.19) | copy-start | bytes 3932164
  6.5 20.3 %collective-permute-start = (bf16[256,512]{1,0:T(8,128)(2,1)}, bf16[256,512]{1,0:T(8,128)(2,1)}, u32[]{:S(2)}, u32[]{:S(2)}) collective-permute-start(bf16[256,512]{1,0:T(8,128)(2,1)} %param.13), channel_id=1, source_target_pairs={{0,224},{16,240},{32,0},{48,16},{64,32},{80,48},{96,64},{112,80},{... | collective-permute-start | bytes 786440 | tf_op jit(solution)/shard_map/ppermute | solution.py:118
  10.7 19.4 %collective-permute-start.3 = (bf16[256,512]{1,0:T(8,128)(2,1)}, bf16[256,512]{1,0:T(8,128)(2,1)}, u32[]{:S(2)}, u32[]{:S(2)}) collective-permute-start(bf16[256,512]{1,0:T(8,128)(2,1)} %param.13), channel_id=1, source_target_pairs={{0,32},{16,48},{32,64},{48,80},{64,96},{80,112},{96,128},{112,144}... | collective-permute-start | bytes 786440 | tf_op jit(solution)/shard_map/ppermute | solution.py:115
  14.3 9.6 %copy-start.13 = (s32[1,8]{1,0:T(1,128)S(1)}, s32[1,8]{1,0:T(1,128)}, u32[]{:S(2)}) copy-start(s32[1,8]{1,0:T(1,128)} %param.11) | copy-start | bytes 100
  14.3 55.9 %all-to-all-start = ((bf16[16,32,2048]{2,1,0:T(8,128)(2,1)}), bf16[16,32,2048]{2,1,0:T(8,128)(2,1)S(1)}, u32[]{:S(2)}, u32[]{:S(2)}) async-start(bf16[16,32,2048]{2,1,0:T(8,128)(2,1)} %broadcast_in_dim.31), calls=%async_computation | async-start | bytes 4194304 | tf_op jit(solution)/shard_map/all_to_all | solution.py:89
  21.5 17.1 %copy-start.11 = (s32[16]{0:T(128)S(1)}, s32[16]{0:T(128)}, u32[]{:S(2)}) copy-start(s32[16]{0:T(128)} %param.12) | copy-start | bytes 196
  21.5 173.7 %all-gather.2.cloned.1.call-start = ((), (), s32[]{:S(2)}) async-start(), calls=%async_computation.5 | async-start | bytes 4456448 | tf_op jit(solution)/shard_map/all_gather | solution.py:162
  26.8 19.5 %collective-permute-start.1 = (bf16[256,512]{1,0:T(8,128)(2,1)}, bf16[256,512]{1,0:T(8,128)(2,1)}, u32[]{:S(2)}, u32[]{:S(2)}) collective-permute-start(bf16[256,512]{1,0:T(8,128)(2,1)} %collective-permute-done), channel_id=1, source_target_pairs={{0,224},{16,240},{32,0},{48,16},{64,32},{80,48},{96,64},{112,80},{... | collective-permute-start | bytes 786440 | tf_op jit(solution)/shard_map/ppermute | solution.py:118
  30.1 8.5 %collective-permute-start.4 = (bf16[256,512]{1,0:T(8,128)(2,1)}, bf16[256,512]{1,0:T(8,128)(2,1)}, u32[]{:S(2)}, u32[]{:S(2)}) collective-permute-start(bf16[256,512]{1,0:T(8,128)(2,1)} %collective-permute-done.3), channel_id=1, source_target_pairs={{0,32},{16,48},{32,64},{48,80},{64,96},{80,112},{96,128},{112,144}... | collective-permute-start | bytes 786440 | tf_op jit(solution)/shard_map/ppermute | solution.py:115
  38.5 12.7 %collective-permute-start.5 = (bf16[256,512]{1,0:T(8,128)(2,1)}, bf16[256,512]{1,0:T(8,128)(2,1)}, u32[]{:S(2)}, u32[]{:S(2)}) collective-permute-start(bf16[256,512]{1,0:T(8,128)(2,1)} %collective-permute-done.4), channel_id=1, source_target_pairs={{0,32},{16,48},{32,64},{48,80},{64,96},{80,112},{96,128},{112,144}... | collective-permute-start | bytes 786440 | tf_op jit(solution)/shard_map/ppermute | solution.py:115
  46.3 7.4 %collective-permute-start.2 = (bf16[256,512]{1,0:T(8,128)(2,1)}, bf16[256,512]{1,0:T(8,128)(2,1)S(1)}, u32[]{:S(2)}, u32[]{:S(2)}) collective-permute-start(bf16[256,512]{1,0:T(8,128)(2,1)} %collective-permute-done.1), channel_id=1, source_target_pairs={{0,224},{16,240},{32,0},{48,16},{64,32},{80,48},{96,64},{112,80},{... | collective-permute-start | bytes 786440 | tf_op jit(solution)/shard_map/ppermute | solution.py:118
  51.2 7.8 %collective-permute-start.6 = (bf16[256,512]{1,0:T(8,128)(2,1)}, bf16[256,512]{1,0:T(8,128)(2,1)S(1)}, u32[]{:S(2)}, u32[]{:S(2)}) collective-permute-start(bf16[256,512]{1,0:T(8,128)(2,1)} %collective-permute-done.5), channel_id=1, source_target_pairs={{0,32},{16,48},{32,64},{48,80},{64,96},{80,112},{96,128},{112,144}... | collective-permute-start | bytes 786440 | tf_op jit(solution)/shard_map/ppermute | solution.py:115
  68.4 14.2 %collective-permute-start.7 = (bf16[256,512]{0,1:T(8,128)(2,1)}, bf16[256,512]{0,1:T(8,128)(2,1)}, u32[]{:S(2)}, u32[]{:S(2)}) collective-permute-start(bf16[256,512]{0,1:T(8,128)(2,1)} %bitcast.144), channel_id=1, source_target_pairs={{0,16},{16,0},{32,48},{48,32},{64,80},{80,64},{96,112},{112,96},{1... | collective-permute-start | bytes 786440 | tf_op jit(solution)/shard_map/ppermute | solution.py:125
  72.7 1.0 copy-start.4
  72.7 9.9 %copy-start.3 = (bf16[1,256,512]{1,2,0:T(8,128)(2,1)S(1)}, bf16[1,256,512]{1,2,0:T(8,128)(2,1)}, u32[]{:S(2)}) copy-start(bf16[1,256,512]{1,2,0:T(8,128)(2,1)} %copy.101) | copy-start | bytes 786436
  73.7 0.6 copy-start.6
  75.5 25.7 %all-to-all-start.1 = ((bf16[16,512,1,64]{1,3,2,0:T(8,128)(2,1)}), bf16[16,512,1,64]{1,3,2,0:T(8,128)(2,1)S(1)}, u32[]{:S(2)}, u32[]{:S(2)}) async-start(bf16[16,512,1,64]{1,3,2,0:T(8,128)(2,1)} %broadcast_in_dim.33), calls=%async_computation.1 | async-start | bytes 2097152 | tf_op jit(solution)/shard_map/all_to_all | solution.py:198
  103.4 1.5 copy-start.9
  103.4 1.5 copy-start.10
  108.9 3.8 %copy-start.8 = (f32[512,16]{0,1:T(8,128)S(1)}, f32[512,16]{0,1:T(8,128)}, u32[]{:S(2)}) copy-start(f32[512,16]{0,1:T(8,128)} %get-tuple-element.10) | copy-start | bytes 98308
  112.8 3.1 %copy-start.7 = (f32[512,16]{0,1:T(8,128)S(1)}, f32[512,16]{0,1:T(8,128)}, u32[]{:S(2)}) copy-start(f32[512,16]{0,1:T(8,128)} %get-tuple-element.7) | copy-start | bytes 98308
  179.8 5.4 %copy-start.1 = (f32[16,32,16,66]{3,2,1,0:T(8,128)}, f32[16,32,16,66]{3,2,1,0:T(8,128)S(1)}, u32[]{:S(2)}) copy-start(f32[16,32,16,66]{3,2,1,0:T(8,128)S(1)} %all_to_all.25) | copy-start | bytes 6488068
  195.2 3.0 %copy-start.2 = (bf16[32,2048]{1,0:T(8,128)(2,1)S(1)}, bf16[32,2048]{1,0:T(8,128)(2,1)}, u32[]{:S(2)}) copy-start(bf16[32,2048]{1,0:T(8,128)(2,1)} %param.10) | copy-start | bytes 393220
  198.7 31.2 %copy-start.12 = (bf16[2,2048,320]{1,2,0:T(8,128)(2,1)S(1)}, bf16[2,2048,320]{1,2,0:T(8,128)(2,1)}, u32[]{:S(2)}) copy-start(bf16[2,2048,320]{1,2,0:T(8,128)(2,1)} %param.18) | copy-start | bytes 7864324
  (1 other events, 0.6 us)
Sparse Core Ops, SparseCore 0:
  24.8 61.0 all-gather.1

commit v5 on v3

--- a/solution.py
+++ b/solution.py
@@ -158,16 +158,39 @@
     value_cols = lax.dynamic_slice_in_dim(value_weight, kv_first * HD, kv_width, 1)
     projection = jnp.concatenate([query_weight, key_cols, value_cols], axis=1)
 
+    quarters = tensor_count // (KVH // local_kv)
+    own_quarter = tensor_rank % quarters
+    own_head = tensor_rank // quarters
     shard_rows = prefix_cache.shape[0]
-    chosen = fetch_slot(prefix_cache, group_prefix, group_rank)
-    out_full = lax.all_gather(out_weight, "tensor", axis=0, tiled=True)
-    by_head = chosen.reshape(shard_rows, 2, KVH // local_kv, kv_width)
-    by_head = jnp.transpose(by_head, (2, 0, 1, 3)).reshape(KVH // local_kv, shard_rows, 2 * kv_width)
-    wanted_by = (jnp.arange(tensor_count) * local_heads // head_ratio) // local_kv
-    outgoing = jnp.take(by_head, wanted_by, axis=0)
-    incoming = lax.all_to_all(outgoing, "tensor", 0, 0, tiled=True)
+    by_head = prefix_cache.reshape(shard_rows, 2, KVH // local_kv, kv_width)
+    spread = []
+    for shift in range(quarters):
+        head_sent = (own_quarter + shift) % quarters
+        block = lax.dynamic_index_in_dim(by_head, head_sent, 2, keepdims=False)
+        pairs = [
+            (quarters * a + b, quarters * ((b + shift) % quarters) + a)
+            for a in range(tensor_count // quarters)
+            for b in range(quarters)
+        ]
+        spread.append(lax.ppermute(block.reshape(shard_rows, 2 * kv_width), "tensor", pairs))
+    spread = jnp.stack(spread)
+    order = (own_head - jnp.arange(quarters)) % quarters
+    spread = jnp.take(spread, order, axis=0).reshape(quarters * shard_rows, 2 * kv_width)
+    mine = fetch_slot(spread, group_prefix, group_rank)
+    held = [mine]
+    for shift in range(1, quarters):
+        pairs = [
+            (quarters * h + q, quarters * h + (q + shift) % quarters)
+            for h in range(tensor_count // quarters)
+            for q in range(quarters)
+        ]
+        held.append(lax.ppermute(mine, "tensor", pairs))
+    held = jnp.stack(held)
+    order = (own_quarter - jnp.arange(quarters)) % quarters
+    incoming = jnp.take(held, order, axis=0)
     seg_rows = tensor_count * shard_rows
     incoming = incoming.reshape(seg_rows, 2 * kv_width)
+    out_full = lax.all_gather(out_weight, "tensor", axis=0, tiled=True)
     keys_block = jnp.repeat(incoming[:, :kv_width].reshape(seg_rows, local_kv, HD), repeat_by, axis=1)
     values_block = jnp.repeat(incoming[:, kv_width:].reshape(seg_rows, local_kv, HD), repeat_by, axis=1)
 

time: 193 us -> 198 us (1.026)
  starting transfers between devices: 25 us -> 32.8 us
  local copies, waits for them, and re-layouts: 15.7 us -> 10.9 us
  other arithmetic: 7 us -> 10.4 us
    all_to_all x1 -> x0, waiting for transfers between devices: 23.1 us -> none  [on_device(): incoming = lax.all_to_all(outgoing, 'tensor', 0, 0, tiled=True)]
    ppermute x0 -> x7, waiting for transfers between devices: none -> 16.8 us  [the longest x3 16.8 us: on_device(): held.append(lax.ppermute(mine, 'tensor', pairs))]
    ppermute x0 -> x7, starting transfers between devices: none -> 15.4 us  [the longest x4 9.94 us: on_device(): lax.ppermute(block.reshape(shard_rows, 2 * kv_width), 'tensor', pairs)]
    ppermute x4, waiting for transfers between devices: 8.93 us -> 17.8 us  [fetch_slot(): ahead = lax.ppermute(ahead, 'dp', onward)]
    all_to_all x1 -> x0, starting transfers between devices: 6.89 us -> none  [on_device(): incoming = lax.all_to_all(outgoing, 'tensor', 0, 0, tiled=True)]
    unnamed x30 -> x28, local copies, waits for them, and re-layouts: 7.37 us -> 4.15 us
    all_to_all x1, blocking collectives: 11.3 us -> 14.3 us  [on_device(): lax.all_to_all(attended.reshape(tensor_count, row_count, query_width), 't...]
    all_to_all x1, blocking collectives: 31.5 us -> 28.6 us  [gather_rows(): received = lax.all_to_all(copies, axis, 0, 0, tiled=True)]
  transfers between devices with their start and end apart: 11 -> 17, of which waited for: 4 -> 7; matrix products, arithmetic and copies ran while one was open for 15% -> 12% of each run, Pallas kernels for 0% -> 0%
where the time goes in v5:
time: 198 us; the launch traced here: 197 us
  blocking collectives  71.7 us (36%)
  waiting for transfers between devices  35.3 us (18%)
  starting transfers between devices  32.8 us (17%)
  between operations  19 us (10%)
  matrix products  16.5 us (8%)
  local copies, waits for them, and re-layouts  10.9 us (6%)
  other arithmetic  10.4 us (5%)
    all_to_all x1, blocking collectives, sum_scatter_rows(): received = lax.all_to_all(parts, axis, 0, 0, tiled=True)  28.8 us
    all_to_all x1, blocking collectives, gather_rows(): received = lax.all_to_all(copies, axis, 0, 0, tiled=True)  28.6 us
    ppermute x4, waiting for transfers between devices, fetch_slot(): ahead = lax.ppermute(ahead, 'dp', onward)  17.8 us
    ppermute x3, waiting for transfers between devices, on_device(): held.append(lax.ppermute(mine, 'tensor', pairs))  16.8 us
    all_to_all x1, blocking collectives, on_device(): lax.all_to_all(attended.reshape(tensor_count, row_count, query_width), 't...  14.3 us
    ppermute x3, starting transfers between devices, fetch_slot(): behind = lax.ppermute(behind, 'dp', backward)  10.6 us
    ppermute x4, starting transfers between devices, on_device(): lax.ppermute(block.reshape(shard_rows, 2 * kv_width), 'tensor', pairs)  9.94 us
    ppermute x3, starting transfers between devices, on_device(): held.append(lax.ppermute(mine, 'tensor', pairs))  5.49 us
  transfers between devices with their start and end apart: 17, of which 7 were waited for; matrix products, arithmetic and copies ran while one was open for 12% of the time, Pallas kernels for 0%

profile of v5, /device:TPU:0, one launch (start us, length us, event | category | flops | bytes accessed | tf_op | source)
XLA Modules:
  0.0 196.6 jit_solution(10435244984221437851)
XLA Ops:
  8.5 2.5 %collective-permute-start.1 = (bf16[256,128]{0,1:T(8,128)(2,1)S(1)}, bf16[256,128]{0,1:T(8,128)(2,1)S(1)}, u32[]{:S(2)}, u32[]{:S(2)}) collective-permute-start(bf16[256,128]{0,1:T(8,128)(2,1)S(1)} %bitcast.175), channel_id=1, source_target_pairs={{0,4},{1,8},{2,12},{3,0},{4,5},{5,9},{6,13},{7,1},{8,6},{9,10},{10... | collective-permute-start | bytes 196616 | tf_op jit(solution)/shard_map/ppermute | solution.py:175
  11.0 4.7 %collective-permute-start.2 = (bf16[256,128]{0,1:T(8,128)(2,1)S(1)}, bf16[256,128]{0,1:T(8,128)(2,1)S(1)}, u32[]{:S(2)}, u32[]{:S(2)}) collective-permute-start(bf16[256,128]{0,1:T(8,128)(2,1)S(1)} %bitcast.173), channel_id=1, source_target_pairs={{0,8},{1,12},{2,0},{3,4},{4,9},{5,13},{6,1},{7,5},{8,10},{9,14},{1... | collective-permute-start | bytes 196616 | tf_op jit(solution)/shard_map/ppermute | solution.py:175
  15.7 2.0 %collective-permute-start.3 = (bf16[256,128]{0,1:T(8,128)(2,1)S(1)}, bf16[256,128]{0,1:T(8,128)(2,1)S(1)}, u32[]{:S(2)}, u32[]{:S(2)}) collective-permute-start(bf16[256,128]{0,1:T(8,128)(2,1)S(1)} %bitcast.172), channel_id=1, source_target_pairs={{0,12},{1,0},{2,4},{3,8},{4,13},{5,1},{6,5},{7,9},{8,14},{9,2},{10... | collective-permute-start | bytes 196616 | tf_op jit(solution)/shard_map/ppermute | solution.py:175
  21.4 4.6 %all-to-all-start = ((bf16[16,32,2048]{2,1,0:T(8,128)(2,1)}), bf16[16,32,2048]{2,1,0:T(8,128)(2,1)}, u32[]{:S(2)}, u32[]{:S(2)}) async-start(bf16[16,32,2048]{2,1,0:T(8,128)(2,1)} %broadcast_in_dim.101), calls=%async_computation | async-start | bytes 4194304 | tf_op jit(solution)/shard_map/all_to_all | solution.py:89
  28.1 2.0 %collective-permute-start.7 = (bf16[1024,128]{1,0:T(8,128)(2,1)S(1)}, bf16[1024,128]{1,0:T(8,128)(2,1)S(1)}, u32[]{:S(2)}, u32[]{:S(2)}) collective-permute-start(bf16[1024,128]{1,0:T(8,128)(2,1)S(1)} %bitcast_select_fusion.2), channel_id=1, source_target_pairs={{0,32},{16,48},{32,64},{48,80},{64,96},{80,112},{96,128},{112,144}... | collective-permute-start | bytes 786440 | tf_op jit(solution)/shard_map/ppermute | solution.py:115
  30.2 4.0 %collective-permute-start.4 = (bf16[1024,128]{1,0:T(8,128)(2,1)S(1)}, bf16[1024,128]{1,0:T(8,128)(2,1)S(1)}, u32[]{:S(2)}, u32[]{:S(2)}) collective-permute-start(bf16[1024,128]{1,0:T(8,128)(2,1)S(1)} %bitcast_select_fusion.2), channel_id=1, source_target_pairs={{0,224},{16,240},{32,0},{48,16},{64,32},{80,48},{96,64},{112,80},{... | collective-permute-start | bytes 786440 | tf_op jit(solution)/shard_map/ppermute | solution.py:118
  34.2 5.2 %collective-permute-done.7 = bf16[1024,128]{1,0:T(8,128)(2,1)S(1)} collective-permute-done((bf16[1024,128]{1,0:T(8,128)(2,1)S(1)}, bf16[1024,128]{1,0:T(8,128)(2,1)S(1)}, u32[]{:S(2)}, u32[]{:S(2)}) %collective-permute-start.7) | collective-permute-done | bytes 262176 | tf_op jit(solution)/shard_map/ppermute | solution.py:115
  39.5 3.3 %collective-permute-start.5 = (bf16[1024,128]{1,0:T(8,128)(2,1)S(1)}, bf16[1024,128]{1,0:T(8,128)(2,1)S(1)}, u32[]{:S(2)}, u32[]{:S(2)}) collective-permute-start(bf16[1024,128]{1,0:T(8,128)(2,1)S(1)} %collective-permute-done.4), channel_id=1, source_target_pairs={{0,224},{16,240},{32,0},{48,16},{64,32},{80,48},{96,64},{112,80},{... | collective-permute-start | bytes 786440 | tf_op jit(solution)/shard_map/ppermute | solution.py:118
  47.4 3.3 %collective-permute-start.6 = (bf16[1024,128]{1,0:T(8,128)(2,1)S(1)}, bf16[1024,128]{1,0:T(8,128)(2,1)S(1)}, u32[]{:S(2)}, u32[]{:S(2)}) collective-permute-start(bf16[1024,128]{1,0:T(8,128)(2,1)S(1)} %collective-permute-done.5), channel_id=1, source_target_pairs={{0,224},{16,240},{32,0},{48,16},{64,32},{80,48},{96,64},{112,80},{... | collective-permute-start | bytes 786440 | tf_op jit(solution)/shard_map/ppermute | solution.py:118
  50.7 4.0 %collective-permute-done.9 = bf16[1024,128]{1,0:T(8,128)(2,1)S(1)} collective-permute-done((bf16[1024,128]{1,0:T(8,128)(2,1)S(1)}, bf16[1024,128]{1,0:T(8,128)(2,1)S(1)}, u32[]{:S(2)}, u32[]{:S(2)}) %collective-permute-start.9) | collective-permute-done | bytes 262176 | tf_op jit(solution)/shard_map/ppermute | solution.py:115
  54.9 7.5 %collective-permute-done.10 = bf16[1024,128]{1,0:T(8,128)(2,1)S(1)} collective-permute-done((bf16[1024,128]{1,0:T(8,128)(2,1)S(1)}, bf16[1024,128]{1,0:T(8,128)(2,1)S(1)}, u32[]{:S(2)}, u32[]{:S(2)}) %collective-permute-start.10) | collective-permute-done | bytes 262176 | tf_op jit(solution)/shard_map/ppermute | solution.py:115
  69.0 2.7 %collective-permute-start.13 = (bf16[1024,128]{1,0:T(8,128)(2,1)S(1)}, bf16[1024,128]{1,0:T(8,128)(2,1)S(1)}, u32[]{:S(2)}, u32[]{:S(2)}) collective-permute-start(bf16[1024,128]{1,0:T(8,128)(2,1)S(1)} %bitcast_select_fusion.1), channel_id=1, source_target_pairs={{0,2},{1,3},{2,0},{3,1},{4,6},{5,7},{6,4},{7,5},{8,10},{9,11},{10,... | collective-permute-start | bytes 786440 | tf_op jit(solution)/shard_map/ppermute | solution.py:187
  74.2 2.4 %constant_dynamic-slice_fusion = (bf16[2048,64]{1,0:T(8,128)(2,1)}, bf16[2048,64]{1,0:T(8,128)(2,1)}) fusion(bf16[2048,256]{1,0:T(8,128)(2,1)S(1)} %copy-done.3, s32[]{:T(128)S(6)} %select_n.215, bf16[2048,256]{1,0:T(8,128)(2,1)} %param.15), kind=kLoop, calls=%fused_computation.139 | loop fusion | bytes 1048580 | tf_op jit(solution)/shard_map/dynamic_slice | solution.py:158
  76.6 2.7 %collective-permute-done.12 = bf16[1024,128]{1,0:T(8,128)(2,1)S(1)} collective-permute-done((bf16[1024,128]{1,0:T(8,128)(2,1)S(1)}, bf16[1024,128]{1,0:T(8,128)(2,1)S(1)}, u32[]{:S(2)}, u32[]{:S(2)}) %collective-permute-start.12) | collective-permute-done | bytes 262176 | tf_op jit(solution)/shard_map/ppermute | solution.py:187
  79.4 12.4 %collective-permute-done.13 = bf16[1024,128]{1,0:T(8,128)(2,1)S(1)} collective-permute-done((bf16[1024,128]{1,0:T(8,128)(2,1)S(1)}, bf16[1024,128]{1,0:T(8,128)(2,1)S(1)}, u32[]{:S(2)}, u32[]{:S(2)}) %collective-permute-start.13) | collective-permute-done | bytes 262176 | tf_op jit(solution)/shard_map/ppermute | solution.py:187
  95.2 2.1 %bitcast_select_fusion = bf16[4096,128]{1,0:T(8,128)(2,1)S(1)} fusion(bf16[4,1024,128]{2,1,0:T(8,128)(2,1)S(1)} %gather_fusion.1, pred[4096]{0:T(1024)(128)(4,1)S(1)} %bitcast.180), kind=kLoop, calls=%fused_computation.44 | loop fusion | flops 524288 | bytes 2101248 | tf_op jit(solution)/shard_map/jit(_take)/select_n | solution.py:190
  97.4 3.1 %fusion.40 = f32[512,192]{0,1:T(8,128)S(1)} fusion(bf16[512,2048]{1,0:T(8,128)(2,1)} %bitcast.29, bf16[2048,64]{1,0:T(8,128)(2,1)} %get-tuple-element.32, bf16[2048,64]{1,0:T(8,128)(2,1)} %get-tuple-element.33, bf16[2048,64]{1,0:T(8,128)(2,1)} %copy.24), kind=kOutput, calls=%fused_computation.38 | convolution fusion | flops 405012480 | bytes 3276800 | tf_op jit(solution)/shard_map/dot_general | solution.py:200
  104.2 1.8 fusion.32
  106.6 14.3 %all_to_all.20 = bf16[16,2,1024]{2,1,0:T(2,128)(2,1)S(1)} all-to-all(bf16[16,2,1024]{2,1,0:T(2,128)(2,1)S(1)} %reshape.529), channel_id=1, replica_groups=mesh['dp'=16,'tensor'=16] {'tensor'}, dimensions={0} | all-to-all | bytes 131072 | tf_op jit(solution)/shard_map/all_to_all | solution.py:241
  121.1 2.9 %convert_reduce_fusion.1 = f32[32,2048]{1,0:T(8,128)S(1)} fusion(bf16[16,32,64]{2,1,0:T(8,128)(2,1)S(1)} %reshape.530, bf16[16,64,2048]{2,1,0:T(8,128)(2,1)} %bitcast.162), kind=kOutput, calls=%fused_computation.9 | convolution fusion | flops 137297920 | bytes 4521984 | tf_op jit(solution)/shard_map/grk,gkd->grd/dot_general | solution.py:245
  124.6 28.6 %all_to_all.21 = bf16[16,32,2048]{2,1,0:T(8,128)(2,1)S(1)} all-to-all(bf16[16,32,2048]{2,1,0:T(8,128)(2,1)S(1)} %broadcast_in_dim.105), channel_id=1, replica_groups=mesh['dp'=16,'tensor'=16] {'tensor'}, dimensions={0} | all-to-all | bytes 4194304 | tf_op jit(solution)/shard_map/all_to_all | solution.py:89
  153.1 1.7 fusion.9
  154.9 5.0 %convolution_convert_fusion = bf16[512,2048]{1,0:T(8,128)(2,1)} fusion(bf16[320,2048]{1,0:T(8,128)(2,1)S(1)} %copy-done, bf16[512,2048]{1,0:T(8,128)(2,1)S(1)} %bitcast.165, bf16[2,2048,320]{1,2,0:T(8,128)(2,1)} %param.18, f32[512,320]{0,1:T(8,128)} %fusion.9), kind=kOutput, calls=%fused_computation.11 | convolution fusion | flops 1344208896 | bytes 7471104 | tf_op jit(solution)/shard_map/dot_general | solution.py:258
  159.8 28.8 %all_to_all.22 = bf16[16,32,2048]{2,1,0:T(8,128)(2,1)S(1)} all-to-all(bf16[16,32,2048]{2,1,0:T(8,128)(2,1)} %bitcast.166), channel_id=1, replica_groups=mesh['dp'=16,'tensor'=16] {'tensor'}, dimensions={0} | all-to-all | bytes 4194304 | tf_op jit(solution)/shard_map/all_to_all | solution.py:96
  (93 shorter events, 25.8 us)
Async XLA Ops:
  6.5 148.3 %copy-start = (bf16[320,2048]{1,0:T(8,128)(2,1)S(1)}, bf16[320,2048]{1,0:T(8,128)(2,1)}, u32[]{:S(2)}) copy-start(bf16[320,2048]{1,0:T(8,128)(2,1)} %param.19) | copy-start | bytes 3932164
  7.8 19.3 %collective-permute-start = (bf16[256,128]{0,1:T(8,128)(2,1)S(1)}, bf16[256,128]{0,1:T(8,128)(2,1)S(1)}, u32[]{:S(2)}, u32[]{:S(2)}) collective-permute-start(bf16[256,128]{0,1:T(8,128)(2,1)S(1)} %bitcast.177), channel_id=1, source_target_pairs={{0,0},{1,4},{2,8},{3,12},{4,1},{5,5},{6,9},{7,13},{8,2},{9,6},{10,... | collective-permute-start | bytes 196616 | tf_op jit(solution)/shard_map/ppermute | solution.py:175
  8.5 18.6 %collective-permute-start.1 = (bf16[256,128]{0,1:T(8,128)(2,1)S(1)}, bf16[256,128]{0,1:T(8,128)(2,1)S(1)}, u32[]{:S(2)}, u32[]{:S(2)}) collective-permute-start(bf16[256,128]{0,1:T(8,128)(2,1)S(1)} %bitcast.175), channel_id=1, source_target_pairs={{0,4},{1,8},{2,12},{3,0},{4,5},{5,9},{6,13},{7,1},{8,6},{9,10},{10... | collective-permute-start | bytes 196616 | tf_op jit(solution)/shard_map/ppermute | solution.py:175
  11.0 16.1 %collective-permute-start.2 = (bf16[256,128]{0,1:T(8,128)(2,1)S(1)}, bf16[256,128]{0,1:T(8,128)(2,1)S(1)}, u32[]{:S(2)}, u32[]{:S(2)}) collective-permute-start(bf16[256,128]{0,1:T(8,128)(2,1)S(1)} %bitcast.173), channel_id=1, source_target_pairs={{0,8},{1,12},{2,0},{3,4},{4,9},{5,13},{6,1},{7,5},{8,10},{9,14},{1... | collective-permute-start | bytes 196616 | tf_op jit(solution)/shard_map/ppermute | solution.py:175
  15.7 11.4 %collective-permute-start.3 = (bf16[256,128]{0,1:T(8,128)(2,1)S(1)}, bf16[256,128]{0,1:T(8,128)(2,1)S(1)}, u32[]{:S(2)}, u32[]{:S(2)}) collective-permute-start(bf16[256,128]{0,1:T(8,128)(2,1)S(1)} %bitcast.172), channel_id=1, source_target_pairs={{0,12},{1,0},{2,4},{3,8},{4,13},{5,1},{6,5},{7,9},{8,14},{9,2},{10... | collective-permute-start | bytes 196616 | tf_op jit(solution)/shard_map/ppermute | solution.py:175
  21.4 5.5 %copy-start.7 = (s32[1,8]{1,0:T(1,128)S(1)}, s32[1,8]{1,0:T(1,128)}, u32[]{:S(2)}) copy-start(s32[1,8]{1,0:T(1,128)} %param.11) | copy-start | bytes 100
  21.4 76.0 %all-to-all-start = ((bf16[16,32,2048]{2,1,0:T(8,128)(2,1)}), bf16[16,32,2048]{2,1,0:T(8,128)(2,1)}, u32[]{:S(2)}, u32[]{:S(2)}) async-start(bf16[16,32,2048]{2,1,0:T(8,128)(2,1)} %broadcast_in_dim.101), calls=%async_computation | async-start | bytes 4194304 | tf_op jit(solution)/shard_map/all_to_all | solution.py:89
  26.0 16.8 %copy-start.5 = (s32[16]{0:T(128)S(1)}, s32[16]{0:T(128)}, u32[]{:S(2)}) copy-start(s32[16]{0:T(128)} %param.12) | copy-start | bytes 196
  26.0 95.1 %all-gather.2.cloned.1.call-start = ((), (), s32[]{:S(2)}) async-start(), calls=%async_computation.4 | async-start | bytes 4456448 | tf_op jit(solution)/shard_map/all_gather | solution.py:193
  28.1 11.3 %collective-permute-start.7 = (bf16[1024,128]{1,0:T(8,128)(2,1)S(1)}, bf16[1024,128]{1,0:T(8,128)(2,1)S(1)}, u32[]{:S(2)}, u32[]{:S(2)}) collective-permute-start(bf16[1024,128]{1,0:T(8,128)(2,1)S(1)} %bitcast_select_fusion.2), channel_id=1, source_target_pairs={{0,32},{16,48},{32,64},{48,80},{64,96},{80,112},{96,128},{112,144}... | collective-permute-start | bytes 786440 | tf_op jit(solution)/shard_map/ppermute | solution.py:115
  30.2 9.3 %collective-permute-start.4 = (bf16[1024,128]{1,0:T(8,128)(2,1)S(1)}, bf16[1024,128]{1,0:T(8,128)(2,1)S(1)}, u32[]{:S(2)}, u32[]{:S(2)}) collective-permute-start(bf16[1024,128]{1,0:T(8,128)(2,1)S(1)} %bitcast_select_fusion.2), channel_id=1, source_target_pairs={{0,224},{16,240},{32,0},{48,16},{64,32},{80,48},{96,64},{112,80},{... | collective-permute-start | bytes 786440 | tf_op jit(solution)/shard_map/ppermute | solution.py:118
  39.4 7.8 %collective-permute-start.8 = (bf16[1024,128]{1,0:T(8,128)(2,1)S(1)}, bf16[1024,128]{1,0:T(8,128)(2,1)S(1)}, u32[]{:S(2)}, u32[]{:S(2)}) collective-permute-start(bf16[1024,128]{1,0:T(8,128)(2,1)S(1)} %collective-permute-done.7), channel_id=1, source_target_pairs={{0,32},{16,48},{32,64},{48,80},{64,96},{80,112},{96,128},{112,144}... | collective-permute-start | bytes 786440 | tf_op jit(solution)/shard_map/ppermute | solution.py:115
  39.5 7.9 %collective-permute-start.5 = (bf16[1024,128]{1,0:T(8,128)(2,1)S(1)}, bf16[1024,128]{1,0:T(8,128)(2,1)S(1)}, u32[]{:S(2)}, u32[]{:S(2)}) collective-permute-start(bf16[1024,128]{1,0:T(8,128)(2,1)S(1)} %collective-permute-done.4), channel_id=1, source_target_pairs={{0,224},{16,240},{32,0},{48,16},{64,32},{80,48},{96,64},{112,80},{... | collective-permute-start | bytes 786440 | tf_op jit(solution)/shard_map/ppermute | solution.py:118
  47.1 7.6 %collective-permute-start.9 = (bf16[1024,128]{1,0:T(8,128)(2,1)S(1)}, bf16[1024,128]{1,0:T(8,128)(2,1)S(1)}, u32[]{:S(2)}, u32[]{:S(2)}) collective-permute-start(bf16[1024,128]{1,0:T(8,128)(2,1)S(1)} %collective-permute-done.8), channel_id=1, source_target_pairs={{0,32},{16,48},{32,64},{48,80},{64,96},{80,112},{96,128},{112,144}... | collective-permute-start | bytes 786440 | tf_op jit(solution)/shard_map/ppermute | solution.py:115
  47.4 7.4 %collective-permute-start.6 = (bf16[1024,128]{1,0:T(8,128)(2,1)S(1)}, bf16[1024,128]{1,0:T(8,128)(2,1)S(1)}, u32[]{:S(2)}, u32[]{:S(2)}) collective-permute-start(bf16[1024,128]{1,0:T(8,128)(2,1)S(1)} %collective-permute-done.5), channel_id=1, source_target_pairs={{0,224},{16,240},{32,0},{48,16},{64,32},{80,48},{96,64},{112,80},{... | collective-permute-start | bytes 786440 | tf_op jit(solution)/shard_map/ppermute | solution.py:118
  54.7 7.6 %collective-permute-start.10 = (bf16[1024,128]{1,0:T(8,128)(2,1)S(1)}, bf16[1024,128]{1,0:T(8,128)(2,1)S(1)}, u32[]{:S(2)}, u32[]{:S(2)}) collective-permute-start(bf16[1024,128]{1,0:T(8,128)(2,1)S(1)} %collective-permute-done.9), channel_id=1, source_target_pairs={{0,32},{16,48},{32,64},{48,80},{64,96},{80,112},{96,128},{112,144}... | collective-permute-start | bytes 786440 | tf_op jit(solution)/shard_map/ppermute | solution.py:115
  54.8 18.4 %copy-start.4 = (bf16[2048,64]{0,1:T(8,128)(2,1)S(1)}, bf16[2048,64]{0,1:T(8,128)(2,1)}, u32[]{:S(2)}) copy-start(bf16[2048,64]{0,1:T(8,128)(2,1)} %param.14) | copy-start | bytes 786436
  54.8 19.4 %copy-start.3 = (bf16[2048,256]{1,0:T(8,128)(2,1)S(1)}, bf16[2048,256]{1,0:T(8,128)(2,1)}, u32[]{:S(2)}) copy-start(bf16[2048,256]{1,0:T(8,128)(2,1)} %param.16) | copy-start | bytes 3145732
  63.9 2.8 %collective-permute-start.11 = (bf16[1024,128]{1,0:T(8,128)(2,1)S(1)}, bf16[1024,128]{1,0:T(8,128)(2,1)S(1)}, u32[]{:S(2)}, u32[]{:S(2)}) collective-permute-start(bf16[1024,128]{1,0:T(8,128)(2,1)S(1)} %dynamic-slice_bitcast_fusion), channel_id=1, source_target_pairs={{0,16},{16,0},{32,48},{48,32},{64,80},{80,64},{96,112},{112,96},{1... | collective-permute-start | bytes 786440 | tf_op jit(solution)/shard_map/ppermute | solution.py:125
  67.7 11.7 %collective-permute-start.12 = (bf16[1024,128]{1,0:T(8,128)(2,1)S(1)}, bf16[1024,128]{1,0:T(8,128)(2,1)S(1)}, u32[]{:S(2)}, u32[]{:S(2)}) collective-permute-start(bf16[1024,128]{1,0:T(8,128)(2,1)S(1)} %bitcast_select_fusion.1), channel_id=1, source_target_pairs={{0,1},{1,2},{2,3},{3,0},{4,5},{5,6},{6,7},{7,4},{8,9},{9,10},{10,1... | collective-permute-start | bytes 786440 | tf_op jit(solution)/shard_map/ppermute | solution.py:187
  69.0 22.7 %collective-permute-start.13 = (bf16[1024,128]{1,0:T(8,128)(2,1)S(1)}, bf16[1024,128]{1,0:T(8,128)(2,1)S(1)}, u32[]{:S(2)}, u32[]{:S(2)}) collective-permute-start(bf16[1024,128]{1,0:T(8,128)(2,1)S(1)} %bitcast_select_fusion.1), channel_id=1, source_target_pairs={{0,2},{1,3},{2,0},{3,1},{4,6},{5,7},{6,4},{7,5},{8,10},{9,11},{10,... | collective-permute-start | bytes 786440 | tf_op jit(solution)/shard_map/ppermute | solution.py:187
  71.7 21.7 %collective-permute-start.14 = (bf16[1024,128]{1,0:T(8,128)(2,1)S(1)}, bf16[1024,128]{1,0:T(8,128)(2,1)}, u32[]{:S(2)}, u32[]{:S(2)}) collective-permute-start(bf16[1024,128]{1,0:T(8,128)(2,1)S(1)} %bitcast_select_fusion.1), channel_id=1, source_target_pairs={{0,3},{1,0},{2,1},{3,2},{4,7},{5,4},{6,5},{7,6},{8,11},{9,8},{10,9... | collective-permute-start | bytes 786440 | tf_op jit(solution)/shard_map/ppermute | solution.py:187
  121.1 3.0 %copy-start.1 = (bf16[32,2048]{1,0:T(8,128)(2,1)S(1)}, bf16[32,2048]{1,0:T(8,128)(2,1)}, u32[]{:S(2)}) copy-start(bf16[32,2048]{1,0:T(8,128)(2,1)} %param.10) | copy-start | bytes 393220
  124.6 28.6 %copy-start.6 = (bf16[2,2048,320]{1,2,0:T(8,128)(2,1)S(1)}, bf16[2,2048,320]{1,2,0:T(8,128)(2,1)}, u32[]{:S(2)}) copy-start(bf16[2,2048,320]{1,2,0:T(8,128)(2,1)} %param.18) | copy-start | bytes 7864324
  (1 other events, 1.4 us)
Sparse Core Ops, SparseCore 0:
  29.2 71.9 all-gather.1

commit v6 on v4

--- a/solution.py
+++ b/solution.py
@@ -98,6 +98,19 @@
 
 
 CORES = 2
+
+
+def merge_states_heads(former, latter):
+    top_one, weight_one, blend_one = former
+    top_two, weight_two, blend_two = latter
+    overall = jnp.maximum(top_one, top_two)
+    factor_one = jnp.exp(top_one - overall)
+    factor_two = jnp.exp(top_two - overall)
+    return (
+        overall,
+        weight_one * factor_one + weight_two * factor_two,
+        blend_one * factor_one[:, :, None] + blend_two * factor_two[:, :, None],
+    )
 
 
 def fetch_slot(prefix_cache, group_prefix, group_rank):
@@ -158,11 +171,12 @@
     value_cols = lax.dynamic_slice_in_dim(value_weight, kv_first * HD, kv_width, 1)
     projection = jnp.concatenate([query_weight, key_cols, value_cols], axis=1)
 
+    shard_rows = prefix_cache.shape[0]
     chosen = fetch_slot(prefix_cache, group_prefix, group_rank)
     out_full = lax.all_gather(out_weight, "tensor", axis=0, tiled=True)
     chunk_rows = chosen.shape[0]
-    chunk_keys = jnp.repeat(chosen[:, :kv_total].reshape(chunk_rows, KVH, HD), head_ratio, axis=1)
-    chunk_values = jnp.repeat(chosen[:, kv_total:].reshape(chunk_rows, KVH, HD), head_ratio, axis=1)
+    chunk_keys = jnp.transpose(chosen[:, :kv_total].reshape(chunk_rows, KVH, HD), (1, 0, 2))
+    chunk_values = jnp.transpose(chosen[:, kv_total:].reshape(chunk_rows, KVH, HD), (1, 0, 2))
 
     normed = norm_rows(tokens)
     segment = gather_rows(normed, "tensor")
@@ -196,10 +210,29 @@
         axis=1,
     )
     every_query = lax.all_to_all(
-        jnp.broadcast_to(queries[None], (tensor_count,) + queries.shape), "tensor", 0, 0, tiled=True
-    )
-    every_query = jnp.transpose(every_query, (1, 0, 2, 3)).reshape(group_tokens, QH, HD)
-    chunk_state = softmax_block(every_query, chunk_keys, chunk_values, scaling, None)
+        jnp.broadcast_to(
+            jnp.transpose(queries, (1, 0, 2))[None], (tensor_count, local_heads, group_tokens, HD)
+        ),
+        "tensor",
+        0,
+        0,
+        tiled=True,
+    ).reshape(KVH, head_ratio * group_tokens, HD)
+    scores = (
+        jnp.einsum("gqd,gkd->gqk", every_query, chunk_keys, preferred_element_type=jnp.float32)
+        * scaling
+    )
+    chunk_top = jnp.max(scores, axis=2)
+    exponent = jnp.exp(scores - chunk_top[:, :, None])
+    chunk_weight = jnp.sum(exponent, axis=2)
+    chunk_blend = jnp.einsum(
+        "gqk,gkd->gqd", exponent.astype(jnp.bfloat16), chunk_values, preferred_element_type=jnp.float32
+    )
+    chunk_state = (
+        chunk_top.reshape(QH, group_tokens),
+        chunk_weight.reshape(QH, group_tokens),
+        chunk_blend.reshape(QH, group_tokens, HD),
+    )
 
     indices = jnp.arange(group_tokens, dtype=jnp.int32)
     allowed = (request[:, None] == request[None, :]) & (indices[None, :] <= indices[:, None])
@@ -209,27 +242,35 @@
     head_first = tensor_rank * local_heads
     suffix_state = (
         lax.dynamic_update_slice_in_dim(
-            jnp.full((group_tokens, QH), NEG_FILL, jnp.float32), suffix_top, head_first, 1
+            jnp.full((QH, group_tokens), NEG_FILL, jnp.float32), suffix_top.T, head_first, 0
         ),
         lax.dynamic_update_slice_in_dim(
-            jnp.zeros((group_tokens, QH), jnp.float32), suffix_weight, head_first, 1
+            jnp.zeros((QH, group_tokens), jnp.float32), suffix_weight.T, head_first, 0
         ),
         lax.dynamic_update_slice_in_dim(
-            jnp.zeros((group_tokens, QH, HD), jnp.float32), suffix_blend, head_first, 1
-        ),
-    )
-    top_score, weight, blended = merge_states(chunk_state, suffix_state)
-    packed = jnp.concatenate([blended, top_score[:, :, None], weight[:, :, None]], axis=2)
-    packed = lax.all_to_all(
-        packed.reshape((tensor_count, row_count) + packed.shape[1:]), "tensor", 0, 0, tiled=True
-    )
-    part_blend = packed[..., :HD]
-    part_top = packed[..., HD]
-    part_weight = packed[..., HD + 1]
+            jnp.zeros((QH, group_tokens, HD), jnp.float32),
+            jnp.transpose(suffix_blend, (1, 0, 2)),
+            head_first,
+            0,
+        ),
+    )
+    top_score, weight, blended = merge_states_heads(chunk_state, suffix_state)
+    partial = (blended / weight[:, :, None]).astype(jnp.bfloat16)
+    partial = partial.reshape(QH, tensor_count, row_count, HD).transpose(1, 2, 0, 3)
+    partial = lax.all_to_all(
+        partial.reshape(tensor_count, row_count, QH * HD), "tensor", 0, 0, tiled=True
+    )
+    stats = jnp.stack([top_score, weight], axis=2).reshape(QH, tensor_count, row_count, 2)
+    stats = lax.all_to_all(
+        stats.transpose(1, 2, 0, 3).reshape(tensor_count, row_count, QH * 2), "tensor", 0, 0, tiled=True
+    ).reshape(tensor_count, row_count, QH, 2)
+    part_top = stats[..., 0]
     overall = jnp.max(part_top, axis=0)
-    factor = jnp.exp(part_top - overall[None])
-    weight = jnp.sum(part_weight * factor, axis=0)
-    blended = jnp.sum(part_blend * factor[..., None], axis=0)
+    factor = stats[..., 1] * jnp.exp(part_top - overall[None])
+    weight = jnp.sum(factor, axis=0)
+    blended = jnp.sum(
+        partial.reshape(tensor_count, row_count, QH, HD).astype(jnp.float32) * factor[..., None], axis=0
+    )
     attended = (blended / weight[:, :, None]).astype(jnp.bfloat16)
     attended = attended.reshape(row_count, tensor_count, query_width).transpose(1, 0, 2)
     feature_groups = out_full.shape[0] // query_width

time: 279 us -> 252 us (0.903)
  blocking collectives: 117 us -> 62.6 us
  waiting for transfers between devices: 23.6 us -> 37.7 us
  starting transfers between devices: 24.9 us -> 35.6 us
  matrix products: 19.8 us -> 25.1 us
  other arithmetic: 22.4 us -> 17.9 us
    all_to_all x1 -> x0, blocking collectives: 53.9 us -> none  [on_device(): lax.all_to_all(packed.reshape((tensor_count, row_count) + packed.shape[1:...]
    all_to_all x1 -> x3, waiting for transfers between devices: 9.15 us -> 23.2 us  [the longest x1 13.8 us: on_device(): lax.all_to_all(jnp.broadcast_to(jnp.transpose(queries, (1, 0, 2))[None],...]
    dot_general x0 -> x2, matrix products: none -> 11.4 us  [the longest x1 6.49 us: on_device(): jnp.einsum('gqd,gkd->gqk', every_query, chunk_keys, preferred_element_typ...]
    all_to_all x1 -> x3, starting transfers between devices: 7.13 us -> 17.8 us  [the longest x1 7.21 us: on_device(): lax.all_to_all(partial.reshape(tensor_count, row_count, QH * HD), 'tensor...]
    reshape x0 -> x6, local copies, waits for them, and re-layouts: none -> 7.1 us  [the longest x1 2.54 us: on_device(): every_query = lax.all_to_all(jnp.broadcast_to(jnp.transpose(queries, (1,...]
    concatenate x1 -> x0, other arithmetic: 6.88 us -> none  [on_device(): jnp.concatenate([blended, top_score[:, :, None], weight[:, :, None]], axi...]
    concatenate x4 -> x0, local copies, waits for them, and re-layouts: 6.23 us -> none  [on_device(): jnp.concatenate([blended, top_score[:, :, None], weight[:, :, None]], axi...]
    mul x1 -> x3, local copies, waits for them, and re-layouts: 0.12 us -> 6.18 us  [on_device(): partial.reshape(tensor_count, row_count, QH, HD).astype(jnp.float32)]
  transfers between devices with their start and end apart: 11 -> 13, of which waited for: 4 -> 5; matrix products, arithmetic and copies ran while one was open for 29% -> 33% of each run, Pallas kernels for 0% -> 0%
where the time goes in v6:
time: 252 us; the launch traced here: 250 us
  blocking collectives  62.6 us (25%)
  local copies, waits for them, and re-layouts  51.8 us (21%)
  waiting for transfers between devices  37.7 us (15%)
  starting transfers between devices  35.6 us (14%)
  matrix products  25.1 us (10%)
  between operations  19 us (8%)
  other arithmetic  17.9 us (7%)
    all_to_all x1, blocking collectives, sum_scatter_rows(): received = lax.all_to_all(parts, axis, 0, 0, tiled=True)  31.7 us
    all_to_all x1, blocking collectives, gather_rows(): received = lax.all_to_all(copies, axis, 0, 0, tiled=True)  30.9 us
    all_to_all x1, waiting for transfers between devices, on_device(): lax.all_to_all(jnp.broadcast_to(jnp.transpose(queries, (1, 0, 2))[None],...  13.8 us
    unnamed x30, local copies, waits for them, and re-layouts  13.1 us
    ppermute x4, waiting for transfers between devices, fetch_slot(): ahead = lax.ppermute(ahead, 'dp', onward)  12.9 us
    ppermute x3, starting transfers between devices, fetch_slot(): behind = lax.ppermute(behind, 'dp', backward)  10.6 us
    all_to_all x1, waiting for transfers between devices, on_device(): lax.all_to_all(partial.reshape(tensor_count, row_count, QH * HD), 'tensor...  9.42 us
    all_to_all x1, starting transfers between devices, on_device(): lax.all_to_all(partial.reshape(tensor_count, row_count, QH * HD), 'tensor...  7.21 us
  transfers between devices with their start and end apart: 13, of which 5 were waited for; matrix products, arithmetic and copies ran while one was open for 33% of the time, Pallas kernels for 0%

profile of v6, /device:TPU:0, one launch (start us, length us, event | category | flops | bytes accessed | tf_op | source)
XLA Modules:
  0.0 249.6 jit_solution(11988268359182999043)
XLA Ops:
  6.5 4.1 %collective-permute-start = (bf16[256,512]{1,0:T(8,128)(2,1)}, bf16[256,512]{1,0:T(8,128)(2,1)}, u32[]{:S(2)}, u32[]{:S(2)}) collective-permute-start(bf16[256,512]{1,0:T(8,128)(2,1)} %param.13), channel_id=1, source_target_pairs={{0,224},{16,240},{32,0},{48,16},{64,32},{80,48},{96,64},{112,80},{... | collective-permute-start | bytes 786440 | tf_op jit(solution)/shard_map/ppermute | solution.py:131
  14.3 7.2 %all-to-all-start = ((bf16[16,32,2048]{2,1,0:T(8,128)(2,1)}), bf16[16,32,2048]{2,1,0:T(8,128)(2,1)S(1)}, u32[]{:S(2)}, u32[]{:S(2)}) async-start(bf16[16,32,2048]{2,1,0:T(8,128)(2,1)} %broadcast_in_dim.25), calls=%async_computation | async-start | bytes 4194304 | tf_op jit(solution)/shard_map/all_to_all | solution.py:89
  24.2 2.5 %constant_dynamic-slice_fusion = (bf16[2048,64]{1,0:T(8,128)(2,1)}, bf16[2048,64]{1,0:T(8,128)(2,1)}) fusion(bf16[2048,256]{1,0:T(8,128)(2,1)} %param.16, s32[]{:T(128)S(6)} %select_n.71, bf16[2048,256]{1,0:T(8,128)(2,1)} %param.15), kind=kLoop, calls=%fused_computation.114 | loop fusion | bytes 1048580 | tf_op jit(solution)/shard_map/dynamic_slice | solution.py:171
  26.8 3.2 %collective-permute-start.1 = (bf16[256,512]{1,0:T(8,128)(2,1)}, bf16[256,512]{1,0:T(8,128)(2,1)}, u32[]{:S(2)}, u32[]{:S(2)}) collective-permute-start(bf16[256,512]{1,0:T(8,128)(2,1)} %collective-permute-done), channel_id=1, source_target_pairs={{0,224},{16,240},{32,0},{48,16},{64,32},{80,48},{96,64},{112,80},{... | collective-permute-start | bytes 786440 | tf_op jit(solution)/shard_map/ppermute | solution.py:131
  30.1 8.4 %collective-permute-done.4 = bf16[256,512]{1,0:T(8,128)(2,1)} collective-permute-done((bf16[256,512]{1,0:T(8,128)(2,1)}, bf16[256,512]{1,0:T(8,128)(2,1)}, u32[]{:S(2)}, u32[]{:S(2)}) %collective-permute-start.4) | collective-permute-done | bytes 262176 | tf_op jit(solution)/shard_map/ppermute | solution.py:128
  46.3 3.2 %collective-permute-start.2 = (bf16[256,512]{1,0:T(8,128)(2,1)}, bf16[256,512]{1,0:T(8,128)(2,1)S(1)}, u32[]{:S(2)}, u32[]{:S(2)}) collective-permute-start(bf16[256,512]{1,0:T(8,128)(2,1)} %collective-permute-done.1), channel_id=1, source_target_pairs={{0,224},{16,240},{32,0},{48,16},{64,32},{80,48},{96,64},{112,80},{... | collective-permute-start | bytes 786440 | tf_op jit(solution)/shard_map/ppermute | solution.py:131
  54.5 4.5 %collective-permute-done.6 = bf16[256,512]{1,0:T(8,128)(2,1)S(1)} collective-permute-done((bf16[256,512]{1,0:T(8,128)(2,1)}, bf16[256,512]{1,0:T(8,128)(2,1)S(1)}, u32[]{:S(2)}, u32[]{:S(2)}) %collective-permute-start.6) | collective-permute-done | bytes 262176 | tf_op jit(solution)/shard_map/ppermute | solution.py:128
  70.8 7.1 %all-to-all-start.1 = ((bf16[16,1,512,64]{2,3,1,0:T(8,128)(2,1)}), bf16[16,1,512,64]{2,3,1,0:T(8,128)(2,1)}, u32[]{:S(2)}, u32[]{:S(2)}) async-start(bf16[16,1,512,64]{2,3,1,0:T(8,128)(2,1)} %broadcast_in_dim.27), calls=%async_computation.1 | async-start | bytes 2097152 | tf_op jit(solution)/shard_map/all_to_all | solution.py:212
  87.1 13.8 %all-to-all-done.1 = bf16[16,1,512,64]{2,3,1,0:T(8,128)(2,1)} async-done(((bf16[16,1,512,64]{2,3,1,0:T(8,128)(2,1)}), bf16[16,1,512,64]{2,3,1,0:T(8,128)(2,1)}, u32[]{:S(2)}, u32[]{:S(2)}) %all-to-all-start.1) | async-done | bytes 1048608 | tf_op jit(solution)/shard_map/all_to_all | solution.py:212
  100.9 2.8 %copy.57 = bf16[16,1,512,64]{2,0,3,1:T(8,128)(2,1)} copy(bf16[16,1,512,64]{2,3,1,0:T(8,128)(2,1)} %all-to-all-done.1) | data formatting | bytes 2097152 | tf_op jit(solution)/shard_map/all_to_all | solution.py:212
  106.3 6.5 %multiply_reduce_fusion = (f32[4,2048]{1,0:T(4,128)S(1)}, f32[4,2048,256]{1,2,0:T(8,128)}) fusion(bf16[4,256,64]{1,2,0:T(8,128)(2,1)S(1)} %bitcast.149, bf16[4,2048,64]{1,0,2:T(4,128)(2,1)} %reshape.279), kind=kOutput, calls=%fused_computation.1 | convolution fusion | flops 272621568 | bytes 9601024 | tf_op jit(solution)/shard_map/gqd,gkd->gqk/dot_general | solution.py:222
  112.8 4.8 %fusion = f32[4,2048]{1,0:T(4,128)S(1)} fusion(f32[4,2048,256]{1,2,0:T(8,128)} %get-tuple-element.26, f32[4,2048]{1,0:T(4,128)S(1)} %get-tuple-element.25), kind=kLoop, calls=%fused_computation.2 | loop fusion | flops 6283264 | bytes 8454144 | tf_op jit(solution)/shard_map/reduce_sum | solution.py:227
  120.2 3.5 %all-to-all-start.3 = ((f32[16,1,1024]{2,1,0:T(1,128)}), f32[16,1,1024]{2,1,0:T(1,128)S(1)}, u32[]{:S(2)}, u32[]{:S(2)}) async-start(f32[16,1,1024]{2,1,0:T(1,128)} %reshape.295), calls=%async_computation.3 | async-start | bytes 131072 | tf_op jit(solution)/shard_map/all_to_all | solution.py:264
  123.7 4.9 %fusion.2 = f32[4,2048,64]{1,2,0:T(8,128)S(1)} fusion(bf16[4,256,64]{1,2,0:T(8,128)(2,1)S(1)} %bitcast.150, f32[4,2048,256]{1,2,0:T(8,128)} %get-tuple-element.26, f32[4,2048]{1,0:T(4,128)S(1)} %get-tuple-element.25), kind=kOutput, calls=%fused_computation.4 | convolution fusion | flops 274726912 | bytes 10649600 | tf_op jit(solution)/shard_map/gqk,gkd->gqd/dot_general | solution.py:228
  132.1 3.8 %divide_convert_fusion = bf16[16,512,64]{1,0,2:T(8,128)(2,1)} fusion(f32[16,512,64]{1,0,2:T(8,128)} %copy-done.1, f32[16,512,64]{1,0,2:T(8,128)} %reshape.282, f32[16,512]{1,0:T(8,128)S(1)} %get-tuple-element.7, f32[16,512]{1,0:T(8,128)} %get-tuple-element.9, f32[16,512]{1,0:T(8,128)S(1)} %get-tuple-element.8), kind=kLoop, calls=%fused_computation.12 | loop fusion | flops 2621440 | bytes 5341184 | tf_op jit(solution)/shard_map/convert_element_type | solution.py:258
  135.9 4.3 %copy.74 = bf16[16,512,64]{2,0,1:T(8,128)(2,1)S(1)} copy(bf16[16,512,64]{1,0,2:T(8,128)(2,1)} %divide_convert_fusion) | data formatting | bytes 2097152 | tf_op jit(solution)/shard_map/transpose | solution.py:259
  142.5 7.2 %all-to-all-start.2 = ((bf16[16,32,1024]{2,1,0:T(8,128)(2,1)}), bf16[16,32,1024]{2,1,0:T(8,128)(2,1)}, u32[]{:S(2)}, u32[]{:S(2)}) async-start(bf16[16,32,1024]{2,1,0:T(8,128)(2,1)} %reshape.289), calls=%async_computation.2 | async-start | bytes 2097152 | tf_op jit(solution)/shard_map/all_to_all | solution.py:260
  151.6 2.6 %mul.181 = f32[16,32,16,64]{3,2,1,0:T(8,128)} broadcast(f32[16,32,16]{2,1,0:T(8,128)S(1)} %copy.70), dimensions={0,1,2} | broadcast | bytes 2129920 | tf_op jit(solution)/shard_map/mul | solution.py:272
  154.2 3.5 %mul.182 = f32[16,32,1024]{2,1,0:T(8,128)S(1)} reshape(f32[16,32,16,64]{3,2,1,0:T(8,128)} %mul.181) | data formatting | bytes 4194304 | tf_op jit(solution)/shard_map/mul | solution.py:272
  157.7 9.4 %all-to-all-done.2 = bf16[16,32,1024]{2,1,0:T(8,128)(2,1)} async-done(((bf16[16,32,1024]{2,1,0:T(8,128)(2,1)}), bf16[16,32,1024]{2,1,0:T(8,128)(2,1)}, u32[]{:S(2)}, u32[]{:S(2)}) %all-to-all-start.2) | async-done | bytes 1048608 | tf_op jit(solution)/shard_map/all_to_all | solution.py:260
  168.9 2.9 %convert_reduce_fusion.1 = f32[32,2048]{1,0:T(8,128)S(1)} fusion(bf16[16,64,2048]{2,1,0:T(8,128)(2,1)} %bitcast.138, bf16[16,32,64]{2,0,1:T(8,128)(2,1)S(1)} %fusion.48), kind=kOutput, calls=%fused_computation.6 | convolution fusion | flops 137297920 | bytes 4521984 | tf_op jit(solution)/shard_map/grk,gkd->grd/dot_general | solution.py:277
  172.4 30.9 %all_to_all.30 = bf16[16,32,2048]{2,1,0:T(8,128)(2,1)S(1)} all-to-all(bf16[16,32,2048]{2,1,0:T(8,128)(2,1)S(1)} %broadcast_in_dim.32), channel_id=1, replica_groups=mesh['dp'=16,'tensor'=16] {'tensor'}, dimensions={0} | all-to-all | bytes 4194304 | tf_op jit(solution)/shard_map/all_to_all | solution.py:89
  205.0 5.0 %convolution_convert_fusion = bf16[512,2048]{1,0:T(8,128)(2,1)} fusion(bf16[320,2048]{1,0:T(8,128)(2,1)S(1)} %copy-done, bf16[512,2048]{1,0:T(8,128)(2,1)S(1)} %bitcast.144, bf16[2,2048,320]{1,2,0:T(8,128)(2,1)} %param.18, f32[512,320]{0,1:T(8,128)} %fusion.9), kind=kOutput, calls=%fused_computation.9 | convolution fusion | flops 1344208896 | bytes 7471104 | tf_op jit(solution)/shard_map/dot_general | solution.py:290
  210.0 31.7 %all_to_all.31 = bf16[16,32,2048]{2,1,0:T(8,128)(2,1)S(1)} all-to-all(bf16[16,32,2048]{2,1,0:T(8,128)(2,1)} %bitcast.145), channel_id=1, replica_groups=mesh['dp'=16,'tensor'=16] {'tensor'}, dimensions={0} | all-to-all | bytes 4194304 | tf_op jit(solution)/shard_map/all_to_all | solution.py:96
  (107 shorter events, 52.8 us)
Async XLA Ops:
  6.5 198.5 %copy-start = (bf16[320,2048]{1,0:T(8,128)(2,1)S(1)}, bf16[320,2048]{1,0:T(8,128)(2,1)}, u32[]{:S(2)}) copy-start(bf16[320,2048]{1,0:T(8,128)(2,1)} %param.19) | copy-start | bytes 3932164
  6.5 20.2 %collective-permute-start = (bf16[256,512]{1,0:T(8,128)(2,1)}, bf16[256,512]{1,0:T(8,128)(2,1)}, u32[]{:S(2)}, u32[]{:S(2)}) collective-permute-start(bf16[256,512]{1,0:T(8,128)(2,1)} %param.13), channel_id=1, source_target_pairs={{0,224},{16,240},{32,0},{48,16},{64,32},{80,48},{96,64},{112,80},{... | collective-permute-start | bytes 786440 | tf_op jit(solution)/shard_map/ppermute | solution.py:131
  10.7 19.3 %collective-permute-start.3 = (bf16[256,512]{1,0:T(8,128)(2,1)}, bf16[256,512]{1,0:T(8,128)(2,1)}, u32[]{:S(2)}, u32[]{:S(2)}) collective-permute-start(bf16[256,512]{1,0:T(8,128)(2,1)} %param.13), channel_id=1, source_target_pairs={{0,32},{16,48},{32,64},{48,80},{64,96},{80,112},{96,128},{112,144}... | collective-permute-start | bytes 786440 | tf_op jit(solution)/shard_map/ppermute | solution.py:128
  14.3 9.6 %copy-start.9 = (s32[1,8]{1,0:T(1,128)S(1)}, s32[1,8]{1,0:T(1,128)}, u32[]{:S(2)}) copy-start(s32[1,8]{1,0:T(1,128)} %param.11) | copy-start | bytes 100
  14.3 52.1 %all-to-all-start = ((bf16[16,32,2048]{2,1,0:T(8,128)(2,1)}), bf16[16,32,2048]{2,1,0:T(8,128)(2,1)S(1)}, u32[]{:S(2)}, u32[]{:S(2)}) async-start(bf16[16,32,2048]{2,1,0:T(8,128)(2,1)} %broadcast_in_dim.25), calls=%async_computation | async-start | bytes 4194304 | tf_op jit(solution)/shard_map/all_to_all | solution.py:89
  21.5 17.0 %copy-start.7 = (s32[16]{0:T(128)S(1)}, s32[16]{0:T(128)}, u32[]{:S(2)}) copy-start(s32[16]{0:T(128)} %param.12) | copy-start | bytes 196
  21.5 147.4 %all-gather.2.cloned.1.call-start = ((), (), s32[]{:S(2)}) async-start(), calls=%async_computation.6 | async-start | bytes 4456448 | tf_op jit(solution)/shard_map/all_gather | solution.py:176
  26.8 19.5 %collective-permute-start.1 = (bf16[256,512]{1,0:T(8,128)(2,1)}, bf16[256,512]{1,0:T(8,128)(2,1)}, u32[]{:S(2)}, u32[]{:S(2)}) collective-permute-start(bf16[256,512]{1,0:T(8,128)(2,1)} %collective-permute-done), channel_id=1, source_target_pairs={{0,224},{16,240},{32,0},{48,16},{64,32},{80,48},{96,64},{112,80},{... | collective-permute-start | bytes 786440 | tf_op jit(solution)/shard_map/ppermute | solution.py:131
  30.0 8.5 %collective-permute-start.4 = (bf16[256,512]{1,0:T(8,128)(2,1)}, bf16[256,512]{1,0:T(8,128)(2,1)}, u32[]{:S(2)}, u32[]{:S(2)}) collective-permute-start(bf16[256,512]{1,0:T(8,128)(2,1)} %collective-permute-done.3), channel_id=1, source_target_pairs={{0,32},{16,48},{32,64},{48,80},{64,96},{80,112},{96,128},{112,144}... | collective-permute-start | bytes 786440 | tf_op jit(solution)/shard_map/ppermute | solution.py:128
  38.5 12.7 %collective-permute-start.5 = (bf16[256,512]{1,0:T(8,128)(2,1)}, bf16[256,512]{1,0:T(8,128)(2,1)}, u32[]{:S(2)}, u32[]{:S(2)}) collective-permute-start(bf16[256,512]{1,0:T(8,128)(2,1)} %collective-permute-done.4), channel_id=1, source_target_pairs={{0,32},{16,48},{32,64},{48,80},{64,96},{80,112},{96,128},{112,144}... | collective-permute-start | bytes 786440 | tf_op jit(solution)/shard_map/ppermute | solution.py:128
  46.3 7.4 %collective-permute-start.2 = (bf16[256,512]{1,0:T(8,128)(2,1)}, bf16[256,512]{1,0:T(8,128)(2,1)S(1)}, u32[]{:S(2)}, u32[]{:S(2)}) collective-permute-start(bf16[256,512]{1,0:T(8,128)(2,1)} %collective-permute-done.1), channel_id=1, source_target_pairs={{0,224},{16,240},{32,0},{48,16},{64,32},{80,48},{96,64},{112,80},{... | collective-permute-start | bytes 786440 | tf_op jit(solution)/shard_map/ppermute | solution.py:131
  51.2 7.8 %collective-permute-start.6 = (bf16[256,512]{1,0:T(8,128)(2,1)}, bf16[256,512]{1,0:T(8,128)(2,1)S(1)}, u32[]{:S(2)}, u32[]{:S(2)}) collective-permute-start(bf16[256,512]{1,0:T(8,128)(2,1)} %collective-permute-done.5), channel_id=1, source_target_pairs={{0,32},{16,48},{32,64},{48,80},{64,96},{80,112},{96,128},{112,144}... | collective-permute-start | bytes 786440 | tf_op jit(solution)/shard_map/ppermute | solution.py:128
  66.4 11.5 %collective-permute-start.7 = (bf16[256,512]{1,0:T(8,128)(2,1)}, bf16[256,512]{1,0:T(8,128)(2,1)}, u32[]{:S(2)}, u32[]{:S(2)}) collective-permute-start(bf16[256,512]{1,0:T(8,128)(2,1)} %dynamic-slice_bitcast_fusion), channel_id=1, source_target_pairs={{0,16},{16,0},{32,48},{48,32},{64,80},{80,64},{96,112},{112,96},{1... | collective-permute-start | bytes 786440 | tf_op jit(solution)/shard_map/ppermute | solution.py:138
  68.9 0.8 copy-start.4
  70.8 30.1 %all-to-all-start.1 = ((bf16[16,1,512,64]{2,3,1,0:T(8,128)(2,1)}), bf16[16,1,512,64]{2,3,1,0:T(8,128)(2,1)}, u32[]{:S(2)}, u32[]{:S(2)}) async-start(bf16[16,1,512,64]{2,3,1,0:T(8,128)(2,1)} %broadcast_in_dim.27), calls=%async_computation.1 | async-start | bytes 2097152 | tf_op jit(solution)/shard_map/all_to_all | solution.py:212
  82.4 0.8 copy-start.5
  87.1 19.2 %copy-start.1 = (f32[16,512,64]{1,0,2:T(8,128)}, f32[16,512,64]{1,0,2:T(8,128)S(1)}, u32[]{:S(2)}) copy-start(f32[16,512,64]{1,0,2:T(8,128)S(1)} %dynamic_update_slice.10) | copy-start | bytes 6291460
  112.8 4.9 %copy-start.6 = (f32[16,512]{1,0:T(8,128)S(1)}, f32[16,512]{1,0:T(8,128)}, u32[]{:S(2)}) copy-start(f32[16,512]{1,0:T(8,128)} %copy-done.5) | copy-start | bytes 98308
  117.6 6.1 %copy-start.3 = (bf16[256,256]{0,1:T(8,128)(2,1)S(1)}, bf16[256,256]{0,1:T(8,128)(2,1)}, u32[]{:S(2)}) copy-start(bf16[256,256]{0,1:T(8,128)(2,1)} %copy.60) | copy-start | bytes 393220
  120.2 22.3 %all-to-all-start.3 = ((f32[16,1,1024]{2,1,0:T(1,128)}), f32[16,1,1024]{2,1,0:T(1,128)S(1)}, u32[]{:S(2)}, u32[]{:S(2)}) async-start(f32[16,1,1024]{2,1,0:T(1,128)} %reshape.295), calls=%async_computation.3 | async-start | bytes 131072 | tf_op jit(solution)/shard_map/all_to_all | solution.py:264
  142.5 24.6 %all-to-all-start.2 = ((bf16[16,32,1024]{2,1,0:T(8,128)(2,1)}), bf16[16,32,1024]{2,1,0:T(8,128)(2,1)}, u32[]{:S(2)}, u32[]{:S(2)}) async-start(bf16[16,32,1024]{2,1,0:T(8,128)(2,1)} %reshape.289), calls=%async_computation.2 | async-start | bytes 2097152 | tf_op jit(solution)/shard_map/all_to_all | solution.py:260
  168.9 3.0 %copy-start.2 = (bf16[32,2048]{1,0:T(8,128)(2,1)S(1)}, bf16[32,2048]{1,0:T(8,128)(2,1)}, u32[]{:S(2)}) copy-start(bf16[32,2048]{1,0:T(8,128)(2,1)} %param.10) | copy-start | bytes 393220
  172.4 30.9 %copy-start.8 = (bf16[2,2048,320]{1,2,0:T(8,128)(2,1)S(1)}, bf16[2,2048,320]{1,2,0:T(8,128)(2,1)}, u32[]{:S(2)}) copy-start(bf16[2,2048,320]{1,2,0:T(8,128)(2,1)} %param.18) | copy-start | bytes 7864324
Sparse Core Ops, SparseCore 0:
  24.8 70.8 all-gather.1

commit v7 on v3

--- a/solution.py
+++ b/solution.py
@@ -171,8 +171,8 @@
     keys_block = jnp.repeat(incoming[:, :kv_width].reshape(seg_rows, local_kv, HD), repeat_by, axis=1)
     values_block = jnp.repeat(incoming[:, kv_width:].reshape(seg_rows, local_kv, HD), repeat_by, axis=1)
 
-    normed = norm_rows(tokens)
-    segment = gather_rows(normed, "tensor")
+    group_rows = gather_rows(tokens, "tensor")
+    segment = norm_rows(group_rows)
     seg_rows = segment.shape[0]
     mapped = jnp.dot(segment, projection, preferred_element_type=jnp.float32)
     query_part = rotate(
@@ -214,20 +214,12 @@
     allowed = (request[:, None] == request[None, :]) & (indices[None, :] <= indices[:, None])
     suffix_state = softmax_block(queries, own_keys, own_values, scaling, allowed[:, None, :])
     top_score, weight, blended = merge_states(prefix_state, suffix_state)
-    attended = (blended / weight[:, :, None]).astype(jnp.bfloat16)
-    attended = lax.all_to_all(
-        attended.reshape(tensor_count, row_count, query_width), "tensor", 0, 0, tiled=True
-    )
-    feature_groups = out_full.shape[0] // query_width
-    partials = jnp.einsum(
-        "grk,gkd->grd",
-        attended,
-        out_full.reshape(feature_groups, query_width, out_full.shape[1]),
-        preferred_element_type=jnp.float32,
-    ).astype(jnp.bfloat16)
-    attn_sum = jnp.sum(partials.astype(jnp.float32), axis=0)
-    middle = (tokens.astype(jnp.float32) + attn_sum).astype(jnp.bfloat16)
-    segment = gather_rows(norm_rows(middle), "tensor")
+    attended = (blended / weight[:, :, None]).astype(jnp.bfloat16).reshape(group_tokens, query_width)
+    every_head = gather_rows(jnp.transpose(attended)[None], "tensor")
+    every_head = jnp.transpose(every_head.reshape(tensor_count * query_width, group_tokens))
+    attn_sum = jnp.dot(every_head, out_full, preferred_element_type=jnp.float32)
+    middle = (group_rows.astype(jnp.float32) + attn_sum).astype(jnp.bfloat16)
+    segment = norm_rows(middle)
     gate_value = jnp.dot(segment, gate_up_weight[0], preferred_element_type=jnp.float32)
     upward = jnp.dot(segment, gate_up_weight[1], preferred_element_type=jnp.float32)
     hidden = (jax.nn.silu(gate_value) * upward).astype(jnp.bfloat16)
@@ -235,7 +227,8 @@
         jnp.dot(hidden, down_weight, preferred_element_type=jnp.float32).astype(jnp.bfloat16),
         "tensor",
     )
-    return (middle.astype(jnp.float32) + ffn_sum).astype(jnp.bfloat16)
+    own_middle = lax.dynamic_slice_in_dim(middle, tensor_rank * row_count, row_count, 0)
+    return (own_middle.astype(jnp.float32) + ffn_sum).astype(jnp.bfloat16)
 
 
 def solution(mesh):

time: 193 us -> 188 us (0.974); the launches traced: 191 us -> 184 us
  blocking collectives: 72.8 us -> 20.3 us
  waiting for transfers between devices: 34.5 us -> 54.7 us
  local copies, waits for them, and re-layouts: 15.7 us -> 34.1 us
  starting transfers between devices: 25 us -> 28.7 us
    all_to_all x2 -> x0, blocking collectives: 41.3 us -> none  [the longest x1 30 us: sum_scatter_rows(): received = lax.all_to_all(parts, axis, 0, 0, tiled=True)]
    all_to_all x0 -> x1, waiting for transfers between devices: none -> 29.6 us  [sum_scatter_rows(): received = lax.all_to_all(parts, axis, 0, 0, tiled=True)]
    all_to_all x1, blocking collectives: 31.5 us -> 20.3 us  [gather_rows(): received = lax.all_to_all(copies, axis, 0, 0, tiled=True)]
    all_to_all x1, waiting for transfers between devices: 23.1 us -> 13.5 us  [on_device(): incoming = lax.all_to_all(outgoing, 'tensor', 0, 0, tiled=True)]
    unnamed x30 -> x32, local copies, waits for them, and re-layouts: 7.37 us -> 15.4 us
    all_to_all x0 -> x1, starting transfers between devices: none -> 3.72 us  [sum_scatter_rows(): received = lax.all_to_all(parts, axis, 0, 0, tiled=True)]
    dot_general x1, matrix products: 2.93 us -> 5.42 us  [on_device(): attn_sum = jnp.dot(every_head, out_full, preferred_element_type=jnp.float32)]
    dynamic_slice x2, local copies, waits for them, and re-layouts: 1.2 us -> 3.66 us  [fetch_slot(): lax.dynamic_index_in_dim(held, (slot_wanted // CORES - chip) % chips, 0,...]
  transfers between devices with their start and end apart: 11 -> 12, of which waited for: 4 -> 5; matrix products, arithmetic and copies ran while one was open for 15% -> 24% of each run, Pallas kernels for 0% -> 0%
where the time goes in v7:
time: 188 us; the launch traced here: 184 us
  waiting for transfers between devices  54.7 us (29%)
  local copies, waits for them, and re-layouts  34.1 us (18%)
  starting transfers between devices  28.7 us (15%)
  blocking collectives  20.3 us (11%)
  matrix products  19 us (10%)
  between operations  18.9 us (10%)
  other arithmetic  8.67 us (5%)
    all_to_all x1, waiting for transfers between devices, sum_scatter_rows(): received = lax.all_to_all(parts, axis, 0, 0, tiled=True)  29.6 us
    all_to_all x1, blocking collectives, gather_rows(): received = lax.all_to_all(copies, axis, 0, 0, tiled=True)  20.3 us
    unnamed x32, local copies, waits for them, and re-layouts  15.4 us
    all_to_all x1, waiting for transfers between devices, on_device(): incoming = lax.all_to_all(outgoing, 'tensor', 0, 0, tiled=True)  13.5 us
    ppermute x3, starting transfers between devices, fetch_slot(): behind = lax.ppermute(behind, 'dp', backward)  10.7 us
    ppermute x4, waiting for transfers between devices, fetch_slot(): ahead = lax.ppermute(ahead, 'dp', onward)  10.1 us
    all_to_all x1, starting transfers between devices, gather_rows(): received = lax.all_to_all(copies, axis, 0, 0, tiled=True)  7.17 us
    all_to_all x1, starting transfers between devices, on_device(): incoming = lax.all_to_all(outgoing, 'tensor', 0, 0, tiled=True)  7 us
  transfers between devices with their start and end apart: 12, of which 5 were waited for; matrix products, arithmetic and copies ran while one was open for 24% of the time, Pallas kernels for 0%

profile of v7, /device:TPU:0, one launch (start us, length us, event | category | flops | bytes accessed | tf_op | source)
XLA Modules:
  0.0 184.4 jit_solution(6661655316693052435)
XLA Ops:
  6.5 4.1 %collective-permute-start = (bf16[256,512]{1,0:T(8,128)(2,1)}, bf16[256,512]{1,0:T(8,128)(2,1)}, u32[]{:S(2)}, u32[]{:S(2)}) collective-permute-start(bf16[256,512]{1,0:T(8,128)(2,1)} %param.13), channel_id=1, source_target_pairs={{0,224},{16,240},{32,0},{48,16},{64,32},{80,48},{96,64},{112,80},{... | collective-permute-start | bytes 786440 | tf_op jit(solution)/shard_map/ppermute | solution.py:118
  10.7 2.5 %broadcast_in_dim.31 = bf16[16,32,2048]{2,1,0:T(8,128)(2,1)} broadcast(bf16[32,2048]{1,0:T(8,128)(2,1)} %param.10), dimensions={1,2} | broadcast | bytes 2228224 | tf_op jit(solution)/shard_map/broadcast_in_dim | solution.py:88
  13.1 7.2 %all-to-all-start = ((bf16[16,32,2048]{2,1,0:T(8,128)(2,1)}), bf16[16,32,2048]{2,1,0:T(8,128)(2,1)S(1)}, u32[]{:S(2)}, u32[]{:S(2)}) async-start(bf16[16,32,2048]{2,1,0:T(8,128)(2,1)} %broadcast_in_dim.31), calls=%async_computation | async-start | bytes 4194304 | tf_op jit(solution)/shard_map/all_to_all | solution.py:89
  23.1 3.3 %collective-permute-start.1 = (bf16[256,512]{1,0:T(8,128)(2,1)}, bf16[256,512]{1,0:T(8,128)(2,1)}, u32[]{:S(2)}, u32[]{:S(2)}) collective-permute-start(bf16[256,512]{1,0:T(8,128)(2,1)} %collective-permute-done), channel_id=1, source_target_pairs={{0,224},{16,240},{32,0},{48,16},{64,32},{80,48},{96,64},{112,80},{... | collective-permute-start | bytes 786440 | tf_op jit(solution)/shard_map/ppermute | solution.py:118
  26.5 5.6 %collective-permute-done.4 = bf16[256,512]{1,0:T(8,128)(2,1)} collective-permute-done((bf16[256,512]{1,0:T(8,128)(2,1)}, bf16[256,512]{1,0:T(8,128)(2,1)}, u32[]{:S(2)}, u32[]{:S(2)}) %collective-permute-start.4) | collective-permute-done | bytes 262176 | tf_op jit(solution)/shard_map/ppermute | solution.py:115
  38.0 3.3 %collective-permute-start.2 = (bf16[256,512]{1,0:T(8,128)(2,1)}, bf16[256,512]{1,0:T(8,128)(2,1)S(1)}, u32[]{:S(2)}, u32[]{:S(2)}) collective-permute-start(bf16[256,512]{1,0:T(8,128)(2,1)} %collective-permute-done.1), channel_id=1, source_target_pairs={{0,224},{16,240},{32,0},{48,16},{64,32},{80,48},{96,64},{112,80},{... | collective-permute-start | bytes 786440 | tf_op jit(solution)/shard_map/ppermute | solution.py:118
  46.2 4.5 %collective-permute-done.6 = bf16[256,512]{1,0:T(8,128)(2,1)S(1)} collective-permute-done((bf16[256,512]{1,0:T(8,128)(2,1)}, bf16[256,512]{1,0:T(8,128)(2,1)S(1)}, u32[]{:S(2)}, u32[]{:S(2)}) %collective-permute-start.6) | collective-permute-done | bytes 262176 | tf_op jit(solution)/shard_map/ppermute | solution.py:115
  56.5 1.9 %constant_dynamic-slice_fusion.3 = (bf16[1,256,512]{2,1,0:T(8,128)(2,1)}, bf16[1,256,512]{2,1,0:T(8,128)(2,1)}) fusion(bf16[8,256,512]{2,1,0:T(8,128)(2,1)} %bitcast_dynamic-update-slice_fusion, s32[]{:T(128)S(6)} %select_n.116, s32[]{:T(128)S(6)} %select_n.120), kind=kLoop, calls=%fused_computation.125 | loop fusion | bytes 1048584 | tf_op jit(solution)/shard_map/jit(dynamic_index_in_dim)/dynamic_slice | solution.py:123
  58.4 1.8 copy.22
  60.2 1.9 %copy.25 = bf16[2048,64]{1,0:T(8,128)(2,1)} copy(bf16[2048,64]{0,1:T(8,128)(2,1)} %param.14) | data formatting | bytes 524288 | tf_op args[4]
  62.2 2.6 %constant_dynamic-slice_fusion = (bf16[2048,64]{1,0:T(8,128)(2,1)}, bf16[2048,64]{1,0:T(8,128)(2,1)}) fusion(bf16[2048,256]{1,0:T(8,128)(2,1)} %param.16, s32[]{:T(128)S(6)} %select_n.126, bf16[2048,256]{1,0:T(8,128)(2,1)} %param.15), kind=kLoop, calls=%fused_computation.122 | loop fusion | bytes 1048580 | tf_op jit(solution)/shard_map/dynamic_slice | solution.py:158
  64.8 1.8 copy.21
  68.3 2.6 %gather_fusion = bf16[16,256,128]{1,2,0:T(8,128)(2,1)} fusion(bf16[4,256,128]{1,2,0:T(8,128)(2,1)} %bitcast.147, s32[1024]{0:T(1024)S(1)} %pad_clamp_fusion), kind=kCustom, calls=%fused_computation | custom fusion | bytes 2097216 | tf_op jit(solution)/shard_map/jit(_take)/gather | solution.py:167
  70.9 2.4 %broadcast_select_fusion = bf16[16,256,128]{1,2,0:T(8,128)(2,1)} fusion(bf16[16,256,128]{1,2,0:T(8,128)(2,1)} %gather_fusion, pred[16]{0:T(512)(128)(4,1)S(1)} %compare_and_fusion), kind=kLoop, calls=%fused_computation.52 | loop fusion | flops 524288 | bytes 2097168 | tf_op jit(solution)/shard_map/jit(_take)/select_n | solution.py:167
  73.3 7.0 %all-to-all-start.1 = ((bf16[16,256,128]{1,2,0:T(8,128)(2,1)}), bf16[16,256,128]{1,2,0:T(8,128)(2,1)}, u32[]{:S(2)}, u32[]{:S(2)}) async-start(bf16[16,256,128]{1,2,0:T(8,128)(2,1)} %broadcast_select_fusion), calls=%async_computation.1 | async-start | bytes 2097152 | tf_op jit(solution)/shard_map/all_to_all | solution.py:168
  85.8 13.5 %all-to-all-done.1 = bf16[16,256,128]{1,2,0:T(8,128)(2,1)} async-done(((bf16[16,256,128]{1,2,0:T(8,128)(2,1)}), bf16[16,256,128]{1,2,0:T(8,128)(2,1)}, u32[]{:S(2)}, u32[]{:S(2)}) %all-to-all-start.1) | async-done | bytes 1048608 | tf_op jit(solution)/shard_map/all_to_all | solution.py:168
  99.2 2.3 %copy.24 = bf16[16,256,128]{2,1,0:T(8,128)(2,1)} copy(bf16[16,256,128]{1,2,0:T(8,128)(2,1)} %all-to-all-done.1) | data formatting | bytes 2097152 | tf_op jit(solution)/shard_map/all_to_all | solution.py:168
  101.5 2.5 %multiply_reduce_fusion = (f32[512]{0:T(512)S(1)}, f32[4096,512]{1,0:T(8,128)S(1)}) fusion(bf16[512,1,32]{0,2,1:T(8,128)(2,1)S(1)} %get-tuple-element.16, bf16[512,1,32]{0,2,1:T(8,128)(2,1)S(1)} %get-tuple-element.17, bf16[4096,128]{1,0:T(8,128)(2,1)} %bitcast.145), kind=kOutput, calls=%fused_computation.3 | convolution fusion | flops 272760320 | bytes 9504768 | tf_op jit(solution)/shard_map/thd,nhd->thn/dot_general | solution.py:56
  105.5 1.8 fusion.37
  108.6 20.3 %all_to_all.20 = bf16[16,1,64,512]{3,2,1,0:T(8,128)(2,1)} all-to-all(bf16[16,1,64,512]{3,2,1,0:T(8,128)(2,1)S(1)} %broadcast_in_dim.38), channel_id=1, replica_groups=mesh['dp'=16,'tensor'=16] {'tensor'}, dimensions={0} | all-to-all | bytes 2097152 | tf_op jit(solution)/shard_map/all_to_all | solution.py:89
  128.9 5.4 %fusion.3 = (f32[512]{0:T(512)S(1)}, bf16[512,2048]{1,0:T(8,128)(2,1)S(1)}) fusion(bf16[1024,512]{1,0:T(8,128)(2,1)} %bitcast.149, bf16[1024,2048]{1,0:T(8,128)(2,1)} %all-gather.2.cloned.1.call-done, bf16[16,32,2048]{2,1,0:T(8,128)(2,1)S(1)} %all-to-all-done), kind=kOutput, calls=%fused_computation.8 | convolution fusion | flops 2153774592 | bytes 9439232 | tf_op jit(solution)/shard_map/dot_general | solution.py:220
  136.8 5.5 %convolution_convert_fusion = bf16[512,2048]{1,0:T(8,128)(2,1)} fusion(bf16[320,2048]{1,0:T(8,128)(2,1)S(1)} %copy-done, bf16[2,2048,320]{1,2,0:T(8,128)(2,1)} %param.18, bf16[512,2048]{1,0:T(8,128)(2,1)} %copy-done.8, f32[512]{0:T(512)S(1)} %add_rsqrt_fusion.1, f32[512,320]{0,1:T(8,128)S(1)} %fusion.14), kind=kOutput, calls=%fused_computation.19 | convolution fusion | flops 1347354624 | bytes 7473152 | tf_op jit(solution)/shard_map/dot_general | solution.py:227
  142.2 3.7 %all-to-all-start.3 = ((bf16[16,32,2048]{2,1,0:T(8,128)(2,1)}), bf16[16,32,2048]{2,1,0:T(8,128)(2,1)S(1)}, u32[]{:S(2)}, u32[]{:S(2)}) async-start(bf16[16,32,2048]{2,1,0:T(8,128)(2,1)} %bitcast.148), calls=%async_computation.3 | async-start | bytes 4194304 | tf_op jit(solution)/shard_map/all_to_all | solution.py:96
  146.0 29.6 %all-to-all-done.3 = bf16[16,32,2048]{2,1,0:T(8,128)(2,1)S(1)} async-done(((bf16[16,32,2048]{2,1,0:T(8,128)(2,1)}), bf16[16,32,2048]{2,1,0:T(8,128)(2,1)S(1)}, u32[]{:S(2)}, u32[]{:S(2)}) %all-to-all-start.3) | async-done | bytes 2097184 | tf_op jit(solution)/shard_map/all_to_all | solution.py:96
  (76 shorter events, 28.5 us)
Async XLA Ops:
  6.5 130.2 %copy-start = (bf16[320,2048]{1,0:T(8,128)(2,1)S(1)}, bf16[320,2048]{1,0:T(8,128)(2,1)}, u32[]{:S(2)}) copy-start(bf16[320,2048]{1,0:T(8,128)(2,1)} %param.19) | copy-start | bytes 3932164
  6.5 16.6 %collective-permute-start = (bf16[256,512]{1,0:T(8,128)(2,1)}, bf16[256,512]{1,0:T(8,128)(2,1)}, u32[]{:S(2)}, u32[]{:S(2)}) collective-permute-start(bf16[256,512]{1,0:T(8,128)(2,1)} %param.13), channel_id=1, source_target_pairs={{0,224},{16,240},{32,0},{48,16},{64,32},{80,48},{96,64},{112,80},{... | collective-permute-start | bytes 786440 | tf_op jit(solution)/shard_map/ppermute | solution.py:118
  10.7 12.4 %collective-permute-start.3 = (bf16[256,512]{1,0:T(8,128)(2,1)}, bf16[256,512]{1,0:T(8,128)(2,1)}, u32[]{:S(2)}, u32[]{:S(2)}) collective-permute-start(bf16[256,512]{1,0:T(8,128)(2,1)} %param.13), channel_id=1, source_target_pairs={{0,32},{16,48},{32,64},{48,80},{64,96},{80,112},{96,128},{112,144}... | collective-permute-start | bytes 786440 | tf_op jit(solution)/shard_map/ppermute | solution.py:115
  13.1 9.6 %copy-start.11 = (s32[1,8]{1,0:T(1,128)S(1)}, s32[1,8]{1,0:T(1,128)}, u32[]{:S(2)}) copy-start(s32[1,8]{1,0:T(1,128)} %param.11) | copy-start | bytes 100
  13.1 19.0 %copy-start.9 = (s32[16]{0:T(128)S(1)}, s32[16]{0:T(128)}, u32[]{:S(2)}) copy-start(s32[16]{0:T(128)} %param.12) | copy-start | bytes 196
  13.1 60.2 %all-to-all-start = ((bf16[16,32,2048]{2,1,0:T(8,128)(2,1)}), bf16[16,32,2048]{2,1,0:T(8,128)(2,1)S(1)}, u32[]{:S(2)}, u32[]{:S(2)}) async-start(bf16[16,32,2048]{2,1,0:T(8,128)(2,1)} %broadcast_in_dim.31), calls=%async_computation | async-start | bytes 4194304 | tf_op jit(solution)/shard_map/all_to_all | solution.py:89
  20.3 108.6 %all-gather.2.cloned.1.call-start = ((), (), s32[]{:S(2)}) async-start(), calls=%async_computation.4 | async-start | bytes 4456448 | tf_op jit(solution)/shard_map/all_gather | solution.py:163
  23.0 9.1 %collective-permute-start.4 = (bf16[256,512]{1,0:T(8,128)(2,1)}, bf16[256,512]{1,0:T(8,128)(2,1)}, u32[]{:S(2)}, u32[]{:S(2)}) collective-permute-start(bf16[256,512]{1,0:T(8,128)(2,1)} %collective-permute-done.3), channel_id=1, source_target_pairs={{0,32},{16,48},{32,64},{48,80},{64,96},{80,112},{96,128},{112,144}... | collective-permute-start | bytes 786440 | tf_op jit(solution)/shard_map/ppermute | solution.py:115
  23.1 14.8 %collective-permute-start.1 = (bf16[256,512]{1,0:T(8,128)(2,1)}, bf16[256,512]{1,0:T(8,128)(2,1)}, u32[]{:S(2)}, u32[]{:S(2)}) collective-permute-start(bf16[256,512]{1,0:T(8,128)(2,1)} %collective-permute-done), channel_id=1, source_target_pairs={{0,224},{16,240},{32,0},{48,16},{64,32},{80,48},{96,64},{112,80},{... | collective-permute-start | bytes 786440 | tf_op jit(solution)/shard_map/ppermute | solution.py:118
  32.1 10.8 %collective-permute-start.5 = (bf16[256,512]{1,0:T(8,128)(2,1)}, bf16[256,512]{1,0:T(8,128)(2,1)}, u32[]{:S(2)}, u32[]{:S(2)}) collective-permute-start(bf16[256,512]{1,0:T(8,128)(2,1)} %collective-permute-done.4), channel_id=1, source_target_pairs={{0,32},{16,48},{32,64},{48,80},{64,96},{80,112},{96,128},{112,144}... | collective-permute-start | bytes 786440 | tf_op jit(solution)/shard_map/ppermute | solution.py:115
  38.0 7.5 %collective-permute-start.2 = (bf16[256,512]{1,0:T(8,128)(2,1)}, bf16[256,512]{1,0:T(8,128)(2,1)S(1)}, u32[]{:S(2)}, u32[]{:S(2)}) collective-permute-start(bf16[256,512]{1,0:T(8,128)(2,1)} %collective-permute-done.1), channel_id=1, source_target_pairs={{0,224},{16,240},{32,0},{48,16},{64,32},{80,48},{96,64},{112,80},{... | collective-permute-start | bytes 786440 | tf_op jit(solution)/shard_map/ppermute | solution.py:118
  42.9 7.8 %collective-permute-start.6 = (bf16[256,512]{1,0:T(8,128)(2,1)}, bf16[256,512]{1,0:T(8,128)(2,1)S(1)}, u32[]{:S(2)}, u32[]{:S(2)}) collective-permute-start(bf16[256,512]{1,0:T(8,128)(2,1)} %collective-permute-done.5), channel_id=1, source_target_pairs={{0,32},{16,48},{32,64},{48,80},{64,96},{80,112},{96,128},{112,144}... | collective-permute-start | bytes 786440 | tf_op jit(solution)/shard_map/ppermute | solution.py:115
  60.2 6.4 %collective-permute-start.7 = (bf16[256,512]{0,1:T(8,128)(2,1)}, bf16[256,512]{0,1:T(8,128)(2,1)}, u32[]{:S(2)}, u32[]{:S(2)}) collective-permute-start(bf16[256,512]{0,1:T(8,128)(2,1)} %bitcast.151), channel_id=1, source_target_pairs={{0,16},{16,0},{32,48},{48,32},{64,80},{80,64},{96,112},{112,96},{1... | collective-permute-start | bytes 786440 | tf_op jit(solution)/shard_map/ppermute | solution.py:125
  73.3 25.9 %all-to-all-start.1 = ((bf16[16,256,128]{1,2,0:T(8,128)(2,1)}), bf16[16,256,128]{1,2,0:T(8,128)(2,1)}, u32[]{:S(2)}, u32[]{:S(2)}) async-start(bf16[16,256,128]{1,2,0:T(8,128)(2,1)} %broadcast_select_fusion), calls=%async_computation.1 | async-start | bytes 2097152 | tf_op jit(solution)/shard_map/all_to_all | solution.py:168
  80.9 1.0 copy-start.4
  80.9 1.2 copy-start.5
  80.9 1.4 copy-start.6
  83.4 0.7 copy-start.7
  84.5 1.0 copy-start.2
  104.0 1.5 copy-start.1
  105.4 1.8 copy-start.3
  128.9 6.8 %copy-start.10 = (bf16[2,2048,320]{1,2,0:T(8,128)(2,1)S(1)}, bf16[2,2048,320]{1,2,0:T(8,128)(2,1)}, u32[]{:S(2)}) copy-start(bf16[2,2048,320]{1,2,0:T(8,128)(2,1)} %param.18) | copy-start | bytes 7864324
  134.4 1.4 copy-start.8
  142.2 33.3 %all-to-all-start.3 = ((bf16[16,32,2048]{2,1,0:T(8,128)(2,1)}), bf16[16,32,2048]{2,1,0:T(8,128)(2,1)S(1)}, u32[]{:S(2)}, u32[]{:S(2)}) async-start(bf16[16,32,2048]{2,1,0:T(8,128)(2,1)} %bitcast.148), calls=%async_computation.3 | async-start | bytes 4194304 | tf_op jit(solution)/shard_map/all_to_all | solution.py:96
Sparse Core Ops, SparseCore 0:
  23.6 61.0 all-gather.1

commit v8 on v7

--- a/solution.py
+++ b/solution.py
@@ -105,23 +105,24 @@
     chips = group_count // CORES
     chip = group_rank // CORES
     core = group_rank % CORES
+    slot_wanted = group_prefix[group_rank]
+    partner_slot = group_prefix[group_rank ^ 1]
+    mine_at = (slot_wanted // CORES - chip) % chips
+    theirs_at = (partner_slot // CORES - chip) % chips
     onward = [(i, (i + CORES) % group_count) for i in range(group_count)]
     backward = [(i, (i - CORES) % group_count) for i in range(group_count)]
-    held = [None] * chips
-    held[0] = prefix_cache
+    mine = prefix_cache
+    theirs = prefix_cache
     ahead = prefix_cache
     behind = prefix_cache
     for step in range(1, chips // 2 + 1):
         ahead = lax.ppermute(ahead, "dp", onward)
-        held[(chips - step) % chips] = ahead
+        mine = jnp.where(mine_at == (chips - step) % chips, ahead, mine)
+        theirs = jnp.where(theirs_at == (chips - step) % chips, ahead, theirs)
         if step < chips - step:
             behind = lax.ppermute(behind, "dp", backward)
-            held[step] = behind
-    held = jnp.stack(held)
-    slot_wanted = group_prefix[group_rank]
-    partner_slot = group_prefix[group_rank ^ 1]
-    mine = lax.dynamic_index_in_dim(held, (slot_wanted // CORES - chip) % chips, 0, keepdims=False)
-    theirs = lax.dynamic_index_in_dim(held, (partner_slot // CORES - chip) % chips, 0, keepdims=False)
+            mine = jnp.where(mine_at == step, behind, mine)
+            theirs = jnp.where(theirs_at == step, behind, theirs)
     swapped = lax.ppermute(theirs, "dp", [(i, i ^ 1) for i in range(group_count)])
     return jnp.where(slot_wanted % CORES == core, mine, swapped)
 
@@ -159,12 +160,12 @@
     projection = jnp.concatenate([query_weight, key_cols, value_cols], axis=1)
 
     shard_rows = prefix_cache.shape[0]
-    chosen = fetch_slot(prefix_cache, group_prefix, group_rank)
+    kv_groups = KVH // local_kv
+    by_head = prefix_cache.reshape(shard_rows, 2, kv_groups, kv_width)
+    by_head = jnp.transpose(by_head, (2, 0, 1, 3)).reshape(kv_groups, shard_rows, 2 * kv_width)
+    chosen = fetch_slot(by_head, group_prefix, group_rank)
     out_full = lax.all_gather(out_weight, "tensor", axis=0, tiled=True)
-    by_head = chosen.reshape(shard_rows, 2, KVH // local_kv, kv_width)
-    by_head = jnp.transpose(by_head, (2, 0, 1, 3)).reshape(KVH // local_kv, shard_rows, 2 * kv_width)
-    wanted_by = (jnp.arange(tensor_count) * local_heads // head_ratio) // local_kv
-    outgoing = jnp.take(by_head, wanted_by, axis=0)
+    outgoing = jnp.repeat(chosen, tensor_count // kv_groups, axis=0)
     incoming = lax.all_to_all(outgoing, "tensor", 0, 0, tiled=True)
     seg_rows = tensor_count * shard_rows
     incoming = incoming.reshape(seg_rows, 2 * kv_width)

time: 188 us -> 182 us (0.968); the launches traced: 184 us -> 180 us
  local copies, waits for them, and re-layouts: 34.1 us -> 17.2 us
  waiting for transfers between devices: 54.7 us -> 65.2 us
    ppermute x3, waiting for transfers between devices: 0.86 us -> 10.9 us  [fetch_slot(): behind = lax.ppermute(behind, 'dp', backward)]
    unnamed x32 -> x24, local copies, waits for them, and re-layouts: 15.4 us -> 6.75 us
    all_to_all x1, waiting for transfers between devices: 13.5 us -> 20 us  [on_device(): incoming = lax.all_to_all(outgoing, 'tensor', 0, 0, tiled=True)]
    ppermute x4, waiting for transfers between devices: 10.1 us -> 3.7 us  [fetch_slot(): ahead = lax.ppermute(ahead, 'dp', onward)]
    dynamic_slice x3 -> x0, local copies, waits for them, and re-layouts: 5.44 us -> none  [the longest x2 3.66 us: fetch_slot(): lax.dynamic_index_in_dim(held, (slot_wanted // CORES - chip) % chips, 0,...]
    gather x1 -> x0, local copies, waits for them, and re-layouts: 2.55 us -> none  [on_device(): outgoing = jnp.take(by_head, wanted_by, axis=0)]
    all_to_all x1 -> x0, local copies, waits for them, and re-layouts: 2.27 us -> none  [on_device(): incoming = lax.all_to_all(outgoing, 'tensor', 0, 0, tiled=True)]
    broadcast_in_dim x0 -> x1, local copies, waits for them, and re-layouts: none -> 2.16 us  [on_device(): outgoing = jnp.repeat(chosen, tensor_count // kv_groups, axis=0)]
  transfers between devices with their start and end apart: 12 -> 12, of which waited for: 5 -> 6; matrix products, arithmetic and copies ran while one was open for 24% -> 16% of each run, Pallas kernels for 0% -> 0%
where the time goes in v8:
time: 182 us; the launch traced here: 180 us
  waiting for transfers between devices  65.2 us (36%)
  starting transfers between devices  29.1 us (16%)
  blocking collectives  20.8 us (11%)
  matrix products  20.3 us (11%)
  between operations  18.8 us (10%)
  local copies, waits for them, and re-layouts  17.2 us (9%)
  other arithmetic  9.01 us (5%)
    all_to_all x1, waiting for transfers between devices, sum_scatter_rows(): received = lax.all_to_all(parts, axis, 0, 0, tiled=True)  29.9 us
    all_to_all x1, blocking collectives, gather_rows(): received = lax.all_to_all(copies, axis, 0, 0, tiled=True)  20.8 us
    all_to_all x1, waiting for transfers between devices, on_device(): incoming = lax.all_to_all(outgoing, 'tensor', 0, 0, tiled=True)  20 us
    ppermute x3, starting transfers between devices, fetch_slot(): behind = lax.ppermute(behind, 'dp', backward)  11.4 us
    ppermute x3, waiting for transfers between devices, fetch_slot(): behind = lax.ppermute(behind, 'dp', backward)  10.9 us
    all_to_all x1, starting transfers between devices, gather_rows(): received = lax.all_to_all(copies, axis, 0, 0, tiled=True)  7.17 us
    unnamed x24, local copies, waits for them, and re-layouts  6.75 us
    all_to_all x1, starting transfers between devices, on_device(): incoming = lax.all_to_all(outgoing, 'tensor', 0, 0, tiled=True)  6.64 us
  transfers between devices with their start and end apart: 12, of which 6 were waited for; matrix products, arithmetic and copies ran while one was open for 16% of the time, Pallas kernels for 0%

profile of v8, /device:TPU:0, one launch (start us, length us, event | category | flops | bytes accessed | tf_op | source)
XLA Modules:
  0.0 180.5 jit_solution(8126588013976371565)
XLA Ops:
  9.3 2.5 %broadcast_in_dim.23 = bf16[16,32,2048]{2,1,0:T(8,128)(2,1)} broadcast(bf16[32,2048]{1,0:T(8,128)(2,1)} %param.10), dimensions={1,2} | broadcast | bytes 2228224 | tf_op jit(solution)/shard_map/broadcast_in_dim | solution.py:88
  11.7 7.2 %all-to-all-start = ((bf16[16,32,2048]{2,1,0:T(8,128)(2,1)}), bf16[16,32,2048]{2,1,0:T(8,128)(2,1)S(1)}, u32[]{:S(2)}, u32[]{:S(2)}) async-start(bf16[16,32,2048]{2,1,0:T(8,128)(2,1)} %broadcast_in_dim.23), calls=%async_computation | async-start | bytes 4194304 | tf_op jit(solution)/shard_map/all_to_all | solution.py:89
  18.9 4.0 %collective-permute-start.4 = (bf16[4,256,128]{1,2,0:T(8,128)(2,1)}, bf16[4,256,128]{1,2,0:T(8,128)(2,1)}, u32[]{:S(2)}, u32[]{:S(2)}) collective-permute-start(bf16[4,256,128]{1,2,0:T(8,128)(2,1)} %bitcast.4), channel_id=1, source_target_pairs={{0,224},{16,240},{32,0},{48,16},{64,32},{80,48},{96,64},{112,80},{... | collective-permute-start | bytes 786440 | tf_op jit(solution)/shard_map/ppermute | solution.py:123
  23.1 5.4 %collective-permute-done.4 = bf16[4,256,128]{1,2,0:T(8,128)(2,1)} collective-permute-done((bf16[4,256,128]{1,2,0:T(8,128)(2,1)}, bf16[4,256,128]{1,2,0:T(8,128)(2,1)}, u32[]{:S(2)}, u32[]{:S(2)}) %collective-permute-start.4) | collective-permute-done | bytes 262176 | tf_op jit(solution)/shard_map/ppermute | solution.py:123
  28.5 3.7 %collective-permute-start.5 = (bf16[4,256,128]{1,2,0:T(8,128)(2,1)}, bf16[4,256,128]{1,2,0:T(8,128)(2,1)}, u32[]{:S(2)}, u32[]{:S(2)}) collective-permute-start(bf16[4,256,128]{1,2,0:T(8,128)(2,1)} %collective-permute-done.4), channel_id=1, source_target_pairs={{0,224},{16,240},{32,0},{48,16},{64,32},{80,48},{96,64},{112,80},{... | collective-permute-start | bytes 786440 | tf_op jit(solution)/shard_map/ppermute | solution.py:123
  32.3 4.6 %collective-permute-done.5 = bf16[4,256,128]{1,2,0:T(8,128)(2,1)} collective-permute-done((bf16[4,256,128]{1,2,0:T(8,128)(2,1)}, bf16[4,256,128]{1,2,0:T(8,128)(2,1)}, u32[]{:S(2)}, u32[]{:S(2)}) %collective-permute-start.5) | collective-permute-done | bytes 262176 | tf_op jit(solution)/shard_map/ppermute | solution.py:123
  36.9 3.7 %collective-permute-start.6 = (bf16[4,256,128]{1,2,0:T(8,128)(2,1)}, bf16[4,256,128]{1,2,0:T(8,128)(2,1)}, u32[]{:S(2)}, u32[]{:S(2)}) collective-permute-start(bf16[4,256,128]{1,2,0:T(8,128)(2,1)} %collective-permute-done.5), channel_id=1, source_target_pairs={{0,224},{16,240},{32,0},{48,16},{64,32},{80,48},{96,64},{112,80},{... | collective-permute-start | bytes 786440 | tf_op jit(solution)/shard_map/ppermute | solution.py:123
  44.8 3.7 %collective-permute-done.3 = bf16[4,256,128]{1,2,0:T(8,128)(2,1)} collective-permute-done((bf16[4,256,128]{1,2,0:T(8,128)(2,1)}, bf16[4,256,128]{1,2,0:T(8,128)(2,1)}, u32[]{:S(2)}, u32[]{:S(2)}) %collective-permute-start.3) | collective-permute-done | bytes 262176 | tf_op jit(solution)/shard_map/ppermute | solution.py:119
  48.5 1.8 %select_select_fusion = bf16[4,256,128]{1,2,0:T(8,128)(2,1)} fusion(bf16[4,256,128]{1,2,0:T(8,128)(2,1)} %collective-permute-done.3, bf16[4,256,128]{1,2,0:T(8,128)(2,1)} %collective-permute-done.6, bf16[4,256,128]{1,2,0:T(8,128)(2,1)} %collective-permute-done.2, bf16[4,256,128]{1,2,0:T(8,128)(2,1)} %collective-permute-done.5, ...), kind=kLoop, calls=%fused_computation.63 | loop fusion | flops 917504 | bytes 2359303 | tf_op jit(solution)/shard_map/jit(_where)/select_n | solution.py:121
  53.0 2.0 %copy.19 = bf16[2048,64]{1,0:T(8,128)(2,1)} copy(bf16[2048,64]{0,1:T(8,128)(2,1)} %param.14) | data formatting | bytes 524288 | tf_op args[4]
  55.0 2.5 %constant_dynamic-slice_fusion = (bf16[2048,64]{1,0:T(8,128)(2,1)}, bf16[2048,64]{1,0:T(8,128)(2,1)}) fusion(bf16[2048,256]{1,0:T(8,128)(2,1)} %param.16, s32[]{:T(128)S(6)} %select_n.185, bf16[2048,256]{1,0:T(8,128)(2,1)} %param.15), kind=kLoop, calls=%fused_computation.107 | loop fusion | bytes 1048580 | tf_op jit(solution)/shard_map/dynamic_slice | solution.py:159
  57.5 1.9 %select_select_fusion.1 = bf16[4,256,128]{1,2,0:T(8,128)(2,1)} fusion(bf16[4,256,128]{1,2,0:T(8,128)(2,1)} %collective-permute-done.7, bf16[4,256,128]{1,2,0:T(8,128)(2,1)} %collective-permute-done.3, bf16[4,256,128]{1,2,0:T(8,128)(2,1)} %collective-permute-done.6, bf16[4,256,128]{1,2,0:T(8,128)(2,1)} %collective-permute-done.2, ...), kind=kLoop, calls=%fused_computation.64 | loop fusion | flops 1048576 | bytes 2621448 | tf_op jit(solution)/shard_map/jit(_where)/select_n | solution.py:127
  59.5 1.8 copy.18
  61.3 2.2 %broadcast_in_dim.25 = bf16[4,4,256,128]{3,2,1,0:T(8,128)(2,1)} broadcast(bf16[4,256,128]{2,1,0:T(8,128)(2,1)} %copy.18), dimensions={0,2,3} | broadcast | bytes 1310720 | tf_op jit(solution)/shard_map/broadcast_in_dim | solution.py:168
  63.4 6.6 %all-to-all-start.1 = ((bf16[16,256,128]{2,1,0:T(8,128)(2,1)}), bf16[16,256,128]{2,1,0:T(8,128)(2,1)}, u32[]{:S(2)}, u32[]{:S(2)}) async-start(bf16[16,256,128]{2,1,0:T(8,128)(2,1)} %bitcast.127), calls=%async_computation.1 | async-start | bytes 2097152 | tf_op jit(solution)/shard_map/all_to_all | solution.py:169
  75.5 20.0 %all-to-all-done.1 = bf16[16,256,128]{2,1,0:T(8,128)(2,1)} async-done(((bf16[16,256,128]{2,1,0:T(8,128)(2,1)}), bf16[16,256,128]{2,1,0:T(8,128)(2,1)}, u32[]{:S(2)}, u32[]{:S(2)}) %all-to-all-start.1) | async-done | bytes 1048608 | tf_op jit(solution)/shard_map/all_to_all | solution.py:169
  95.5 2.5 %multiply_reduce_fusion = (f32[512]{0:T(512)S(1)}, f32[4096,512]{1,0:T(8,128)S(1)}) fusion(bf16[512,1,32]{0,2,1:T(8,128)(2,1)S(1)} %get-tuple-element.14, bf16[512,1,32]{0,2,1:T(8,128)(2,1)S(1)} %get-tuple-element.15, bf16[4096,128]{1,0:T(8,128)(2,1)} %bitcast.7), kind=kOutput, calls=%fused_computation.2 | convolution fusion | flops 272760320 | bytes 9504768 | tf_op jit(solution)/shard_map/thd,nhd->thn/dot_general | solution.py:56
  99.4 3.1 %fusion.37 = f32[1,64,512]{2,1,0:T(8,128)S(1)} fusion(f32[4096,512]{1,0:T(8,128)S(1)} %get-tuple-element.21, f32[512]{0:T(512)S(1)} %get-tuple-element.20, bf16[4096,128]{1,0:T(8,128)(2,1)} %bitcast.7, f32[512]{0:T(512)S(1)} %get-tuple-element.7, f32[512]{0:T(512)S(1)} %get-tuple-element.17, f32[512]{0:T(512)S(1)} %get-tuple-element.16), kind=kOutput, calls=%fused_computation.37 | convolution fusion | flops 274825216 | bytes 9576448 | tf_op jit(solution)/shard_map/thn,nhd->thd/dot_general | solution.py:64
  103.9 20.8 %all_to_all.20 = bf16[16,1,64,512]{3,2,1,0:T(8,128)(2,1)} all-to-all(bf16[16,1,64,512]{3,2,1,0:T(8,128)(2,1)S(1)} %broadcast_in_dim.29), channel_id=1, replica_groups=mesh['dp'=16,'tensor'=16] {'tensor'}, dimensions={0} | all-to-all | bytes 2097152 | tf_op jit(solution)/shard_map/all_to_all | solution.py:89
  124.7 5.4 %fusion.3 = (f32[512]{0:T(512)S(1)}, bf16[512,2048]{1,0:T(8,128)(2,1)S(1)}) fusion(bf16[1024,512]{1,0:T(8,128)(2,1)} %bitcast.129, bf16[1024,2048]{1,0:T(8,128)(2,1)} %all-gather.2.cloned.1.call-done, bf16[16,32,2048]{2,1,0:T(8,128)(2,1)S(1)} %all-to-all-done), kind=kOutput, calls=%fused_computation.7 | convolution fusion | flops 2153774592 | bytes 9439232 | tf_op jit(solution)/shard_map/dot_general | solution.py:221
  132.5 5.5 %convolution_convert_fusion = bf16[512,2048]{1,0:T(8,128)(2,1)} fusion(bf16[320,2048]{1,0:T(8,128)(2,1)S(1)} %copy-done, bf16[2,2048,320]{1,2,0:T(8,128)(2,1)} %param.18, bf16[512,2048]{1,0:T(8,128)(2,1)} %copy-done.7, f32[512]{0:T(512)S(1)} %add_rsqrt_fusion.1, f32[512,320]{0,1:T(8,128)S(1)} %fusion.14), kind=kOutput, calls=%fused_computation.18 | convolution fusion | flops 1347354624 | bytes 7473152 | tf_op jit(solution)/shard_map/dot_general | solution.py:228
  138.0 3.7 %all-to-all-start.3 = ((bf16[16,32,2048]{2,1,0:T(8,128)(2,1)}), bf16[16,32,2048]{2,1,0:T(8,128)(2,1)S(1)}, u32[]{:S(2)}, u32[]{:S(2)}) async-start(bf16[16,32,2048]{2,1,0:T(8,128)(2,1)} %bitcast.128), calls=%async_computation.3 | async-start | bytes 4194304 | tf_op jit(solution)/shard_map/all_to_all | solution.py:96
  141.7 29.9 %all-to-all-done.3 = bf16[16,32,2048]{2,1,0:T(8,128)(2,1)S(1)} async-done(((bf16[16,32,2048]{2,1,0:T(8,128)(2,1)}), bf16[16,32,2048]{2,1,0:T(8,128)(2,1)S(1)}, u32[]{:S(2)}, u32[]{:S(2)}) %all-to-all-start.3) | async-done | bytes 2097184 | tf_op jit(solution)/shard_map/all_to_all | solution.py:96
  172.0 1.6 add_convert_fusion
  (61 shorter events, 15.5 us)
Async XLA Ops:
  6.5 126.0 %copy-start = (bf16[320,2048]{1,0:T(8,128)(2,1)S(1)}, bf16[320,2048]{1,0:T(8,128)(2,1)}, u32[]{:S(2)}) copy-start(bf16[320,2048]{1,0:T(8,128)(2,1)} %param.19) | copy-start | bytes 3932164
  6.5 118.1 %all-gather.2.cloned.1.call-start = ((), (), s32[]{:S(2)}) async-start(), calls=%async_computation.4 | async-start | bytes 4456448 | tf_op jit(solution)/shard_map/all_gather | solution.py:167
  9.1 13.9 %collective-permute-start = (bf16[4,256,128]{1,2,0:T(8,128)(2,1)}, bf16[4,256,128]{1,2,0:T(8,128)(2,1)}, u32[]{:S(2)}, u32[]{:S(2)}) collective-permute-start(bf16[4,256,128]{1,2,0:T(8,128)(2,1)} %bitcast.4), channel_id=1, source_target_pairs={{0,32},{16,48},{32,64},{48,80},{64,96},{80,112},{96,128},{112,144}... | collective-permute-start | bytes 786440 | tf_op jit(solution)/shard_map/ppermute | solution.py:119
  11.7 11.2 %copy-start.10 = (s32[1,8]{1,0:T(1,128)S(1)}, s32[1,8]{1,0:T(1,128)}, u32[]{:S(2)}) copy-start(s32[1,8]{1,0:T(1,128)} %param.11) | copy-start | bytes 100
  11.7 29.0 %copy-start.8 = (s32[16]{0:T(128)S(1)}, s32[16]{0:T(128)}, u32[]{:S(2)}) copy-start(s32[16]{0:T(128)} %param.12) | copy-start | bytes 196
  11.7 49.5 %all-to-all-start = ((bf16[16,32,2048]{2,1,0:T(8,128)(2,1)}), bf16[16,32,2048]{2,1,0:T(8,128)(2,1)S(1)}, u32[]{:S(2)}, u32[]{:S(2)}) async-start(bf16[16,32,2048]{2,1,0:T(8,128)(2,1)} %broadcast_in_dim.23), calls=%async_computation | async-start | bytes 4194304 | tf_op jit(solution)/shard_map/all_to_all | solution.py:89
  18.9 9.6 %collective-permute-start.4 = (bf16[4,256,128]{1,2,0:T(8,128)(2,1)}, bf16[4,256,128]{1,2,0:T(8,128)(2,1)}, u32[]{:S(2)}, u32[]{:S(2)}) collective-permute-start(bf16[4,256,128]{1,2,0:T(8,128)(2,1)} %bitcast.4), channel_id=1, source_target_pairs={{0,224},{16,240},{32,0},{48,16},{64,32},{80,48},{96,64},{112,80},{... | collective-permute-start | bytes 786440 | tf_op jit(solution)/shard_map/ppermute | solution.py:123
  22.9 9.3 %collective-permute-start.1 = (bf16[4,256,128]{1,2,0:T(8,128)(2,1)}, bf16[4,256,128]{1,2,0:T(8,128)(2,1)}, u32[]{:S(2)}, u32[]{:S(2)}) collective-permute-start(bf16[4,256,128]{1,2,0:T(8,128)(2,1)} %collective-permute-done), channel_id=1, source_target_pairs={{0,32},{16,48},{32,64},{48,80},{64,96},{80,112},{96,128},{112,144}... | collective-permute-start | bytes 786440 | tf_op jit(solution)/shard_map/ppermute | solution.py:119
  28.5 8.4 %collective-permute-start.5 = (bf16[4,256,128]{1,2,0:T(8,128)(2,1)}, bf16[4,256,128]{1,2,0:T(8,128)(2,1)}, u32[]{:S(2)}, u32[]{:S(2)}) collective-permute-start(bf16[4,256,128]{1,2,0:T(8,128)(2,1)} %collective-permute-done.4), channel_id=1, source_target_pairs={{0,224},{16,240},{32,0},{48,16},{64,32},{80,48},{96,64},{112,80},{... | collective-permute-start | bytes 786440 | tf_op jit(solution)/shard_map/ppermute | solution.py:123
  32.2 8.4 %collective-permute-start.2 = (bf16[4,256,128]{1,2,0:T(8,128)(2,1)}, bf16[4,256,128]{1,2,0:T(8,128)(2,1)}, u32[]{:S(2)}, u32[]{:S(2)}) collective-permute-start(bf16[4,256,128]{1,2,0:T(8,128)(2,1)} %collective-permute-done.1), channel_id=1, source_target_pairs={{0,32},{16,48},{32,64},{48,80},{64,96},{80,112},{96,128},{112,144}... | collective-permute-start | bytes 786440 | tf_op jit(solution)/shard_map/ppermute | solution.py:119
  36.9 7.9 %collective-permute-start.6 = (bf16[4,256,128]{1,2,0:T(8,128)(2,1)}, bf16[4,256,128]{1,2,0:T(8,128)(2,1)}, u32[]{:S(2)}, u32[]{:S(2)}) collective-permute-start(bf16[4,256,128]{1,2,0:T(8,128)(2,1)} %collective-permute-done.5), channel_id=1, source_target_pairs={{0,224},{16,240},{32,0},{48,16},{64,32},{80,48},{96,64},{112,80},{... | collective-permute-start | bytes 786440 | tf_op jit(solution)/shard_map/ppermute | solution.py:123
  40.6 7.9 %collective-permute-start.3 = (bf16[4,256,128]{1,2,0:T(8,128)(2,1)}, bf16[4,256,128]{1,2,0:T(8,128)(2,1)}, u32[]{:S(2)}, u32[]{:S(2)}) collective-permute-start(bf16[4,256,128]{1,2,0:T(8,128)(2,1)} %collective-permute-done.2), channel_id=1, source_target_pairs={{0,32},{16,48},{32,64},{48,80},{64,96},{80,112},{96,128},{112,144}... | collective-permute-start | bytes 786440 | tf_op jit(solution)/shard_map/ppermute | solution.py:119
  50.3 7.2 %collective-permute-start.7 = (bf16[4,256,128]{1,2,0:T(8,128)(2,1)}, bf16[4,256,128]{1,2,0:T(8,128)(2,1)}, u32[]{:S(2)}, u32[]{:S(2)}) collective-permute-start(bf16[4,256,128]{1,2,0:T(8,128)(2,1)} %select_select_fusion), channel_id=1, source_target_pairs={{0,16},{16,0},{32,48},{48,32},{64,80},{80,64},{96,112},{112,96},{1... | collective-permute-start | bytes 786440 | tf_op jit(solution)/shard_map/ppermute | solution.py:126
  63.4 32.1 %all-to-all-start.1 = ((bf16[16,256,128]{2,1,0:T(8,128)(2,1)}), bf16[16,256,128]{2,1,0:T(8,128)(2,1)}, u32[]{:S(2)}, u32[]{:S(2)}) async-start(bf16[16,256,128]{2,1,0:T(8,128)(2,1)} %bitcast.127), calls=%async_computation.1 | async-start | bytes 2097152 | tf_op jit(solution)/shard_map/all_to_all | solution.py:169
  70.6 1.0 copy-start.3
  70.6 1.2 copy-start.4
  70.6 1.4 copy-start.5
  73.2 0.8 copy-start.6
  74.3 1.0 copy-start.1
  99.4 3.2 %copy-start.2 = (f32[512,1,512]{0,2,1:T(8,128)S(1)}, f32[512,1,512]{0,2,1:T(8,128)}, u32[]{:S(2)}) copy-start(f32[512,1,512]{0,2,1:T(8,128)} %copy-done.1) | copy-start | bytes 3145732
  124.7 6.8 %copy-start.9 = (bf16[2,2048,320]{1,2,0:T(8,128)(2,1)S(1)}, bf16[2,2048,320]{1,2,0:T(8,128)(2,1)}, u32[]{:S(2)}) copy-start(bf16[2,2048,320]{1,2,0:T(8,128)(2,1)} %param.18) | copy-start | bytes 7864324
  130.1 1.4 copy-start.7
  138.0 33.6 %all-to-all-start.3 = ((bf16[16,32,2048]{2,1,0:T(8,128)(2,1)}), bf16[16,32,2048]{2,1,0:T(8,128)(2,1)S(1)}, u32[]{:S(2)}, u32[]{:S(2)}) async-start(bf16[16,32,2048]{2,1,0:T(8,128)(2,1)} %bitcast.128), calls=%async_computation.3 | async-start | bytes 4194304 | tf_op jit(solution)/shard_map/all_to_all | solution.py:96
Sparse Core Ops, SparseCore 0:
  9.8 82.2 all-gather.1

commit v9 on v8

--- a/solution.py
+++ b/solution.py
@@ -100,7 +100,7 @@
 CORES = 2
 
 
-def fetch_slot(prefix_cache, group_prefix, group_rank):
+def fetch_slot(prefix_cache, group_prefix, group_rank, rider):
     group_count = lax.axis_size("dp")
     chips = group_count // CORES
     chip = group_rank // CORES
@@ -123,8 +123,11 @@
             behind = lax.ppermute(behind, "dp", backward)
             mine = jnp.where(mine_at == step, behind, mine)
             theirs = jnp.where(theirs_at == step, behind, theirs)
+        if step == 1:
+            ahead, behind, rider = lax.optimization_barrier((ahead, behind, rider))
+        mine, theirs, ahead, behind = lax.optimization_barrier((mine, theirs, ahead, behind))
     swapped = lax.ppermute(theirs, "dp", [(i, i ^ 1) for i in range(group_count)])
-    return jnp.where(slot_wanted % CORES == core, mine, swapped)
+    return slot_wanted % CORES == core, mine, swapped, rider
 
 
 def on_device(
@@ -163,9 +166,13 @@
     kv_groups = KVH // local_kv
     by_head = prefix_cache.reshape(shard_rows, 2, kv_groups, kv_width)
     by_head = jnp.transpose(by_head, (2, 0, 1, 3)).reshape(kv_groups, shard_rows, 2 * kv_width)
-    chosen = fetch_slot(by_head, group_prefix, group_rank)
+    on_core, mine, swapped, projection = fetch_slot(by_head, group_prefix, group_rank, projection)
     out_full = lax.all_gather(out_weight, "tensor", axis=0, tiled=True)
-    outgoing = jnp.repeat(chosen, tensor_count // kv_groups, axis=0)
+    outgoing = jnp.where(
+        on_core,
+        jnp.repeat(mine, tensor_count // kv_groups, axis=0),
+        jnp.repeat(swapped, tensor_count // kv_groups, axis=0),
+    )
     incoming = lax.all_to_all(outgoing, "tensor", 0, 0, tiled=True)
     seg_rows = tensor_count * shard_rows
     incoming = incoming.reshape(seg_rows, 2 * kv_width)

time: 182 us -> 179 us (0.984)
  other arithmetic: 9.01 us -> 16.4 us
  local copies, waits for them, and re-layouts: 17.2 us -> 13 us
  starting transfers between devices: 29.1 us -> 26.1 us
  waiting for transfers between devices: 65.2 us -> 62.8 us
    all_to_all x1, waiting for transfers between devices: 20 us -> 12.4 us  [on_device(): incoming = lax.all_to_all(outgoing, 'tensor', 0, 0, tiled=True)]
    ppermute x4, waiting for transfers between devices: 3.7 us -> 11.1 us  [fetch_slot(): ahead = lax.ppermute(ahead, 'dp', onward)]
    ppermute x3, waiting for transfers between devices: 10.9 us -> 4.33 us  [fetch_slot(): behind = lax.ppermute(behind, 'dp', backward)]
    select_n x1 -> x4, other arithmetic: 1.93 us -> 7.75 us  [the longest x3 6.05 us: fetch_slot(): theirs = jnp.where(theirs_at == step, behind, theirs)]
    all_to_all x1, waiting for transfers between devices: 0.01 us -> 3.34 us  [gather_rows(): received = lax.all_to_all(copies, axis, 0, 0, tiled=True)]
    all_to_all x1, starting transfers between devices: 6.64 us -> 4.53 us  [on_device(): incoming = lax.all_to_all(outgoing, 'tensor', 0, 0, tiled=True)]
    ppermute x1, waiting for transfers between devices: 0.01 us -> 1.83 us  [fetch_slot(): lax.ppermute(theirs, 'dp', [(i, i ^ 1) for i in range(group_count)])]
  transfers between devices with their start and end apart: 12 -> 12, of which waited for: 6 -> 7; matrix products, arithmetic and copies ran while one was open for 16% -> 17% of each run, Pallas kernels for 0% -> 0%
where the time goes in v9:
time: 179 us; the launch traced here: 178 us
  waiting for transfers between devices  62.8 us (35%)
  starting transfers between devices  26.1 us (15%)
  blocking collectives  20.9 us (12%)
  matrix products  20 us (11%)
  between operations  18.9 us (11%)
  other arithmetic  16.4 us (9%)
  local copies, waits for them, and re-layouts  13 us (7%)
    all_to_all x1, waiting for transfers between devices, sum_scatter_rows(): received = lax.all_to_all(parts, axis, 0, 0, tiled=True)  29.8 us
    all_to_all x1, blocking collectives, gather_rows(): received = lax.all_to_all(copies, axis, 0, 0, tiled=True)  20.9 us
    all_to_all x1, waiting for transfers between devices, on_device(): incoming = lax.all_to_all(outgoing, 'tensor', 0, 0, tiled=True)  12.4 us
    ppermute x4, waiting for transfers between devices, fetch_slot(): ahead = lax.ppermute(ahead, 'dp', onward)  11.1 us
    ppermute x3, starting transfers between devices, fetch_slot(): behind = lax.ppermute(behind, 'dp', backward)  10.7 us
    all_to_all x1, starting transfers between devices, gather_rows(): received = lax.all_to_all(copies, axis, 0, 0, tiled=True)  7.17 us
    select_n x3, other arithmetic, fetch_slot(): theirs = jnp.where(theirs_at == step, behind, theirs)  6.05 us
    dot_general x1, matrix products, on_device(): jnp.dot(hidden, down_weight, preferred_element_type=jnp.float32)  5.51 us
  transfers between devices with their start and end apart: 12, of which 7 were waited for; matrix products, arithmetic and copies ran while one was open for 17% of the time, Pallas kernels for 0%

profile of v9, /device:TPU:0, one launch (start us, length us, event | category | flops | bytes accessed | tf_op | source)
XLA Modules:
  0.0 178.0 jit_solution(3315398929442548335)
XLA Ops:
  7.8 4.2 %collective-permute-start = (bf16[4,256,128]{1,2,0:T(8,128)(2,1)S(1)}, bf16[4,256,128]{1,2,0:T(8,128)(2,1)}, u32[]{:S(2)}, u32[]{:S(2)}) collective-permute-start(bf16[4,256,128]{1,2,0:T(8,128)(2,1)S(1)} %bitcast.130), channel_id=1, source_target_pairs={{0,224},{16,240},{32,0},{48,16},{64,32},{80,48},{96,64},{112,80},{... | collective-permute-start | bytes 786440 | tf_op jit(solution)/shard_map/ppermute | solution.py:123
  21.3 1.9 %select_select_fusion.4 = (bf16[4,256,128]{1,2,0:T(8,128)(2,1)}, bf16[4,256,128]{1,2,0:T(8,128)(2,1)}) fusion(bf16[4,256,128]{1,2,0:T(8,128)(2,1)} %collective-permute-done, bf16[4,256,128]{1,2,0:T(8,128)(2,1)} %collective-permute-done.1, pred[]{:T(512)S(6)} %eq.77, pred[]{:T(512)S(6)} %eq.76, bf16[4,256,2,64]{1,3,2,0:T(8,128)(2,1)S(1)} %copy.17, ...), kind=kLoop, calls=%fused_computation.62 | loop fusion | flops 524288 | bytes 1310724 | tf_op jit(solution)/shard_map/jit(_where)/select_n | solution.py:125
  23.2 3.2 %collective-permute-start.2 = (bf16[4,256,128]{1,2,0:T(8,128)(2,1)}, bf16[4,256,128]{1,2,0:T(8,128)(2,1)}, u32[]{:S(2)}, u32[]{:S(2)}) collective-permute-start(bf16[4,256,128]{1,2,0:T(8,128)(2,1)} %collective-permute-done), channel_id=1, source_target_pairs={{0,224},{16,240},{32,0},{48,16},{64,32},{80,48},{96,64},{112,80},{... | collective-permute-start | bytes 786440 | tf_op jit(solution)/shard_map/ppermute | solution.py:123
  28.0 7.2 %all-to-all-start = ((bf16[16,32,2048]{2,1,0:T(8,128)(2,1)}), bf16[16,32,2048]{2,1,0:T(8,128)(2,1)S(1)}, u32[]{:S(2)}, u32[]{:S(2)}) async-start(bf16[16,32,2048]{2,1,0:T(8,128)(2,1)} %broadcast_in_dim.23), calls=%async_computation | async-start | bytes 4194304 | tf_op jit(solution)/shard_map/all_to_all | solution.py:89
  35.3 2.1 %select_select_fusion.2 = (bf16[4,256,128]{1,2,0:T(8,128)(2,1)}, bf16[4,256,128]{1,2,0:T(8,128)(2,1)}) fusion(bf16[4,256,128]{1,2,0:T(8,128)(2,1)} %collective-permute-done.2, bf16[4,256,128]{1,2,0:T(8,128)(2,1)} %collective-permute-done.3, bf16[4,256,128]{1,2,0:T(8,128)(2,1)} %get-tuple-element.26, pred[]{:T(512)S(6)} %eq.80, pred[]{:T(512)S(6)} %eq.79, ...), kind=kLoop, calls=%fused_computation.60 | loop fusion | flops 524288 | bytes 1572868 | tf_op jit(solution)/shard_map/jit(_where)/select_n | solution.py:125
  37.3 3.2 %collective-permute-start.4 = (bf16[4,256,128]{1,2,0:T(8,128)(2,1)}, bf16[4,256,128]{1,2,0:T(8,128)(2,1)}, u32[]{:S(2)}, u32[]{:S(2)}) collective-permute-start(bf16[4,256,128]{1,2,0:T(8,128)(2,1)} %collective-permute-done.2), channel_id=1, source_target_pairs={{0,224},{16,240},{32,0},{48,16},{64,32},{80,48},{96,64},{112,80},{... | collective-permute-start | bytes 786440 | tf_op jit(solution)/shard_map/ppermute | solution.py:123
  40.7 4.3 %collective-permute-done.4 = bf16[4,256,128]{1,2,0:T(8,128)(2,1)} collective-permute-done((bf16[4,256,128]{1,2,0:T(8,128)(2,1)}, bf16[4,256,128]{1,2,0:T(8,128)(2,1)}, u32[]{:S(2)}, u32[]{:S(2)}) %collective-permute-start.4) | collective-permute-done | bytes 262176 | tf_op jit(solution)/shard_map/ppermute | solution.py:123
  45.1 3.4 %collective-permute-done.5 = bf16[4,256,128]{1,2,0:T(8,128)(2,1)} collective-permute-done((bf16[4,256,128]{1,2,0:T(8,128)(2,1)}, bf16[4,256,128]{1,2,0:T(8,128)(2,1)}, u32[]{:S(2)}, u32[]{:S(2)}) %collective-permute-start.5) | collective-permute-done | bytes 262176 | tf_op jit(solution)/shard_map/ppermute | solution.py:119
  48.5 2.1 %select_select_fusion = (bf16[4,256,128]{1,2,0:T(8,128)(2,1)}, bf16[4,256,128]{1,2,0:T(8,128)(2,1)}) fusion(bf16[4,256,128]{1,2,0:T(8,128)(2,1)} %collective-permute-done.4, bf16[4,256,128]{1,2,0:T(8,128)(2,1)} %collective-permute-done.5, bf16[4,256,128]{1,2,0:T(8,128)(2,1)} %get-tuple-element.30, pred[]{:T(512)S(6)} %eq.83, pred[]{:T(512)S(6)} %eq.82, ...), kind=kLoop, calls=%fused_computation.58 | loop fusion | flops 524288 | bytes 1572868 | tf_op jit(solution)/shard_map/jit(_where)/select_n | solution.py:125
  50.7 7.7 %collective-permute-done.6 = bf16[4,256,128]{1,2,0:T(8,128)(2,1)} collective-permute-done((bf16[4,256,128]{1,2,0:T(8,128)(2,1)}, bf16[4,256,128]{1,2,0:T(8,128)(2,1)}, u32[]{:S(2)}, u32[]{:S(2)}) %collective-permute-start.6) | collective-permute-done | bytes 262176 | tf_op jit(solution)/shard_map/ppermute | solution.py:119
  58.4 1.9 %broadcast_select_fusion = (bf16[4,256,128]{1,2,0:T(8,128)(2,1)}, bf16[4,256,128]{1,2,0:T(8,128)(2,1)}) fusion(bf16[4,256,128]{1,2,0:T(8,128)(2,1)} %collective-permute-done.6, bf16[4,256,128]{1,2,0:T(8,128)(2,1)} %get-tuple-element.33, pred[]{:T(512)S(6)} %eq.84, bf16[4,256,128]{1,2,0:T(8,128)(2,1)} %get-tuple-element.32, pred[]{:T(512)S(6)} %eq.71), kind=kLoop, calls=%fused_computation.64 | loop fusion | flops 262144 | bytes 1310722 | tf_op jit(solution)/shard_map/jit(_where)/select_n | solution.py:121
  60.4 1.8 %collective-permute-done.7 = bf16[4,256,128]{1,2,0:T(8,128)(2,1)} collective-permute-done((bf16[4,256,128]{1,2,0:T(8,128)(2,1)}, bf16[4,256,128]{1,2,0:T(8,128)(2,1)}, u32[]{:S(2)}, u32[]{:S(2)}) %collective-permute-start.7) | collective-permute-done | bytes 262176 | tf_op jit(solution)/shard_map/ppermute | solution.py:129
  63.9 1.8 %copy.19 = bf16[4,256,128]{2,1,0:T(8,128)(2,1)} copy(bf16[4,256,128]{1,2,0:T(8,128)(2,1)} %broadcast_select_fusion.2) | data formatting | bytes 524288 | tf_op jit(solution)/shard_map/jit(_where)/select_n | solution.py:171
  65.7 3.3 %all-to-all-done = bf16[16,32,2048]{2,1,0:T(8,128)(2,1)S(1)} async-done(((bf16[16,32,2048]{2,1,0:T(8,128)(2,1)}), bf16[16,32,2048]{2,1,0:T(8,128)(2,1)S(1)}, u32[]{:S(2)}, u32[]{:S(2)}) %all-to-all-start) | async-done | bytes 2097184 | tf_op jit(solution)/shard_map/all_to_all | solution.py:89
  69.0 2.1 %broadcast_in_dim.25 = bf16[4,4,256,128]{3,2,1,0:T(8,128)(2,1)} broadcast(bf16[4,256,128]{2,1,0:T(8,128)(2,1)} %copy.19), dimensions={0,2,3} | broadcast | bytes 1310720 | tf_op jit(solution)/shard_map/broadcast_in_dim | solution.py:173
  71.2 4.5 %all-to-all-start.1 = ((bf16[16,256,128]{2,1,0:T(8,128)(2,1)}), bf16[16,256,128]{2,1,0:T(8,128)(2,1)}, u32[]{:S(2)}, u32[]{:S(2)}) async-start(bf16[16,256,128]{2,1,0:T(8,128)(2,1)} %bitcast.128), calls=%async_computation.1 | async-start | bytes 2097152 | tf_op jit(solution)/shard_map/all_to_all | solution.py:176
  80.7 12.4 %all-to-all-done.1 = bf16[16,256,128]{2,1,0:T(8,128)(2,1)} async-done(((bf16[16,256,128]{2,1,0:T(8,128)(2,1)}), bf16[16,256,128]{2,1,0:T(8,128)(2,1)}, u32[]{:S(2)}, u32[]{:S(2)}) %all-to-all-start.1) | async-done | bytes 1048608 | tf_op jit(solution)/shard_map/all_to_all | solution.py:176
  93.1 2.5 %multiply_reduce_fusion = (f32[512]{0:T(512)S(1)}, f32[4096,512]{1,0:T(8,128)S(1)}) fusion(bf16[512,1,32]{0,2,1:T(8,128)(2,1)S(1)} %get-tuple-element.54, bf16[512,1,32]{0,2,1:T(8,128)(2,1)S(1)} %get-tuple-element.55, bf16[4096,128]{1,0:T(8,128)(2,1)} %bitcast.7), kind=kOutput, calls=%fused_computation.2 | convolution fusion | flops 272760320 | bytes 9504768 | tf_op jit(solution)/shard_map/thd,nhd->thn/dot_general | solution.py:56
  97.0 3.1 %fusion.37 = f32[1,64,512]{2,1,0:T(8,128)S(1)} fusion(f32[4096,512]{1,0:T(8,128)S(1)} %get-tuple-element.61, f32[512]{0:T(512)S(1)} %get-tuple-element.60, bf16[4096,128]{1,0:T(8,128)(2,1)} %bitcast.7, f32[512]{0:T(512)S(1)} %get-tuple-element.39, f32[512]{0:T(512)S(1)} %get-tuple-element.57, f32[512]{0:T(512)S(1)} %get-tuple-element.56), kind=kOutput, calls=%fused_computation.37 | convolution fusion | flops 274825216 | bytes 9576448 | tf_op jit(solution)/shard_map/thn,nhd->thd/dot_general | solution.py:64
  101.5 20.9 %all_to_all.20 = bf16[16,1,64,512]{3,2,1,0:T(8,128)(2,1)} all-to-all(bf16[16,1,64,512]{3,2,1,0:T(8,128)(2,1)S(1)} %broadcast_in_dim.29), channel_id=1, replica_groups=mesh['dp'=16,'tensor'=16] {'tensor'}, dimensions={0} | all-to-all | bytes 2097152 | tf_op jit(solution)/shard_map/all_to_all | solution.py:89
  122.4 5.4 %fusion.3 = (f32[512]{0:T(512)S(1)}, bf16[512,2048]{1,0:T(8,128)(2,1)S(1)}) fusion(bf16[1024,512]{1,0:T(8,128)(2,1)} %bitcast.132, bf16[1024,2048]{1,0:T(8,128)(2,1)} %all-gather.2.cloned.1.call-done, bf16[16,32,2048]{2,1,0:T(8,128)(2,1)S(1)} %all-to-all-done), kind=kOutput, calls=%fused_computation.7 | convolution fusion | flops 2153774592 | bytes 9439232 | tf_op jit(solution)/shard_map/dot_general | solution.py:228
  130.2 5.5 %convolution_convert_fusion = bf16[512,2048]{1,0:T(8,128)(2,1)} fusion(bf16[320,2048]{1,0:T(8,128)(2,1)S(1)} %copy-done, bf16[2,2048,320]{1,2,0:T(8,128)(2,1)} %param.18, bf16[512,2048]{1,0:T(8,128)(2,1)} %copy-done.7, f32[512]{0:T(512)S(1)} %add_rsqrt_fusion.1, f32[512,320]{0,1:T(8,128)S(1)} %fusion.14), kind=kOutput, calls=%fused_computation.18 | convolution fusion | flops 1347354624 | bytes 7473152 | tf_op jit(solution)/shard_map/dot_general | solution.py:235
  135.7 3.7 %all-to-all-start.3 = ((bf16[16,32,2048]{2,1,0:T(8,128)(2,1)}), bf16[16,32,2048]{2,1,0:T(8,128)(2,1)S(1)}, u32[]{:S(2)}, u32[]{:S(2)}) async-start(bf16[16,32,2048]{2,1,0:T(8,128)(2,1)} %bitcast.129), calls=%async_computation.3 | async-start | bytes 4194304 | tf_op jit(solution)/shard_map/all_to_all | solution.py:96
  139.4 29.8 %all-to-all-done.3 = bf16[16,32,2048]{2,1,0:T(8,128)(2,1)S(1)} async-done(((bf16[16,32,2048]{2,1,0:T(8,128)(2,1)}), bf16[16,32,2048]{2,1,0:T(8,128)(2,1)S(1)}, u32[]{:S(2)}, u32[]{:S(2)}) %all-to-all-start.3) | async-done | bytes 2097184 | tf_op jit(solution)/shard_map/all_to_all | solution.py:96
  (65 shorter events, 21.0 us)
Async XLA Ops:
  6.5 123.6 %copy-start = (bf16[320,2048]{1,0:T(8,128)(2,1)S(1)}, bf16[320,2048]{1,0:T(8,128)(2,1)}, u32[]{:S(2)}) copy-start(bf16[320,2048]{1,0:T(8,128)(2,1)} %param.19) | copy-start | bytes 3932164
  6.5 7.1 %copy-start.8 = (s32[16]{0:T(128)S(1)}, s32[16]{0:T(128)}, u32[]{:S(2)}) copy-start(s32[16]{0:T(128)} %param.12) | copy-start | bytes 196
  6.5 12.9 %copy-start.5 = (bf16[2048,64]{0,1:T(8,128)(2,1)S(1)}, bf16[2048,64]{0,1:T(8,128)(2,1)}, u32[]{:S(2)}) copy-start(bf16[2048,64]{0,1:T(8,128)(2,1)} %param.14) | copy-start | bytes 786436
  6.5 115.8 %all-gather.2.cloned.1.call-start = ((), (), s32[]{:S(2)}) async-start(), calls=%async_computation.4 | async-start | bytes 4456448 | tf_op jit(solution)/shard_map/all_gather | solution.py:170
  7.8 13.5 %collective-permute-start = (bf16[4,256,128]{1,2,0:T(8,128)(2,1)S(1)}, bf16[4,256,128]{1,2,0:T(8,128)(2,1)}, u32[]{:S(2)}, u32[]{:S(2)}) collective-permute-start(bf16[4,256,128]{1,2,0:T(8,128)(2,1)S(1)} %bitcast.130), channel_id=1, source_target_pairs={{0,224},{16,240},{32,0},{48,16},{64,32},{80,48},{96,64},{112,80},{... | collective-permute-start | bytes 786440 | tf_op jit(solution)/shard_map/ppermute | solution.py:123
  12.0 9.3 %collective-permute-start.1 = (bf16[4,256,128]{1,2,0:T(8,128)(2,1)S(1)}, bf16[4,256,128]{1,2,0:T(8,128)(2,1)}, u32[]{:S(2)}, u32[]{:S(2)}) collective-permute-start(bf16[4,256,128]{1,2,0:T(8,128)(2,1)S(1)} %bitcast.131), channel_id=1, source_target_pairs={{0,32},{16,48},{32,64},{48,80},{64,96},{80,112},{96,128},{112,144}... | collective-permute-start | bytes 786440 | tf_op jit(solution)/shard_map/ppermute | solution.py:119
  13.6 12.9 %copy-start.6 = (bf16[32,2048]{1,0:T(8,128)(2,1)S(1)}, bf16[32,2048]{1,0:T(8,128)(2,1)}, u32[]{:S(2)}) copy-start(bf16[32,2048]{1,0:T(8,128)(2,1)} %param.10) | copy-start | bytes 393220
  23.2 12.0 %collective-permute-start.2 = (bf16[4,256,128]{1,2,0:T(8,128)(2,1)}, bf16[4,256,128]{1,2,0:T(8,128)(2,1)}, u32[]{:S(2)}, u32[]{:S(2)}) collective-permute-start(bf16[4,256,128]{1,2,0:T(8,128)(2,1)} %collective-permute-done), channel_id=1, source_target_pairs={{0,224},{16,240},{32,0},{48,16},{64,32},{80,48},{96,64},{112,80},{... | collective-permute-start | bytes 786440 | tf_op jit(solution)/shard_map/ppermute | solution.py:123
  26.5 8.8 %collective-permute-start.3 = (bf16[4,256,128]{1,2,0:T(8,128)(2,1)}, bf16[4,256,128]{1,2,0:T(8,128)(2,1)}, u32[]{:S(2)}, u32[]{:S(2)}) collective-permute-start(bf16[4,256,128]{1,2,0:T(8,128)(2,1)} %collective-permute-done.1), channel_id=1, source_target_pairs={{0,32},{16,48},{32,64},{48,80},{64,96},{80,112},{96,128},{112,144}... | collective-permute-start | bytes 786440 | tf_op jit(solution)/shard_map/ppermute | solution.py:119
  28.0 12.5 %copy-start.10 = (s32[1,8]{1,0:T(1,128)S(1)}, s32[1,8]{1,0:T(1,128)}, u32[]{:S(2)}) copy-start(s32[1,8]{1,0:T(1,128)} %param.11) | copy-start | bytes 100
  28.0 41.0 %all-to-all-start = ((bf16[16,32,2048]{2,1,0:T(8,128)(2,1)}), bf16[16,32,2048]{2,1,0:T(8,128)(2,1)S(1)}, u32[]{:S(2)}, u32[]{:S(2)}) async-start(bf16[16,32,2048]{2,1,0:T(8,128)(2,1)} %broadcast_in_dim.23), calls=%async_computation | async-start | bytes 4194304 | tf_op jit(solution)/shard_map/all_to_all | solution.py:89
  37.3 7.7 %collective-permute-start.4 = (bf16[4,256,128]{1,2,0:T(8,128)(2,1)}, bf16[4,256,128]{1,2,0:T(8,128)(2,1)}, u32[]{:S(2)}, u32[]{:S(2)}) collective-permute-start(bf16[4,256,128]{1,2,0:T(8,128)(2,1)} %collective-permute-done.2), channel_id=1, source_target_pairs={{0,224},{16,240},{32,0},{48,16},{64,32},{80,48},{96,64},{112,80},{... | collective-permute-start | bytes 786440 | tf_op jit(solution)/shard_map/ppermute | solution.py:123
  40.5 7.9 %collective-permute-start.5 = (bf16[4,256,128]{1,2,0:T(8,128)(2,1)}, bf16[4,256,128]{1,2,0:T(8,128)(2,1)}, u32[]{:S(2)}, u32[]{:S(2)}) collective-permute-start(bf16[4,256,128]{1,2,0:T(8,128)(2,1)} %collective-permute-done.3), channel_id=1, source_target_pairs={{0,32},{16,48},{32,64},{48,80},{64,96},{80,112},{96,128},{112,144}... | collective-permute-start | bytes 786440 | tf_op jit(solution)/shard_map/ppermute | solution.py:119
  50.5 7.9 %collective-permute-start.6 = (bf16[4,256,128]{1,2,0:T(8,128)(2,1)}, bf16[4,256,128]{1,2,0:T(8,128)(2,1)}, u32[]{:S(2)}, u32[]{:S(2)}) collective-permute-start(bf16[4,256,128]{1,2,0:T(8,128)(2,1)} %collective-permute-done.5), channel_id=1, source_target_pairs={{0,32},{16,48},{32,64},{48,80},{64,96},{80,112},{96,128},{112,144}... | collective-permute-start | bytes 786440 | tf_op jit(solution)/shard_map/ppermute | solution.py:119
  60.3 1.9 %collective-permute-start.7 = (bf16[4,256,128]{1,2,0:T(8,128)(2,1)}, bf16[4,256,128]{1,2,0:T(8,128)(2,1)}, u32[]{:S(2)}, u32[]{:S(2)}) collective-permute-start(bf16[4,256,128]{1,2,0:T(8,128)(2,1)} %get-tuple-element.35), channel_id=1, source_target_pairs={{0,16},{16,0},{32,48},{48,32},{64,80},{80,64},{96,112},{112,96},{1... | collective-permute-start | bytes 786440 | tf_op jit(solution)/shard_map/ppermute | solution.py:129
  71.2 21.9 %all-to-all-start.1 = ((bf16[16,256,128]{2,1,0:T(8,128)(2,1)}), bf16[16,256,128]{2,1,0:T(8,128)(2,1)}, u32[]{:S(2)}, u32[]{:S(2)}) async-start(bf16[16,256,128]{2,1,0:T(8,128)(2,1)} %bitcast.128), calls=%async_computation.1 | async-start | bytes 2097152 | tf_op jit(solution)/shard_map/all_to_all | solution.py:176
  76.3 1.2 copy-start.1
  78.4 0.7 copy-start.4
  79.5 1.0 copy-start.2
  97.0 3.2 %copy-start.3 = (f32[512,1,512]{0,2,1:T(8,128)S(1)}, f32[512,1,512]{0,2,1:T(8,128)}, u32[]{:S(2)}) copy-start(f32[512,1,512]{0,2,1:T(8,128)} %copy-done.2) | copy-start | bytes 3145732
  122.4 6.8 %copy-start.9 = (bf16[2,2048,320]{1,2,0:T(8,128)(2,1)S(1)}, bf16[2,2048,320]{1,2,0:T(8,128)(2,1)}, u32[]{:S(2)}) copy-start(bf16[2,2048,320]{1,2,0:T(8,128)(2,1)} %param.18) | copy-start | bytes 7864324
  127.8 1.3 copy-start.7
  135.7 33.5 %all-to-all-start.3 = ((bf16[16,32,2048]{2,1,0:T(8,128)(2,1)}), bf16[16,32,2048]{2,1,0:T(8,128)(2,1)S(1)}, u32[]{:S(2)}, u32[]{:S(2)}) async-start(bf16[16,32,2048]{2,1,0:T(8,128)(2,1)} %bitcast.129), calls=%async_computation.3 | async-start | bytes 4194304 | tf_op jit(solution)/shard_map/all_to_all | solution.py:96
Sparse Core Ops, SparseCore 0:
  12.1 66.7 all-gather.1

commit v10 on v9

--- a/solution.py
+++ b/solution.py
@@ -164,22 +164,33 @@
 
     shard_rows = prefix_cache.shape[0]
     kv_groups = KVH // local_kv
-    by_head = prefix_cache.reshape(shard_rows, 2, kv_groups, kv_width)
-    by_head = jnp.transpose(by_head, (2, 0, 1, 3)).reshape(kv_groups, shard_rows, 2 * kv_width)
-    on_core, mine, swapped, projection = fetch_slot(by_head, group_prefix, group_rank, projection)
+    token_copies = jnp.broadcast_to(tokens[None], (tensor_count,) + tokens.shape)
+    ring_input, token_copies = lax.optimization_barrier((prefix_cache, token_copies))
+    group_rows = lax.all_to_all(token_copies, "tensor", 0, 0, tiled=True).reshape(
+        group_tokens, tokens.shape[1]
+    )
+    on_core, mine, swapped, projection = fetch_slot(ring_input, group_prefix, group_rank, projection)
     out_full = lax.all_gather(out_weight, "tensor", axis=0, tiled=True)
-    outgoing = jnp.where(
-        on_core,
-        jnp.repeat(mine, tensor_count // kv_groups, axis=0),
-        jnp.repeat(swapped, tensor_count // kv_groups, axis=0),
-    )
+    chosen = jnp.where(on_core, mine, swapped)
+    by_head = jnp.stack(
+        [
+            jnp.concatenate(
+                [
+                    chosen[:, head * kv_width : (head + 1) * kv_width],
+                    chosen[:, kv_total + head * kv_width : kv_total + (head + 1) * kv_width],
+                ],
+                axis=1,
+            )
+            for head in range(kv_groups)
+        ]
+    )
+    outgoing = jnp.repeat(by_head, tensor_count // kv_groups, axis=0)
     incoming = lax.all_to_all(outgoing, "tensor", 0, 0, tiled=True)
     seg_rows = tensor_count * shard_rows
     incoming = incoming.reshape(seg_rows, 2 * kv_width)
     keys_block = jnp.repeat(incoming[:, :kv_width].reshape(seg_rows, local_kv, HD), repeat_by, axis=1)
     values_block = jnp.repeat(incoming[:, kv_width:].reshape(seg_rows, local_kv, HD), repeat_by, axis=1)
 
-    group_rows = gather_rows(tokens, "tensor")
     segment = norm_rows(group_rows)
     seg_rows = segment.shape[0]
     mapped = jnp.dot(segment, projection, preferred_element_type=jnp.float32)

time: 179 us -> 192 us (1.073)
  waiting for transfers between devices: 62.8 us -> 81.2 us
  blocking collectives: 20.9 us -> 18.6 us
    all_to_all x1, waiting for transfers between devices: 12.4 us -> 22.6 us  [on_device(): incoming = lax.all_to_all(outgoing, 'tensor', 0, 0, tiled=True)]
    all_to_all x1, waiting for transfers between devices: 3.34 us -> 13.3 us  [on_device(): lax.all_to_all(token_copies, 'tensor', 0, 0, tiled=True)]
    ppermute x3, starting transfers between devices: 10.7 us -> 7.71 us  [fetch_slot(): behind = lax.ppermute(behind, 'dp', backward)]
    broadcast_in_dim x1 -> x2, local copies, waits for them, and re-layouts: 2.14 us -> 4.77 us  [the longest x1 2.63 us: on_device(): jnp.broadcast_to(tokens[None], (tensor_count,) + tokens.shape)]
    all_to_all x1, waiting for transfers between devices: 29.8 us -> 27.2 us  [sum_scatter_rows(): received = lax.all_to_all(parts, axis, 0, 0, tiled=True)]
    all_to_all x1, blocking collectives: 20.9 us -> 18.6 us  [gather_rows(): received = lax.all_to_all(copies, axis, 0, 0, tiled=True)]
    unnamed x24 -> x23, local copies, waits for them, and re-layouts: 5.01 us -> 4.75 us
  transfers between devices with their start and end apart: 12 -> 12, of which waited for: 7 -> 7; matrix products, arithmetic and copies ran while one was open for 17% -> 14% of each run, Pallas kernels for 0% -> 0%
where the time goes in v10:
time: 192 us; the launch traced here: 191 us
  waiting for transfers between devices  81.2 us (42%)
  starting transfers between devices  24.8 us (13%)
  matrix products  20 us (10%)
  between operations  19 us (10%)
  blocking collectives  18.6 us (10%)
  other arithmetic  15.8 us (8%)
  local copies, waits for them, and re-layouts  11.9 us (6%)
    all_to_all x1, waiting for transfers between devices, sum_scatter_rows(): received = lax.all_to_all(parts, axis, 0, 0, tiled=True)  27.2 us
    all_to_all x1, waiting for transfers between devices, on_device(): incoming = lax.all_to_all(outgoing, 'tensor', 0, 0, tiled=True)  22.6 us
    all_to_all x1, blocking collectives, gather_rows(): received = lax.all_to_all(copies, axis, 0, 0, tiled=True)  18.6 us
    all_to_all x1, waiting for transfers between devices, on_device(): lax.all_to_all(token_copies, 'tensor', 0, 0, tiled=True)  13.3 us
    ppermute x4, waiting for transfers between devices, fetch_slot(): ahead = lax.ppermute(ahead, 'dp', onward)  11.1 us
    ppermute x3, starting transfers between devices, fetch_slot(): behind = lax.ppermute(behind, 'dp', backward)  7.71 us
    all_to_all x1, starting transfers between devices, on_device(): lax.all_to_all(token_copies, 'tensor', 0, 0, tiled=True)  7.04 us
    dot_general x1, matrix products, on_device(): jnp.dot(hidden, down_weight, preferred_element_type=jnp.float32)  5.5 us
  transfers between devices with their start and end apart: 12, of which 7 were waited for; matrix products, arithmetic and copies ran while one was open for 14% of the time, Pallas kernels for 0%

profile of v10, /device:TPU:0, one launch (start us, length us, event | category | flops | bytes accessed | tf_op | source)
XLA Modules:
  0.0 191.3 jit_solution(8567873236394405118)
XLA Ops:
  6.5 2.6 %broadcast_in_dim.23 = bf16[16,32,2048]{2,1,0:T(8,128)(2,1)} broadcast(bf16[32,2048]{1,0:T(8,128)(2,1)} %param.10), dimensions={1,2} | broadcast | bytes 2228224 | tf_op jit(solution)/shard_map/broadcast_in_dim | solution.py:167
  9.2 4.1 %collective-permute-start = (bf16[256,512]{1,0:T(8,128)(2,1)}, bf16[256,512]{1,0:T(8,128)(2,1)}, u32[]{:S(2)}, u32[]{:S(2)}) collective-permute-start(bf16[256,512]{1,0:T(8,128)(2,1)} %param.13), channel_id=1, source_target_pairs={{0,224},{16,240},{32,0},{48,16},{64,32},{80,48},{96,64},{112,80},{... | collective-permute-start | bytes 786440 | tf_op jit(solution)/shard_map/ppermute | solution.py:123
  24.6 3.3 %collective-permute-start.2 = (bf16[256,512]{1,0:T(8,128)(2,1)}, bf16[256,512]{1,0:T(8,128)(2,1)}, u32[]{:S(2)}, u32[]{:S(2)}) collective-permute-start(bf16[256,512]{1,0:T(8,128)(2,1)} %collective-permute-done), channel_id=1, source_target_pairs={{0,224},{16,240},{32,0},{48,16},{64,32},{80,48},{96,64},{112,80},{... | collective-permute-start | bytes 786440 | tf_op jit(solution)/shard_map/ppermute | solution.py:123
  27.9 5.3 %collective-permute-done.2 = bf16[256,512]{1,0:T(8,128)(2,1)} collective-permute-done((bf16[256,512]{1,0:T(8,128)(2,1)}, bf16[256,512]{1,0:T(8,128)(2,1)}, u32[]{:S(2)}, u32[]{:S(2)}) %collective-permute-start.2) | collective-permute-done | bytes 262176 | tf_op jit(solution)/shard_map/ppermute | solution.py:123
  33.2 3.4 %collective-permute-done.3 = bf16[256,512]{1,0:T(8,128)(2,1)} collective-permute-done((bf16[256,512]{1,0:T(8,128)(2,1)}, bf16[256,512]{1,0:T(8,128)(2,1)}, u32[]{:S(2)}, u32[]{:S(2)}) %collective-permute-start.3) | collective-permute-done | bytes 262176 | tf_op jit(solution)/shard_map/ppermute | solution.py:119
  36.6 1.9 select_select_fusion.2
  38.8 1.7 collective-permute-start.5
  40.6 7.0 %all-to-all-start = ((bf16[16,32,2048]{2,1,0:T(8,128)(2,1)}), bf16[16,32,2048]{2,1,0:T(8,128)(2,1)S(1)}, u32[]{:S(2)}, u32[]{:S(2)}) async-start(bf16[16,32,2048]{2,1,0:T(8,128)(2,1)} %broadcast_in_dim.23), calls=%async_computation | async-start | bytes 4194304 | tf_op jit(solution)/shard_map/all_to_all | solution.py:169
  47.8 2.0 %select_select_fusion = (bf16[256,512]{1,0:T(8,128)(2,1)}, bf16[256,512]{1,0:T(8,128)(2,1)}) fusion(bf16[256,512]{1,0:T(8,128)(2,1)} %collective-permute-done.4, bf16[256,512]{1,0:T(8,128)(2,1)} %collective-permute-done.5, bf16[256,512]{1,0:T(8,128)(2,1)} %get-tuple-element.34, pred[]{:T(512)S(6)} %eq.83, pred[]{:T(512)S(6)} %eq.82, ...), kind=kLoop, calls=%fused_computation.59 | loop fusion | flops 524288 | bytes 1572868 | tf_op jit(solution)/shard_map/jit(_where)/select_n | solution.py:125
  50.0 7.6 %collective-permute-done.6 = bf16[256,512]{1,0:T(8,128)(2,1)} collective-permute-done((bf16[256,512]{1,0:T(8,128)(2,1)}, bf16[256,512]{1,0:T(8,128)(2,1)}, u32[]{:S(2)}, u32[]{:S(2)}) %collective-permute-start.6) | collective-permute-done | bytes 262176 | tf_op jit(solution)/shard_map/ppermute | solution.py:119
  57.7 2.0 %broadcast_select_fusion = (bf16[256,512]{1,0:T(8,128)(2,1)}, bf16[256,512]{1,0:T(8,128)(2,1)}) fusion(bf16[256,512]{1,0:T(8,128)(2,1)} %collective-permute-done.6, bf16[256,512]{1,0:T(8,128)(2,1)} %get-tuple-element.37, pred[]{:T(512)S(6)} %eq.84, bf16[256,512]{1,0:T(8,128)(2,1)} %get-tuple-element.36, pred[]{:T(512)S(6)} %eq.71), kind=kLoop, calls=%fused_computation.65 | loop fusion | flops 262144 | bytes 1310722 | tf_op jit(solution)/shard_map/jit(_where)/select_n | solution.py:121
  59.7 1.8 collective-permute-done.7
  63.8 13.3 %all-to-all-done = bf16[16,32,2048]{2,1,0:T(8,128)(2,1)S(1)} async-done(((bf16[16,32,2048]{2,1,0:T(8,128)(2,1)}), bf16[16,32,2048]{2,1,0:T(8,128)(2,1)S(1)}, u32[]{:S(2)}, u32[]{:S(2)}) %all-to-all-start) | async-done | bytes 2097184 | tf_op jit(solution)/shard_map/all_to_all | solution.py:169
  77.0 2.1 %broadcast_in_dim.25 = bf16[4,4,256,128]{3,2,1,0:T(8,128)(2,1)} broadcast(bf16[4,256,128]{2,1,0:T(8,128)(2,1)} %pad_maximum_fusion.1), dimensions={0,2,3} | broadcast | bytes 1310720 | tf_op jit(solution)/shard_map/broadcast_in_dim | solution.py:187
  79.2 4.5 %all-to-all-start.1 = ((bf16[16,256,128]{2,1,0:T(8,128)(2,1)}), bf16[16,256,128]{2,1,0:T(8,128)(2,1)}, u32[]{:S(2)}, u32[]{:S(2)}) async-start(bf16[16,256,128]{2,1,0:T(8,128)(2,1)} %bitcast.130), calls=%async_computation.1 | async-start | bytes 2097152 | tf_op jit(solution)/shard_map/all_to_all | solution.py:188
  88.7 22.6 %all-to-all-done.1 = bf16[16,256,128]{2,1,0:T(8,128)(2,1)} async-done(((bf16[16,256,128]{2,1,0:T(8,128)(2,1)}), bf16[16,256,128]{2,1,0:T(8,128)(2,1)}, u32[]{:S(2)}, u32[]{:S(2)}) %all-to-all-start.1) | async-done | bytes 1048608 | tf_op jit(solution)/shard_map/all_to_all | solution.py:188
  111.3 2.5 %multiply_reduce_fusion = (f32[512]{0:T(512)S(1)}, f32[4096,512]{1,0:T(8,128)S(1)}) fusion(bf16[512,1,32]{0,2,1:T(8,128)(2,1)S(1)} %get-tuple-element.66, bf16[512,1,32]{0,2,1:T(8,128)(2,1)S(1)} %get-tuple-element.67, bf16[4096,128]{1,0:T(8,128)(2,1)} %bitcast.8), kind=kOutput, calls=%fused_computation.2 | convolution fusion | flops 272760320 | bytes 9504768 | tf_op jit(solution)/shard_map/thd,nhd->thn/dot_general | solution.py:56
  115.2 3.1 %fusion.37 = f32[1,64,512]{2,1,0:T(8,128)S(1)} fusion(f32[4096,512]{1,0:T(8,128)S(1)} %get-tuple-element.73, f32[512]{0:T(512)S(1)} %get-tuple-element.72, bf16[4096,128]{1,0:T(8,128)(2,1)} %bitcast.8, f32[512]{0:T(512)S(1)} %get-tuple-element.43, f32[512]{0:T(512)S(1)} %get-tuple-element.69, f32[512]{0:T(512)S(1)} %get-tuple-element.68), kind=kOutput, calls=%fused_computation.37 | convolution fusion | flops 274825216 | bytes 9576448 | tf_op jit(solution)/shard_map/thn,nhd->thd/dot_general | solution.py:64
  119.7 18.6 %all_to_all.20 = bf16[16,1,64,512]{3,2,1,0:T(8,128)(2,1)} all-to-all(bf16[16,1,64,512]{3,2,1,0:T(8,128)(2,1)S(1)} %broadcast_in_dim.29), channel_id=1, replica_groups=mesh['dp'=16,'tensor'=16] {'tensor'}, dimensions={0} | all-to-all | bytes 2097152 | tf_op jit(solution)/shard_map/all_to_all | solution.py:89
  138.3 5.4 %fusion.3 = (f32[512]{0:T(512)S(1)}, bf16[512,2048]{1,0:T(8,128)(2,1)S(1)}) fusion(bf16[1024,512]{1,0:T(8,128)(2,1)} %bitcast.132, bf16[1024,2048]{1,0:T(8,128)(2,1)} %all-gather.2.cloned.1.call-done, bf16[16,32,2048]{2,1,0:T(8,128)(2,1)S(1)} %all-to-all-done), kind=kOutput, calls=%fused_computation.7 | convolution fusion | flops 2153774592 | bytes 9439232 | tf_op jit(solution)/shard_map/dot_general | solution.py:239
  146.1 5.5 %convolution_convert_fusion = bf16[512,2048]{1,0:T(8,128)(2,1)} fusion(bf16[320,2048]{1,0:T(8,128)(2,1)S(1)} %copy-done, bf16[2,2048,320]{1,2,0:T(8,128)(2,1)} %param.18, bf16[512,2048]{1,0:T(8,128)(2,1)} %copy-done.7, f32[512]{0:T(512)S(1)} %add_rsqrt_fusion.1, f32[512,320]{0,1:T(8,128)S(1)} %fusion.14), kind=kOutput, calls=%fused_computation.18 | convolution fusion | flops 1347354624 | bytes 7473152 | tf_op jit(solution)/shard_map/dot_general | solution.py:246
  151.6 3.7 %all-to-all-start.3 = ((bf16[16,32,2048]{2,1,0:T(8,128)(2,1)}), bf16[16,32,2048]{2,1,0:T(8,128)(2,1)S(1)}, u32[]{:S(2)}, u32[]{:S(2)}) async-start(bf16[16,32,2048]{2,1,0:T(8,128)(2,1)} %bitcast.131), calls=%async_computation.3 | async-start | bytes 4194304 | tf_op jit(solution)/shard_map/all_to_all | solution.py:96
  155.3 27.2 %all-to-all-done.3 = bf16[16,32,2048]{2,1,0:T(8,128)(2,1)S(1)} async-done(((bf16[16,32,2048]{2,1,0:T(8,128)(2,1)}), bf16[16,32,2048]{2,1,0:T(8,128)(2,1)S(1)}, u32[]{:S(2)}, u32[]{:S(2)}) %all-to-all-start.3) | async-done | bytes 2097184 | tf_op jit(solution)/shard_map/all_to_all | solution.py:96
  182.9 1.6 add_convert_fusion
  (68 shorter events, 19.3 us)
Async XLA Ops:
  6.5 139.6 %copy-start = (bf16[320,2048]{1,0:T(8,128)(2,1)S(1)}, bf16[320,2048]{1,0:T(8,128)(2,1)}, u32[]{:S(2)}) copy-start(bf16[320,2048]{1,0:T(8,128)(2,1)} %param.19) | copy-start | bytes 3932164
  6.5 6.8 %copy-start.5 = (bf16[2048,256]{1,0:T(8,128)(2,1)S(1)}, bf16[2048,256]{1,0:T(8,128)(2,1)}, u32[]{:S(2)}) copy-start(bf16[2048,256]{1,0:T(8,128)(2,1)} %param.16) | copy-start | bytes 3145732
  6.5 8.2 %copy-start.8 = (s32[16]{0:T(128)S(1)}, s32[16]{0:T(128)}, u32[]{:S(2)}) copy-start(s32[16]{0:T(128)} %param.12) | copy-start | bytes 196
  6.5 131.8 %all-gather.2.cloned.1.call-start = ((), (), s32[]{:S(2)}) async-start(), calls=%async_computation.4 | async-start | bytes 4456448 | tf_op jit(solution)/shard_map/all_gather | solution.py:173
  9.2 14.3 %collective-permute-start = (bf16[256,512]{1,0:T(8,128)(2,1)}, bf16[256,512]{1,0:T(8,128)(2,1)}, u32[]{:S(2)}, u32[]{:S(2)}) collective-permute-start(bf16[256,512]{1,0:T(8,128)(2,1)} %param.13), channel_id=1, source_target_pairs={{0,224},{16,240},{32,0},{48,16},{64,32},{80,48},{96,64},{112,80},{... | collective-permute-start | bytes 786440 | tf_op jit(solution)/shard_map/ppermute | solution.py:123
  13.3 10.2 %collective-permute-start.1 = (bf16[256,512]{1,0:T(8,128)(2,1)}, bf16[256,512]{1,0:T(8,128)(2,1)}, u32[]{:S(2)}, u32[]{:S(2)}) collective-permute-start(bf16[256,512]{1,0:T(8,128)(2,1)} %param.13), channel_id=1, source_target_pairs={{0,32},{16,48},{32,64},{48,80},{64,96},{80,112},{96,128},{112,144}... | collective-permute-start | bytes 786440 | tf_op jit(solution)/shard_map/ppermute | solution.py:119
  14.7 8.8 %copy-start.6 = (bf16[256,512]{1,0:T(8,128)(2,1)S(1)}, bf16[256,512]{1,0:T(8,128)(2,1)}, u32[]{:S(2)}) copy-start(bf16[256,512]{1,0:T(8,128)(2,1)} %param.13) | copy-start | bytes 786436
  24.6 8.6 %collective-permute-start.2 = (bf16[256,512]{1,0:T(8,128)(2,1)}, bf16[256,512]{1,0:T(8,128)(2,1)}, u32[]{:S(2)}, u32[]{:S(2)}) collective-permute-start(bf16[256,512]{1,0:T(8,128)(2,1)} %collective-permute-done), channel_id=1, source_target_pairs={{0,224},{16,240},{32,0},{48,16},{64,32},{80,48},{96,64},{112,80},{... | collective-permute-start | bytes 786440 | tf_op jit(solution)/shard_map/ppermute | solution.py:123
  27.9 8.7 %collective-permute-start.3 = (bf16[256,512]{1,0:T(8,128)(2,1)}, bf16[256,512]{1,0:T(8,128)(2,1)}, u32[]{:S(2)}, u32[]{:S(2)}) collective-permute-start(bf16[256,512]{1,0:T(8,128)(2,1)} %collective-permute-done.1), channel_id=1, source_target_pairs={{0,32},{16,48},{32,64},{48,80},{64,96},{80,112},{96,128},{112,144}... | collective-permute-start | bytes 786440 | tf_op jit(solution)/shard_map/ppermute | solution.py:119
  27.9 19.7 %copy-start.10 = (s32[1,8]{1,0:T(1,128)S(1)}, s32[1,8]{1,0:T(1,128)}, u32[]{:S(2)}) copy-start(s32[1,8]{1,0:T(1,128)} %param.11) | copy-start | bytes 100
  38.5 9.3 %collective-permute-start.4 = (bf16[256,512]{1,0:T(8,128)(2,1)}, bf16[256,512]{1,0:T(8,128)(2,1)}, u32[]{:S(2)}, u32[]{:S(2)}) collective-permute-start(bf16[256,512]{1,0:T(8,128)(2,1)} %collective-permute-done.2), channel_id=1, source_target_pairs={{0,224},{16,240},{32,0},{48,16},{64,32},{80,48},{96,64},{112,80},{... | collective-permute-start | bytes 786440 | tf_op jit(solution)/shard_map/ppermute | solution.py:123
  38.8 9.0 %collective-permute-start.5 = (bf16[256,512]{1,0:T(8,128)(2,1)}, bf16[256,512]{1,0:T(8,128)(2,1)}, u32[]{:S(2)}, u32[]{:S(2)}) collective-permute-start(bf16[256,512]{1,0:T(8,128)(2,1)} %collective-permute-done.3), channel_id=1, source_target_pairs={{0,32},{16,48},{32,64},{48,80},{64,96},{80,112},{96,128},{112,144}... | collective-permute-start | bytes 786440 | tf_op jit(solution)/shard_map/ppermute | solution.py:119
  40.6 36.5 %all-to-all-start = ((bf16[16,32,2048]{2,1,0:T(8,128)(2,1)}), bf16[16,32,2048]{2,1,0:T(8,128)(2,1)S(1)}, u32[]{:S(2)}, u32[]{:S(2)}) async-start(bf16[16,32,2048]{2,1,0:T(8,128)(2,1)} %broadcast_in_dim.23), calls=%async_computation | async-start | bytes 4194304 | tf_op jit(solution)/shard_map/all_to_all | solution.py:169
  49.8 7.9 %collective-permute-start.6 = (bf16[256,512]{1,0:T(8,128)(2,1)}, bf16[256,512]{1,0:T(8,128)(2,1)}, u32[]{:S(2)}, u32[]{:S(2)}) collective-permute-start(bf16[256,512]{1,0:T(8,128)(2,1)} %collective-permute-done.5), channel_id=1, source_target_pairs={{0,32},{16,48},{32,64},{48,80},{64,96},{80,112},{96,128},{112,144}... | collective-permute-start | bytes 786440 | tf_op jit(solution)/shard_map/ppermute | solution.py:119
  59.7 1.9 collective-permute-start.7
  79.2 32.1 %all-to-all-start.1 = ((bf16[16,256,128]{2,1,0:T(8,128)(2,1)}), bf16[16,256,128]{2,1,0:T(8,128)(2,1)}, u32[]{:S(2)}, u32[]{:S(2)}) async-start(bf16[16,256,128]{2,1,0:T(8,128)(2,1)} %bitcast.130), calls=%async_computation.1 | async-start | bytes 2097152 | tf_op jit(solution)/shard_map/all_to_all | solution.py:188
  84.3 1.2 copy-start.1
  86.4 0.7 copy-start.4
  87.5 1.0 copy-start.2
  115.2 3.1 %copy-start.3 = (f32[512,1,512]{0,2,1:T(8,128)S(1)}, f32[512,1,512]{0,2,1:T(8,128)}, u32[]{:S(2)}) copy-start(f32[512,1,512]{0,2,1:T(8,128)} %copy-done.2) | copy-start | bytes 3145732
  138.3 6.8 %copy-start.9 = (bf16[2,2048,320]{1,2,0:T(8,128)(2,1)S(1)}, bf16[2,2048,320]{1,2,0:T(8,128)(2,1)}, u32[]{:S(2)}) copy-start(bf16[2,2048,320]{1,2,0:T(8,128)(2,1)} %param.18) | copy-start | bytes 7864324
  143.7 1.3 copy-start.7
  151.6 30.9 %all-to-all-start.3 = ((bf16[16,32,2048]{2,1,0:T(8,128)(2,1)}), bf16[16,32,2048]{2,1,0:T(8,128)(2,1)S(1)}, u32[]{:S(2)}, u32[]{:S(2)}) async-start(bf16[16,32,2048]{2,1,0:T(8,128)(2,1)} %bitcast.131), calls=%async_computation.3 | async-start | bytes 4194304 | tf_op jit(solution)/shard_map/all_to_all | solution.py:96
Sparse Core Ops, SparseCore 0:
  28.0 83.1 all-gather.1

commit v11 on v9

--- a/solution.py
+++ b/solution.py
@@ -179,7 +179,7 @@
     keys_block = jnp.repeat(incoming[:, :kv_width].reshape(seg_rows, local_kv, HD), repeat_by, axis=1)
     values_block = jnp.repeat(incoming[:, kv_width:].reshape(seg_rows, local_kv, HD), repeat_by, axis=1)
 
-    group_rows = gather_rows(tokens, "tensor")
+    group_rows = lax.all_gather(tokens, "tensor", axis=0, tiled=True)
     segment = norm_rows(group_rows)
     seg_rows = segment.shape[0]
     mapped = jnp.dot(segment, projection, preferred_element_type=jnp.float32)

time: 179 us -> 194 us (1.084)
  waiting for transfers between devices: 62.8 us -> 94.5 us
  other arithmetic: 16.4 us -> 9.21 us
  local copies, waits for them, and re-layouts: 13 us -> 6.4 us
  starting transfers between devices: 26.1 us -> 22.9 us
    all_gather x1, waiting for transfers between devices: 0.01 us -> 26.9 us  [on_device(): out_full = lax.all_gather(out_weight, 'tensor', axis=0, tiled=True)]
    all_to_all x1 -> x0, starting transfers between devices: 7.17 us -> none  [gather_rows(): received = lax.all_to_all(copies, axis, 0, 0, tiled=True)]
    ppermute x3, waiting for transfers between devices: 4.33 us -> 9.47 us  [fetch_slot(): behind = lax.ppermute(behind, 'dp', backward)]
    select_n x3, other arithmetic: 6.05 us -> 1.2 us  [fetch_slot(): theirs = jnp.where(theirs_at == step, behind, theirs)]
    all_to_all x1 -> x0, waiting for transfers between devices: 3.34 us -> none  [gather_rows(): received = lax.all_to_all(copies, axis, 0, 0, tiled=True)]
    ppermute x3, starting transfers between devices: 10.7 us -> 7.87 us  [fetch_slot(): behind = lax.ppermute(behind, 'dp', backward)]
    ppermute x4, starting transfers between devices: 0.01 us -> 2.63 us  [fetch_slot(): ahead = lax.ppermute(ahead, 'dp', onward)]
    all_to_all x1, starting transfers between devices: 4.53 us -> 7.04 us  [on_device(): incoming = lax.all_to_all(outgoing, 'tensor', 0, 0, tiled=True)]
  transfers between devices with their start and end apart: 12 -> 12, of which waited for: 7 -> 9; matrix products, arithmetic and copies ran while one was open for 17% -> 10% of each run, Pallas kernels for 0% -> 0%
where the time goes in v11:
time: 194 us; the launch traced here: 192 us
  waiting for transfers between devices  94.5 us (49%)
  starting transfers between devices  22.9 us (12%)
  blocking collectives  20.8 us (11%)
  matrix products  19.5 us (10%)
  between operations  18.8 us (10%)
  other arithmetic  9.21 us (5%)
  local copies, waits for them, and re-layouts  6.4 us (3%)
    all_to_all x1, waiting for transfers between devices, sum_scatter_rows(): received = lax.all_to_all(parts, axis, 0, 0, tiled=True)  31.7 us
    all_gather x1, waiting for transfers between devices, on_device(): out_full = lax.all_gather(out_weight, 'tensor', axis=0, tiled=True)  26.9 us
    all_to_all x1, blocking collectives, gather_rows(): received = lax.all_to_all(copies, axis, 0, 0, tiled=True)  20.8 us
    all_to_all x1, waiting for transfers between devices, on_device(): incoming = lax.all_to_all(outgoing, 'tensor', 0, 0, tiled=True)  12.2 us
    ppermute x4, waiting for transfers between devices, fetch_slot(): ahead = lax.ppermute(ahead, 'dp', onward)  11.4 us
    ppermute x3, waiting for transfers between devices, fetch_slot(): behind = lax.ppermute(behind, 'dp', backward)  9.47 us
    ppermute x3, starting transfers between devices, fetch_slot(): behind = lax.ppermute(behind, 'dp', backward)  7.87 us
    all_to_all x1, starting transfers between devices, on_device(): incoming = lax.all_to_all(outgoing, 'tensor', 0, 0, tiled=True)  7.04 us
  transfers between devices with their start and end apart: 12, of which 9 were waited for; matrix products, arithmetic and copies ran while one was open for 10% of the time, Pallas kernels for 0%

profile of v11, /device:TPU:0, one launch (start us, length us, event | category | flops | bytes accessed | tf_op | source)
XLA Modules:
  0.0 192.1 jit_solution(11447685624349679845)
XLA Ops:
  9.1 4.2 %collective-permute-start = (bf16[4,256,128]{1,2,0:T(8,128)(2,1)S(1)}, bf16[4,256,128]{1,2,0:T(8,128)(2,1)}, u32[]{:S(2)}, u32[]{:S(2)}) collective-permute-start(bf16[4,256,128]{1,2,0:T(8,128)(2,1)S(1)} %bitcast.123), channel_id=1, source_target_pairs={{0,224},{16,240},{32,0},{48,16},{64,32},{80,48},{96,64},{112,80},{... | collective-permute-start | bytes 786440 | tf_op jit(solution)/shard_map/ppermute | solution.py:123
  13.3 1.6 constant_dynamic-slice_fusion
  21.0 1.5 pad_maximum_fusion
  23.6 3.3 %collective-permute-start.2 = (bf16[4,256,128]{1,2,0:T(8,128)(2,1)}, bf16[4,256,128]{1,2,0:T(8,128)(2,1)S(1)}, u32[]{:S(2)}, u32[]{:S(2)}) collective-permute-start(bf16[4,256,128]{1,2,0:T(8,128)(2,1)} %collective-permute-done), channel_id=1, source_target_pairs={{0,224},{16,240},{32,0},{48,16},{64,32},{80,48},{96,64},{112,80},{... | collective-permute-start | bytes 786440 | tf_op jit(solution)/shard_map/ppermute | solution.py:123
  26.9 5.3 %collective-permute-done.2 = bf16[4,256,128]{1,2,0:T(8,128)(2,1)S(1)} collective-permute-done((bf16[4,256,128]{1,2,0:T(8,128)(2,1)}, bf16[4,256,128]{1,2,0:T(8,128)(2,1)S(1)}, u32[]{:S(2)}, u32[]{:S(2)}) %collective-permute-start.2) | collective-permute-done | bytes 262176 | tf_op jit(solution)/shard_map/ppermute | solution.py:123
  32.2 3.3 %collective-permute-done.3 = bf16[4,256,128]{1,2,0:T(8,128)(2,1)S(1)} collective-permute-done((bf16[4,256,128]{1,2,0:T(8,128)(2,1)}, bf16[4,256,128]{1,2,0:T(8,128)(2,1)S(1)}, u32[]{:S(2)}, u32[]{:S(2)}) %collective-permute-start.3) | collective-permute-done | bytes 262176 | tf_op jit(solution)/shard_map/ppermute | solution.py:119
  35.9 1.7 collective-permute-start.5
  37.8 4.2 %collective-permute-done.4 = bf16[4,256,128]{1,2,0:T(8,128)(2,1)S(1)} collective-permute-done((bf16[4,256,128]{1,2,0:T(8,128)(2,1)S(1)}, bf16[4,256,128]{1,2,0:T(8,128)(2,1)S(1)}, u32[]{:S(2)}, u32[]{:S(2)}) %collective-permute-start.4) | collective-permute-done | bytes 262176 | tf_op jit(solution)/shard_map/ppermute | solution.py:123
  42.0 1.5 collective-permute-done.5
  44.6 6.6 %collective-permute-done.6 = bf16[4,256,128]{1,2,0:T(8,128)(2,1)S(1)} collective-permute-done((bf16[4,256,128]{1,2,0:T(8,128)(2,1)S(1)}, bf16[4,256,128]{1,2,0:T(8,128)(2,1)S(1)}, u32[]{:S(2)}, u32[]{:S(2)}) %collective-permute-start.6) | collective-permute-done | bytes 262176 | tf_op jit(solution)/shard_map/ppermute | solution.py:119
  51.4 1.5 collective-permute-done.7
  54.3 7.0 %all-to-all-start = ((bf16[16,256,128]{2,1,0:T(8,128)(2,1)}), bf16[16,256,128]{2,1,0:T(8,128)(2,1)S(1)}, u32[]{:S(2)}, u32[]{:S(2)}) async-start(bf16[16,256,128]{2,1,0:T(8,128)(2,1)} %bitcast.5), calls=%async_computation | async-start | bytes 2097152 | tf_op jit(solution)/shard_map/all_to_all | solution.py:176
  61.4 2.1 %fusion.5 = f32[512]{0:T(512)S(1)} fusion(bf16[512,2048]{1,0:T(8,128)(2,1)} %all-gather.3.cloned.1.call-done), kind=kLoop, calls=%fused_computation.12 | loop fusion | flops 3145216 | bytes 2099200 | tf_op jit(solution)/shard_map/reduce_sum | solution.py:49
  63.5 2.5 %fusion.11 = f32[512,192]{0,1:T(8,128)S(1)} fusion(bf16[2048,192]{1,0:T(8,128)(2,1)S(1)} %copy-done.1, bf16[512,2048]{1,0:T(8,128)(2,1)} %all-gather.3.cloned.1.call-done, f32[512]{0:T(512)S(1)} %add_rsqrt_fusion.1), kind=kOutput, calls=%fused_computation.19 | convolution fusion | flops 405798912 | bytes 3278848 | tf_op jit(solution)/shard_map/dot_general | solution.py:185
  67.0 12.2 %all-to-all-done = bf16[16,256,128]{2,1,0:T(8,128)(2,1)S(1)} async-done(((bf16[16,256,128]{2,1,0:T(8,128)(2,1)}), bf16[16,256,128]{2,1,0:T(8,128)(2,1)S(1)}, u32[]{:S(2)}, u32[]{:S(2)}) %all-to-all-start) | async-done | bytes 1048608 | tf_op jit(solution)/shard_map/all_to_all | solution.py:176
  80.4 1.4 fusion.1
  81.9 1.8 fusion.40
  85.0 20.8 %all_to_all.15 = bf16[16,1,64,512]{3,2,1,0:T(8,128)(2,1)S(1)} all-to-all(bf16[16,1,64,512]{3,2,1,0:T(8,128)(2,1)S(1)} %broadcast_in_dim.26), channel_id=1, replica_groups=mesh['dp'=16,'tensor'=16] {'tensor'}, dimensions={0} | all-to-all | bytes 2097152 | tf_op jit(solution)/shard_map/all_to_all | solution.py:89
  105.8 26.9 %all-gather.5.cloned.1.call-done = bf16[1024,2048]{1,0:T(8,128)(2,1)} async-done(((bf16[64,2048]{1,0:T(8,128)(2,1)}), bf16[1024,2048]{1,0:T(8,128)(2,1)}) %all-gather.5.cloned.1.call-update) | async-done | bytes 4194320 | tf_op jit(solution)/shard_map/all_gather | solution.py:170
  132.7 5.8 %fusion.3 = (f32[512]{0:T(512)S(1)}, bf16[512,2048]{1,0:T(8,128)(2,1)S(1)}) fusion(bf16[1024,512]{1,0:T(8,128)(2,1)S(1)} %bitcast.125, bf16[1024,2048]{1,0:T(8,128)(2,1)} %all-gather.5.cloned.1.call-done, bf16[512,2048]{1,0:T(8,128)(2,1)} %all-gather.3.cloned.1.call-done), kind=kOutput, calls=%fused_computation.10 | convolution fusion | flops 2153774592 | bytes 9439232 | tf_op jit(solution)/shard_map/dot_general | solution.py:228
  140.9 5.5 %convolution_convert_fusion = bf16[512,2048]{1,0:T(8,128)(2,1)} fusion(bf16[320,2048]{1,0:T(8,128)(2,1)S(1)} %copy-done, bf16[2,2048,320]{1,2,0:T(8,128)(2,1)} %param.18, bf16[512,2048]{1,0:T(8,128)(2,1)} %copy-done.4, f32[512]{0:T(512)S(1)} %add_rsqrt_fusion, f32[512,320]{0,1:T(8,128)S(1)} %fusion.17), kind=kOutput, calls=%fused_computation.18 | convolution fusion | flops 1347354624 | bytes 7473152 | tf_op jit(solution)/shard_map/dot_general | solution.py:235
  146.4 5.3 %all-to-all-start.2 = ((bf16[16,32,2048]{2,1,0:T(8,128)(2,1)}), bf16[16,32,2048]{2,1,0:T(8,128)(2,1)S(1)}, u32[]{:S(2)}, u32[]{:S(2)}) async-start(bf16[16,32,2048]{2,1,0:T(8,128)(2,1)} %bitcast.122), calls=%async_computation.2 | async-start | bytes 4194304 | tf_op jit(solution)/shard_map/all_to_all | solution.py:96
  151.7 31.7 %all-to-all-done.2 = bf16[16,32,2048]{2,1,0:T(8,128)(2,1)S(1)} async-done(((bf16[16,32,2048]{2,1,0:T(8,128)(2,1)}), bf16[16,32,2048]{2,1,0:T(8,128)(2,1)S(1)}, u32[]{:S(2)}, u32[]{:S(2)}) %all-to-all-start.2) | async-done | bytes 2097184 | tf_op jit(solution)/shard_map/all_to_all | solution.py:96
  183.7 1.6 add_convert_fusion
  (57 shorter events, 14.1 us)
Async XLA Ops:
  6.5 134.4 %copy-start = (bf16[320,2048]{1,0:T(8,128)(2,1)S(1)}, bf16[320,2048]{1,0:T(8,128)(2,1)}, u32[]{:S(2)}) copy-start(bf16[320,2048]{1,0:T(8,128)(2,1)} %param.19) | copy-start | bytes 3932164
  6.5 8.4 %copy-start.5 = (s32[16]{0:T(128)S(1)}, s32[16]{0:T(128)}, u32[]{:S(2)}) copy-start(s32[16]{0:T(128)} %param.12) | copy-start | bytes 196
  6.5 14.1 %copy-start.3 = (bf16[2048,64]{0,1:T(8,128)(2,1)S(1)}, bf16[2048,64]{0,1:T(8,128)(2,1)}, u32[]{:S(2)}) copy-start(bf16[2048,64]{0,1:T(8,128)(2,1)} %param.14) | copy-start | bytes 786436
  6.5 54.9 %all-gather.3.cloned.1.call-start = ((), (), s32[]{:S(2)}) async-start(), calls=%async_computation.3 | async-start | bytes 2228224 | tf_op jit(solution)/shard_map/all_gather | solution.py:182
  7.3 125.5 %all-gather.5.cloned.1.call-start = ((), (), s32[]{:S(2)}) async-start(), calls=%async_computation.4 | async-start | bytes 4456448 | tf_op jit(solution)/shard_map/all_gather | solution.py:170
  9.1 13.3 %collective-permute-start = (bf16[4,256,128]{1,2,0:T(8,128)(2,1)S(1)}, bf16[4,256,128]{1,2,0:T(8,128)(2,1)}, u32[]{:S(2)}, u32[]{:S(2)}) collective-permute-start(bf16[4,256,128]{1,2,0:T(8,128)(2,1)S(1)} %bitcast.123), channel_id=1, source_target_pairs={{0,224},{16,240},{32,0},{48,16},{64,32},{80,48},{96,64},{112,80},{... | collective-permute-start | bytes 786440 | tf_op jit(solution)/shard_map/ppermute | solution.py:123
  13.3 9.1 %collective-permute-start.1 = (bf16[4,256,128]{1,2,0:T(8,128)(2,1)S(1)}, bf16[4,256,128]{1,2,0:T(8,128)(2,1)}, u32[]{:S(2)}, u32[]{:S(2)}) collective-permute-start(bf16[4,256,128]{1,2,0:T(8,128)(2,1)S(1)} %bitcast.124), channel_id=1, source_target_pairs={{0,32},{16,48},{32,64},{48,80},{64,96},{80,112},{96,128},{112,144}... | collective-permute-start | bytes 786440 | tf_op jit(solution)/shard_map/ppermute | solution.py:119
  20.9 16.7 %copy-start.7 = (s32[1,8]{1,0:T(1,128)S(1)}, s32[1,8]{1,0:T(1,128)}, u32[]{:S(2)}) copy-start(s32[1,8]{1,0:T(1,128)} %param.11) | copy-start | bytes 100
  23.6 8.6 %collective-permute-start.2 = (bf16[4,256,128]{1,2,0:T(8,128)(2,1)}, bf16[4,256,128]{1,2,0:T(8,128)(2,1)S(1)}, u32[]{:S(2)}, u32[]{:S(2)}) collective-permute-start(bf16[4,256,128]{1,2,0:T(8,128)(2,1)} %collective-permute-done), channel_id=1, source_target_pairs={{0,224},{16,240},{32,0},{48,16},{64,32},{80,48},{96,64},{112,80},{... | collective-permute-start | bytes 786440 | tf_op jit(solution)/shard_map/ppermute | solution.py:123
  26.9 8.6 %collective-permute-start.3 = (bf16[4,256,128]{1,2,0:T(8,128)(2,1)}, bf16[4,256,128]{1,2,0:T(8,128)(2,1)S(1)}, u32[]{:S(2)}, u32[]{:S(2)}) collective-permute-start(bf16[4,256,128]{1,2,0:T(8,128)(2,1)} %collective-permute-done.1), channel_id=1, source_target_pairs={{0,32},{16,48},{32,64},{48,80},{64,96},{80,112},{96,128},{112,144}... | collective-permute-start | bytes 786440 | tf_op jit(solution)/shard_map/ppermute | solution.py:119
  35.6 6.5 %collective-permute-start.4 = (bf16[4,256,128]{1,2,0:T(8,128)(2,1)S(1)}, bf16[4,256,128]{1,2,0:T(8,128)(2,1)S(1)}, u32[]{:S(2)}, u32[]{:S(2)}) collective-permute-start(bf16[4,256,128]{1,2,0:T(8,128)(2,1)S(1)} %collective-permute-done.2), channel_id=1, source_target_pairs={{0,224},{16,240},{32,0},{48,16},{64,32},{80,48},{96,64},{112,80},{... | collective-permute-start | bytes 786440 | tf_op jit(solution)/shard_map/ppermute | solution.py:123
  35.9 7.6 %collective-permute-start.5 = (bf16[4,256,128]{1,2,0:T(8,128)(2,1)S(1)}, bf16[4,256,128]{1,2,0:T(8,128)(2,1)S(1)}, u32[]{:S(2)}, u32[]{:S(2)}) collective-permute-start(bf16[4,256,128]{1,2,0:T(8,128)(2,1)S(1)} %collective-permute-done.3), channel_id=1, source_target_pairs={{0,32},{16,48},{32,64},{48,80},{64,96},{80,112},{96,128},{112,144}... | collective-permute-start | bytes 786440 | tf_op jit(solution)/shard_map/ppermute | solution.py:119
  43.6 7.7 %collective-permute-start.6 = (bf16[4,256,128]{1,2,0:T(8,128)(2,1)S(1)}, bf16[4,256,128]{1,2,0:T(8,128)(2,1)S(1)}, u32[]{:S(2)}, u32[]{:S(2)}) collective-permute-start(bf16[4,256,128]{1,2,0:T(8,128)(2,1)S(1)} %collective-permute-done.5), channel_id=1, source_target_pairs={{0,32},{16,48},{32,64},{48,80},{64,96},{80,112},{96,128},{112,144}... | collective-permute-start | bytes 786440 | tf_op jit(solution)/shard_map/ppermute | solution.py:119
  51.3 1.6 collective-permute-start.7
  53.1 10.4 %copy-start.1 = (bf16[2048,192]{1,0:T(8,128)(2,1)S(1)}, bf16[2048,192]{1,0:T(8,128)(2,1)}, u32[]{:S(2)}) copy-start(bf16[2048,192]{1,0:T(8,128)(2,1)} %pad_maximum_fusion) | copy-start | bytes 2359300
  54.3 24.8 %all-to-all-start = ((bf16[16,256,128]{2,1,0:T(8,128)(2,1)}), bf16[16,256,128]{2,1,0:T(8,128)(2,1)S(1)}, u32[]{:S(2)}, u32[]{:S(2)}) async-start(bf16[16,256,128]{2,1,0:T(8,128)(2,1)} %bitcast.5), calls=%async_computation | async-start | bytes 2097152 | tf_op jit(solution)/shard_map/all_to_all | solution.py:176
  66.0 0.8 copy-start.2
  132.7 7.1 %copy-start.6 = (bf16[2,2048,320]{1,2,0:T(8,128)(2,1)S(1)}, bf16[2,2048,320]{1,2,0:T(8,128)(2,1)}, u32[]{:S(2)}) copy-start(bf16[2,2048,320]{1,2,0:T(8,128)(2,1)} %param.18) | copy-start | bytes 7864324
  138.5 1.4 copy-start.4
  146.4 36.9 %all-to-all-start.2 = ((bf16[16,32,2048]{2,1,0:T(8,128)(2,1)}), bf16[16,32,2048]{2,1,0:T(8,128)(2,1)S(1)}, u32[]{:S(2)}, u32[]{:S(2)}) async-start(bf16[16,32,2048]{2,1,0:T(8,128)(2,1)} %bitcast.122), calls=%async_computation.2 | async-start | bytes 4194304 | tf_op jit(solution)/shard_map/all_to_all | solution.py:96
Sparse Core Ops, SparseCore 0:
  9.8 51.1 all-gather.2
  63.4 69.2 all-gather.4

commit v12 on v11

--- a/solution.py
+++ b/solution.py
@@ -124,7 +124,9 @@
             mine = jnp.where(mine_at == step, behind, mine)
             theirs = jnp.where(theirs_at == step, behind, theirs)
         if step == 1:
-            ahead, behind, rider = lax.optimization_barrier((ahead, behind, rider))
+            ahead, behind, rider[0] = lax.optimization_barrier((ahead, behind, rider[0]))
+        if step == 3:
+            ahead, behind, rider[1] = lax.optimization_barrier((ahead, behind, rider[1]))
         mine, theirs, ahead, behind = lax.optimization_barrier((mine, theirs, ahead, behind))
     swapped = lax.ppermute(theirs, "dp", [(i, i ^ 1) for i in range(group_count)])
     return slot_wanted % CORES == core, mine, swapped, rider
@@ -166,8 +168,12 @@
     kv_groups = KVH // local_kv
     by_head = prefix_cache.reshape(shard_rows, 2, kv_groups, kv_width)
     by_head = jnp.transpose(by_head, (2, 0, 1, 3)).reshape(kv_groups, shard_rows, 2 * kv_width)
-    on_core, mine, swapped, projection = fetch_slot(by_head, group_prefix, group_rank, projection)
-    out_full = lax.all_gather(out_weight, "tensor", axis=0, tiled=True)
+    half_cols = out_weight.shape[1] // 2
+    out_right = gather_rows(out_weight[:, half_cols:], "tensor")
+    on_core, mine, swapped, (projection, out_right) = fetch_slot(
+        by_head, group_prefix, group_rank, [projection, out_right]
+    )
+    out_left = lax.all_gather(out_weight[:, :half_cols], "tensor", axis=0, tiled=True)
     outgoing = jnp.where(
         on_core,
         jnp.repeat(mine, tensor_count // kv_groups, axis=0),
@@ -225,7 +231,13 @@
     attended = (blended / weight[:, :, None]).astype(jnp.bfloat16).reshape(group_tokens, query_width)
     every_head = gather_rows(jnp.transpose(attended)[None], "tensor")
     every_head = jnp.transpose(every_head.reshape(tensor_count * query_width, group_tokens))
-    attn_sum = jnp.dot(every_head, out_full, preferred_element_type=jnp.float32)
+    attn_sum = jnp.concatenate(
+        [
+            jnp.dot(every_head, out_left, preferred_element_type=jnp.float32),
+            jnp.dot(every_head, out_right, preferred_element_type=jnp.float32),
+        ],
+        axis=1,
+    )
     middle = (group_rows.astype(jnp.float32) + attn_sum).astype(jnp.bfloat16)
     segment = norm_rows(middle)
     gate_value = jnp.dot(segment, gate_up_weight[0], preferred_element_type=jnp.float32)

time: 194 us -> 201 us (1.036)
  waiting for transfers between devices: 94.5 us -> 70.1 us
  local copies, waits for them, and re-layouts: 6.4 us -> 17.6 us
  other arithmetic: 9.21 us -> 19.8 us
  blocking collectives: 20.8 us -> 26.6 us
  starting transfers between devices: 22.9 us -> 27.6 us
    all_gather x1, waiting for transfers between devices: 26.9 us -> 0.01 us  [on_device(): lax.all_gather(out_weight[:, :half_cols], 'tensor', axis=0, tiled=True)]
    all_to_all x1, blocking collectives: 20.8 us -> 26.6 us  [gather_rows(): received = lax.all_to_all(copies, axis, 0, 0, tiled=True)]
    all_to_all x0 -> x1, starting transfers between devices: none -> 5.3 us  [gather_rows(): received = lax.all_to_all(copies, axis, 0, 0, tiled=True)]
    select_n x3, other arithmetic: 1.2 us -> 6.04 us  [fetch_slot(): theirs = jnp.where(theirs_at == step, behind, theirs)]
    unnamed x18 -> x24, local copies, waits for them, and re-layouts: 2.72 us -> 5.43 us
    all_to_all x1, waiting for transfers between devices: 12.2 us -> 14.8 us  [on_device(): incoming = lax.all_to_all(outgoing, 'tensor', 0, 0, tiled=True)]
    dot_general x1 -> x2, matrix products: 5.78 us -> 5.59 us  [the longest x1 3 us: on_device(): jnp.dot(every_head, out_left, preferred_element_type=jnp.float32)]
  transfers between devices with their start and end apart: 12 -> 13, of which waited for: 9 -> 8; matrix products, arithmetic and copies ran while one was open for 10% -> 21% of each run, Pallas kernels for 0% -> 0%
where the time goes in v12:
time: 201 us; the launch traced here: 200 us
  waiting for transfers between devices  70.1 us (35%)
  starting transfers between devices  27.6 us (14%)
  blocking collectives  26.6 us (13%)
  other arithmetic  19.8 us (10%)
  matrix products  19.4 us (10%)
  between operations  18.4 us (9%)
  local copies, waits for them, and re-layouts  17.6 us (9%)
    all_to_all x1, waiting for transfers between devices, sum_scatter_rows(): received = lax.all_to_all(parts, axis, 0, 0, tiled=True)  30.9 us
    all_to_all x1, blocking collectives, gather_rows(): received = lax.all_to_all(copies, axis, 0, 0, tiled=True)  26.6 us
    all_to_all x1, waiting for transfers between devices, on_device(): incoming = lax.all_to_all(outgoing, 'tensor', 0, 0, tiled=True)  14.8 us
    ppermute x4, waiting for transfers between devices, fetch_slot(): ahead = lax.ppermute(ahead, 'dp', onward)  12.3 us
    ppermute x3, waiting for transfers between devices, fetch_slot(): behind = lax.ppermute(behind, 'dp', backward)  9.48 us
    ppermute x3, starting transfers between devices, fetch_slot(): behind = lax.ppermute(behind, 'dp', backward)  9.45 us
    all_to_all x1, starting transfers between devices, on_device(): incoming = lax.all_to_all(outgoing, 'tensor', 0, 0, tiled=True)  6.93 us
    select_n x3, other arithmetic, fetch_slot(): theirs = jnp.where(theirs_at == step, behind, theirs)  6.04 us
  transfers between devices with their start and end apart: 13, of which 8 were waited for; matrix products, arithmetic and copies ran while one was open for 21% of the time, Pallas kernels for 0%

profile of v12, /device:TPU:0, one launch (start us, length us, event | category | flops | bytes accessed | tf_op | source)
XLA Modules:
  0.0 199.6 jit_solution(5095812641902978982)
XLA Ops:
  10.5 5.3 %all-to-all-start = ((bf16[16,64,1024]{2,1,0:T(8,128)(2,1)}), bf16[16,64,1024]{2,1,0:T(8,128)(2,1)S(1)}, u32[]{:S(2)}, u32[]{:S(2)}) async-start(bf16[16,64,1024]{2,1,0:T(8,128)(2,1)} %broadcast_in_dim.24), calls=%async_computation | async-start | bytes 4194304 | tf_op jit(solution)/shard_map/all_to_all | solution.py:89
  19.3 5.9 %collective-permute-start = (bf16[4,256,128]{1,2,0:T(8,128)(2,1)}, bf16[4,256,128]{1,2,0:T(8,128)(2,1)}, u32[]{:S(2)}, u32[]{:S(2)}) collective-permute-start(bf16[4,256,128]{1,2,0:T(8,128)(2,1)} %bitcast.3), channel_id=1, source_target_pairs={{0,224},{16,240},{32,0},{48,16},{64,32},{80,48},{96,64},{112,80},{... | collective-permute-start | bytes 786440 | tf_op jit(solution)/shard_map/ppermute | solution.py:123
  25.2 2.5 %constant_dynamic-slice_fusion = (bf16[2048,64]{1,0:T(8,128)(2,1)}, bf16[2048,64]{1,0:T(8,128)(2,1)}) fusion(bf16[2048,256]{1,0:T(8,128)(2,1)} %param.16, s32[]{:T(128)S(6)} %select_n.173, bf16[2048,256]{1,0:T(8,128)(2,1)} %param.15), kind=kLoop, calls=%fused_computation.111 | loop fusion | bytes 1048580 | tf_op jit(solution)/shard_map/dynamic_slice | solution.py:164
  33.1 2.0 %copy.18 = bf16[2048,64]{1,0:T(8,128)(2,1)} copy(bf16[2048,64]{0,1:T(8,128)(2,1)} %param.14) | data formatting | bytes 524288 | tf_op args[4]
  35.1 2.9 %pad_maximum_fusion = bf16[2048,192]{1,0:T(8,128)(2,1)} fusion(bf16[2048,64]{1,0:T(8,128)(2,1)} %get-tuple-element.72, bf16[2048,64]{1,0:T(8,128)(2,1)} %get-tuple-element.73, bf16[2048,64]{1,0:T(8,128)(2,1)} %copy.18), kind=kLoop, calls=%fused_computation.45 | loop fusion | flops 2359296 | bytes 1572864 | tf_op jit(solution)/shard_map/concatenate | solution.py:165
  38.0 2.0 select_select_fusion.4
  40.0 3.2 %collective-permute-start.2 = (bf16[4,256,128]{1,2,0:T(8,128)(2,1)}, bf16[4,256,128]{1,2,0:T(8,128)(2,1)}, u32[]{:S(2)}, u32[]{:S(2)}) collective-permute-start(bf16[4,256,128]{1,2,0:T(8,128)(2,1)} %collective-permute-done), channel_id=1, source_target_pairs={{0,224},{16,240},{32,0},{48,16},{64,32},{80,48},{96,64},{112,80},{... | collective-permute-start | bytes 786440 | tf_op jit(solution)/shard_map/ppermute | solution.py:123
  43.2 5.1 %collective-permute-done.2 = bf16[4,256,128]{1,2,0:T(8,128)(2,1)} collective-permute-done((bf16[4,256,128]{1,2,0:T(8,128)(2,1)}, bf16[4,256,128]{1,2,0:T(8,128)(2,1)}, u32[]{:S(2)}, u32[]{:S(2)}) %collective-permute-start.2) | collective-permute-done | bytes 262176 | tf_op jit(solution)/shard_map/ppermute | solution.py:123
  48.3 3.4 %collective-permute-done.3 = bf16[4,256,128]{1,2,0:T(8,128)(2,1)} collective-permute-done((bf16[4,256,128]{1,2,0:T(8,128)(2,1)}, bf16[4,256,128]{1,2,0:T(8,128)(2,1)}, u32[]{:S(2)}, u32[]{:S(2)}) %collective-permute-start.3) | collective-permute-done | bytes 262176 | tf_op jit(solution)/shard_map/ppermute | solution.py:119
  51.7 2.0 %select_select_fusion.2 = (bf16[4,256,128]{1,2,0:T(8,128)(2,1)}, bf16[4,256,128]{1,2,0:T(8,128)(2,1)}) fusion(bf16[4,256,128]{1,2,0:T(8,128)(2,1)} %collective-permute-done.2, bf16[4,256,128]{1,2,0:T(8,128)(2,1)} %collective-permute-done.3, bf16[4,256,128]{1,2,0:T(8,128)(2,1)} %get-tuple-element.28, pred[]{:T(512)S(6)} %eq.80, pred[]{:T(512)S(6)} %eq.79, ...), kind=kLoop, calls=%fused_computation.62 | loop fusion | flops 524288 | bytes 1572868 | tf_op jit(solution)/shard_map/jit(_where)/select_n | solution.py:125
  56.0 4.4 %collective-permute-done.4 = bf16[4,256,128]{1,2,0:T(8,128)(2,1)} collective-permute-done((bf16[4,256,128]{1,2,0:T(8,128)(2,1)}, bf16[4,256,128]{1,2,0:T(8,128)(2,1)}, u32[]{:S(2)}, u32[]{:S(2)}) %collective-permute-start.4) | collective-permute-done | bytes 262176 | tf_op jit(solution)/shard_map/ppermute | solution.py:123
  62.0 2.1 %select_select_fusion = (bf16[4,256,128]{1,2,0:T(8,128)(2,1)}, bf16[4,256,128]{1,2,0:T(8,128)(2,1)}) fusion(bf16[4,256,128]{1,2,0:T(8,128)(2,1)} %collective-permute-done.4, bf16[4,256,128]{1,2,0:T(8,128)(2,1)} %collective-permute-done.5, bf16[4,256,128]{1,2,0:T(8,128)(2,1)} %get-tuple-element.32, pred[]{:T(512)S(6)} %eq.83, pred[]{:T(512)S(6)} %eq.82, ...), kind=kLoop, calls=%fused_computation.60 | loop fusion | flops 524288 | bytes 1572868 | tf_op jit(solution)/shard_map/jit(_where)/select_n | solution.py:125
  64.7 7.3 %collective-permute-done.6 = bf16[4,256,128]{1,2,0:T(8,128)(2,1)} collective-permute-done((bf16[4,256,128]{1,2,0:T(8,128)(2,1)}, bf16[4,256,128]{1,2,0:T(8,128)(2,1)}, u32[]{:S(2)}, u32[]{:S(2)}) %collective-permute-start.6) | collective-permute-done | bytes 262176 | tf_op jit(solution)/shard_map/ppermute | solution.py:119
  79.2 2.2 %broadcast_in_dim.25 = bf16[4,4,256,128]{3,2,1,0:T(8,128)(2,1)} broadcast(bf16[4,256,128]{2,1,0:T(8,128)(2,1)} %copy.19), dimensions={0,2,3} | broadcast | bytes 1310720 | tf_op jit(solution)/shard_map/broadcast_in_dim | solution.py:179
  81.4 6.9 %all-to-all-start.1 = ((bf16[16,256,128]{2,1,0:T(8,128)(2,1)}), bf16[16,256,128]{2,1,0:T(8,128)(2,1)S(1)}, u32[]{:S(2)}, u32[]{:S(2)}) async-start(bf16[16,256,128]{2,1,0:T(8,128)(2,1)} %bitcast.128), calls=%async_computation.1 | async-start | bytes 2097152 | tf_op jit(solution)/shard_map/all_to_all | solution.py:182
  88.4 2.3 %fusion.5 = f32[512]{0:T(512)S(1)} fusion(bf16[512,2048]{1,0:T(8,128)(2,1)} %all-gather.3.cloned.1.call-done), kind=kLoop, calls=%fused_computation.12 | loop fusion | flops 3145216 | bytes 2099200 | tf_op jit(solution)/shard_map/reduce_sum | solution.py:49
  90.7 2.2 %fusion.11 = f32[512,192]{0,1:T(8,128)S(1)} fusion(bf16[2048,192]{1,0:T(8,128)(2,1)} %pad_maximum_fusion, bf16[512,2048]{1,0:T(8,128)(2,1)S(1)} %copy-done.1, f32[512]{0:T(512)S(1)} %add_rsqrt_fusion.1), kind=kOutput, calls=%fused_computation.19 | convolution fusion | flops 405798912 | bytes 3278848 | tf_op jit(solution)/shard_map/dot_general | solution.py:191
  94.2 14.8 %all-to-all-done.1 = bf16[16,256,128]{2,1,0:T(8,128)(2,1)S(1)} async-done(((bf16[16,256,128]{2,1,0:T(8,128)(2,1)}), bf16[16,256,128]{2,1,0:T(8,128)(2,1)S(1)}, u32[]{:S(2)}, u32[]{:S(2)}) %all-to-all-start.1) | async-done | bytes 1048608 | tf_op jit(solution)/shard_map/all_to_all | solution.py:182
  115.1 26.6 %all_to_all.20 = bf16[16,1,64,512]{3,2,1,0:T(8,128)(2,1)S(1)} all-to-all(bf16[16,1,64,512]{3,2,1,0:T(8,128)(2,1)S(1)} %broadcast_in_dim.29), channel_id=1, replica_groups=mesh['dp'=16,'tensor'=16] {'tensor'}, dimensions={0} | all-to-all | bytes 2097152 | tf_op jit(solution)/shard_map/all_to_all | solution.py:89
  141.7 2.6 %fusion.100 = f32[512,1024]{1,0:T(8,128)} fusion(bf16[1024,512]{1,0:T(8,128)(2,1)S(1)} %bitcast.125, bf16[1024,1024]{1,0:T(8,128)(2,1)S(1)} %bitcast.127), kind=kOutput, calls=%fused_computation.124 | convolution fusion | flops 1073741824 | bytes 5242880 | tf_op jit(solution)/shard_map/dot_general | solution.py:237
  144.3 3.0 %fusion.99 = f32[512,1024]{1,0:T(8,128)S(1)} fusion(bf16[1024,512]{1,0:T(8,128)(2,1)S(1)} %bitcast.126, bf16[1024,1024]{1,0:T(8,128)(2,1)} %all-gather.5.cloned.1.call-done), kind=kOutput, calls=%fused_computation.123 | convolution fusion | flops 1073741824 | bytes 5242880 | tf_op jit(solution)/shard_map/dot_general | solution.py:236
  151.1 5.0 %convolution_convert_fusion = bf16[512,2048]{1,0:T(8,128)(2,1)} fusion(bf16[320,2048]{1,0:T(8,128)(2,1)S(1)} %copy-done, bf16[2,2048,320]{1,2,0:T(8,128)(2,1)} %param.18, bf16[512,2048]{1,0:T(8,128)(2,1)S(1)} %get-tuple-element.42, f32[512]{0:T(512)S(1)} %add_rsqrt_fusion, f32[512,320]{0,1:T(8,128)} %fusion.17), kind=kOutput, calls=%fused_computation.18 | convolution fusion | flops 1347354624 | bytes 7473152 | tf_op jit(solution)/shard_map/dot_general | solution.py:247
  156.1 3.7 %all-to-all-start.3 = ((bf16[16,32,2048]{2,1,0:T(8,128)(2,1)}), bf16[16,32,2048]{2,1,0:T(8,128)(2,1)S(1)}, u32[]{:S(2)}, u32[]{:S(2)}) async-start(bf16[16,32,2048]{2,1,0:T(8,128)(2,1)} %bitcast.129), calls=%async_computation.3 | async-start | bytes 4194304 | tf_op jit(solution)/shard_map/all_to_all | solution.py:96
  159.8 30.9 %all-to-all-done.3 = bf16[16,32,2048]{2,1,0:T(8,128)(2,1)S(1)} async-done(((bf16[16,32,2048]{2,1,0:T(8,128)(2,1)}), bf16[16,32,2048]{2,1,0:T(8,128)(2,1)S(1)}, u32[]{:S(2)}, u32[]{:S(2)}) %all-to-all-start.3) | async-done | bytes 2097184 | tf_op jit(solution)/shard_map/all_to_all | solution.py:96
  (69 shorter events, 32.8 us)
Async XLA Ops:
  6.5 144.6 %copy-start = (bf16[320,2048]{1,0:T(8,128)(2,1)S(1)}, bf16[320,2048]{1,0:T(8,128)(2,1)}, u32[]{:S(2)}) copy-start(bf16[320,2048]{1,0:T(8,128)(2,1)} %param.19) | copy-start | bytes 3932164
  6.5 81.8 %all-gather.3.cloned.1.call-start = ((), (), s32[]{:S(2)}) async-start(), calls=%async_computation.4 | async-start | bytes 2228224 | tf_op jit(solution)/shard_map/all_gather | solution.py:188
  10.5 53.5 %all-to-all-start = ((bf16[16,64,1024]{2,1,0:T(8,128)(2,1)}), bf16[16,64,1024]{2,1,0:T(8,128)(2,1)S(1)}, u32[]{:S(2)}, u32[]{:S(2)}) async-start(bf16[16,64,1024]{2,1,0:T(8,128)(2,1)} %broadcast_in_dim.24), calls=%async_computation | async-start | bytes 4194304 | tf_op jit(solution)/shard_map/all_to_all | solution.py:89
  15.8 11.9 %copy-start.8 = (s32[16]{0:T(128)S(1)}, s32[16]{0:T(128)}, u32[]{:S(2)}) copy-start(s32[16]{0:T(128)} %param.12) | copy-start | bytes 196
  15.8 128.5 %all-gather.5.cloned.1.call-start = ((), (), s32[]{:S(2)}) async-start(), calls=%async_computation.5 | async-start | bytes 2228224 | tf_op jit(solution)/shard_map/all_gather | solution.py:176
  19.3 18.7 %collective-permute-start = (bf16[4,256,128]{1,2,0:T(8,128)(2,1)}, bf16[4,256,128]{1,2,0:T(8,128)(2,1)}, u32[]{:S(2)}, u32[]{:S(2)}) collective-permute-start(bf16[4,256,128]{1,2,0:T(8,128)(2,1)} %bitcast.3), channel_id=1, source_target_pairs={{0,224},{16,240},{32,0},{48,16},{64,32},{80,48},{96,64},{112,80},{... | collective-permute-start | bytes 786440 | tf_op jit(solution)/shard_map/ppermute | solution.py:123
  25.2 12.8 %collective-permute-start.1 = (bf16[4,256,128]{1,2,0:T(8,128)(2,1)}, bf16[4,256,128]{1,2,0:T(8,128)(2,1)}, u32[]{:S(2)}, u32[]{:S(2)}) collective-permute-start(bf16[4,256,128]{1,2,0:T(8,128)(2,1)} %bitcast.3), channel_id=1, source_target_pairs={{0,32},{16,48},{32,64},{48,80},{64,96},{80,112},{96,128},{112,144}... | collective-permute-start | bytes 786440 | tf_op jit(solution)/shard_map/ppermute | solution.py:119
  38.0 17.8 %copy-start.10 = (s32[1,8]{1,0:T(1,128)S(1)}, s32[1,8]{1,0:T(1,128)}, u32[]{:S(2)}) copy-start(s32[1,8]{1,0:T(1,128)} %param.11) | copy-start | bytes 100
  40.0 8.3 %collective-permute-start.2 = (bf16[4,256,128]{1,2,0:T(8,128)(2,1)}, bf16[4,256,128]{1,2,0:T(8,128)(2,1)}, u32[]{:S(2)}, u32[]{:S(2)}) collective-permute-start(bf16[4,256,128]{1,2,0:T(8,128)(2,1)} %collective-permute-done), channel_id=1, source_target_pairs={{0,224},{16,240},{32,0},{48,16},{64,32},{80,48},{96,64},{112,80},{... | collective-permute-start | bytes 786440 | tf_op jit(solution)/shard_map/ppermute | solution.py:123
  43.2 8.5 %collective-permute-start.3 = (bf16[4,256,128]{1,2,0:T(8,128)(2,1)}, bf16[4,256,128]{1,2,0:T(8,128)(2,1)}, u32[]{:S(2)}, u32[]{:S(2)}) collective-permute-start(bf16[4,256,128]{1,2,0:T(8,128)(2,1)} %collective-permute-done.1), channel_id=1, source_target_pairs={{0,32},{16,48},{32,64},{48,80},{64,96},{80,112},{96,128},{112,144}... | collective-permute-start | bytes 786440 | tf_op jit(solution)/shard_map/ppermute | solution.py:119
  53.7 6.7 %collective-permute-start.4 = (bf16[4,256,128]{1,2,0:T(8,128)(2,1)}, bf16[4,256,128]{1,2,0:T(8,128)(2,1)}, u32[]{:S(2)}, u32[]{:S(2)}) collective-permute-start(bf16[4,256,128]{1,2,0:T(8,128)(2,1)} %collective-permute-done.2), channel_id=1, source_target_pairs={{0,224},{16,240},{32,0},{48,16},{64,32},{80,48},{96,64},{112,80},{... | collective-permute-start | bytes 786440 | tf_op jit(solution)/shard_map/ppermute | solution.py:123
  54.1 7.9 %collective-permute-start.5 = (bf16[4,256,128]{1,2,0:T(8,128)(2,1)}, bf16[4,256,128]{1,2,0:T(8,128)(2,1)}, u32[]{:S(2)}, u32[]{:S(2)}) collective-permute-start(bf16[4,256,128]{1,2,0:T(8,128)(2,1)} %collective-permute-done.3), channel_id=1, source_target_pairs={{0,32},{16,48},{32,64},{48,80},{64,96},{80,112},{96,128},{112,144}... | collective-permute-start | bytes 786440 | tf_op jit(solution)/shard_map/ppermute | solution.py:119
  64.0 17.4 %copy-start.4 = (bf16[16,64,1024]{2,1,0:T(8,128)(2,1)}, bf16[16,64,1024]{2,1,0:T(8,128)(2,1)S(1)}, u32[]{:S(2)}) copy-start(bf16[16,64,1024]{2,1,0:T(8,128)(2,1)S(1)} %all-to-all-done) | copy-start | bytes 6291460
  64.0 7.9 %collective-permute-start.6 = (bf16[4,256,128]{1,2,0:T(8,128)(2,1)}, bf16[4,256,128]{1,2,0:T(8,128)(2,1)}, u32[]{:S(2)}, u32[]{:S(2)}) collective-permute-start(bf16[4,256,128]{1,2,0:T(8,128)(2,1)} %collective-permute-done.5), channel_id=1, source_target_pairs={{0,32},{16,48},{32,64},{48,80},{64,96},{80,112},{96,128},{112,144}... | collective-permute-start | bytes 786440 | tf_op jit(solution)/shard_map/ppermute | solution.py:119
  73.8 1.9 collective-permute-start.7
  81.4 27.6 %all-to-all-start.1 = ((bf16[16,256,128]{2,1,0:T(8,128)(2,1)}), bf16[16,256,128]{2,1,0:T(8,128)(2,1)S(1)}, u32[]{:S(2)}, u32[]{:S(2)}) async-start(bf16[16,256,128]{2,1,0:T(8,128)(2,1)} %bitcast.128), calls=%async_computation.1 | async-start | bytes 2097152 | tf_op jit(solution)/shard_map/all_to_all | solution.py:182
  88.4 2.3 %copy-start.1 = (bf16[512,2048]{1,0:T(8,128)(2,1)S(1)}, bf16[512,2048]{1,0:T(8,128)(2,1)}, u32[]{:S(2)}) copy-start(bf16[512,2048]{1,0:T(8,128)(2,1)} %all-gather.3.cloned.1.call-done) | copy-start | bytes 6291460
  92.9 0.8 copy-start.7
  113.6 28.1 %copy-start.5 = (bf16[16,64,1024]{2,1,0:T(8,128)(2,1)S(1)}, bf16[16,64,1024]{2,1,0:T(8,128)(2,1)}, u32[]{:S(2)}) copy-start(bf16[16,64,1024]{2,1,0:T(8,128)(2,1)} %copy-done.4) | copy-start | bytes 6291460
  144.3 3.0 %copy-start.2 = (bf16[512,2048]{1,0:T(8,128)(2,1)S(1)}, bf16[512,2048]{1,0:T(8,128)(2,1)}, u32[]{:S(2)}) copy-start(bf16[512,2048]{1,0:T(8,128)(2,1)} %all-gather.3.cloned.1.call-done) | copy-start | bytes 6291460
  144.3 3.0 %copy-start.3 = (f32[512,1024]{1,0:T(8,128)S(1)}, f32[512,1024]{1,0:T(8,128)}, u32[]{:S(2)}) copy-start(f32[512,1024]{1,0:T(8,128)} %fusion.100) | copy-start | bytes 6291460
  147.3 1.9 copy-start.9
  148.0 3.0 %copy-start.6 = (bf16[512,2048]{1,0:T(8,128)(2,1)}, bf16[512,2048]{1,0:T(8,128)(2,1)S(1)}, u32[]{:S(2)}) copy-start(bf16[512,2048]{1,0:T(8,128)(2,1)S(1)} %get-tuple-element.42) | copy-start | bytes 6291460
  156.1 34.7 %all-to-all-start.3 = ((bf16[16,32,2048]{2,1,0:T(8,128)(2,1)}), bf16[16,32,2048]{2,1,0:T(8,128)(2,1)S(1)}, u32[]{:S(2)}, u32[]{:S(2)}) async-start(bf16[16,32,2048]{2,1,0:T(8,128)(2,1)} %bitcast.129), calls=%async_computation.3 | async-start | bytes 4194304 | tf_op jit(solution)/shard_map/all_to_all | solution.py:96
Sparse Core Ops, SparseCore 0:
  9.8 64.3 all-gather.2
  76.6 63.3 all-gather.4

commit v13 on v9

--- a/solution.py
+++ b/solution.py
@@ -123,7 +123,7 @@
             behind = lax.ppermute(behind, "dp", backward)
             mine = jnp.where(mine_at == step, behind, mine)
             theirs = jnp.where(theirs_at == step, behind, theirs)
-        if step == 1:
+        if step == 2:
             ahead, behind, rider = lax.optimization_barrier((ahead, behind, rider))
         mine, theirs, ahead, behind = lax.optimization_barrier((mine, theirs, ahead, behind))
     swapped = lax.ppermute(theirs, "dp", [(i, i ^ 1) for i in range(group_count)])

time: 179 us -> 188 us (1.050)
  local copies, waits for them, and re-layouts: 13 us -> 17.3 us
    all_to_all x1, waiting for transfers between devices: 3.34 us -> 0.01 us  [gather_rows(): received = lax.all_to_all(copies, axis, 0, 0, tiled=True)]
    all_to_all x1, waiting for transfers between devices: 12.4 us -> 15.4 us  [on_device(): incoming = lax.all_to_all(outgoing, 'tensor', 0, 0, tiled=True)]
    all_to_all x1, starting transfers between devices: 4.53 us -> 7.22 us  [on_device(): incoming = lax.all_to_all(outgoing, 'tensor', 0, 0, tiled=True)]
  transfers between devices with their start and end apart: 12 -> 12, of which waited for: 7 -> 7; matrix products, arithmetic and copies ran while one was open for 17% -> 19% of each run, Pallas kernels for 0% -> 0%
where the time goes in v13:
time: 188 us; the launch traced here: 186 us
  waiting for transfers between devices  64 us (34%)
  starting transfers between devices  27.9 us (15%)
  blocking collectives  20.6 us (11%)
  matrix products  20 us (11%)
  between operations  18.8 us (10%)
  other arithmetic  17.8 us (9%)
  local copies, waits for them, and re-layouts  17.3 us (9%)
    all_to_all x1, waiting for transfers between devices, sum_scatter_rows(): received = lax.all_to_all(parts, axis, 0, 0, tiled=True)  29.7 us
    all_to_all x1, blocking collectives, gather_rows(): received = lax.all_to_all(copies, axis, 0, 0, tiled=True)  20.6 us
    all_to_all x1, waiting for transfers between devices, on_device(): incoming = lax.all_to_all(outgoing, 'tensor', 0, 0, tiled=True)  15.4 us
    ppermute x4, waiting for transfers between devices, fetch_slot(): ahead = lax.ppermute(ahead, 'dp', onward)  12 us
    ppermute x3, starting transfers between devices, fetch_slot(): behind = lax.ppermute(behind, 'dp', backward)  9.7 us
    all_to_all x1, starting transfers between devices, on_device(): incoming = lax.all_to_all(outgoing, 'tensor', 0, 0, tiled=True)  7.22 us
    all_to_all x1, starting transfers between devices, gather_rows(): received = lax.all_to_all(copies, axis, 0, 0, tiled=True)  7.17 us
    unnamed x24, local copies, waits for them, and re-layouts  6.75 us
  transfers between devices with their start and end apart: 12, of which 7 were waited for; matrix products, arithmetic and copies ran while one was open for 19% of the time, Pallas kernels for 0%

profile of v13, /device:TPU:0, one launch (start us, length us, event | category | flops | bytes accessed | tf_op | source)
XLA Modules:
  0.0 186.4 jit_solution(9006540691867379111)
XLA Ops:
  8.5 4.1 %collective-permute-start = (bf16[4,256,128]{1,2,0:T(8,128)(2,1)}, bf16[4,256,128]{1,2,0:T(8,128)(2,1)}, u32[]{:S(2)}, u32[]{:S(2)}) collective-permute-start(bf16[4,256,128]{1,2,0:T(8,128)(2,1)} %bitcast.4), channel_id=1, source_target_pairs={{0,224},{16,240},{32,0},{48,16},{64,32},{80,48},{96,64},{112,80},{... | collective-permute-start | bytes 786440 | tf_op jit(solution)/shard_map/ppermute | solution.py:123
  12.6 2.5 %broadcast_in_dim.23 = bf16[16,32,2048]{2,1,0:T(8,128)(2,1)} broadcast(bf16[32,2048]{1,0:T(8,128)(2,1)} %param.10), dimensions={1,2} | broadcast | bytes 2228224 | tf_op jit(solution)/shard_map/broadcast_in_dim | solution.py:88
  15.1 7.2 %all-to-all-start = ((bf16[16,32,2048]{2,1,0:T(8,128)(2,1)}), bf16[16,32,2048]{2,1,0:T(8,128)(2,1)S(1)}, u32[]{:S(2)}, u32[]{:S(2)}) async-start(bf16[16,32,2048]{2,1,0:T(8,128)(2,1)} %broadcast_in_dim.23), calls=%async_computation | async-start | bytes 4194304 | tf_op jit(solution)/shard_map/all_to_all | solution.py:89
  28.8 2.0 %select_select_fusion.4 = (bf16[4,256,128]{1,2,0:T(8,128)(2,1)}, bf16[4,256,128]{1,2,0:T(8,128)(2,1)}) fusion(bf16[4,256,128]{1,2,0:T(8,128)(2,1)} %collective-permute-done, bf16[4,256,128]{1,2,0:T(8,128)(2,1)} %collective-permute-done.1, pred[]{:T(512)S(6)} %eq.77, pred[]{:T(512)S(6)} %eq.76, bf16[4,256,2,64]{1,3,2,0:T(8,128)(2,1)} %copy.17, pred[]{:T(512)S(6)} %eq.75, ...), kind=kLoop, calls=%fused_computation.62 | loop fusion | flops 524288 | bytes 1310724 | tf_op jit(solution)/shard_map/jit(_where)/select_n | solution.py:125
  30.8 3.2 %collective-permute-start.2 = (bf16[4,256,128]{1,2,0:T(8,128)(2,1)}, bf16[4,256,128]{1,2,0:T(8,128)(2,1)}, u32[]{:S(2)}, u32[]{:S(2)}) collective-permute-start(bf16[4,256,128]{1,2,0:T(8,128)(2,1)} %collective-permute-done), channel_id=1, source_target_pairs={{0,224},{16,240},{32,0},{48,16},{64,32},{80,48},{96,64},{112,80},{... | collective-permute-start | bytes 786440 | tf_op jit(solution)/shard_map/ppermute | solution.py:123
  34.0 2.6 %constant_dynamic-slice_fusion = (bf16[2048,64]{1,0:T(8,128)(2,1)}, bf16[2048,64]{1,0:T(8,128)(2,1)}) fusion(bf16[2048,256]{1,0:T(8,128)(2,1)} %param.16, s32[]{:T(128)S(6)} %select_n.180, bf16[2048,256]{1,0:T(8,128)(2,1)} %param.15), kind=kLoop, calls=%fused_computation.109 | loop fusion | bytes 1048580 | tf_op jit(solution)/shard_map/dynamic_slice | solution.py:162
  36.6 2.0 %copy.18 = bf16[2048,64]{1,0:T(8,128)(2,1)} copy(bf16[2048,64]{0,1:T(8,128)(2,1)} %param.14) | data formatting | bytes 524288 | tf_op args[4]
  38.6 2.9 %pad_maximum_fusion = bf16[2048,192]{1,0:T(8,128)(2,1)} fusion(bf16[2048,64]{1,0:T(8,128)(2,1)} %get-tuple-element.66, bf16[2048,64]{1,0:T(8,128)(2,1)} %get-tuple-element.67, bf16[2048,64]{1,0:T(8,128)(2,1)} %copy.18), kind=kLoop, calls=%fused_computation.43 | loop fusion | flops 2359296 | bytes 1572864 | tf_op jit(solution)/shard_map/concatenate | solution.py:163
  44.4 2.3 %collective-permute-start.4 = (bf16[4,256,128]{1,2,0:T(8,128)(2,1)}, bf16[4,256,128]{1,2,0:T(8,128)(2,1)}, u32[]{:S(2)}, u32[]{:S(2)}) collective-permute-start(bf16[4,256,128]{1,2,0:T(8,128)(2,1)} %collective-permute-done.2), channel_id=1, source_target_pairs={{0,224},{16,240},{32,0},{48,16},{64,32},{80,48},{96,64},{112,80},{... | collective-permute-start | bytes 786440 | tf_op jit(solution)/shard_map/ppermute | solution.py:123
  46.9 4.3 %collective-permute-done.4 = bf16[4,256,128]{1,2,0:T(8,128)(2,1)} collective-permute-done((bf16[4,256,128]{1,2,0:T(8,128)(2,1)}, bf16[4,256,128]{1,2,0:T(8,128)(2,1)}, u32[]{:S(2)}, u32[]{:S(2)}) %collective-permute-start.4) | collective-permute-done | bytes 262176 | tf_op jit(solution)/shard_map/ppermute | solution.py:123
  51.3 3.4 %collective-permute-done.5 = bf16[4,256,128]{1,2,0:T(8,128)(2,1)} collective-permute-done((bf16[4,256,128]{1,2,0:T(8,128)(2,1)}, bf16[4,256,128]{1,2,0:T(8,128)(2,1)}, u32[]{:S(2)}, u32[]{:S(2)}) %collective-permute-start.5) | collective-permute-done | bytes 262176 | tf_op jit(solution)/shard_map/ppermute | solution.py:119
  54.7 2.1 %select_select_fusion = (bf16[4,256,128]{1,2,0:T(8,128)(2,1)}, bf16[4,256,128]{1,2,0:T(8,128)(2,1)}) fusion(bf16[4,256,128]{1,2,0:T(8,128)(2,1)} %collective-permute-done.4, bf16[4,256,128]{1,2,0:T(8,128)(2,1)} %collective-permute-done.5, bf16[4,256,128]{1,2,0:T(8,128)(2,1)} %get-tuple-element.30, pred[]{:T(512)S(6)} %eq.83, pred[]{:T(512)S(6)} %eq.82, ...), kind=kLoop, calls=%fused_computation.58 | loop fusion | flops 524288 | bytes 1572868 | tf_op jit(solution)/shard_map/jit(_where)/select_n | solution.py:125
  56.9 7.7 %collective-permute-done.6 = bf16[4,256,128]{1,2,0:T(8,128)(2,1)} collective-permute-done((bf16[4,256,128]{1,2,0:T(8,128)(2,1)}, bf16[4,256,128]{1,2,0:T(8,128)(2,1)}, u32[]{:S(2)}, u32[]{:S(2)}) %collective-permute-start.6) | collective-permute-done | bytes 262176 | tf_op jit(solution)/shard_map/ppermute | solution.py:119
  64.7 2.0 %broadcast_select_fusion = (bf16[4,256,128]{1,2,0:T(8,128)(2,1)}, bf16[4,256,128]{1,2,0:T(8,128)(2,1)}) fusion(bf16[4,256,128]{1,2,0:T(8,128)(2,1)} %collective-permute-done.6, bf16[4,256,128]{1,2,0:T(8,128)(2,1)} %get-tuple-element.33, pred[]{:T(512)S(6)} %eq.84, bf16[4,256,128]{1,2,0:T(8,128)(2,1)} %get-tuple-element.32, pred[]{:T(512)S(6)} %eq.71), kind=kLoop, calls=%fused_computation.64 | loop fusion | flops 262144 | bytes 1310722 | tf_op jit(solution)/shard_map/jit(_where)/select_n | solution.py:121
  72.0 2.1 %broadcast_in_dim.25 = bf16[4,4,256,128]{3,2,1,0:T(8,128)(2,1)} broadcast(bf16[4,256,128]{2,1,0:T(8,128)(2,1)} %copy.19), dimensions={0,2,3} | broadcast | bytes 1310720 | tf_op jit(solution)/shard_map/broadcast_in_dim | solution.py:173
  74.1 7.2 %all-to-all-start.1 = ((bf16[16,256,128]{2,1,0:T(8,128)(2,1)}), bf16[16,256,128]{2,1,0:T(8,128)(2,1)}, u32[]{:S(2)}, u32[]{:S(2)}) async-start(bf16[16,256,128]{2,1,0:T(8,128)(2,1)} %bitcast.128), calls=%async_computation.1 | async-start | bytes 2097152 | tf_op jit(solution)/shard_map/all_to_all | solution.py:176
  86.3 15.4 %all-to-all-done.1 = bf16[16,256,128]{2,1,0:T(8,128)(2,1)} async-done(((bf16[16,256,128]{2,1,0:T(8,128)(2,1)}), bf16[16,256,128]{2,1,0:T(8,128)(2,1)}, u32[]{:S(2)}, u32[]{:S(2)}) %all-to-all-start.1) | async-done | bytes 1048608 | tf_op jit(solution)/shard_map/all_to_all | solution.py:176
  101.8 2.5 %multiply_reduce_fusion = (f32[512]{0:T(512)S(1)}, f32[4096,512]{1,0:T(8,128)S(1)}) fusion(bf16[512,1,32]{0,2,1:T(8,128)(2,1)S(1)} %get-tuple-element.54, bf16[512,1,32]{0,2,1:T(8,128)(2,1)S(1)} %get-tuple-element.55, bf16[4096,128]{1,0:T(8,128)(2,1)} %bitcast.7), kind=kOutput, calls=%fused_computation.2 | convolution fusion | flops 272760320 | bytes 9504768 | tf_op jit(solution)/shard_map/thd,nhd->thn/dot_general | solution.py:56
  105.7 3.1 %fusion.37 = f32[1,64,512]{2,1,0:T(8,128)S(1)} fusion(f32[4096,512]{1,0:T(8,128)S(1)} %get-tuple-element.61, f32[512]{0:T(512)S(1)} %get-tuple-element.60, bf16[4096,128]{1,0:T(8,128)(2,1)} %bitcast.7, f32[512]{0:T(512)S(1)} %get-tuple-element.39, f32[512]{0:T(512)S(1)} %get-tuple-element.57, f32[512]{0:T(512)S(1)} %get-tuple-element.56), kind=kOutput, calls=%fused_computation.37 | convolution fusion | flops 274825216 | bytes 9576448 | tf_op jit(solution)/shard_map/thn,nhd->thd/dot_general | solution.py:64
  110.2 20.6 %all_to_all.20 = bf16[16,1,64,512]{3,2,1,0:T(8,128)(2,1)} all-to-all(bf16[16,1,64,512]{3,2,1,0:T(8,128)(2,1)S(1)} %broadcast_in_dim.29), channel_id=1, replica_groups=mesh['dp'=16,'tensor'=16] {'tensor'}, dimensions={0} | all-to-all | bytes 2097152 | tf_op jit(solution)/shard_map/all_to_all | solution.py:89
  130.8 5.4 %fusion.3 = (f32[512]{0:T(512)S(1)}, bf16[512,2048]{1,0:T(8,128)(2,1)S(1)}) fusion(bf16[1024,512]{1,0:T(8,128)(2,1)} %bitcast.130, bf16[1024,2048]{1,0:T(8,128)(2,1)} %all-gather.2.cloned.1.call-done, bf16[16,32,2048]{2,1,0:T(8,128)(2,1)S(1)} %all-to-all-done), kind=kOutput, calls=%fused_computation.7 | convolution fusion | flops 2153774592 | bytes 9439232 | tf_op jit(solution)/shard_map/dot_general | solution.py:228
  138.6 5.5 %convolution_convert_fusion = bf16[512,2048]{1,0:T(8,128)(2,1)} fusion(bf16[320,2048]{1,0:T(8,128)(2,1)S(1)} %copy-done, bf16[2,2048,320]{1,2,0:T(8,128)(2,1)} %param.18, bf16[512,2048]{1,0:T(8,128)(2,1)} %copy-done.7, f32[512]{0:T(512)S(1)} %add_rsqrt_fusion.1, f32[512,320]{0,1:T(8,128)S(1)} %fusion.14), kind=kOutput, calls=%fused_computation.18 | convolution fusion | flops 1347354624 | bytes 7473152 | tf_op jit(solution)/shard_map/dot_general | solution.py:235
  144.1 3.7 %all-to-all-start.3 = ((bf16[16,32,2048]{2,1,0:T(8,128)(2,1)}), bf16[16,32,2048]{2,1,0:T(8,128)(2,1)S(1)}, u32[]{:S(2)}, u32[]{:S(2)}) async-start(bf16[16,32,2048]{2,1,0:T(8,128)(2,1)} %bitcast.129), calls=%async_computation.3 | async-start | bytes 4194304 | tf_op jit(solution)/shard_map/all_to_all | solution.py:96
  147.9 29.7 %all-to-all-done.3 = bf16[16,32,2048]{2,1,0:T(8,128)(2,1)S(1)} async-done(((bf16[16,32,2048]{2,1,0:T(8,128)(2,1)}), bf16[16,32,2048]{2,1,0:T(8,128)(2,1)S(1)}, u32[]{:S(2)}, u32[]{:S(2)}) %all-to-all-start.3) | async-done | bytes 2097184 | tf_op jit(solution)/shard_map/all_to_all | solution.py:96
  (65 shorter events, 23.8 us)
Async XLA Ops:
  6.5 132.1 %copy-start = (bf16[320,2048]{1,0:T(8,128)(2,1)S(1)}, bf16[320,2048]{1,0:T(8,128)(2,1)}, u32[]{:S(2)}) copy-start(bf16[320,2048]{1,0:T(8,128)(2,1)} %param.19) | copy-start | bytes 3932164
  8.5 20.4 %collective-permute-start = (bf16[4,256,128]{1,2,0:T(8,128)(2,1)}, bf16[4,256,128]{1,2,0:T(8,128)(2,1)}, u32[]{:S(2)}, u32[]{:S(2)}) collective-permute-start(bf16[4,256,128]{1,2,0:T(8,128)(2,1)} %bitcast.4), channel_id=1, source_target_pairs={{0,224},{16,240},{32,0},{48,16},{64,32},{80,48},{96,64},{112,80},{... | collective-permute-start | bytes 786440 | tf_op jit(solution)/shard_map/ppermute | solution.py:123
  12.6 16.2 %collective-permute-start.1 = (bf16[4,256,128]{1,2,0:T(8,128)(2,1)}, bf16[4,256,128]{1,2,0:T(8,128)(2,1)}, u32[]{:S(2)}, u32[]{:S(2)}) collective-permute-start(bf16[4,256,128]{1,2,0:T(8,128)(2,1)} %bitcast.4), channel_id=1, source_target_pairs={{0,32},{16,48},{32,64},{48,80},{64,96},{80,112},{96,128},{112,144}... | collective-permute-start | bytes 786440 | tf_op jit(solution)/shard_map/ppermute | solution.py:119
  15.1 7.9 %copy-start.8 = (s32[16]{0:T(128)S(1)}, s32[16]{0:T(128)}, u32[]{:S(2)}) copy-start(s32[16]{0:T(128)} %param.12) | copy-start | bytes 196
  15.1 56.9 %all-to-all-start = ((bf16[16,32,2048]{2,1,0:T(8,128)(2,1)}), bf16[16,32,2048]{2,1,0:T(8,128)(2,1)S(1)}, u32[]{:S(2)}, u32[]{:S(2)}) async-start(bf16[16,32,2048]{2,1,0:T(8,128)(2,1)} %broadcast_in_dim.23), calls=%async_computation | async-start | bytes 4194304 | tf_op jit(solution)/shard_map/all_to_all | solution.py:89
  22.2 108.6 %all-gather.2.cloned.1.call-start = ((), (), s32[]{:S(2)}) async-start(), calls=%async_computation.4 | async-start | bytes 4456448 | tf_op jit(solution)/shard_map/all_gather | solution.py:170
  30.8 10.8 %collective-permute-start.2 = (bf16[4,256,128]{1,2,0:T(8,128)(2,1)}, bf16[4,256,128]{1,2,0:T(8,128)(2,1)}, u32[]{:S(2)}, u32[]{:S(2)}) collective-permute-start(bf16[4,256,128]{1,2,0:T(8,128)(2,1)} %collective-permute-done), channel_id=1, source_target_pairs={{0,224},{16,240},{32,0},{48,16},{64,32},{80,48},{96,64},{112,80},{... | collective-permute-start | bytes 786440 | tf_op jit(solution)/shard_map/ppermute | solution.py:123
  34.0 8.5 %collective-permute-start.3 = (bf16[4,256,128]{1,2,0:T(8,128)(2,1)}, bf16[4,256,128]{1,2,0:T(8,128)(2,1)}, u32[]{:S(2)}, u32[]{:S(2)}) collective-permute-start(bf16[4,256,128]{1,2,0:T(8,128)(2,1)} %collective-permute-done.1), channel_id=1, source_target_pairs={{0,32},{16,48},{32,64},{48,80},{64,96},{80,112},{96,128},{112,144}... | collective-permute-start | bytes 786440 | tf_op jit(solution)/shard_map/ppermute | solution.py:119
  36.6 10.2 %copy-start.10 = (s32[1,8]{1,0:T(1,128)S(1)}, s32[1,8]{1,0:T(1,128)}, u32[]{:S(2)}) copy-start(s32[1,8]{1,0:T(1,128)} %param.11) | copy-start | bytes 100
  38.6 3.8 %copy-start.5 = (bf16[4,256,128]{1,2,0:T(8,128)(2,1)S(1)}, bf16[4,256,128]{1,2,0:T(8,128)(2,1)}, u32[]{:S(2)}) copy-start(bf16[4,256,128]{1,2,0:T(8,128)(2,1)} %get-tuple-element.24) | copy-start | bytes 786436
  38.6 3.8 %copy-start.6 = (bf16[4,256,128]{1,2,0:T(8,128)(2,1)S(1)}, bf16[4,256,128]{1,2,0:T(8,128)(2,1)}, u32[]{:S(2)}) copy-start(bf16[4,256,128]{1,2,0:T(8,128)(2,1)} %get-tuple-element.23) | copy-start | bytes 786436
  44.4 6.9 %collective-permute-start.4 = (bf16[4,256,128]{1,2,0:T(8,128)(2,1)}, bf16[4,256,128]{1,2,0:T(8,128)(2,1)}, u32[]{:S(2)}, u32[]{:S(2)}) collective-permute-start(bf16[4,256,128]{1,2,0:T(8,128)(2,1)} %collective-permute-done.2), channel_id=1, source_target_pairs={{0,224},{16,240},{32,0},{48,16},{64,32},{80,48},{96,64},{112,80},{... | collective-permute-start | bytes 786440 | tf_op jit(solution)/shard_map/ppermute | solution.py:123
  46.8 7.9 %collective-permute-start.5 = (bf16[4,256,128]{1,2,0:T(8,128)(2,1)}, bf16[4,256,128]{1,2,0:T(8,128)(2,1)}, u32[]{:S(2)}, u32[]{:S(2)}) collective-permute-start(bf16[4,256,128]{1,2,0:T(8,128)(2,1)} %collective-permute-done.3), channel_id=1, source_target_pairs={{0,32},{16,48},{32,64},{48,80},{64,96},{80,112},{96,128},{112,144}... | collective-permute-start | bytes 786440 | tf_op jit(solution)/shard_map/ppermute | solution.py:119
  56.8 7.9 %collective-permute-start.6 = (bf16[4,256,128]{1,2,0:T(8,128)(2,1)}, bf16[4,256,128]{1,2,0:T(8,128)(2,1)}, u32[]{:S(2)}, u32[]{:S(2)}) collective-permute-start(bf16[4,256,128]{1,2,0:T(8,128)(2,1)} %collective-permute-done.5), channel_id=1, source_target_pairs={{0,32},{16,48},{32,64},{48,80},{64,96},{80,112},{96,128},{112,144}... | collective-permute-start | bytes 786440 | tf_op jit(solution)/shard_map/ppermute | solution.py:119
  66.6 1.9 %collective-permute-start.7 = (bf16[4,256,128]{1,2,0:T(8,128)(2,1)}, bf16[4,256,128]{1,2,0:T(8,128)(2,1)}, u32[]{:S(2)}, u32[]{:S(2)}) collective-permute-start(bf16[4,256,128]{1,2,0:T(8,128)(2,1)} %get-tuple-element.35), channel_id=1, source_target_pairs={{0,16},{16,0},{32,48},{48,32},{64,80},{80,64},{96,112},{112,96},{1... | collective-permute-start | bytes 786440 | tf_op jit(solution)/shard_map/ppermute | solution.py:129
  74.1 27.7 %all-to-all-start.1 = ((bf16[16,256,128]{2,1,0:T(8,128)(2,1)}), bf16[16,256,128]{2,1,0:T(8,128)(2,1)}, u32[]{:S(2)}, u32[]{:S(2)}) async-start(bf16[16,256,128]{2,1,0:T(8,128)(2,1)} %bitcast.128), calls=%async_computation.1 | async-start | bytes 2097152 | tf_op jit(solution)/shard_map/all_to_all | solution.py:176
  81.9 1.2 copy-start.1
  84.0 0.7 copy-start.4
  85.1 1.0 copy-start.2
  105.7 3.1 %copy-start.3 = (f32[512,1,512]{0,2,1:T(8,128)S(1)}, f32[512,1,512]{0,2,1:T(8,128)}, u32[]{:S(2)}) copy-start(f32[512,1,512]{0,2,1:T(8,128)} %copy-done.2) | copy-start | bytes 3145732
  130.8 6.8 %copy-start.9 = (bf16[2,2048,320]{1,2,0:T(8,128)(2,1)S(1)}, bf16[2,2048,320]{1,2,0:T(8,128)(2,1)}, u32[]{:S(2)}) copy-start(bf16[2,2048,320]{1,2,0:T(8,128)(2,1)} %param.18) | copy-start | bytes 7864324
  136.2 1.3 copy-start.7
  144.1 33.4 %all-to-all-start.3 = ((bf16[16,32,2048]{2,1,0:T(8,128)(2,1)}), bf16[16,32,2048]{2,1,0:T(8,128)(2,1)S(1)}, u32[]{:S(2)}, u32[]{:S(2)}) async-start(bf16[16,32,2048]{2,1,0:T(8,128)(2,1)} %bitcast.129), calls=%async_computation.3 | async-start | bytes 4194304 | tf_op jit(solution)/shard_map/all_to_all | solution.py:96
Sparse Core Ops, SparseCore 0:
  25.5 66.7 all-gather.1

commit v14 on v9

--- a/solution.py
+++ b/solution.py
@@ -167,7 +167,15 @@
     by_head = prefix_cache.reshape(shard_rows, 2, kv_groups, kv_width)
     by_head = jnp.transpose(by_head, (2, 0, 1, 3)).reshape(kv_groups, shard_rows, 2 * kv_width)
     on_core, mine, swapped, projection = fetch_slot(by_head, group_prefix, group_rank, projection)
-    out_full = lax.all_gather(out_weight, "tensor", axis=0, tiled=True)
+    group_count = lax.axis_size("dp")
+    core = group_rank % CORES
+    half_cols = out_weight.shape[1] // CORES
+    own_cols = lax.dynamic_slice_in_dim(out_weight, core * half_cols, half_cols, 1)
+    own_cols = lax.all_gather(own_cols, "tensor", axis=0, tiled=True)
+    other_cols = lax.ppermute(own_cols, "dp", [(i, i ^ 1) for i in range(group_count)])
+    out_full = jnp.zeros((own_cols.shape[0], out_weight.shape[1]), own_cols.dtype)
+    out_full = lax.dynamic_update_slice_in_dim(out_full, own_cols, core * half_cols, 1)
+    out_full = lax.dynamic_update_slice_in_dim(out_full, other_cols, (1 - core) * half_cols, 1)
     outgoing = jnp.where(
         on_core,
         jnp.repeat(mine, tensor_count // kv_groups, axis=0),

time: 179 us -> 199 us (1.11)
  blocking collectives: 20.9 us -> 0 us
  waiting for transfers between devices: 62.8 us -> 77.5 us
  local copies, waits for them, and re-layouts: 13 us -> 23.4 us
  starting transfers between devices: 26.1 us -> 33.5 us
  other arithmetic: 16.4 us -> 19.8 us
  matrix products: 20 us -> 23.2 us
    all_to_all x1 -> x0, blocking collectives: 20.9 us -> none  [gather_rows(): received = lax.all_to_all(copies, axis, 0, 0, tiled=True)]
    all_to_all x1 -> x2, waiting for transfers between devices: 3.34 us -> 12.4 us  [gather_rows(): received = lax.all_to_all(copies, axis, 0, 0, tiled=True)]
    all_to_all x1, waiting for transfers between devices: 12.4 us -> 17.6 us  [on_device(): incoming = lax.all_to_all(outgoing, 'tensor', 0, 0, tiled=True)]
    dynamic_update_slice x0 -> x2, local copies, waits for them, and re-layouts: none -> 4.64 us  [the longest x1 3.13 us: on_device(): lax.dynamic_update_slice_in_dim(out_full, other_cols, (1 - core) * half_c...]
    all_to_all x1 -> x2, starting transfers between devices: 7.17 us -> 11.7 us  [gather_rows(): received = lax.all_to_all(copies, axis, 0, 0, tiled=True)]
    reduce_sum x2, other arithmetic: 1.64 us -> 5.17 us  [softmax_block(): weight = jnp.sum(exponent, axis=2)]
    dot_general x2, matrix products: 2.84 us -> 6.05 us  [softmax_block(): jnp.einsum('thd,nhd->thn', queries, keys_block, preferred_element_type=jn...]
    all_to_all x1, starting transfers between devices: 4.53 us -> 7.27 us  [on_device(): incoming = lax.all_to_all(outgoing, 'tensor', 0, 0, tiled=True)]
  transfers between devices with their start and end apart: 12 -> 14, of which waited for: 7 -> 7; matrix products, arithmetic and copies ran while one was open for 17% -> 23% of each run, Pallas kernels for 0% -> 0%
where the time goes in v14:
time: 199 us; the launch traced here: 196 us
  waiting for transfers between devices  77.5 us (39%)
  starting transfers between devices  33.5 us (17%)
  local copies, waits for them, and re-layouts  23.4 us (12%)
  matrix products  23.2 us (12%)
  other arithmetic  19.8 us (10%)
  between operations  18.9 us (9%)
    all_to_all x1, waiting for transfers between devices, sum_scatter_rows(): received = lax.all_to_all(parts, axis, 0, 0, tiled=True)  31.9 us
    all_to_all x1, waiting for transfers between devices, on_device(): incoming = lax.all_to_all(outgoing, 'tensor', 0, 0, tiled=True)  17.6 us
    all_to_all x2, waiting for transfers between devices, gather_rows(): received = lax.all_to_all(copies, axis, 0, 0, tiled=True)  12.4 us
    all_to_all x2, starting transfers between devices, gather_rows(): received = lax.all_to_all(copies, axis, 0, 0, tiled=True)  11.7 us
    ppermute x4, waiting for transfers between devices, fetch_slot(): ahead = lax.ppermute(ahead, 'dp', onward)  11.1 us
    ppermute x3, starting transfers between devices, fetch_slot(): behind = lax.ppermute(behind, 'dp', backward)  10.7 us
    all_to_all x1, starting transfers between devices, on_device(): incoming = lax.all_to_all(outgoing, 'tensor', 0, 0, tiled=True)  7.27 us
    dot_general x2, matrix products, softmax_block(): jnp.einsum('thd,nhd->thn', queries, keys_block, preferred_element_type=jn...  6.05 us
  transfers between devices with their start and end apart: 14, of which 7 were waited for; matrix products, arithmetic and copies ran while one was open for 23% of the time, Pallas kernels for 0%

profile of v14, /device:TPU:0, one launch (start us, length us, event | category | flops | bytes accessed | tf_op | source)
XLA Modules:
  0.0 196.3 jit_solution(1999559229860886059)
XLA Ops:
  7.8 4.2 %collective-permute-start = (bf16[4,256,128]{1,2,0:T(8,128)(2,1)S(1)}, bf16[4,256,128]{1,2,0:T(8,128)(2,1)}, u32[]{:S(2)}, u32[]{:S(2)}) collective-permute-start(bf16[4,256,128]{1,2,0:T(8,128)(2,1)S(1)} %bitcast.130), channel_id=1, source_target_pairs={{0,224},{16,240},{32,0},{48,16},{64,32},{80,48},{96,64},{112,80},{... | collective-permute-start | bytes 786440 | tf_op jit(solution)/shard_map/ppermute | solution.py:123
  23.0 3.2 %collective-permute-start.2 = (bf16[4,256,128]{1,2,0:T(8,128)(2,1)}, bf16[4,256,128]{1,2,0:T(8,128)(2,1)}, u32[]{:S(2)}, u32[]{:S(2)}) collective-permute-start(bf16[4,256,128]{1,2,0:T(8,128)(2,1)} %collective-permute-done), channel_id=1, source_target_pairs={{0,224},{16,240},{32,0},{48,16},{64,32},{80,48},{96,64},{112,80},{... | collective-permute-start | bytes 786440 | tf_op jit(solution)/shard_map/ppermute | solution.py:123
  27.9 7.2 %all-to-all-start = ((bf16[16,32,2048]{2,1,0:T(8,128)(2,1)}), bf16[16,32,2048]{2,1,0:T(8,128)(2,1)S(1)}, u32[]{:S(2)}, u32[]{:S(2)}) async-start(bf16[16,32,2048]{2,1,0:T(8,128)(2,1)} %broadcast_in_dim.25), calls=%async_computation | async-start | bytes 4194304 | tf_op jit(solution)/shard_map/all_to_all | solution.py:89
  35.1 2.0 %select_select_fusion.2 = (bf16[4,256,128]{1,2,0:T(8,128)(2,1)}, bf16[4,256,128]{1,2,0:T(8,128)(2,1)}) fusion(bf16[4,256,128]{1,2,0:T(8,128)(2,1)} %collective-permute-done.2, bf16[4,256,128]{1,2,0:T(8,128)(2,1)} %collective-permute-done.3, bf16[4,256,128]{1,2,0:T(8,128)(2,1)} %get-tuple-element.26, pred[]{:T(512)S(6)} %eq.81, pred[]{:T(512)S(6)} %eq.80, ...), kind=kLoop, calls=%fused_computation.60 | loop fusion | flops 524288 | bytes 1572868 | tf_op jit(solution)/shard_map/jit(_where)/select_n | solution.py:125
  37.1 3.3 %collective-permute-start.4 = (bf16[4,256,128]{1,2,0:T(8,128)(2,1)}, bf16[4,256,128]{1,2,0:T(8,128)(2,1)}, u32[]{:S(2)}, u32[]{:S(2)}) collective-permute-start(bf16[4,256,128]{1,2,0:T(8,128)(2,1)} %collective-permute-done.2), channel_id=1, source_target_pairs={{0,224},{16,240},{32,0},{48,16},{64,32},{80,48},{96,64},{112,80},{... | collective-permute-start | bytes 786440 | tf_op jit(solution)/shard_map/ppermute | solution.py:123
  42.2 2.7 %collective-permute-done.4 = bf16[4,256,128]{1,2,0:T(8,128)(2,1)} collective-permute-done((bf16[4,256,128]{1,2,0:T(8,128)(2,1)}, bf16[4,256,128]{1,2,0:T(8,128)(2,1)}, u32[]{:S(2)}, u32[]{:S(2)}) %collective-permute-start.4) | collective-permute-done | bytes 262176 | tf_op jit(solution)/shard_map/ppermute | solution.py:123
  44.9 3.4 %collective-permute-done.5 = bf16[4,256,128]{1,2,0:T(8,128)(2,1)} collective-permute-done((bf16[4,256,128]{1,2,0:T(8,128)(2,1)}, bf16[4,256,128]{1,2,0:T(8,128)(2,1)}, u32[]{:S(2)}, u32[]{:S(2)}) %collective-permute-start.5) | collective-permute-done | bytes 262176 | tf_op jit(solution)/shard_map/ppermute | solution.py:119
  48.3 2.0 %select_select_fusion = (bf16[4,256,128]{1,2,0:T(8,128)(2,1)}, bf16[4,256,128]{1,2,0:T(8,128)(2,1)}) fusion(bf16[4,256,128]{1,2,0:T(8,128)(2,1)} %collective-permute-done.4, bf16[4,256,128]{1,2,0:T(8,128)(2,1)} %collective-permute-done.5, bf16[4,256,128]{1,2,0:T(8,128)(2,1)} %get-tuple-element.30, pred[]{:T(512)S(6)} %eq.84, pred[]{:T(512)S(6)} %eq.83, ...), kind=kLoop, calls=%fused_computation.58 | loop fusion | flops 524288 | bytes 1572868 | tf_op jit(solution)/shard_map/jit(_where)/select_n | solution.py:125
  50.5 7.7 %collective-permute-done.6 = bf16[4,256,128]{1,2,0:T(8,128)(2,1)} collective-permute-done((bf16[4,256,128]{1,2,0:T(8,128)(2,1)}, bf16[4,256,128]{1,2,0:T(8,128)(2,1)}, u32[]{:S(2)}, u32[]{:S(2)}) %collective-permute-start.6) | collective-permute-done | bytes 262176 | tf_op jit(solution)/shard_map/ppermute | solution.py:119
  58.2 2.0 %broadcast_select_fusion = (bf16[4,256,128]{1,2,0:T(8,128)(2,1)}, bf16[4,256,128]{1,2,0:T(8,128)(2,1)}) fusion(bf16[4,256,128]{1,2,0:T(8,128)(2,1)} %collective-permute-done.6, bf16[4,256,128]{1,2,0:T(8,128)(2,1)} %get-tuple-element.33, pred[]{:T(512)S(6)} %eq.85, bf16[4,256,128]{1,2,0:T(8,128)(2,1)} %get-tuple-element.32, pred[]{:T(512)S(6)} %eq.72), kind=kLoop, calls=%fused_computation.64 | loop fusion | flops 262144 | bytes 1310722 | tf_op jit(solution)/shard_map/jit(_where)/select_n | solution.py:121
  65.6 2.2 %broadcast_in_dim.27 = bf16[4,4,256,128]{3,2,1,0:T(8,128)(2,1)} broadcast(bf16[4,256,128]{2,1,0:T(8,128)(2,1)} %copy.19), dimensions={0,2,3} | broadcast | bytes 1310720 | tf_op jit(solution)/shard_map/broadcast_in_dim | solution.py:181
  67.7 7.3 %all-to-all-start.1 = ((bf16[16,256,128]{2,1,0:T(8,128)(2,1)}), bf16[16,256,128]{2,1,0:T(8,128)(2,1)}, u32[]{:S(2)}, u32[]{:S(2)}) async-start(bf16[16,256,128]{2,1,0:T(8,128)(2,1)} %bitcast.128), calls=%async_computation.1 | async-start | bytes 2097152 | tf_op jit(solution)/shard_map/all_to_all | solution.py:184
  80.0 17.6 %all-to-all-done.1 = bf16[16,256,128]{2,1,0:T(8,128)(2,1)} async-done(((bf16[16,256,128]{2,1,0:T(8,128)(2,1)}), bf16[16,256,128]{2,1,0:T(8,128)(2,1)}, u32[]{:S(2)}, u32[]{:S(2)}) %all-to-all-start.1) | async-done | bytes 1048608 | tf_op jit(solution)/shard_map/all_to_all | solution.py:184
  97.5 5.7 %multiply_reduce_fusion = (f32[512]{0:T(512)S(1)}, f32[4096,512]{1,0:T(8,128)}) fusion(bf16[512,1,32]{0,2,1:T(8,128)(2,1)S(1)} %get-tuple-element.54, bf16[512,1,32]{0,2,1:T(8,128)(2,1)S(1)} %get-tuple-element.55, bf16[4096,128]{1,0:T(8,128)(2,1)} %bitcast.7), kind=kOutput, calls=%fused_computation.2 | convolution fusion | flops 272760320 | bytes 9504768 | tf_op jit(solution)/shard_map/thd,nhd->thn/dot_general | solution.py:56
  103.2 5.0 %fusion.1 = f32[512]{0:T(512)S(1)} fusion(f32[4096,512]{1,0:T(8,128)} %get-tuple-element.61, f32[512]{0:T(512)S(1)} %get-tuple-element.60), kind=kLoop, calls=%fused_computation.3 | loop fusion | flops 6290944 | bytes 8392704 | tf_op jit(solution)/shard_map/reduce_sum | solution.py:63
  109.0 3.1 %fusion.37 = f32[1,64,512]{2,1,0:T(8,128)S(1)} fusion(f32[4096,512]{1,0:T(8,128)S(1)} %copy-done.1, f32[512]{0:T(512)S(1)} %get-tuple-element.60, bf16[4096,128]{1,0:T(8,128)(2,1)} %bitcast.7, f32[512]{0:T(512)S(1)} %get-tuple-element.39, f32[512]{0:T(512)S(1)} %get-tuple-element.57, f32[512]{0:T(512)S(1)} %get-tuple-element.56), kind=kOutput, calls=%fused_computation.37 | convolution fusion | flops 274825216 | bytes 9576448 | tf_op jit(solution)/shard_map/thn,nhd->thd/dot_general | solution.py:64
  114.4 4.6 %all-to-all-start.2 = ((bf16[16,1,64,512]{3,2,1,0:T(8,128)(2,1)}), bf16[16,1,64,512]{3,2,1,0:T(8,128)(2,1)}, u32[]{:S(2)}, u32[]{:S(2)}) async-start(bf16[16,1,64,512]{3,2,1,0:T(8,128)(2,1)} %broadcast_in_dim.31), calls=%async_computation.2 | async-start | bytes 2097152 | tf_op jit(solution)/shard_map/all_to_all | solution.py:89
  119.0 2.5 %broadcast_in_dim.32 = bf16[1024,2048]{1,0:T(8,128)(2,1)} broadcast(bf16[]{:T(256)} %constant.124.clone.1), dimensions={} | broadcast | bytes 4194306 | tf_op jit(solution)/shard_map/broadcast_in_dim | solution.py:176
  123.0 3.1 %constant_dynamic-update-slice_fusion = bf16[1024,2048]{1,0:T(8,128)(2,1)} fusion(bf16[1024,2048]{1,0:T(8,128)(2,1)} %constant_dynamic-update-slice_fusion.1, bf16[1024,1024]{1,0:T(8,128)(2,1)} %collective-permute-done.8, s32[]{:T(128)S(6)} %select_n.205), kind=kLoop, calls=%fused_computation.109 | loop fusion | bytes 4194308 | tf_op jit(solution)/shard_map/dynamic_update_slice | solution.py:178
  126.2 12.4 %all-to-all-done.2 = bf16[16,1,64,512]{3,2,1,0:T(8,128)(2,1)} async-done(((bf16[16,1,64,512]{3,2,1,0:T(8,128)(2,1)}), bf16[16,1,64,512]{3,2,1,0:T(8,128)(2,1)}, u32[]{:S(2)}, u32[]{:S(2)}) %all-to-all-start.2) | async-done | bytes 1048608 | tf_op jit(solution)/shard_map/all_to_all | solution.py:89
  138.5 5.4 %fusion.3 = (f32[512]{0:T(512)S(1)}, bf16[512,2048]{1,0:T(8,128)(2,1)S(1)}) fusion(bf16[1024,512]{1,0:T(8,128)(2,1)} %bitcast.27, bf16[1024,2048]{1,0:T(8,128)(2,1)} %constant_dynamic-update-slice_fusion, bf16[16,32,2048]{2,1,0:T(8,128)(2,1)S(1)} %all-to-all-done), kind=kOutput, calls=%fused_computation.7 | convolution fusion | flops 2153774592 | bytes 9439232 | tf_op jit(solution)/shard_map/dot_general | solution.py:236
  146.4 5.5 %convolution_convert_fusion = bf16[512,2048]{1,0:T(8,128)(2,1)} fusion(bf16[320,2048]{1,0:T(8,128)(2,1)S(1)} %copy-done, bf16[2,2048,320]{1,2,0:T(8,128)(2,1)} %param.18, bf16[512,2048]{1,0:T(8,128)(2,1)} %copy-done.9, f32[512]{0:T(512)S(1)} %add_rsqrt_fusion.1, f32[512,320]{0,1:T(8,128)S(1)} %fusion.14), kind=kOutput, calls=%fused_computation.18 | convolution fusion | flops 1347354624 | bytes 7473152 | tf_op jit(solution)/shard_map/dot_general | solution.py:243
  151.9 3.7 %all-to-all-start.3 = ((bf16[16,32,2048]{2,1,0:T(8,128)(2,1)}), bf16[16,32,2048]{2,1,0:T(8,128)(2,1)S(1)}, u32[]{:S(2)}, u32[]{:S(2)}) async-start(bf16[16,32,2048]{2,1,0:T(8,128)(2,1)} %bitcast.129), calls=%async_computation.3 | async-start | bytes 4194304 | tf_op jit(solution)/shard_map/all_to_all | solution.py:96
  155.6 31.9 %all-to-all-done.3 = bf16[16,32,2048]{2,1,0:T(8,128)(2,1)S(1)} async-done(((bf16[16,32,2048]{2,1,0:T(8,128)(2,1)}), bf16[16,32,2048]{2,1,0:T(8,128)(2,1)S(1)}, u32[]{:S(2)}, u32[]{:S(2)}) %all-to-all-start.3) | async-done | bytes 2097184 | tf_op jit(solution)/shard_map/all_to_all | solution.py:96
  (76 shorter events, 29.9 us)
Async XLA Ops:
  6.5 139.8 %copy-start = (bf16[320,2048]{1,0:T(8,128)(2,1)S(1)}, bf16[320,2048]{1,0:T(8,128)(2,1)}, u32[]{:S(2)}) copy-start(bf16[320,2048]{1,0:T(8,128)(2,1)} %param.19) | copy-start | bytes 3932164
  6.5 7.0 %copy-start.10 = (s32[16]{0:T(128)S(1)}, s32[16]{0:T(128)}, u32[]{:S(2)}) copy-start(s32[16]{0:T(128)} %param.12) | copy-start | bytes 196
  6.5 12.8 %copy-start.7 = (bf16[2048,64]{0,1:T(8,128)(2,1)S(1)}, bf16[2048,64]{0,1:T(8,128)(2,1)}, u32[]{:S(2)}) copy-start(bf16[2048,64]{0,1:T(8,128)(2,1)} %param.14) | copy-start | bytes 786436
  7.8 13.4 %collective-permute-start = (bf16[4,256,128]{1,2,0:T(8,128)(2,1)S(1)}, bf16[4,256,128]{1,2,0:T(8,128)(2,1)}, u32[]{:S(2)}, u32[]{:S(2)}) collective-permute-start(bf16[4,256,128]{1,2,0:T(8,128)(2,1)S(1)} %bitcast.130), channel_id=1, source_target_pairs={{0,224},{16,240},{32,0},{48,16},{64,32},{80,48},{96,64},{112,80},{... | collective-permute-start | bytes 786440 | tf_op jit(solution)/shard_map/ppermute | solution.py:123
  12.0 9.2 %collective-permute-start.1 = (bf16[4,256,128]{1,2,0:T(8,128)(2,1)S(1)}, bf16[4,256,128]{1,2,0:T(8,128)(2,1)}, u32[]{:S(2)}, u32[]{:S(2)}) collective-permute-start(bf16[4,256,128]{1,2,0:T(8,128)(2,1)S(1)} %bitcast.131), channel_id=1, source_target_pairs={{0,32},{16,48},{32,64},{48,80},{64,96},{80,112},{96,128},{112,144}... | collective-permute-start | bytes 786440 | tf_op jit(solution)/shard_map/ppermute | solution.py:119
  13.5 12.7 %copy-start.8 = (bf16[32,2048]{1,0:T(8,128)(2,1)S(1)}, bf16[32,2048]{1,0:T(8,128)(2,1)}, u32[]{:S(2)}) copy-start(bf16[32,2048]{1,0:T(8,128)(2,1)} %param.10) | copy-start | bytes 393220
  23.0 12.1 %collective-permute-start.2 = (bf16[4,256,128]{1,2,0:T(8,128)(2,1)}, bf16[4,256,128]{1,2,0:T(8,128)(2,1)}, u32[]{:S(2)}, u32[]{:S(2)}) collective-permute-start(bf16[4,256,128]{1,2,0:T(8,128)(2,1)} %collective-permute-done), channel_id=1, source_target_pairs={{0,224},{16,240},{32,0},{48,16},{64,32},{80,48},{96,64},{112,80},{... | collective-permute-start | bytes 786440 | tf_op jit(solution)/shard_map/ppermute | solution.py:123
  26.3 8.8 %collective-permute-start.3 = (bf16[4,256,128]{1,2,0:T(8,128)(2,1)}, bf16[4,256,128]{1,2,0:T(8,128)(2,1)}, u32[]{:S(2)}, u32[]{:S(2)}) collective-permute-start(bf16[4,256,128]{1,2,0:T(8,128)(2,1)} %collective-permute-done.1), channel_id=1, source_target_pairs={{0,32},{16,48},{32,64},{48,80},{64,96},{80,112},{96,128},{112,144}... | collective-permute-start | bytes 786440 | tf_op jit(solution)/shard_map/ppermute | solution.py:119
  27.9 14.1 %copy-start.12 = (s32[1,8]{1,0:T(1,128)S(1)}, s32[1,8]{1,0:T(1,128)}, u32[]{:S(2)}) copy-start(s32[1,8]{1,0:T(1,128)} %param.11) | copy-start | bytes 100
  27.9 37.7 %all-to-all-start = ((bf16[16,32,2048]{2,1,0:T(8,128)(2,1)}), bf16[16,32,2048]{2,1,0:T(8,128)(2,1)S(1)}, u32[]{:S(2)}, u32[]{:S(2)}) async-start(bf16[16,32,2048]{2,1,0:T(8,128)(2,1)} %broadcast_in_dim.25), calls=%async_computation | async-start | bytes 4194304 | tf_op jit(solution)/shard_map/all_to_all | solution.py:89
  35.0 68.1 %all-gather.2.cloned.1.call-start = ((), (), s32[]{:S(2)}) async-start(), calls=%async_computation.4 | async-start | bytes 2228224 | tf_op jit(solution)/shard_map/all_gather | solution.py:174
  37.1 7.8 %collective-permute-start.4 = (bf16[4,256,128]{1,2,0:T(8,128)(2,1)}, bf16[4,256,128]{1,2,0:T(8,128)(2,1)}, u32[]{:S(2)}, u32[]{:S(2)}) collective-permute-start(bf16[4,256,128]{1,2,0:T(8,128)(2,1)} %collective-permute-done.2), channel_id=1, source_target_pairs={{0,224},{16,240},{32,0},{48,16},{64,32},{80,48},{96,64},{112,80},{... | collective-permute-start | bytes 786440 | tf_op jit(solution)/shard_map/ppermute | solution.py:123
  40.4 7.9 %collective-permute-start.5 = (bf16[4,256,128]{1,2,0:T(8,128)(2,1)}, bf16[4,256,128]{1,2,0:T(8,128)(2,1)}, u32[]{:S(2)}, u32[]{:S(2)}) collective-permute-start(bf16[4,256,128]{1,2,0:T(8,128)(2,1)} %collective-permute-done.3), channel_id=1, source_target_pairs={{0,32},{16,48},{32,64},{48,80},{64,96},{80,112},{96,128},{112,144}... | collective-permute-start | bytes 786440 | tf_op jit(solution)/shard_map/ppermute | solution.py:119
  50.3 7.9 %collective-permute-start.6 = (bf16[4,256,128]{1,2,0:T(8,128)(2,1)}, bf16[4,256,128]{1,2,0:T(8,128)(2,1)}, u32[]{:S(2)}, u32[]{:S(2)}) collective-permute-start(bf16[4,256,128]{1,2,0:T(8,128)(2,1)} %collective-permute-done.5), channel_id=1, source_target_pairs={{0,32},{16,48},{32,64},{48,80},{64,96},{80,112},{96,128},{112,144}... | collective-permute-start | bytes 786440 | tf_op jit(solution)/shard_map/ppermute | solution.py:119
  60.2 1.9 collective-permute-start.7
  67.7 29.8 %all-to-all-start.1 = ((bf16[16,256,128]{2,1,0:T(8,128)(2,1)}), bf16[16,256,128]{2,1,0:T(8,128)(2,1)}, u32[]{:S(2)}, u32[]{:S(2)}) async-start(bf16[16,256,128]{2,1,0:T(8,128)(2,1)} %bitcast.128), calls=%async_computation.1 | async-start | bytes 2097152 | tf_op jit(solution)/shard_map/all_to_all | solution.py:184
  103.2 19.8 %collective-permute-start.8 = (bf16[1024,1024]{1,0:T(8,128)(2,1)}, bf16[1024,1024]{1,0:T(8,128)(2,1)}, u32[]{:S(2)}, u32[]{:S(2)}) collective-permute-start(bf16[1024,1024]{1,0:T(8,128)(2,1)} %all-gather.2.cloned.1.call-done), channel_id=1, source_target_pairs={{0,16},{16,0},{32,48},{48,32},{64,80},{80,64},{96,112},{112,96},{1... | collective-permute-start | bytes 6291464 | tf_op jit(solution)/shard_map/ppermute | solution.py:175
  103.2 5.8 %copy-start.1 = (f32[4096,512]{1,0:T(8,128)S(1)}, f32[4096,512]{1,0:T(8,128)}, u32[]{:S(2)}) copy-start(f32[4096,512]{1,0:T(8,128)} %get-tuple-element.61) | copy-start | bytes 25165828
  109.0 3.2 %copy-start.4 = (f32[512,1,512]{0,2,1:T(8,128)S(1)}, f32[512,1,512]{0,2,1:T(8,128)}, u32[]{:S(2)}) copy-start(f32[512,1,512]{0,2,1:T(8,128)} %copy-done.3) | copy-start | bytes 3145732
  114.4 24.1 %all-to-all-start.2 = ((bf16[16,1,64,512]{3,2,1,0:T(8,128)(2,1)}), bf16[16,1,64,512]{3,2,1,0:T(8,128)(2,1)}, u32[]{:S(2)}, u32[]{:S(2)}) async-start(bf16[16,1,64,512]{3,2,1,0:T(8,128)(2,1)} %broadcast_in_dim.31), calls=%async_computation.2 | async-start | bytes 2097152 | tf_op jit(solution)/shard_map/all_to_all | solution.py:89
  119.0 2.5 %copy-start.5 = (bf16[1024,1024]{1,0:T(8,128)(2,1)S(1)}, bf16[1024,1024]{1,0:T(8,128)(2,1)}, u32[]{:S(2)}) copy-start(bf16[1024,1024]{1,0:T(8,128)(2,1)} %all-gather.2.cloned.1.call-done) | copy-start | bytes 6291460
  138.5 6.8 %copy-start.11 = (bf16[2,2048,320]{1,2,0:T(8,128)(2,1)S(1)}, bf16[2,2048,320]{1,2,0:T(8,128)(2,1)}, u32[]{:S(2)}) copy-start(bf16[2,2048,320]{1,2,0:T(8,128)(2,1)} %param.18) | copy-start | bytes 7864324
  144.0 1.3 copy-start.9
  151.9 35.6 %all-to-all-start.3 = ((bf16[16,32,2048]{2,1,0:T(8,128)(2,1)}), bf16[16,32,2048]{2,1,0:T(8,128)(2,1)S(1)}, u32[]{:S(2)}, u32[]{:S(2)}) async-start(bf16[16,32,2048]{2,1,0:T(8,128)(2,1)} %bitcast.129), calls=%async_computation.3 | async-start | bytes 4194304 | tf_op jit(solution)/shard_map/all_to_all | solution.py:96
  (3 other events, 3.0 us)
Sparse Core Ops, SparseCore 0:
  42.1 59.3 all-gather.1

commit v15 on v9

--- a/solution.py
+++ b/solution.py
@@ -116,6 +116,14 @@
     ahead = prefix_cache
     behind = prefix_cache
     for step in range(1, chips // 2 + 1):
+        if step == chips - step:
+            rows = ahead.shape[1] // 2
+            first = lax.ppermute(ahead[:, :rows], "dp", onward)
+            second = lax.ppermute(behind[:, rows:], "dp", backward)
+            far = jnp.concatenate([first, second], axis=1)
+            mine = jnp.where(mine_at == step, far, mine)
+            theirs = jnp.where(theirs_at == step, far, theirs)
+            break
         ahead = lax.ppermute(ahead, "dp", onward)
         mine = jnp.where(mine_at == (chips - step) % chips, ahead, mine)
         theirs = jnp.where(theirs_at == (chips - step) % chips, ahead, theirs)

time: 179 us -> 181 us (1.011)
  waiting for transfers between devices: 62.8 us -> 55 us
  local copies, waits for them, and re-layouts: 13 us -> 18 us
  starting transfers between devices: 26.1 us -> 31 us
    ppermute x4 -> x3, waiting for transfers between devices: 11.1 us -> 3.42 us  [fetch_slot(): ahead = lax.ppermute(ahead, 'dp', onward)]
    ppermute x0 -> x2, starting transfers between devices: none -> 3.31 us  [the longest x1 3.22 us: fetch_slot(): second = lax.ppermute(behind[:, rows:], 'dp', backward)]
    slice x0 -> x2, local copies, waits for them, and re-layouts: none -> 2.48 us  [the longest x1 1.57 us: fetch_slot(): second = lax.ppermute(behind[:, rows:], 'dp', backward)]
    all_to_all x1, waiting for transfers between devices: 3.34 us -> 1.11 us  [gather_rows(): received = lax.all_to_all(copies, axis, 0, 0, tiled=True)]
    ppermute x0 -> x2, waiting for transfers between devices: none -> 1.82 us  [the longest x1 1.31 us: fetch_slot(): first = lax.ppermute(ahead[:, :rows], 'dp', onward)]
    unnamed x24 -> x27, local copies, waits for them, and re-layouts: 5.01 us -> 6.61 us
  transfers between devices with their start and end apart: 12 -> 13, of which waited for: 7 -> 8; matrix products, arithmetic and copies ran while one was open for 17% -> 19% of each run, Pallas kernels for 0% -> 0%
where the time goes in v15:
time: 181 us; the launch traced here: 180 us
  waiting for transfers between devices  55 us (30%)
  starting transfers between devices  31 us (17%)
  blocking collectives  20.4 us (11%)
  matrix products  20 us (11%)
  between operations  19.1 us (11%)
  local copies, waits for them, and re-layouts  18 us (10%)
  other arithmetic  16.3 us (9%)
    all_to_all x1, waiting for transfers between devices, sum_scatter_rows(): received = lax.all_to_all(parts, axis, 0, 0, tiled=True)  29.7 us
    all_to_all x1, blocking collectives, gather_rows(): received = lax.all_to_all(copies, axis, 0, 0, tiled=True)  20.4 us
    all_to_all x1, waiting for transfers between devices, on_device(): incoming = lax.all_to_all(outgoing, 'tensor', 0, 0, tiled=True)  12.9 us
    ppermute x3, starting transfers between devices, fetch_slot(): behind = lax.ppermute(behind, 'dp', backward)  10.6 us
    all_to_all x1, starting transfers between devices, gather_rows(): received = lax.all_to_all(copies, axis, 0, 0, tiled=True)  7.17 us
    unnamed x27, local copies, waits for them, and re-layouts  6.61 us
    all_to_all x1, starting transfers between devices, on_device(): incoming = lax.all_to_all(outgoing, 'tensor', 0, 0, tiled=True)  6.17 us
    select_n x3, other arithmetic, fetch_slot(): theirs = jnp.where(theirs_at == step, behind, theirs)  6 us
  transfers between devices with their start and end apart: 13, of which 8 were waited for; matrix products, arithmetic and copies ran while one was open for 19% of the time, Pallas kernels for 0%

profile of v15, /device:TPU:0, one launch (start us, length us, event | category | flops | bytes accessed | tf_op | source)
XLA Modules:
  0.0 179.7 jit_solution(15387314362183295897)
XLA Ops:
  7.8 4.2 %collective-permute-start = (bf16[4,256,128]{1,2,0:T(8,128)(2,1)S(1)}, bf16[4,256,128]{1,2,0:T(8,128)(2,1)}, u32[]{:S(2)}, u32[]{:S(2)}) collective-permute-start(bf16[4,256,128]{1,2,0:T(8,128)(2,1)S(1)} %bitcast.130), channel_id=1, source_target_pairs={{0,224},{16,240},{32,0},{48,16},{64,32},{80,48},{96,64},{112,80},{... | collective-permute-start | bytes 786440 | tf_op jit(solution)/shard_map/ppermute | solution.py:131
  21.5 1.9 %select_select_fusion.5 = (bf16[4,256,128]{1,2,0:T(8,128)(2,1)}, bf16[4,256,128]{1,2,0:T(8,128)(2,1)}) fusion(bf16[4,256,128]{1,2,0:T(8,128)(2,1)} %collective-permute-done, bf16[4,256,128]{1,2,0:T(8,128)(2,1)} %collective-permute-done.1, pred[]{:T(512)S(6)} %eq.77, pred[]{:T(512)S(6)} %eq.76, bf16[4,256,2,64]{1,3,2,0:T(8,128)(2,1)S(1)} %copy.17, ...), kind=kLoop, calls=%fused_computation.63 | loop fusion | flops 524288 | bytes 1310724 | tf_op jit(solution)/shard_map/jit(_where)/select_n | solution.py:133
  23.4 3.2 %collective-permute-start.2 = (bf16[4,256,128]{1,2,0:T(8,128)(2,1)}, bf16[4,256,128]{1,2,0:T(8,128)(2,1)}, u32[]{:S(2)}, u32[]{:S(2)}) collective-permute-start(bf16[4,256,128]{1,2,0:T(8,128)(2,1)} %collective-permute-done), channel_id=1, source_target_pairs={{0,224},{16,240},{32,0},{48,16},{64,32},{80,48},{96,64},{112,80},{... | collective-permute-start | bytes 786440 | tf_op jit(solution)/shard_map/ppermute | solution.py:131
  28.2 7.2 %all-to-all-start = ((bf16[16,32,2048]{2,1,0:T(8,128)(2,1)}), bf16[16,32,2048]{2,1,0:T(8,128)(2,1)S(1)}, u32[]{:S(2)}, u32[]{:S(2)}) async-start(bf16[16,32,2048]{2,1,0:T(8,128)(2,1)} %broadcast_in_dim.23), calls=%async_computation | async-start | bytes 4194304 | tf_op jit(solution)/shard_map/all_to_all | solution.py:89
  35.4 2.1 %select_select_fusion.3 = (bf16[4,256,128]{1,2,0:T(8,128)(2,1)}, bf16[4,256,128]{1,2,0:T(8,128)(2,1)}) fusion(bf16[4,256,128]{1,2,0:T(8,128)(2,1)} %collective-permute-done.2, bf16[4,256,128]{1,2,0:T(8,128)(2,1)} %collective-permute-done.3, bf16[4,256,128]{1,2,0:T(8,128)(2,1)} %get-tuple-element.25, pred[]{:T(512)S(6)} %eq.80, pred[]{:T(512)S(6)} %eq.79, ...), kind=kLoop, calls=%fused_computation.61 | loop fusion | flops 524288 | bytes 1572868 | tf_op jit(solution)/shard_map/jit(_where)/select_n | solution.py:133
  37.5 3.2 %collective-permute-start.4 = (bf16[4,256,128]{1,2,0:T(8,128)(2,1)}, bf16[4,256,128]{1,2,0:T(8,128)(2,1)}, u32[]{:S(2)}, u32[]{:S(2)}) collective-permute-start(bf16[4,256,128]{1,2,0:T(8,128)(2,1)} %collective-permute-done.2), channel_id=1, source_target_pairs={{0,224},{16,240},{32,0},{48,16},{64,32},{80,48},{96,64},{112,80},{... | collective-permute-start | bytes 786440 | tf_op jit(solution)/shard_map/ppermute | solution.py:131
  40.8 4.3 %collective-permute-done.4 = bf16[4,256,128]{1,2,0:T(8,128)(2,1)} collective-permute-done((bf16[4,256,128]{1,2,0:T(8,128)(2,1)}, bf16[4,256,128]{1,2,0:T(8,128)(2,1)}, u32[]{:S(2)}, u32[]{:S(2)}) %collective-permute-start.4) | collective-permute-done | bytes 262176 | tf_op jit(solution)/shard_map/ppermute | solution.py:131
  45.1 3.4 %collective-permute-done.5 = bf16[4,256,128]{1,2,0:T(8,128)(2,1)} collective-permute-done((bf16[4,256,128]{1,2,0:T(8,128)(2,1)}, bf16[4,256,128]{1,2,0:T(8,128)(2,1)}, u32[]{:S(2)}, u32[]{:S(2)}) %collective-permute-start.5) | collective-permute-done | bytes 262176 | tf_op jit(solution)/shard_map/ppermute | solution.py:127
  48.5 2.0 %select_select_fusion.1 = (bf16[4,256,128]{1,2,0:T(8,128)(2,1)}, bf16[4,256,128]{1,2,0:T(8,128)(2,1)}) fusion(bf16[4,256,128]{1,2,0:T(8,128)(2,1)} %collective-permute-done.4, bf16[4,256,128]{1,2,0:T(8,128)(2,1)} %collective-permute-done.5, bf16[4,256,128]{1,2,0:T(8,128)(2,1)} %get-tuple-element.29, pred[]{:T(512)S(6)} %eq.83, pred[]{:T(512)S(6)} %eq.82, ...), kind=kLoop, calls=%fused_computation.59 | loop fusion | flops 524288 | bytes 1572868 | tf_op jit(solution)/shard_map/jit(_where)/select_n | solution.py:133
  53.2 3.2 %collective-permute-start.7 = (bf16[4,128,128]{1,2,0:T(8,128)(2,1)}, bf16[4,128,128]{1,2,0:T(8,128)(2,1)}, u32[]{:S(2)}, u32[]{:S(2)}) collective-permute-start(bf16[4,128,128]{1,2,0:T(8,128)(2,1)} %slice.44), channel_id=1, source_target_pairs={{0,224},{16,240},{32,0},{48,16},{64,32},{80,48},{96,64},{112,80},{... | collective-permute-start | bytes 393224 | tf_op jit(solution)/shard_map/ppermute | solution.py:122
  60.9 1.7 broadcast_select_fusion
  62.7 1.8 %collective-permute-done.8 = bf16[4,256,128]{1,2,0:T(8,128)(2,1)} collective-permute-done((bf16[4,256,128]{1,2,0:T(8,128)(2,1)}, bf16[4,256,128]{1,2,0:T(8,128)(2,1)}, u32[]{:S(2)}, u32[]{:S(2)}) %collective-permute-start.8) | collective-permute-done | bytes 262176 | tf_op jit(solution)/shard_map/ppermute | solution.py:137
  64.5 1.8 %select_select_fusion = bf16[4,256,128]{1,2,0:T(8,128)(2,1)} fusion(bf16[4,256,128]{1,2,0:T(8,128)(2,1)} %collective-permute-done.8, bf16[4,256,128]{1,2,0:T(8,128)(2,1)} %copy-done.4, bf16[4,256,128]{1,2,0:T(8,128)(2,1)} %get-tuple-element.32, pred[]{:T(512)S(6)} %eq.71, pred[]{:T(512)S(6)} %eq.70), kind=kLoop, calls=%fused_computation.58 | loop fusion | flops 262144 | bytes 1048578 | tf_op jit(solution)/shard_map/jit(_where)/select_n | solution.py:179
  66.3 1.8 copy.19
  69.2 2.2 %broadcast_in_dim.25 = bf16[4,4,256,128]{3,2,1,0:T(8,128)(2,1)} broadcast(bf16[4,256,128]{2,1,0:T(8,128)(2,1)} %copy.19), dimensions={0,2,3} | broadcast | bytes 1310720 | tf_op jit(solution)/shard_map/broadcast_in_dim | solution.py:181
  71.4 6.2 %all-to-all-start.1 = ((bf16[16,256,128]{2,1,0:T(8,128)(2,1)}), bf16[16,256,128]{2,1,0:T(8,128)(2,1)}, u32[]{:S(2)}, u32[]{:S(2)}) async-start(bf16[16,256,128]{2,1,0:T(8,128)(2,1)} %bitcast.128), calls=%async_computation.1 | async-start | bytes 2097152 | tf_op jit(solution)/shard_map/all_to_all | solution.py:184
  82.5 12.9 %all-to-all-done.1 = bf16[16,256,128]{2,1,0:T(8,128)(2,1)} async-done(((bf16[16,256,128]{2,1,0:T(8,128)(2,1)}), bf16[16,256,128]{2,1,0:T(8,128)(2,1)}, u32[]{:S(2)}, u32[]{:S(2)}) %all-to-all-start.1) | async-done | bytes 1048608 | tf_op jit(solution)/shard_map/all_to_all | solution.py:184
  95.4 2.5 %multiply_reduce_fusion = (f32[512]{0:T(512)S(1)}, f32[4096,512]{1,0:T(8,128)S(1)}) fusion(bf16[512,1,32]{0,2,1:T(8,128)(2,1)S(1)} %get-tuple-element.50, bf16[512,1,32]{0,2,1:T(8,128)(2,1)S(1)} %get-tuple-element.51, bf16[4096,128]{1,0:T(8,128)(2,1)} %bitcast.7), kind=kOutput, calls=%fused_computation.2 | convolution fusion | flops 272760320 | bytes 9504768 | tf_op jit(solution)/shard_map/thd,nhd->thn/dot_general | solution.py:56
  99.3 3.1 %fusion.37 = f32[1,64,512]{2,1,0:T(8,128)S(1)} fusion(f32[4096,512]{1,0:T(8,128)S(1)} %get-tuple-element.57, f32[512]{0:T(512)S(1)} %get-tuple-element.56, bf16[4096,128]{1,0:T(8,128)(2,1)} %bitcast.7, f32[512]{0:T(512)S(1)} %get-tuple-element.37, f32[512]{0:T(512)S(1)} %get-tuple-element.53, f32[512]{0:T(512)S(1)} %get-tuple-element.52), kind=kOutput, calls=%fused_computation.37 | convolution fusion | flops 274825216 | bytes 9576448 | tf_op jit(solution)/shard_map/thn,nhd->thd/dot_general | solution.py:64
  103.8 20.4 %all_to_all.20 = bf16[16,1,64,512]{3,2,1,0:T(8,128)(2,1)} all-to-all(bf16[16,1,64,512]{3,2,1,0:T(8,128)(2,1)S(1)} %broadcast_in_dim.29), channel_id=1, replica_groups=mesh['dp'=16,'tensor'=16] {'tensor'}, dimensions={0} | all-to-all | bytes 2097152 | tf_op jit(solution)/shard_map/all_to_all | solution.py:89
  124.2 5.4 %fusion.3 = (f32[512]{0:T(512)S(1)}, bf16[512,2048]{1,0:T(8,128)(2,1)S(1)}) fusion(bf16[1024,512]{1,0:T(8,128)(2,1)} %bitcast.132, bf16[1024,2048]{1,0:T(8,128)(2,1)} %all-gather.2.cloned.1.call-done, bf16[16,32,2048]{2,1,0:T(8,128)(2,1)S(1)} %all-to-all-done), kind=kOutput, calls=%fused_computation.7 | convolution fusion | flops 2153774592 | bytes 9439232 | tf_op jit(solution)/shard_map/dot_general | solution.py:236
  132.0 5.5 %convolution_convert_fusion = bf16[512,2048]{1,0:T(8,128)(2,1)} fusion(bf16[320,2048]{1,0:T(8,128)(2,1)S(1)} %copy-done, bf16[2,2048,320]{1,2,0:T(8,128)(2,1)} %param.18, bf16[512,2048]{1,0:T(8,128)(2,1)} %copy-done.8, f32[512]{0:T(512)S(1)} %add_rsqrt_fusion.1, f32[512,320]{0,1:T(8,128)S(1)} %fusion.14), kind=kOutput, calls=%fused_computation.18 | convolution fusion | flops 1347354624 | bytes 7473152 | tf_op jit(solution)/shard_map/dot_general | solution.py:243
  137.5 3.7 %all-to-all-start.3 = ((bf16[16,32,2048]{2,1,0:T(8,128)(2,1)}), bf16[16,32,2048]{2,1,0:T(8,128)(2,1)S(1)}, u32[]{:S(2)}, u32[]{:S(2)}) async-start(bf16[16,32,2048]{2,1,0:T(8,128)(2,1)} %bitcast.129), calls=%async_computation.3 | async-start | bytes 4194304 | tf_op jit(solution)/shard_map/all_to_all | solution.py:96
  141.2 29.7 %all-to-all-done.3 = bf16[16,32,2048]{2,1,0:T(8,128)(2,1)S(1)} async-done(((bf16[16,32,2048]{2,1,0:T(8,128)(2,1)}), bf16[16,32,2048]{2,1,0:T(8,128)(2,1)S(1)}, u32[]{:S(2)}, u32[]{:S(2)}) %all-to-all-start.3) | async-done | bytes 2097184 | tf_op jit(solution)/shard_map/all_to_all | solution.py:96
  (73 shorter events, 27.3 us)
Async XLA Ops:
  6.5 125.4 %copy-start = (bf16[320,2048]{1,0:T(8,128)(2,1)S(1)}, bf16[320,2048]{1,0:T(8,128)(2,1)}, u32[]{:S(2)}) copy-start(bf16[320,2048]{1,0:T(8,128)(2,1)} %param.19) | copy-start | bytes 3932164
  6.5 7.1 %copy-start.9 = (s32[16]{0:T(128)S(1)}, s32[16]{0:T(128)}, u32[]{:S(2)}) copy-start(s32[16]{0:T(128)} %param.12) | copy-start | bytes 196
  6.5 13.1 %copy-start.6 = (bf16[2048,64]{0,1:T(8,128)(2,1)S(1)}, bf16[2048,64]{0,1:T(8,128)(2,1)}, u32[]{:S(2)}) copy-start(bf16[2048,64]{0,1:T(8,128)(2,1)} %param.14) | copy-start | bytes 786436
  6.5 117.6 %all-gather.2.cloned.1.call-start = ((), (), s32[]{:S(2)}) async-start(), calls=%async_computation.4 | async-start | bytes 4456448 | tf_op jit(solution)/shard_map/all_gather | solution.py:178
  7.8 13.7 %collective-permute-start = (bf16[4,256,128]{1,2,0:T(8,128)(2,1)S(1)}, bf16[4,256,128]{1,2,0:T(8,128)(2,1)}, u32[]{:S(2)}, u32[]{:S(2)}) collective-permute-start(bf16[4,256,128]{1,2,0:T(8,128)(2,1)S(1)} %bitcast.130), channel_id=1, source_target_pairs={{0,224},{16,240},{32,0},{48,16},{64,32},{80,48},{96,64},{112,80},{... | collective-permute-start | bytes 786440 | tf_op jit(solution)/shard_map/ppermute | solution.py:131
  12.0 9.5 %collective-permute-start.1 = (bf16[4,256,128]{1,2,0:T(8,128)(2,1)S(1)}, bf16[4,256,128]{1,2,0:T(8,128)(2,1)}, u32[]{:S(2)}, u32[]{:S(2)}) collective-permute-start(bf16[4,256,128]{1,2,0:T(8,128)(2,1)S(1)} %bitcast.131), channel_id=1, source_target_pairs={{0,32},{16,48},{32,64},{48,80},{64,96},{80,112},{96,128},{112,144}... | collective-permute-start | bytes 786440 | tf_op jit(solution)/shard_map/ppermute | solution.py:127
  13.6 13.0 %copy-start.7 = (bf16[32,2048]{1,0:T(8,128)(2,1)S(1)}, bf16[32,2048]{1,0:T(8,128)(2,1)}, u32[]{:S(2)}) copy-start(bf16[32,2048]{1,0:T(8,128)(2,1)} %param.10) | copy-start | bytes 393220
  23.4 12.0 %collective-permute-start.2 = (bf16[4,256,128]{1,2,0:T(8,128)(2,1)}, bf16[4,256,128]{1,2,0:T(8,128)(2,1)}, u32[]{:S(2)}, u32[]{:S(2)}) collective-permute-start(bf16[4,256,128]{1,2,0:T(8,128)(2,1)} %collective-permute-done), channel_id=1, source_target_pairs={{0,224},{16,240},{32,0},{48,16},{64,32},{80,48},{96,64},{112,80},{... | collective-permute-start | bytes 786440 | tf_op jit(solution)/shard_map/ppermute | solution.py:131
  26.6 8.8 %collective-permute-start.3 = (bf16[4,256,128]{1,2,0:T(8,128)(2,1)}, bf16[4,256,128]{1,2,0:T(8,128)(2,1)}, u32[]{:S(2)}, u32[]{:S(2)}) collective-permute-start(bf16[4,256,128]{1,2,0:T(8,128)(2,1)} %collective-permute-done.1), channel_id=1, source_target_pairs={{0,32},{16,48},{32,64},{48,80},{64,96},{80,112},{96,128},{112,144}... | collective-permute-start | bytes 786440 | tf_op jit(solution)/shard_map/ppermute | solution.py:127
  28.2 12.4 %copy-start.11 = (s32[1,8]{1,0:T(1,128)S(1)}, s32[1,8]{1,0:T(1,128)}, u32[]{:S(2)}) copy-start(s32[1,8]{1,0:T(1,128)} %param.11) | copy-start | bytes 100
  28.2 41.0 %all-to-all-start = ((bf16[16,32,2048]{2,1,0:T(8,128)(2,1)}), bf16[16,32,2048]{2,1,0:T(8,128)(2,1)S(1)}, u32[]{:S(2)}, u32[]{:S(2)}) async-start(bf16[16,32,2048]{2,1,0:T(8,128)(2,1)} %broadcast_in_dim.23), calls=%async_computation | async-start | bytes 4194304 | tf_op jit(solution)/shard_map/all_to_all | solution.py:89
  37.5 7.7 %collective-permute-start.4 = (bf16[4,256,128]{1,2,0:T(8,128)(2,1)}, bf16[4,256,128]{1,2,0:T(8,128)(2,1)}, u32[]{:S(2)}, u32[]{:S(2)}) collective-permute-start(bf16[4,256,128]{1,2,0:T(8,128)(2,1)} %collective-permute-done.2), channel_id=1, source_target_pairs={{0,224},{16,240},{32,0},{48,16},{64,32},{80,48},{96,64},{112,80},{... | collective-permute-start | bytes 786440 | tf_op jit(solution)/shard_map/ppermute | solution.py:131
  40.6 7.9 %collective-permute-start.5 = (bf16[4,256,128]{1,2,0:T(8,128)(2,1)}, bf16[4,256,128]{1,2,0:T(8,128)(2,1)}, u32[]{:S(2)}, u32[]{:S(2)}) collective-permute-start(bf16[4,256,128]{1,2,0:T(8,128)(2,1)} %collective-permute-done.3), channel_id=1, source_target_pairs={{0,32},{16,48},{32,64},{48,80},{64,96},{80,112},{96,128},{112,144}... | collective-permute-start | bytes 786440 | tf_op jit(solution)/shard_map/ppermute | solution.py:127
  51.5 6.4 %collective-permute-start.6 = (bf16[4,128,128]{1,2,0:T(8,128)(2,1)S(1)}, bf16[4,128,128]{1,2,0:T(8,128)(2,1)}, u32[]{:S(2)}, u32[]{:S(2)}) collective-permute-start(bf16[4,128,128]{1,2,0:T(8,128)(2,1)S(1)} %slice.43), channel_id=1, source_target_pairs={{0,32},{16,48},{32,64},{48,80},{64,96},{80,112},{96,128},{112,144}... | collective-permute-start | bytes 393224 | tf_op jit(solution)/shard_map/ppermute | solution.py:121
  53.2 6.1 %collective-permute-start.7 = (bf16[4,128,128]{1,2,0:T(8,128)(2,1)}, bf16[4,128,128]{1,2,0:T(8,128)(2,1)}, u32[]{:S(2)}, u32[]{:S(2)}) collective-permute-start(bf16[4,128,128]{1,2,0:T(8,128)(2,1)} %slice.44), channel_id=1, source_target_pairs={{0,224},{16,240},{32,0},{48,16},{64,32},{80,48},{96,64},{112,80},{... | collective-permute-start | bytes 393224 | tf_op jit(solution)/shard_map/ppermute | solution.py:122
  62.6 1.9 %collective-permute-start.8 = (bf16[4,256,128]{1,2,0:T(8,128)(2,1)}, bf16[4,256,128]{1,2,0:T(8,128)(2,1)}, u32[]{:S(2)}, u32[]{:S(2)}) collective-permute-start(bf16[4,256,128]{1,2,0:T(8,128)(2,1)} %broadcast_select_fusion), channel_id=1, source_target_pairs={{0,16},{16,0},{32,48},{48,32},{64,80},{80,64},{96,112},{112,96},{1... | collective-permute-start | bytes 786440 | tf_op jit(solution)/shard_map/ppermute | solution.py:137
  71.4 24.0 %all-to-all-start.1 = ((bf16[16,256,128]{2,1,0:T(8,128)(2,1)}), bf16[16,256,128]{2,1,0:T(8,128)(2,1)}, u32[]{:S(2)}, u32[]{:S(2)}) async-start(bf16[16,256,128]{2,1,0:T(8,128)(2,1)} %bitcast.128), calls=%async_computation.1 | async-start | bytes 2097152 | tf_op jit(solution)/shard_map/all_to_all | solution.py:184
  78.1 1.2 copy-start.1
  80.2 0.7 copy-start.5
  81.3 1.0 copy-start.2
  99.3 3.2 %copy-start.3 = (f32[512,1,512]{0,2,1:T(8,128)S(1)}, f32[512,1,512]{0,2,1:T(8,128)}, u32[]{:S(2)}) copy-start(f32[512,1,512]{0,2,1:T(8,128)} %copy-done.2) | copy-start | bytes 3145732
  124.2 6.8 %copy-start.10 = (bf16[2,2048,320]{1,2,0:T(8,128)(2,1)S(1)}, bf16[2,2048,320]{1,2,0:T(8,128)(2,1)}, u32[]{:S(2)}) copy-start(bf16[2,2048,320]{1,2,0:T(8,128)(2,1)} %param.18) | copy-start | bytes 7864324
  129.6 1.3 copy-start.8
  137.5 33.4 %all-to-all-start.3 = ((bf16[16,32,2048]{2,1,0:T(8,128)(2,1)}), bf16[16,32,2048]{2,1,0:T(8,128)(2,1)S(1)}, u32[]{:S(2)}, u32[]{:S(2)}) async-start(bf16[16,32,2048]{2,1,0:T(8,128)(2,1)} %bitcast.129), calls=%async_computation.3 | async-start | bytes 4194304 | tf_op jit(solution)/shard_map/all_to_all | solution.py:96
  (1 other events, 0.7 us)
Sparse Core Ops, SparseCore 0:
  12.1 66.8 all-gather.1

commit v16 on v9

--- a/solution.py
+++ b/solution.py
@@ -210,18 +210,14 @@
         repeat_by,
         axis=1,
     )
-    start_state = (
-        jnp.full((group_tokens, local_heads), NEG_FILL, jnp.float32),
-        jnp.zeros((group_tokens, local_heads), jnp.float32),
-        jnp.zeros((group_tokens, local_heads, HD), jnp.float32),
-    )
-    prefix_state = merge_states(
-        start_state, softmax_block(queries, keys_block, values_block, scaling, None)
-    )
+    every_key = jnp.concatenate([keys_block, own_keys], axis=0)
+    every_value = jnp.concatenate([values_block, own_values], axis=0)
     indices = jnp.arange(group_tokens, dtype=jnp.int32)
     allowed = (request[:, None] == request[None, :]) & (indices[None, :] <= indices[:, None])
-    suffix_state = softmax_block(queries, own_keys, own_values, scaling, allowed[:, None, :])
-    top_score, weight, blended = merge_states(prefix_state, suffix_state)
+    allowed = jnp.concatenate([jnp.ones((group_tokens, keys_block.shape[0]), bool), allowed], axis=1)
+    top_score, weight, blended = softmax_block(
+        queries, every_key, every_value, scaling, allowed[:, None, :]
+    )
     attended = (blended / weight[:, :, None]).astype(jnp.bfloat16).reshape(group_tokens, query_width)
     every_head = gather_rows(jnp.transpose(attended)[None], "tensor")
     every_head = jnp.transpose(every_head.reshape(tensor_count * query_width, group_tokens))

time: 179 us -> 177 us (0.989)
  local copies, waits for them, and re-layouts: 13 us -> 17.7 us
  matrix products: 20 us -> 15.8 us
  waiting for transfers between devices: 62.8 us -> 59.5 us
    another operation x0 -> x3, local copies, waits for them, and re-layouts: none -> 4.54 us  [the longest x2 2.49 us: on_device(): jnp.repeat(projected[:, query_width + kv_width:].reshape(group_tokens, lo...]
    all_to_all x1, waiting for transfers between devices: 12.4 us -> 9.4 us  [on_device(): incoming = lax.all_to_all(outgoing, 'tensor', 0, 0, tiled=True)]
    dot_general x2 -> x1, matrix products: 4.34 us -> 1.61 us  [softmax_block(): jnp.einsum('thn,nhd->thd', exponent.astype(jnp.bfloat16), values_block, p...]
    unnamed x24 -> x28, local copies, waits for them, and re-layouts: 5.01 us -> 4.43 us
  transfers between devices with their start and end apart: 12 -> 12, of which waited for: 7 -> 7; matrix products, arithmetic and copies ran while one was open for 17% -> 18% of each run, Pallas kernels for 0% -> 0%
where the time goes in v16:
time: 177 us; the launch traced here: 176 us
  waiting for transfers between devices  59.5 us (34%)
  starting transfers between devices  26.2 us (15%)
  blocking collectives  21 us (12%)
  between operations  18.9 us (11%)
  local copies, waits for them, and re-layouts  17.7 us (10%)
  other arithmetic  16.6 us (9%)
  matrix products  15.8 us (9%)
    all_to_all x1, waiting for transfers between devices, sum_scatter_rows(): received = lax.all_to_all(parts, axis, 0, 0, tiled=True)  29.5 us
    all_to_all x1, blocking collectives, gather_rows(): received = lax.all_to_all(copies, axis, 0, 0, tiled=True)  21 us
    ppermute x4, waiting for transfers between devices, fetch_slot(): ahead = lax.ppermute(ahead, 'dp', onward)  11.2 us
    ppermute x3, starting transfers between devices, fetch_slot(): behind = lax.ppermute(behind, 'dp', backward)  10.7 us
    all_to_all x1, waiting for transfers between devices, on_device(): incoming = lax.all_to_all(outgoing, 'tensor', 0, 0, tiled=True)  9.4 us
    all_to_all x1, starting transfers between devices, gather_rows(): received = lax.all_to_all(copies, axis, 0, 0, tiled=True)  7.17 us
    dot_general x1, matrix products, on_device(): jnp.dot(hidden, down_weight, preferred_element_type=jnp.float32)  5.51 us
    dot_general x1, matrix products, on_device(): attn_sum = jnp.dot(every_head, out_full, preferred_element_type=jnp.float32)  5.42 us
  transfers between devices with their start and end apart: 12, of which 7 were waited for; matrix products, arithmetic and copies ran while one was open for 18% of the time, Pallas kernels for 0%

profile of v16, /device:TPU:0, one launch (start us, length us, event | category | flops | bytes accessed | tf_op | source)
XLA Modules:
  0.0 175.7 jit_solution(10403447160852026960)
XLA Ops:
  7.8 4.2 %collective-permute-start = (bf16[4,256,128]{1,2,0:T(8,128)(2,1)S(1)}, bf16[4,256,128]{1,2,0:T(8,128)(2,1)}, u32[]{:S(2)}, u32[]{:S(2)}) collective-permute-start(bf16[4,256,128]{1,2,0:T(8,128)(2,1)S(1)} %bitcast.108), channel_id=1, source_target_pairs={{0,224},{16,240},{32,0},{48,16},{64,32},{80,48},{96,64},{112,80},{... | collective-permute-start | bytes 786440 | tf_op jit(solution)/shard_map/ppermute | solution.py:123
  21.3 1.9 %select_select_fusion.4 = (bf16[4,256,128]{1,2,0:T(8,128)(2,1)}, bf16[4,256,128]{1,2,0:T(8,128)(2,1)}) fusion(bf16[4,256,128]{1,2,0:T(8,128)(2,1)} %collective-permute-done, bf16[4,256,128]{1,2,0:T(8,128)(2,1)} %collective-permute-done.1, pred[]{:T(512)S(6)} %eq.70, pred[]{:T(512)S(6)} %eq.69, bf16[4,256,2,64]{1,3,2,0:T(8,128)(2,1)S(1)} %copy.21, ...), kind=kLoop, calls=%fused_computation.53 | loop fusion | flops 524288 | bytes 1310724 | tf_op jit(solution)/shard_map/jit(_where)/select_n | solution.py:125
  23.2 3.2 %collective-permute-start.2 = (bf16[4,256,128]{1,2,0:T(8,128)(2,1)}, bf16[4,256,128]{1,2,0:T(8,128)(2,1)}, u32[]{:S(2)}, u32[]{:S(2)}) collective-permute-start(bf16[4,256,128]{1,2,0:T(8,128)(2,1)} %collective-permute-done), channel_id=1, source_target_pairs={{0,224},{16,240},{32,0},{48,16},{64,32},{80,48},{96,64},{112,80},{... | collective-permute-start | bytes 786440 | tf_op jit(solution)/shard_map/ppermute | solution.py:123
  26.4 1.6 broadcast_in_dim.21
  28.0 7.2 %all-to-all-start = ((bf16[16,32,2048]{2,1,0:T(8,128)(2,1)}), bf16[16,32,2048]{2,1,0:T(8,128)(2,1)S(1)}, u32[]{:S(2)}, u32[]{:S(2)}) async-start(bf16[16,32,2048]{2,1,0:T(8,128)(2,1)} %broadcast_in_dim.21), calls=%async_computation | async-start | bytes 4194304 | tf_op jit(solution)/shard_map/all_to_all | solution.py:89
  36.7 3.3 %collective-permute-start.4 = (bf16[4,256,128]{1,2,0:T(8,128)(2,1)}, bf16[4,256,128]{1,2,0:T(8,128)(2,1)S(1)}, u32[]{:S(2)}, u32[]{:S(2)}) collective-permute-start(bf16[4,256,128]{1,2,0:T(8,128)(2,1)} %collective-permute-done.2), channel_id=1, source_target_pairs={{0,224},{16,240},{32,0},{48,16},{64,32},{80,48},{96,64},{112,80},{... | collective-permute-start | bytes 786440 | tf_op jit(solution)/shard_map/ppermute | solution.py:123
  40.1 4.4 %collective-permute-done.4 = bf16[4,256,128]{1,2,0:T(8,128)(2,1)S(1)} collective-permute-done((bf16[4,256,128]{1,2,0:T(8,128)(2,1)}, bf16[4,256,128]{1,2,0:T(8,128)(2,1)S(1)}, u32[]{:S(2)}, u32[]{:S(2)}) %collective-permute-start.4) | collective-permute-done | bytes 262176 | tf_op jit(solution)/shard_map/ppermute | solution.py:123
  44.5 3.4 %collective-permute-done.5 = bf16[4,256,128]{1,2,0:T(8,128)(2,1)} collective-permute-done((bf16[4,256,128]{1,2,0:T(8,128)(2,1)}, bf16[4,256,128]{1,2,0:T(8,128)(2,1)}, u32[]{:S(2)}, u32[]{:S(2)}) %collective-permute-start.5) | collective-permute-done | bytes 262176 | tf_op jit(solution)/shard_map/ppermute | solution.py:119
  47.9 1.8 %select_select_fusion = (bf16[4,256,128]{1,2,0:T(8,128)(2,1)}, bf16[4,256,128]{1,2,0:T(8,128)(2,1)}) fusion(bf16[4,256,128]{1,2,0:T(8,128)(2,1)S(1)} %collective-permute-done.4, bf16[4,256,128]{1,2,0:T(8,128)(2,1)} %collective-permute-done.5, bf16[4,256,128]{1,2,0:T(8,128)(2,1)S(1)} %get-tuple-element.30, pred[]{:T(512)S(6)} %eq.76, pred[]{:T(512)S(6)} %eq.75, ...), kind=kLoop, calls=%fused_computation.49 | loop fusion | flops 524288 | bytes 1572868 | tf_op jit(solution)/shard_map/jit(_where)/select_n | solution.py:125
  49.8 7.8 %collective-permute-done.6 = bf16[4,256,128]{1,2,0:T(8,128)(2,1)} collective-permute-done((bf16[4,256,128]{1,2,0:T(8,128)(2,1)}, bf16[4,256,128]{1,2,0:T(8,128)(2,1)}, u32[]{:S(2)}, u32[]{:S(2)}) %collective-permute-start.6) | collective-permute-done | bytes 262176 | tf_op jit(solution)/shard_map/ppermute | solution.py:119
  57.6 2.0 %broadcast_select_fusion = (bf16[4,256,128]{1,2,0:T(8,128)(2,1)}, bf16[4,256,128]{1,2,0:T(8,128)(2,1)}) fusion(bf16[4,256,128]{1,2,0:T(8,128)(2,1)} %collective-permute-done.6, bf16[4,256,128]{1,2,0:T(8,128)(2,1)} %get-tuple-element.33, pred[]{:T(512)S(6)} %eq.77, bf16[4,256,128]{1,2,0:T(8,128)(2,1)} %get-tuple-element.32, pred[]{:T(512)S(6)} %eq.64), kind=kLoop, calls=%fused_computation.55 | loop fusion | flops 262144 | bytes 1310722 | tf_op jit(solution)/shard_map/jit(_where)/select_n | solution.py:121
  61.5 1.7 broadcast_select_fusion.2
  63.2 1.8 %copy.23 = bf16[4,256,128]{2,1,0:T(8,128)(2,1)} copy(bf16[4,256,128]{1,2,0:T(8,128)(2,1)} %broadcast_select_fusion.2) | data formatting | bytes 524288 | tf_op jit(solution)/shard_map/jit(_where)/select_n | solution.py:171
  65.0 4.0 %all-to-all-done = bf16[16,32,2048]{2,1,0:T(8,128)(2,1)S(1)} async-done(((bf16[16,32,2048]{2,1,0:T(8,128)(2,1)}), bf16[16,32,2048]{2,1,0:T(8,128)(2,1)S(1)}, u32[]{:S(2)}, u32[]{:S(2)}) %all-to-all-start) | async-done | bytes 2097184 | tf_op jit(solution)/shard_map/all_to_all | solution.py:89
  69.0 2.2 %broadcast_in_dim.22 = bf16[4,4,256,128]{3,2,1,0:T(8,128)(2,1)} broadcast(bf16[4,256,128]{2,1,0:T(8,128)(2,1)} %copy.23), dimensions={0,2,3} | broadcast | bytes 1310720 | tf_op jit(solution)/shard_map/broadcast_in_dim | solution.py:173
  71.2 4.5 %all-to-all-start.1 = ((bf16[16,256,128]{2,1,0:T(8,128)(2,1)}), bf16[16,256,128]{2,1,0:T(8,128)(2,1)}, u32[]{:S(2)}, u32[]{:S(2)}) async-start(bf16[16,256,128]{2,1,0:T(8,128)(2,1)} %bitcast.106), calls=%async_computation.1 | async-start | bytes 2097152 | tf_op jit(solution)/shard_map/all_to_all | solution.py:176
  83.4 9.4 %all-to-all-done.1 = bf16[16,256,128]{2,1,0:T(8,128)(2,1)} async-done(((bf16[16,256,128]{2,1,0:T(8,128)(2,1)}), bf16[16,256,128]{2,1,0:T(8,128)(2,1)}, u32[]{:S(2)}, u32[]{:S(2)}) %all-to-all-start.1) | async-done | bytes 1048608 | tf_op jit(solution)/shard_map/all_to_all | solution.py:176
  92.8 2.1 %slice_bitcast_fusion.1 = (bf16[4096,1,64]{2,0,1:T(8,128)(2,1)S(1)}, bf16[4096,1,64]{2,0,1:T(8,128)(2,1)S(1)}) fusion(bf16[4096,128]{1,0:T(8,128)(2,1)} %bitcast.7), kind=kLoop, calls=%fused_computation.38 | loop fusion | bytes 2097152 | tf_op jit(solution)/shard_map/reshape;broadcast_in_dim;reshape | solution.py:180
  97.6 1.6 fusion.36
  99.3 21.0 %all_to_all.20 = bf16[16,1,64,512]{3,2,1,0:T(8,128)(2,1)} all-to-all(bf16[16,1,64,512]{3,2,1,0:T(8,128)(2,1)S(1)} %broadcast_in_dim.26), channel_id=1, replica_groups=mesh['dp'=16,'tensor'=16] {'tensor'}, dimensions={0} | all-to-all | bytes 2097152 | tf_op jit(solution)/shard_map/all_to_all | solution.py:89
  120.3 5.4 %fusion.6 = (f32[512]{0:T(512)S(1)}, bf16[512,2048]{1,0:T(8,128)(2,1)S(1)}) fusion(bf16[1024,512]{1,0:T(8,128)(2,1)} %bitcast.110, bf16[1024,2048]{1,0:T(8,128)(2,1)} %all-gather.2.cloned.1.call-done, bf16[16,32,2048]{2,1,0:T(8,128)(2,1)S(1)} %all-to-all-done), kind=kOutput, calls=%fused_computation.9 | convolution fusion | flops 2153774592 | bytes 9439232 | tf_op jit(solution)/shard_map/dot_general | solution.py:224
  128.1 5.5 %convolution_convert_fusion = bf16[512,2048]{1,0:T(8,128)(2,1)} fusion(bf16[320,2048]{1,0:T(8,128)(2,1)S(1)} %copy-done, bf16[2,2048,320]{1,2,0:T(8,128)(2,1)} %param.18, bf16[512,2048]{1,0:T(8,128)(2,1)} %copy-done.9, f32[512]{0:T(512)S(1)} %add_rsqrt_fusion.1, f32[512,320]{0,1:T(8,128)S(1)} %fusion.13), kind=kOutput, calls=%fused_computation.18 | convolution fusion | flops 1347354624 | bytes 7473152 | tf_op jit(solution)/shard_map/dot_general | solution.py:231
  133.6 3.7 %all-to-all-start.3 = ((bf16[16,32,2048]{2,1,0:T(8,128)(2,1)}), bf16[16,32,2048]{2,1,0:T(8,128)(2,1)S(1)}, u32[]{:S(2)}, u32[]{:S(2)}) async-start(bf16[16,32,2048]{2,1,0:T(8,128)(2,1)} %bitcast.107), calls=%async_computation.3 | async-start | bytes 4194304 | tf_op jit(solution)/shard_map/all_to_all | solution.py:96
  137.3 29.5 %all-to-all-done.3 = bf16[16,32,2048]{2,1,0:T(8,128)(2,1)S(1)} async-done(((bf16[16,32,2048]{2,1,0:T(8,128)(2,1)}), bf16[16,32,2048]{2,1,0:T(8,128)(2,1)S(1)}, u32[]{:S(2)}, u32[]{:S(2)}) %all-to-all-start.3) | async-done | bytes 2097184 | tf_op jit(solution)/shard_map/all_to_all | solution.py:96
  (71 shorter events, 23.5 us)
Async XLA Ops:
  6.5 121.6 %copy-start = (bf16[320,2048]{1,0:T(8,128)(2,1)S(1)}, bf16[320,2048]{1,0:T(8,128)(2,1)}, u32[]{:S(2)}) copy-start(bf16[320,2048]{1,0:T(8,128)(2,1)} %param.19) | copy-start | bytes 3932164
  6.5 7.1 %copy-start.10 = (s32[16]{0:T(128)S(1)}, s32[16]{0:T(128)}, u32[]{:S(2)}) copy-start(s32[16]{0:T(128)} %param.12) | copy-start | bytes 196
  6.5 12.9 %copy-start.3 = (bf16[2048,64]{0,1:T(8,128)(2,1)S(1)}, bf16[2048,64]{0,1:T(8,128)(2,1)}, u32[]{:S(2)}) copy-start(bf16[2048,64]{0,1:T(8,128)(2,1)} %param.14) | copy-start | bytes 786436
  6.5 113.7 %all-gather.2.cloned.1.call-start = ((), (), s32[]{:S(2)}) async-start(), calls=%async_computation.4 | async-start | bytes 4456448 | tf_op jit(solution)/shard_map/all_gather | solution.py:170
  7.8 13.5 %collective-permute-start = (bf16[4,256,128]{1,2,0:T(8,128)(2,1)S(1)}, bf16[4,256,128]{1,2,0:T(8,128)(2,1)}, u32[]{:S(2)}, u32[]{:S(2)}) collective-permute-start(bf16[4,256,128]{1,2,0:T(8,128)(2,1)S(1)} %bitcast.108), channel_id=1, source_target_pairs={{0,224},{16,240},{32,0},{48,16},{64,32},{80,48},{96,64},{112,80},{... | collective-permute-start | bytes 786440 | tf_op jit(solution)/shard_map/ppermute | solution.py:123
  12.0 9.3 %collective-permute-start.1 = (bf16[4,256,128]{1,2,0:T(8,128)(2,1)S(1)}, bf16[4,256,128]{1,2,0:T(8,128)(2,1)}, u32[]{:S(2)}, u32[]{:S(2)}) collective-permute-start(bf16[4,256,128]{1,2,0:T(8,128)(2,1)S(1)} %bitcast.109), channel_id=1, source_target_pairs={{0,32},{16,48},{32,64},{48,80},{64,96},{80,112},{96,128},{112,144}... | collective-permute-start | bytes 786440 | tf_op jit(solution)/shard_map/ppermute | solution.py:119
  19.4 7.0 %copy-start.5 = (bf16[32,2048]{1,0:T(8,128)(2,1)S(1)}, bf16[32,2048]{1,0:T(8,128)(2,1)}, u32[]{:S(2)}) copy-start(bf16[32,2048]{1,0:T(8,128)(2,1)} %param.10) | copy-start | bytes 393220
  23.2 12.2 %collective-permute-start.2 = (bf16[4,256,128]{1,2,0:T(8,128)(2,1)}, bf16[4,256,128]{1,2,0:T(8,128)(2,1)}, u32[]{:S(2)}, u32[]{:S(2)}) collective-permute-start(bf16[4,256,128]{1,2,0:T(8,128)(2,1)} %collective-permute-done), channel_id=1, source_target_pairs={{0,224},{16,240},{32,0},{48,16},{64,32},{80,48},{96,64},{112,80},{... | collective-permute-start | bytes 786440 | tf_op jit(solution)/shard_map/ppermute | solution.py:123
  26.4 9.0 %collective-permute-start.3 = (bf16[4,256,128]{1,2,0:T(8,128)(2,1)}, bf16[4,256,128]{1,2,0:T(8,128)(2,1)}, u32[]{:S(2)}, u32[]{:S(2)}) collective-permute-start(bf16[4,256,128]{1,2,0:T(8,128)(2,1)} %collective-permute-done.1), channel_id=1, source_target_pairs={{0,32},{16,48},{32,64},{48,80},{64,96},{80,112},{96,128},{112,144}... | collective-permute-start | bytes 786440 | tf_op jit(solution)/shard_map/ppermute | solution.py:119
  28.0 7.2 %copy-start.12 = (s32[1,8]{1,0:T(1,128)S(1)}, s32[1,8]{1,0:T(1,128)}, u32[]{:S(2)}) copy-start(s32[1,8]{1,0:T(1,128)} %param.11) | copy-start | bytes 100
  28.0 41.0 %all-to-all-start = ((bf16[16,32,2048]{2,1,0:T(8,128)(2,1)}), bf16[16,32,2048]{2,1,0:T(8,128)(2,1)S(1)}, u32[]{:S(2)}, u32[]{:S(2)}) async-start(bf16[16,32,2048]{2,1,0:T(8,128)(2,1)} %broadcast_in_dim.21), calls=%async_computation | async-start | bytes 4194304 | tf_op jit(solution)/shard_map/all_to_all | solution.py:89
  36.7 7.8 %collective-permute-start.4 = (bf16[4,256,128]{1,2,0:T(8,128)(2,1)}, bf16[4,256,128]{1,2,0:T(8,128)(2,1)S(1)}, u32[]{:S(2)}, u32[]{:S(2)}) collective-permute-start(bf16[4,256,128]{1,2,0:T(8,128)(2,1)} %collective-permute-done.2), channel_id=1, source_target_pairs={{0,224},{16,240},{32,0},{48,16},{64,32},{80,48},{96,64},{112,80},{... | collective-permute-start | bytes 786440 | tf_op jit(solution)/shard_map/ppermute | solution.py:123
  40.0 7.9 %collective-permute-start.5 = (bf16[4,256,128]{1,2,0:T(8,128)(2,1)}, bf16[4,256,128]{1,2,0:T(8,128)(2,1)}, u32[]{:S(2)}, u32[]{:S(2)}) collective-permute-start(bf16[4,256,128]{1,2,0:T(8,128)(2,1)} %collective-permute-done.3), channel_id=1, source_target_pairs={{0,32},{16,48},{32,64},{48,80},{64,96},{80,112},{96,128},{112,144}... | collective-permute-start | bytes 786440 | tf_op jit(solution)/shard_map/ppermute | solution.py:119
  49.7 7.9 %collective-permute-start.6 = (bf16[4,256,128]{1,2,0:T(8,128)(2,1)}, bf16[4,256,128]{1,2,0:T(8,128)(2,1)}, u32[]{:S(2)}, u32[]{:S(2)}) collective-permute-start(bf16[4,256,128]{1,2,0:T(8,128)(2,1)} %collective-permute-done.5), channel_id=1, source_target_pairs={{0,32},{16,48},{32,64},{48,80},{64,96},{80,112},{96,128},{112,144}... | collective-permute-start | bytes 786440 | tf_op jit(solution)/shard_map/ppermute | solution.py:119
  59.6 1.9 %collective-permute-start.7 = (bf16[4,256,128]{1,2,0:T(8,128)(2,1)}, bf16[4,256,128]{1,2,0:T(8,128)(2,1)}, u32[]{:S(2)}, u32[]{:S(2)}) collective-permute-start(bf16[4,256,128]{1,2,0:T(8,128)(2,1)} %get-tuple-element.35), channel_id=1, source_target_pairs={{0,16},{16,0},{32,48},{48,32},{64,80},{80,64},{96,112},{112,96},{1... | collective-permute-start | bytes 786440 | tf_op jit(solution)/shard_map/ppermute | solution.py:129
  71.2 21.6 %all-to-all-start.1 = ((bf16[16,256,128]{2,1,0:T(8,128)(2,1)}), bf16[16,256,128]{2,1,0:T(8,128)(2,1)}, u32[]{:S(2)}, u32[]{:S(2)}) async-start(bf16[16,256,128]{2,1,0:T(8,128)(2,1)} %bitcast.106), calls=%async_computation.1 | async-start | bytes 2097152 | tf_op jit(solution)/shard_map/all_to_all | solution.py:176
  76.3 1.2 copy-start.1
  92.8 2.1 %copy-start.4 = (pred[512,512]{0,1:T(32,128)(4,1)S(1)}, pred[512,512]{0,1:T(32,128)(4,1)}, u32[]{:S(2)}) copy-start(pred[512,512]{0,1:T(32,128)(4,1)} %fusion.39) | copy-start | bytes 786436
  92.8 2.1 %copy-start.6 = (bf16[512,1,64]{2,0,1:T(8,128)(2,1)S(1)}, bf16[512,1,64]{2,0,1:T(8,128)(2,1)}, u32[]{:S(2)}) copy-start(bf16[512,1,64]{2,0,1:T(8,128)(2,1)} %copy.25) | copy-start | bytes 196612
  92.8 2.1 %copy-start.7 = (bf16[512,1,32]{0,2,1:T(8,128)(2,1)S(1)}, bf16[512,1,32]{0,2,1:T(8,128)(2,1)}, u32[]{:S(2)}) copy-start(bf16[512,1,32]{0,2,1:T(8,128)(2,1)} %get-tuple-element.49) | copy-start | bytes 98308
  92.8 2.1 %copy-start.8 = (bf16[512,1,32]{0,2,1:T(8,128)(2,1)S(1)}, bf16[512,1,32]{0,2,1:T(8,128)(2,1)}, u32[]{:S(2)}) copy-start(bf16[512,1,32]{0,2,1:T(8,128)(2,1)} %get-tuple-element.50) | copy-start | bytes 98308
  120.3 6.8 %copy-start.11 = (bf16[2,2048,320]{1,2,0:T(8,128)(2,1)S(1)}, bf16[2,2048,320]{1,2,0:T(8,128)(2,1)}, u32[]{:S(2)}) copy-start(bf16[2,2048,320]{1,2,0:T(8,128)(2,1)} %param.18) | copy-start | bytes 7864324
  125.7 1.3 copy-start.9
  133.6 33.2 %all-to-all-start.3 = ((bf16[16,32,2048]{2,1,0:T(8,128)(2,1)}), bf16[16,32,2048]{2,1,0:T(8,128)(2,1)S(1)}, u32[]{:S(2)}, u32[]{:S(2)}) async-start(bf16[16,32,2048]{2,1,0:T(8,128)(2,1)} %bitcast.107), calls=%async_computation.3 | async-start | bytes 4194304 | tf_op jit(solution)/shard_map/all_to_all | solution.py:96
  (1 other events, 0.8 us)
Sparse Core Ops, SparseCore 0:
  12.1 66.8 all-gather.1

commit v17 on v16

--- a/solution.py
+++ b/solution.py
@@ -164,15 +164,22 @@
 
     shard_rows = prefix_cache.shape[0]
     kv_groups = KVH // local_kv
-    by_head = prefix_cache.reshape(shard_rows, 2, kv_groups, kv_width)
-    by_head = jnp.transpose(by_head, (2, 0, 1, 3)).reshape(kv_groups, shard_rows, 2 * kv_width)
-    on_core, mine, swapped, projection = fetch_slot(by_head, group_prefix, group_rank, projection)
+    on_core, mine, swapped, projection = fetch_slot(prefix_cache, group_prefix, group_rank, projection)
     out_full = lax.all_gather(out_weight, "tensor", axis=0, tiled=True)
-    outgoing = jnp.where(
-        on_core,
-        jnp.repeat(mine, tensor_count // kv_groups, axis=0),
-        jnp.repeat(swapped, tensor_count // kv_groups, axis=0),
-    )
+    chosen = jnp.where(on_core, mine, swapped)
+    by_head = jnp.stack(
+        [
+            jnp.concatenate(
+                [
+                    chosen[:, head * kv_width : (head + 1) * kv_width],
+                    chosen[:, kv_total + head * kv_width : kv_total + (head + 1) * kv_width],
+                ],
+                axis=1,
+            )
+            for head in range(kv_groups)
+        ]
+    )
+    outgoing = jnp.repeat(by_head, tensor_count // kv_groups, axis=0)
     incoming = lax.all_to_all(outgoing, "tensor", 0, 0, tiled=True)
     seg_rows = tensor_count * shard_rows
     incoming = incoming.reshape(seg_rows, 2 * kv_width)

time: 177 us -> 178 us (level)
  waiting for transfers between devices: 59.5 us -> 64.1 us
  blocking collectives: 21 us -> 17.5 us
  local copies, waits for them, and re-layouts: 17.7 us -> 15.6 us
    all_to_all x1, waiting for transfers between devices: 9.4 us -> 18.8 us  [on_device(): incoming = lax.all_to_all(outgoing, 'tensor', 0, 0, tiled=True)]
    all_to_all x1, blocking collectives: 21 us -> 17.5 us  [gather_rows(): received = lax.all_to_all(copies, axis, 0, 0, tiled=True)]
    all_to_all x1, waiting for transfers between devices: 4.03 us -> 1.19 us  [gather_rows(): received = lax.all_to_all(copies, axis, 0, 0, tiled=True)]
    all_to_all x1, waiting for transfers between devices: 29.5 us -> 26.9 us  [sum_scatter_rows(): received = lax.all_to_all(parts, axis, 0, 0, tiled=True)]
    select_n x1 -> x0, local copies, waits for them, and re-layouts: 1.79 us -> none  [on_device(): jnp.where(on_core, jnp.repeat(mine, tensor_count // kv_groups, axis=0), j...]
    unnamed x28 -> x27, local copies, waits for them, and re-layouts: 4.43 us -> 3.21 us
  transfers between devices with their start and end apart: 12 -> 12, of which waited for: 7 -> 7; matrix products, arithmetic and copies ran while one was open for 18% -> 17% of each run, Pallas kernels for 0% -> 0%
where the time goes in v17:
time: 178 us; the launch traced here: 177 us
  waiting for transfers between devices  64.1 us (36%)
  starting transfers between devices  27.7 us (16%)
  between operations  19.1 us (11%)
  blocking collectives  17.5 us (10%)
  other arithmetic  16.9 us (9%)
  matrix products  15.8 us (9%)
  local copies, waits for them, and re-layouts  15.6 us (9%)
    all_to_all x1, waiting for transfers between devices, sum_scatter_rows(): received = lax.all_to_all(parts, axis, 0, 0, tiled=True)  26.9 us
    all_to_all x1, waiting for transfers between devices, on_device(): incoming = lax.all_to_all(outgoing, 'tensor', 0, 0, tiled=True)  18.8 us
    all_to_all x1, blocking collectives, gather_rows(): received = lax.all_to_all(copies, axis, 0, 0, tiled=True)  17.5 us
    ppermute x4, waiting for transfers between devices, fetch_slot(): ahead = lax.ppermute(ahead, 'dp', onward)  11.2 us
    ppermute x3, starting transfers between devices, fetch_slot(): behind = lax.ppermute(behind, 'dp', backward)  10.7 us
    all_to_all x1, starting transfers between devices, gather_rows(): received = lax.all_to_all(copies, axis, 0, 0, tiled=True)  7.17 us
    all_to_all x1, starting transfers between devices, on_device(): incoming = lax.all_to_all(outgoing, 'tensor', 0, 0, tiled=True)  6.12 us
    dot_general x1, matrix products, on_device(): jnp.dot(hidden, down_weight, preferred_element_type=jnp.float32)  5.51 us
  transfers between devices with their start and end apart: 12, of which 7 were waited for; matrix products, arithmetic and copies ran while one was open for 17% of the time, Pallas kernels for 0%

profile of v17, /device:TPU:0, one launch (start us, length us, event | category | flops | bytes accessed | tf_op | source)
XLA Modules:
  0.0 176.9 jit_solution(18121345882950144060)
XLA Ops:
  6.5 4.1 %collective-permute-start = (bf16[256,512]{1,0:T(8,128)(2,1)}, bf16[256,512]{1,0:T(8,128)(2,1)}, u32[]{:S(2)}, u32[]{:S(2)}) collective-permute-start(bf16[256,512]{1,0:T(8,128)(2,1)} %param.13), channel_id=1, source_target_pairs={{0,224},{16,240},{32,0},{48,16},{64,32},{80,48},{96,64},{112,80},{... | collective-permute-start | bytes 786440 | tf_op jit(solution)/shard_map/ppermute | solution.py:123
  10.7 1.6 constant_dynamic-slice_fusion
  20.9 1.9 %select_select_fusion.4 = (bf16[256,512]{1,0:T(8,128)(2,1)}, bf16[256,512]{1,0:T(8,128)(2,1)}) fusion(bf16[256,512]{1,0:T(8,128)(2,1)} %collective-permute-done, bf16[256,512]{1,0:T(8,128)(2,1)} %collective-permute-done.1, bf16[256,512]{1,0:T(8,128)(2,1)S(1)} %copy-done.4, pred[]{:T(512)S(6)} %eq.70, pred[]{:T(512)S(6)} %eq.69, pred[]{:T(512)S(6)} %eq.68, ...), kind=kLoop, calls=%fused_computation.54 | loop fusion | flops 524288 | bytes 1310724 | tf_op jit(solution)/shard_map/jit(_where)/select_n | solution.py:125
  22.8 3.2 %collective-permute-start.2 = (bf16[256,512]{1,0:T(8,128)(2,1)}, bf16[256,512]{1,0:T(8,128)(2,1)}, u32[]{:S(2)}, u32[]{:S(2)}) collective-permute-start(bf16[256,512]{1,0:T(8,128)(2,1)} %collective-permute-done), channel_id=1, source_target_pairs={{0,224},{16,240},{32,0},{48,16},{64,32},{80,48},{96,64},{112,80},{... | collective-permute-start | bytes 786440 | tf_op jit(solution)/shard_map/ppermute | solution.py:123
  26.1 1.6 broadcast_in_dim.21
  27.7 7.2 %all-to-all-start = ((bf16[16,32,2048]{2,1,0:T(8,128)(2,1)}), bf16[16,32,2048]{2,1,0:T(8,128)(2,1)S(1)}, u32[]{:S(2)}, u32[]{:S(2)}) async-start(bf16[16,32,2048]{2,1,0:T(8,128)(2,1)} %broadcast_in_dim.21), calls=%async_computation | async-start | bytes 4194304 | tf_op jit(solution)/shard_map/all_to_all | solution.py:89
  37.1 3.3 %collective-permute-start.4 = (bf16[256,512]{1,0:T(8,128)(2,1)}, bf16[256,512]{1,0:T(8,128)(2,1)S(1)}, u32[]{:S(2)}, u32[]{:S(2)}) collective-permute-start(bf16[256,512]{1,0:T(8,128)(2,1)} %collective-permute-done.2), channel_id=1, source_target_pairs={{0,224},{16,240},{32,0},{48,16},{64,32},{80,48},{96,64},{112,80},{... | collective-permute-start | bytes 786440 | tf_op jit(solution)/shard_map/ppermute | solution.py:123
  40.5 4.4 %collective-permute-done.4 = bf16[256,512]{1,0:T(8,128)(2,1)S(1)} collective-permute-done((bf16[256,512]{1,0:T(8,128)(2,1)}, bf16[256,512]{1,0:T(8,128)(2,1)S(1)}, u32[]{:S(2)}, u32[]{:S(2)}) %collective-permute-start.4) | collective-permute-done | bytes 262176 | tf_op jit(solution)/shard_map/ppermute | solution.py:123
  44.9 3.4 %collective-permute-done.5 = bf16[256,512]{1,0:T(8,128)(2,1)} collective-permute-done((bf16[256,512]{1,0:T(8,128)(2,1)}, bf16[256,512]{1,0:T(8,128)(2,1)}, u32[]{:S(2)}, u32[]{:S(2)}) %collective-permute-start.5) | collective-permute-done | bytes 262176 | tf_op jit(solution)/shard_map/ppermute | solution.py:119
  48.3 1.8 %select_select_fusion = (bf16[256,512]{1,0:T(8,128)(2,1)}, bf16[256,512]{1,0:T(8,128)(2,1)}) fusion(bf16[256,512]{1,0:T(8,128)(2,1)S(1)} %collective-permute-done.4, bf16[256,512]{1,0:T(8,128)(2,1)} %collective-permute-done.5, bf16[256,512]{1,0:T(8,128)(2,1)S(1)} %get-tuple-element.30, pred[]{:T(512)S(6)} %eq.76, pred[]{:T(512)S(6)} %eq.75, ...), kind=kLoop, calls=%fused_computation.50 | loop fusion | flops 524288 | bytes 1572868 | tf_op jit(solution)/shard_map/jit(_where)/select_n | solution.py:125
  50.2 7.8 %collective-permute-done.6 = bf16[256,512]{1,0:T(8,128)(2,1)} collective-permute-done((bf16[256,512]{1,0:T(8,128)(2,1)}, bf16[256,512]{1,0:T(8,128)(2,1)}, u32[]{:S(2)}, u32[]{:S(2)}) %collective-permute-start.6) | collective-permute-done | bytes 262176 | tf_op jit(solution)/shard_map/ppermute | solution.py:119
  58.0 1.9 %broadcast_select_fusion = (bf16[256,512]{1,0:T(8,128)(2,1)}, bf16[256,512]{1,0:T(8,128)(2,1)}) fusion(bf16[256,512]{1,0:T(8,128)(2,1)} %collective-permute-done.6, bf16[256,512]{1,0:T(8,128)(2,1)} %get-tuple-element.33, pred[]{:T(512)S(6)} %eq.77, bf16[256,512]{1,0:T(8,128)(2,1)} %get-tuple-element.32, pred[]{:T(512)S(6)} %eq.64), kind=kLoop, calls=%fused_computation.56 | loop fusion | flops 262144 | bytes 1310722 | tf_op jit(solution)/shard_map/jit(_where)/select_n | solution.py:121
  65.3 2.1 %broadcast_in_dim.22 = bf16[4,4,256,128]{3,2,1,0:T(8,128)(2,1)} broadcast(bf16[4,256,128]{2,1,0:T(8,128)(2,1)} %pad_maximum_fusion.1), dimensions={0,2,3} | broadcast | bytes 1310720 | tf_op jit(solution)/shard_map/broadcast_in_dim | solution.py:182
  67.4 6.1 %all-to-all-start.1 = ((bf16[16,256,128]{2,1,0:T(8,128)(2,1)}), bf16[16,256,128]{2,1,0:T(8,128)(2,1)}, u32[]{:S(2)}, u32[]{:S(2)}) async-start(bf16[16,256,128]{2,1,0:T(8,128)(2,1)} %bitcast.108), calls=%async_computation.1 | async-start | bytes 2097152 | tf_op jit(solution)/shard_map/all_to_all | solution.py:183
  78.7 1.5 fusion.67
  81.2 18.8 %all-to-all-done.1 = bf16[16,256,128]{2,1,0:T(8,128)(2,1)} async-done(((bf16[16,256,128]{2,1,0:T(8,128)(2,1)}), bf16[16,256,128]{2,1,0:T(8,128)(2,1)}, u32[]{:S(2)}, u32[]{:S(2)}) %all-to-all-start.1) | async-done | bytes 1048608 | tf_op jit(solution)/shard_map/all_to_all | solution.py:183
  100.1 2.0 %slice_bitcast_fusion.1 = (bf16[4096,1,64]{2,0,1:T(8,128)(2,1)S(1)}, bf16[4096,1,64]{2,0,1:T(8,128)(2,1)S(1)}) fusion(bf16[4096,128]{1,0:T(8,128)(2,1)} %bitcast.8), kind=kLoop, calls=%fused_computation.38 | loop fusion | bytes 2097152 | tf_op jit(solution)/shard_map/reshape;broadcast_in_dim;reshape | solution.py:187
  104.9 1.6 fusion.36
  106.6 17.5 %all_to_all.20 = bf16[16,1,64,512]{3,2,1,0:T(8,128)(2,1)} all-to-all(bf16[16,1,64,512]{3,2,1,0:T(8,128)(2,1)S(1)} %broadcast_in_dim.26), channel_id=1, replica_groups=mesh['dp'=16,'tensor'=16] {'tensor'}, dimensions={0} | all-to-all | bytes 2097152 | tf_op jit(solution)/shard_map/all_to_all | solution.py:89
  124.1 5.4 %fusion.6 = (f32[512]{0:T(512)S(1)}, bf16[512,2048]{1,0:T(8,128)(2,1)S(1)}) fusion(bf16[1024,512]{1,0:T(8,128)(2,1)} %bitcast.110, bf16[1024,2048]{1,0:T(8,128)(2,1)} %all-gather.2.cloned.1.call-done, bf16[16,32,2048]{2,1,0:T(8,128)(2,1)S(1)} %all-to-all-done), kind=kOutput, calls=%fused_computation.9 | convolution fusion | flops 2153774592 | bytes 9439232 | tf_op jit(solution)/shard_map/dot_general | solution.py:231
  131.9 5.5 %convolution_convert_fusion = bf16[512,2048]{1,0:T(8,128)(2,1)} fusion(bf16[320,2048]{1,0:T(8,128)(2,1)S(1)} %copy-done, bf16[2,2048,320]{1,2,0:T(8,128)(2,1)} %param.18, bf16[512,2048]{1,0:T(8,128)(2,1)} %copy-done.10, f32[512]{0:T(512)S(1)} %add_rsqrt_fusion.1, f32[512,320]{0,1:T(8,128)S(1)} %fusion.13), kind=kOutput, calls=%fused_computation.18 | convolution fusion | flops 1347354624 | bytes 7473152 | tf_op jit(solution)/shard_map/dot_general | solution.py:238
  137.4 3.7 %all-to-all-start.3 = ((bf16[16,32,2048]{2,1,0:T(8,128)(2,1)}), bf16[16,32,2048]{2,1,0:T(8,128)(2,1)S(1)}, u32[]{:S(2)}, u32[]{:S(2)}) async-start(bf16[16,32,2048]{2,1,0:T(8,128)(2,1)} %bitcast.109), calls=%async_computation.3 | async-start | bytes 4194304 | tf_op jit(solution)/shard_map/all_to_all | solution.py:96
  141.2 26.9 %all-to-all-done.3 = bf16[16,32,2048]{2,1,0:T(8,128)(2,1)S(1)} async-done(((bf16[16,32,2048]{2,1,0:T(8,128)(2,1)}), bf16[16,32,2048]{2,1,0:T(8,128)(2,1)S(1)}, u32[]{:S(2)}, u32[]{:S(2)}) %all-to-all-start.3) | async-done | bytes 2097184 | tf_op jit(solution)/shard_map/all_to_all | solution.py:96
  168.4 1.6 add_convert_fusion
  (74 shorter events, 22.5 us)
Async XLA Ops:
  6.5 125.4 %copy-start = (bf16[320,2048]{1,0:T(8,128)(2,1)S(1)}, bf16[320,2048]{1,0:T(8,128)(2,1)}, u32[]{:S(2)}) copy-start(bf16[320,2048]{1,0:T(8,128)(2,1)} %param.19) | copy-start | bytes 3932164
  6.5 12.6 %copy-start.3 = (bf16[2048,64]{0,1:T(8,128)(2,1)S(1)}, bf16[2048,64]{0,1:T(8,128)(2,1)}, u32[]{:S(2)}) copy-start(bf16[2048,64]{0,1:T(8,128)(2,1)} %param.14) | copy-start | bytes 786436
  6.5 14.4 %collective-permute-start = (bf16[256,512]{1,0:T(8,128)(2,1)}, bf16[256,512]{1,0:T(8,128)(2,1)}, u32[]{:S(2)}, u32[]{:S(2)}) collective-permute-start(bf16[256,512]{1,0:T(8,128)(2,1)} %param.13), channel_id=1, source_target_pairs={{0,224},{16,240},{32,0},{48,16},{64,32},{80,48},{96,64},{112,80},{... | collective-permute-start | bytes 786440 | tf_op jit(solution)/shard_map/ppermute | solution.py:123
  10.7 10.3 %collective-permute-start.1 = (bf16[256,512]{1,0:T(8,128)(2,1)}, bf16[256,512]{1,0:T(8,128)(2,1)}, u32[]{:S(2)}, u32[]{:S(2)}) collective-permute-start(bf16[256,512]{1,0:T(8,128)(2,1)} %param.13), channel_id=1, source_target_pairs={{0,32},{16,48},{32,64},{48,80},{64,96},{80,112},{96,128},{112,144}... | collective-permute-start | bytes 786440 | tf_op jit(solution)/shard_map/ppermute | solution.py:119
  10.7 10.3 %copy-start.4 = (bf16[256,512]{1,0:T(8,128)(2,1)S(1)}, bf16[256,512]{1,0:T(8,128)(2,1)}, u32[]{:S(2)}) copy-start(bf16[256,512]{1,0:T(8,128)(2,1)} %param.13) | copy-start | bytes 786436
  19.1 7.0 %copy-start.6 = (bf16[32,2048]{1,0:T(8,128)(2,1)S(1)}, bf16[32,2048]{1,0:T(8,128)(2,1)}, u32[]{:S(2)}) copy-start(bf16[32,2048]{1,0:T(8,128)(2,1)} %param.10) | copy-start | bytes 393220
  22.8 13.0 %collective-permute-start.2 = (bf16[256,512]{1,0:T(8,128)(2,1)}, bf16[256,512]{1,0:T(8,128)(2,1)}, u32[]{:S(2)}, u32[]{:S(2)}) collective-permute-start(bf16[256,512]{1,0:T(8,128)(2,1)} %collective-permute-done), channel_id=1, source_target_pairs={{0,224},{16,240},{32,0},{48,16},{64,32},{80,48},{96,64},{112,80},{... | collective-permute-start | bytes 786440 | tf_op jit(solution)/shard_map/ppermute | solution.py:123
  26.1 9.8 %collective-permute-start.3 = (bf16[256,512]{1,0:T(8,128)(2,1)}, bf16[256,512]{1,0:T(8,128)(2,1)}, u32[]{:S(2)}, u32[]{:S(2)}) collective-permute-start(bf16[256,512]{1,0:T(8,128)(2,1)} %collective-permute-done.1), channel_id=1, source_target_pairs={{0,32},{16,48},{32,64},{48,80},{64,96},{80,112},{96,128},{112,144}... | collective-permute-start | bytes 786440 | tf_op jit(solution)/shard_map/ppermute | solution.py:119
  27.7 7.9 %copy-start.12 = (s32[1,8]{1,0:T(1,128)S(1)}, s32[1,8]{1,0:T(1,128)}, u32[]{:S(2)}) copy-start(s32[1,8]{1,0:T(1,128)} %param.11) | copy-start | bytes 100
  27.7 37.6 %all-to-all-start = ((bf16[16,32,2048]{2,1,0:T(8,128)(2,1)}), bf16[16,32,2048]{2,1,0:T(8,128)(2,1)S(1)}, u32[]{:S(2)}, u32[]{:S(2)}) async-start(bf16[16,32,2048]{2,1,0:T(8,128)(2,1)} %broadcast_in_dim.21), calls=%async_computation | async-start | bytes 4194304 | tf_op jit(solution)/shard_map/all_to_all | solution.py:89
  34.9 89.2 %all-gather.2.cloned.1.call-start = ((), (), s32[]{:S(2)}) async-start(), calls=%async_computation.4 | async-start | bytes 4456448 | tf_op jit(solution)/shard_map/all_gather | solution.py:168
  37.1 7.8 %collective-permute-start.4 = (bf16[256,512]{1,0:T(8,128)(2,1)}, bf16[256,512]{1,0:T(8,128)(2,1)S(1)}, u32[]{:S(2)}, u32[]{:S(2)}) collective-permute-start(bf16[256,512]{1,0:T(8,128)(2,1)} %collective-permute-done.2), channel_id=1, source_target_pairs={{0,224},{16,240},{32,0},{48,16},{64,32},{80,48},{96,64},{112,80},{... | collective-permute-start | bytes 786440 | tf_op jit(solution)/shard_map/ppermute | solution.py:123
  40.4 7.9 %collective-permute-start.5 = (bf16[256,512]{1,0:T(8,128)(2,1)}, bf16[256,512]{1,0:T(8,128)(2,1)}, u32[]{:S(2)}, u32[]{:S(2)}) collective-permute-start(bf16[256,512]{1,0:T(8,128)(2,1)} %collective-permute-done.3), channel_id=1, source_target_pairs={{0,32},{16,48},{32,64},{48,80},{64,96},{80,112},{96,128},{112,144}... | collective-permute-start | bytes 786440 | tf_op jit(solution)/shard_map/ppermute | solution.py:119
  50.1 7.9 %collective-permute-start.6 = (bf16[256,512]{1,0:T(8,128)(2,1)}, bf16[256,512]{1,0:T(8,128)(2,1)}, u32[]{:S(2)}, u32[]{:S(2)}) collective-permute-start(bf16[256,512]{1,0:T(8,128)(2,1)} %collective-permute-done.5), channel_id=1, source_target_pairs={{0,32},{16,48},{32,64},{48,80},{64,96},{80,112},{96,128},{112,144}... | collective-permute-start | bytes 786440 | tf_op jit(solution)/shard_map/ppermute | solution.py:119
  59.9 1.9 %collective-permute-start.7 = (bf16[256,512]{1,0:T(8,128)(2,1)}, bf16[256,512]{1,0:T(8,128)(2,1)}, u32[]{:S(2)}, u32[]{:S(2)}) collective-permute-start(bf16[256,512]{1,0:T(8,128)(2,1)} %get-tuple-element.35), channel_id=1, source_target_pairs={{0,16},{16,0},{32,48},{48,32},{64,80},{80,64},{96,112},{112,96},{1... | collective-permute-start | bytes 786440 | tf_op jit(solution)/shard_map/ppermute | solution.py:129
  67.4 32.6 %all-to-all-start.1 = ((bf16[16,256,128]{2,1,0:T(8,128)(2,1)}), bf16[16,256,128]{2,1,0:T(8,128)(2,1)}, u32[]{:S(2)}, u32[]{:S(2)}) async-start(bf16[16,256,128]{2,1,0:T(8,128)(2,1)} %bitcast.108), calls=%async_computation.1 | async-start | bytes 2097152 | tf_op jit(solution)/shard_map/all_to_all | solution.py:183
  74.1 1.2 copy-start.1
  100.1 2.0 %copy-start.5 = (pred[512,512]{0,1:T(32,128)(4,1)S(1)}, pred[512,512]{0,1:T(32,128)(4,1)}, u32[]{:S(2)}) copy-start(pred[512,512]{0,1:T(32,128)(4,1)} %fusion.39) | copy-start | bytes 786436
  100.1 2.0 %copy-start.7 = (bf16[512,1,64]{2,0,1:T(8,128)(2,1)S(1)}, bf16[512,1,64]{2,0,1:T(8,128)(2,1)}, u32[]{:S(2)}) copy-start(bf16[512,1,64]{2,0,1:T(8,128)(2,1)} %copy.16) | copy-start | bytes 196612
  100.1 2.0 %copy-start.8 = (bf16[512,1,32]{0,2,1:T(8,128)(2,1)S(1)}, bf16[512,1,32]{0,2,1:T(8,128)(2,1)}, u32[]{:S(2)}) copy-start(bf16[512,1,32]{0,2,1:T(8,128)(2,1)} %get-tuple-element.57) | copy-start | bytes 98308
  100.1 2.1 %copy-start.9 = (bf16[512,1,32]{0,2,1:T(8,128)(2,1)S(1)}, bf16[512,1,32]{0,2,1:T(8,128)(2,1)}, u32[]{:S(2)}) copy-start(bf16[512,1,32]{0,2,1:T(8,128)(2,1)} %get-tuple-element.58) | copy-start | bytes 98308
  124.1 6.8 %copy-start.11 = (bf16[2,2048,320]{1,2,0:T(8,128)(2,1)S(1)}, bf16[2,2048,320]{1,2,0:T(8,128)(2,1)}, u32[]{:S(2)}) copy-start(bf16[2,2048,320]{1,2,0:T(8,128)(2,1)} %param.18) | copy-start | bytes 7864324
  129.5 1.3 copy-start.10
  137.4 30.6 %all-to-all-start.3 = ((bf16[16,32,2048]{2,1,0:T(8,128)(2,1)}), bf16[16,32,2048]{2,1,0:T(8,128)(2,1)S(1)}, u32[]{:S(2)}, u32[]{:S(2)}) async-start(bf16[16,32,2048]{2,1,0:T(8,128)(2,1)} %bitcast.109), calls=%async_computation.3 | async-start | bytes 4194304 | tf_op jit(solution)/shard_map/all_to_all | solution.py:96
  (1 other events, 0.8 us)
Sparse Core Ops, SparseCore 0:
  38.1 67.9 all-gather.1

commit v18 on v16

--- a/solution.py
+++ b/solution.py
@@ -210,13 +210,23 @@
         repeat_by,
         axis=1,
     )
-    every_key = jnp.concatenate([keys_block, own_keys], axis=0)
-    every_value = jnp.concatenate([values_block, own_values], axis=0)
     indices = jnp.arange(group_tokens, dtype=jnp.int32)
     allowed = (request[:, None] == request[None, :]) & (indices[None, :] <= indices[:, None])
-    allowed = jnp.concatenate([jnp.ones((group_tokens, keys_block.shape[0]), bool), allowed], axis=1)
-    top_score, weight, blended = softmax_block(
-        queries, every_key, every_value, scaling, allowed[:, None, :]
+    prefix_scores = (
+        jnp.einsum("thd,nhd->thn", queries, keys_block, preferred_element_type=jnp.float32) * scaling
+    )
+    own_scores = (
+        jnp.einsum("thd,nhd->thn", queries, own_keys, preferred_element_type=jnp.float32) * scaling
+    )
+    own_scores = jnp.where(allowed[:, None, :], own_scores, NEG_FILL)
+    top_score = jnp.maximum(jnp.max(prefix_scores, axis=2), jnp.max(own_scores, axis=2))
+    prefix_exp = jnp.exp(prefix_scores - top_score[:, :, None])
+    own_exp = jnp.exp(own_scores - top_score[:, :, None])
+    weight = jnp.sum(prefix_exp, axis=2) + jnp.sum(own_exp, axis=2)
+    blended = jnp.einsum(
+        "thn,nhd->thd", prefix_exp.astype(jnp.bfloat16), values_block, preferred_element_type=jnp.float32
+    ) + jnp.einsum(
+        "thn,nhd->thd", own_exp.astype(jnp.bfloat16), own_values, preferred_element_type=jnp.float32
     )
     attended = (blended / weight[:, :, None]).astype(jnp.bfloat16).reshape(group_tokens, query_width)
     every_head = gather_rows(jnp.transpose(attended)[None], "tensor")

time: 177 us -> 179 us (1.011)
  local copies, waits for them, and re-layouts: 17.7 us -> 12.4 us
  matrix products: 15.8 us -> 20.9 us
  waiting for transfers between devices: 59.5 us -> 62.6 us
    dot_general x2 -> x4, matrix products: 3.02 us -> 8.17 us  [the longest x1 3.04 us: on_device(): jnp.einsum('thn,nhd->thd', prefix_exp.astype(jnp.bfloat16), values_block,...]
    another operation x3 -> x0, local copies, waits for them, and re-layouts: 4.54 us -> none  [the longest x2 2.49 us: on_device(): jnp.repeat(projected[:, query_width + kv_width:].reshape(group_tokens, lo...]
    all_to_all x1, waiting for transfers between devices: 9.4 us -> 12.3 us  [on_device(): incoming = lax.all_to_all(outgoing, 'tensor', 0, 0, tiled=True)]
    unnamed x28 -> x22, local copies, waits for them, and re-layouts: 4.43 us -> 4.39 us
where the time goes in v18:
time: 179 us; the launch traced here: 178 us
  waiting for transfers between devices  62.6 us (35%)
  starting transfers between devices  26.1 us (15%)
  matrix products  20.9 us (12%)
  blocking collectives  20.9 us (12%)
  between operations  18.8 us (11%)
  other arithmetic  16.3 us (9%)
  local copies, waits for them, and re-layouts  12.4 us (7%)
    all_to_all x1, waiting for transfers between devices, sum_scatter_rows(): received = lax.all_to_all(parts, axis, 0, 0, tiled=True)  29.7 us
    all_to_all x1, blocking collectives, gather_rows(): received = lax.all_to_all(copies, axis, 0, 0, tiled=True)  20.9 us
    all_to_all x1, waiting for transfers between devices, on_device(): incoming = lax.all_to_all(outgoing, 'tensor', 0, 0, tiled=True)  12.3 us
    ppermute x4, waiting for transfers between devices, fetch_slot(): ahead = lax.ppermute(ahead, 'dp', onward)  11.1 us
    ppermute x3, starting transfers between devices, fetch_slot(): behind = lax.ppermute(behind, 'dp', backward)  10.7 us
    all_to_all x1, starting transfers between devices, gather_rows(): received = lax.all_to_all(copies, axis, 0, 0, tiled=True)  7.17 us
    select_n x3, other arithmetic, fetch_slot(): theirs = jnp.where(theirs_at == step, behind, theirs)  5.97 us
    dot_general x1, matrix products, on_device(): jnp.dot(hidden, down_weight, preferred_element_type=jnp.float32)  5.49 us
  transfers between devices with their start and end apart: 12, of which 7 were waited for; matrix products, arithmetic and copies ran while one was open for 18% of the time, Pallas kernels for 0%

profile of v18, /device:TPU:0, one launch (start us, length us, event | category | flops | bytes accessed | tf_op | source)
XLA Modules:
  0.0 178.0 jit_solution(15236445431147240364)
XLA Ops:
  7.8 4.2 %collective-permute-start = (bf16[4,256,128]{1,2,0:T(8,128)(2,1)S(1)}, bf16[4,256,128]{1,2,0:T(8,128)(2,1)}, u32[]{:S(2)}, u32[]{:S(2)}) collective-permute-start(bf16[4,256,128]{1,2,0:T(8,128)(2,1)S(1)} %bitcast.102), channel_id=1, source_target_pairs={{0,224},{16,240},{32,0},{48,16},{64,32},{80,48},{96,64},{112,80},{... | collective-permute-start | bytes 786440 | tf_op jit(solution)/shard_map/ppermute | solution.py:123
  21.1 1.9 %select_select_fusion.4 = (bf16[4,256,128]{1,2,0:T(8,128)(2,1)}, bf16[4,256,128]{1,2,0:T(8,128)(2,1)}) fusion(bf16[4,256,128]{1,2,0:T(8,128)(2,1)} %collective-permute-done, bf16[4,256,128]{1,2,0:T(8,128)(2,1)} %collective-permute-done.1, pred[]{:T(512)S(6)} %eq.77, pred[]{:T(512)S(6)} %eq.76, bf16[4,256,2,64]{1,3,2,0:T(8,128)(2,1)S(1)} %copy.17, ...), kind=kLoop, calls=%fused_computation.57 | loop fusion | flops 524288 | bytes 1310724 | tf_op jit(solution)/shard_map/jit(_where)/select_n | solution.py:125
  23.1 3.2 %collective-permute-start.2 = (bf16[4,256,128]{1,2,0:T(8,128)(2,1)}, bf16[4,256,128]{1,2,0:T(8,128)(2,1)}, u32[]{:S(2)}, u32[]{:S(2)}) collective-permute-start(bf16[4,256,128]{1,2,0:T(8,128)(2,1)} %collective-permute-done), channel_id=1, source_target_pairs={{0,224},{16,240},{32,0},{48,16},{64,32},{80,48},{96,64},{112,80},{... | collective-permute-start | bytes 786440 | tf_op jit(solution)/shard_map/ppermute | solution.py:123
  27.9 7.2 %all-to-all-start = ((bf16[16,32,2048]{2,1,0:T(8,128)(2,1)}), bf16[16,32,2048]{2,1,0:T(8,128)(2,1)S(1)}, u32[]{:S(2)}, u32[]{:S(2)}) async-start(bf16[16,32,2048]{2,1,0:T(8,128)(2,1)} %broadcast_in_dim.19), calls=%async_computation | async-start | bytes 4194304 | tf_op jit(solution)/shard_map/all_to_all | solution.py:89
  35.1 2.0 %select_select_fusion.2 = (bf16[4,256,128]{1,2,0:T(8,128)(2,1)}, bf16[4,256,128]{1,2,0:T(8,128)(2,1)}) fusion(bf16[4,256,128]{1,2,0:T(8,128)(2,1)} %collective-permute-done.2, bf16[4,256,128]{1,2,0:T(8,128)(2,1)} %collective-permute-done.3, bf16[4,256,128]{1,2,0:T(8,128)(2,1)} %get-tuple-element.26, pred[]{:T(512)S(6)} %eq.80, pred[]{:T(512)S(6)} %eq.79, ...), kind=kLoop, calls=%fused_computation.55 | loop fusion | flops 524288 | bytes 1572868 | tf_op jit(solution)/shard_map/jit(_where)/select_n | solution.py:125
  37.1 3.2 %collective-permute-start.4 = (bf16[4,256,128]{1,2,0:T(8,128)(2,1)}, bf16[4,256,128]{1,2,0:T(8,128)(2,1)}, u32[]{:S(2)}, u32[]{:S(2)}) collective-permute-start(bf16[4,256,128]{1,2,0:T(8,128)(2,1)} %collective-permute-done.2), channel_id=1, source_target_pairs={{0,224},{16,240},{32,0},{48,16},{64,32},{80,48},{96,64},{112,80},{... | collective-permute-start | bytes 786440 | tf_op jit(solution)/shard_map/ppermute | solution.py:123
  40.6 4.3 %collective-permute-done.4 = bf16[4,256,128]{1,2,0:T(8,128)(2,1)} collective-permute-done((bf16[4,256,128]{1,2,0:T(8,128)(2,1)}, bf16[4,256,128]{1,2,0:T(8,128)(2,1)}, u32[]{:S(2)}, u32[]{:S(2)}) %collective-permute-start.4) | collective-permute-done | bytes 262176 | tf_op jit(solution)/shard_map/ppermute | solution.py:123
  44.9 3.4 %collective-permute-done.5 = bf16[4,256,128]{1,2,0:T(8,128)(2,1)} collective-permute-done((bf16[4,256,128]{1,2,0:T(8,128)(2,1)}, bf16[4,256,128]{1,2,0:T(8,128)(2,1)}, u32[]{:S(2)}, u32[]{:S(2)}) %collective-permute-start.5) | collective-permute-done | bytes 262176 | tf_op jit(solution)/shard_map/ppermute | solution.py:119
  48.3 2.0 %select_select_fusion = (bf16[4,256,128]{1,2,0:T(8,128)(2,1)}, bf16[4,256,128]{1,2,0:T(8,128)(2,1)}) fusion(bf16[4,256,128]{1,2,0:T(8,128)(2,1)} %collective-permute-done.4, bf16[4,256,128]{1,2,0:T(8,128)(2,1)} %collective-permute-done.5, bf16[4,256,128]{1,2,0:T(8,128)(2,1)} %get-tuple-element.30, pred[]{:T(512)S(6)} %eq.83, pred[]{:T(512)S(6)} %eq.82, ...), kind=kLoop, calls=%fused_computation.53 | loop fusion | flops 524288 | bytes 1572868 | tf_op jit(solution)/shard_map/jit(_where)/select_n | solution.py:125
  50.5 7.7 %collective-permute-done.6 = bf16[4,256,128]{1,2,0:T(8,128)(2,1)} collective-permute-done((bf16[4,256,128]{1,2,0:T(8,128)(2,1)}, bf16[4,256,128]{1,2,0:T(8,128)(2,1)}, u32[]{:S(2)}, u32[]{:S(2)}) %collective-permute-start.6) | collective-permute-done | bytes 262176 | tf_op jit(solution)/shard_map/ppermute | solution.py:119
  58.2 1.9 %broadcast_select_fusion = (bf16[4,256,128]{1,2,0:T(8,128)(2,1)}, bf16[4,256,128]{1,2,0:T(8,128)(2,1)}) fusion(bf16[4,256,128]{1,2,0:T(8,128)(2,1)} %collective-permute-done.6, bf16[4,256,128]{1,2,0:T(8,128)(2,1)} %get-tuple-element.33, pred[]{:T(512)S(6)} %eq.84, bf16[4,256,128]{1,2,0:T(8,128)(2,1)} %get-tuple-element.32, pred[]{:T(512)S(6)} %eq.71), kind=kLoop, calls=%fused_computation.59 | loop fusion | flops 262144 | bytes 1310722 | tf_op jit(solution)/shard_map/jit(_where)/select_n | solution.py:121
  60.2 1.8 %collective-permute-done.7 = bf16[4,256,128]{1,2,0:T(8,128)(2,1)} collective-permute-done((bf16[4,256,128]{1,2,0:T(8,128)(2,1)}, bf16[4,256,128]{1,2,0:T(8,128)(2,1)}, u32[]{:S(2)}, u32[]{:S(2)}) %collective-permute-start.7) | collective-permute-done | bytes 262176 | tf_op jit(solution)/shard_map/ppermute | solution.py:129
  63.7 1.8 %copy.19 = bf16[4,256,128]{2,1,0:T(8,128)(2,1)} copy(bf16[4,256,128]{1,2,0:T(8,128)(2,1)} %broadcast_select_fusion.2) | data formatting | bytes 524288 | tf_op jit(solution)/shard_map/jit(_where)/select_n | solution.py:171
  65.5 3.3 %all-to-all-done = bf16[16,32,2048]{2,1,0:T(8,128)(2,1)S(1)} async-done(((bf16[16,32,2048]{2,1,0:T(8,128)(2,1)}), bf16[16,32,2048]{2,1,0:T(8,128)(2,1)S(1)}, u32[]{:S(2)}, u32[]{:S(2)}) %all-to-all-start) | async-done | bytes 2097184 | tf_op jit(solution)/shard_map/all_to_all | solution.py:89
  68.8 2.2 %broadcast_in_dim.20 = bf16[4,4,256,128]{3,2,1,0:T(8,128)(2,1)} broadcast(bf16[4,256,128]{2,1,0:T(8,128)(2,1)} %copy.19), dimensions={0,2,3} | broadcast | bytes 1310720 | tf_op jit(solution)/shard_map/broadcast_in_dim | solution.py:173
  71.0 4.5 %all-to-all-start.1 = ((bf16[16,256,128]{2,1,0:T(8,128)(2,1)}), bf16[16,256,128]{2,1,0:T(8,128)(2,1)}, u32[]{:S(2)}, u32[]{:S(2)}) async-start(bf16[16,256,128]{2,1,0:T(8,128)(2,1)} %bitcast.100), calls=%async_computation.1 | async-start | bytes 2097152 | tf_op jit(solution)/shard_map/all_to_all | solution.py:176
  80.6 12.3 %all-to-all-done.1 = bf16[16,256,128]{2,1,0:T(8,128)(2,1)} async-done(((bf16[16,256,128]{2,1,0:T(8,128)(2,1)}), bf16[16,256,128]{2,1,0:T(8,128)(2,1)}, u32[]{:S(2)}, u32[]{:S(2)}) %all-to-all-start.1) | async-done | bytes 1048608 | tf_op jit(solution)/shard_map/all_to_all | solution.py:176
  92.9 2.6 %multiply_reduce_fusion = (f32[512]{0:T(512)S(1)}, f32[4096,512]{1,0:T(8,128)S(1)}) fusion(bf16[512,1,32]{0,2,1:T(8,128)(2,1)S(1)} %get-tuple-element.51, bf16[512,1,32]{0,2,1:T(8,128)(2,1)S(1)} %get-tuple-element.52, bf16[4096,128]{1,0:T(8,128)(2,1)} %bitcast.7), kind=kOutput, calls=%fused_computation.2 | convolution fusion | flops 272760320 | bytes 9504768 | tf_op jit(solution)/shard_map/thd,nhd->thn/dot_general | solution.py:216
  97.2 3.0 %fusion.9 = f32[64,512]{1,0:T(8,128)S(1)} fusion(f32[4096,512]{1,0:T(8,128)S(1)} %get-tuple-element.56, f32[512]{0:T(512)S(1)} %max.9, bf16[4096,128]{1,0:T(8,128)(2,1)} %bitcast.7), kind=kOutput, calls=%fused_computation.17 | convolution fusion | flops 274726912 | bytes 9570304 | tf_op jit(solution)/shard_map/thn,nhd->thd/dot_general | solution.py:226
  101.5 20.9 %all_to_all.20 = bf16[16,1,64,512]{3,2,1,0:T(8,128)(2,1)} all-to-all(bf16[16,1,64,512]{3,2,1,0:T(8,128)(2,1)S(1)} %broadcast_in_dim.23), channel_id=1, replica_groups=mesh['dp'=16,'tensor'=16] {'tensor'}, dimensions={0} | all-to-all | bytes 2097152 | tf_op jit(solution)/shard_map/all_to_all | solution.py:89
  122.4 5.4 %fusion.3 = (f32[512]{0:T(512)S(1)}, bf16[512,2048]{1,0:T(8,128)(2,1)S(1)}) fusion(bf16[1024,512]{1,0:T(8,128)(2,1)} %bitcast.104, bf16[1024,2048]{1,0:T(8,128)(2,1)} %all-gather.2.cloned.1.call-done, bf16[16,32,2048]{2,1,0:T(8,128)(2,1)S(1)} %all-to-all-done), kind=kOutput, calls=%fused_computation.7 | convolution fusion | flops 2153774592 | bytes 9439232 | tf_op jit(solution)/shard_map/dot_general | solution.py:234
  130.3 5.5 %convolution_convert_fusion = bf16[512,2048]{1,0:T(8,128)(2,1)} fusion(bf16[320,2048]{1,0:T(8,128)(2,1)S(1)} %copy-done, bf16[2,2048,320]{1,2,0:T(8,128)(2,1)} %param.18, bf16[512,2048]{1,0:T(8,128)(2,1)} %copy-done.6, f32[512]{0:T(512)S(1)} %add_rsqrt_fusion.1, f32[512,320]{0,1:T(8,128)S(1)} %fusion.14), kind=kOutput, calls=%fused_computation.18 | convolution fusion | flops 1347354624 | bytes 7473152 | tf_op jit(solution)/shard_map/dot_general | solution.py:241
  135.7 3.7 %all-to-all-start.3 = ((bf16[16,32,2048]{2,1,0:T(8,128)(2,1)}), bf16[16,32,2048]{2,1,0:T(8,128)(2,1)S(1)}, u32[]{:S(2)}, u32[]{:S(2)}) async-start(bf16[16,32,2048]{2,1,0:T(8,128)(2,1)} %bitcast.101), calls=%async_computation.3 | async-start | bytes 4194304 | tf_op jit(solution)/shard_map/all_to_all | solution.py:96
  139.5 29.7 %all-to-all-done.3 = bf16[16,32,2048]{2,1,0:T(8,128)(2,1)S(1)} async-done(((bf16[16,32,2048]{2,1,0:T(8,128)(2,1)}), bf16[16,32,2048]{2,1,0:T(8,128)(2,1)S(1)}, u32[]{:S(2)}, u32[]{:S(2)}) %all-to-all-start.3) | async-done | bytes 2097184 | tf_op jit(solution)/shard_map/all_to_all | solution.py:96
  (64 shorter events, 21.3 us)
Async XLA Ops:
  6.5 123.7 %copy-start = (bf16[320,2048]{1,0:T(8,128)(2,1)S(1)}, bf16[320,2048]{1,0:T(8,128)(2,1)}, u32[]{:S(2)}) copy-start(bf16[320,2048]{1,0:T(8,128)(2,1)} %param.19) | copy-start | bytes 3932164
  6.5 7.1 %copy-start.7 = (s32[16]{0:T(128)S(1)}, s32[16]{0:T(128)}, u32[]{:S(2)}) copy-start(s32[16]{0:T(128)} %param.12) | copy-start | bytes 196
  6.5 12.8 %copy-start.4 = (bf16[2048,64]{0,1:T(8,128)(2,1)S(1)}, bf16[2048,64]{0,1:T(8,128)(2,1)}, u32[]{:S(2)}) copy-start(bf16[2048,64]{0,1:T(8,128)(2,1)} %param.14) | copy-start | bytes 786436
  6.5 115.9 %all-gather.2.cloned.1.call-start = ((), (), s32[]{:S(2)}) async-start(), calls=%async_computation.4 | async-start | bytes 4456448 | tf_op jit(solution)/shard_map/all_gather | solution.py:170
  7.8 13.4 %collective-permute-start = (bf16[4,256,128]{1,2,0:T(8,128)(2,1)S(1)}, bf16[4,256,128]{1,2,0:T(8,128)(2,1)}, u32[]{:S(2)}, u32[]{:S(2)}) collective-permute-start(bf16[4,256,128]{1,2,0:T(8,128)(2,1)S(1)} %bitcast.102), channel_id=1, source_target_pairs={{0,224},{16,240},{32,0},{48,16},{64,32},{80,48},{96,64},{112,80},{... | collective-permute-start | bytes 786440 | tf_op jit(solution)/shard_map/ppermute | solution.py:123
  12.0 9.2 %collective-permute-start.1 = (bf16[4,256,128]{1,2,0:T(8,128)(2,1)S(1)}, bf16[4,256,128]{1,2,0:T(8,128)(2,1)}, u32[]{:S(2)}, u32[]{:S(2)}) collective-permute-start(bf16[4,256,128]{1,2,0:T(8,128)(2,1)S(1)} %bitcast.103), channel_id=1, source_target_pairs={{0,32},{16,48},{32,64},{48,80},{64,96},{80,112},{96,128},{112,144}... | collective-permute-start | bytes 786440 | tf_op jit(solution)/shard_map/ppermute | solution.py:119
  13.6 12.7 %copy-start.5 = (bf16[32,2048]{1,0:T(8,128)(2,1)S(1)}, bf16[32,2048]{1,0:T(8,128)(2,1)}, u32[]{:S(2)}) copy-start(bf16[32,2048]{1,0:T(8,128)(2,1)} %param.10) | copy-start | bytes 393220
  23.1 12.0 %collective-permute-start.2 = (bf16[4,256,128]{1,2,0:T(8,128)(2,1)}, bf16[4,256,128]{1,2,0:T(8,128)(2,1)}, u32[]{:S(2)}, u32[]{:S(2)}) collective-permute-start(bf16[4,256,128]{1,2,0:T(8,128)(2,1)} %collective-permute-done), channel_id=1, source_target_pairs={{0,224},{16,240},{32,0},{48,16},{64,32},{80,48},{96,64},{112,80},{... | collective-permute-start | bytes 786440 | tf_op jit(solution)/shard_map/ppermute | solution.py:123
  26.3 8.8 %collective-permute-start.3 = (bf16[4,256,128]{1,2,0:T(8,128)(2,1)}, bf16[4,256,128]{1,2,0:T(8,128)(2,1)}, u32[]{:S(2)}, u32[]{:S(2)}) collective-permute-start(bf16[4,256,128]{1,2,0:T(8,128)(2,1)} %collective-permute-done.1), channel_id=1, source_target_pairs={{0,32},{16,48},{32,64},{48,80},{64,96},{80,112},{96,128},{112,144}... | collective-permute-start | bytes 786440 | tf_op jit(solution)/shard_map/ppermute | solution.py:119
  27.9 12.5 %copy-start.9 = (s32[1,8]{1,0:T(1,128)S(1)}, s32[1,8]{1,0:T(1,128)}, u32[]{:S(2)}) copy-start(s32[1,8]{1,0:T(1,128)} %param.11) | copy-start | bytes 100
  27.9 40.9 %all-to-all-start = ((bf16[16,32,2048]{2,1,0:T(8,128)(2,1)}), bf16[16,32,2048]{2,1,0:T(8,128)(2,1)S(1)}, u32[]{:S(2)}, u32[]{:S(2)}) async-start(bf16[16,32,2048]{2,1,0:T(8,128)(2,1)} %broadcast_in_dim.19), calls=%async_computation | async-start | bytes 4194304 | tf_op jit(solution)/shard_map/all_to_all | solution.py:89
  37.1 7.7 %collective-permute-start.4 = (bf16[4,256,128]{1,2,0:T(8,128)(2,1)}, bf16[4,256,128]{1,2,0:T(8,128)(2,1)}, u32[]{:S(2)}, u32[]{:S(2)}) collective-permute-start(bf16[4,256,128]{1,2,0:T(8,128)(2,1)} %collective-permute-done.2), channel_id=1, source_target_pairs={{0,224},{16,240},{32,0},{48,16},{64,32},{80,48},{96,64},{112,80},{... | collective-permute-start | bytes 786440 | tf_op jit(solution)/shard_map/ppermute | solution.py:123
  40.4 7.9 %collective-permute-start.5 = (bf16[4,256,128]{1,2,0:T(8,128)(2,1)}, bf16[4,256,128]{1,2,0:T(8,128)(2,1)}, u32[]{:S(2)}, u32[]{:S(2)}) collective-permute-start(bf16[4,256,128]{1,2,0:T(8,128)(2,1)} %collective-permute-done.3), channel_id=1, source_target_pairs={{0,32},{16,48},{32,64},{48,80},{64,96},{80,112},{96,128},{112,144}... | collective-permute-start | bytes 786440 | tf_op jit(solution)/shard_map/ppermute | solution.py:119
  50.3 7.9 %collective-permute-start.6 = (bf16[4,256,128]{1,2,0:T(8,128)(2,1)}, bf16[4,256,128]{1,2,0:T(8,128)(2,1)}, u32[]{:S(2)}, u32[]{:S(2)}) collective-permute-start(bf16[4,256,128]{1,2,0:T(8,128)(2,1)} %collective-permute-done.5), channel_id=1, source_target_pairs={{0,32},{16,48},{32,64},{48,80},{64,96},{80,112},{96,128},{112,144}... | collective-permute-start | bytes 786440 | tf_op jit(solution)/shard_map/ppermute | solution.py:119
  60.1 1.9 %collective-permute-start.7 = (bf16[4,256,128]{1,2,0:T(8,128)(2,1)}, bf16[4,256,128]{1,2,0:T(8,128)(2,1)}, u32[]{:S(2)}, u32[]{:S(2)}) collective-permute-start(bf16[4,256,128]{1,2,0:T(8,128)(2,1)} %get-tuple-element.35), channel_id=1, source_target_pairs={{0,16},{16,0},{32,48},{48,32},{64,80},{80,64},{96,112},{112,96},{1... | collective-permute-start | bytes 786440 | tf_op jit(solution)/shard_map/ppermute | solution.py:129
  71.0 22.0 %all-to-all-start.1 = ((bf16[16,256,128]{2,1,0:T(8,128)(2,1)}), bf16[16,256,128]{2,1,0:T(8,128)(2,1)}, u32[]{:S(2)}, u32[]{:S(2)}) async-start(bf16[16,256,128]{2,1,0:T(8,128)(2,1)} %bitcast.100), calls=%async_computation.1 | async-start | bytes 2097152 | tf_op jit(solution)/shard_map/all_to_all | solution.py:176
  76.1 1.2 copy-start.1
  78.1 0.7 copy-start.3
  92.9 2.6 %copy-start.2 = (f32[512,1,512]{0,2,1:T(8,128)S(1)}, f32[512,1,512]{0,2,1:T(8,128)}, u32[]{:S(2)}) copy-start(f32[512,1,512]{0,2,1:T(8,128)} %get-tuple-element.58) | copy-start | bytes 3145732
  122.4 6.8 %copy-start.8 = (bf16[2,2048,320]{1,2,0:T(8,128)(2,1)S(1)}, bf16[2,2048,320]{1,2,0:T(8,128)(2,1)}, u32[]{:S(2)}) copy-start(bf16[2,2048,320]{1,2,0:T(8,128)(2,1)} %param.18) | copy-start | bytes 7864324
  127.9 1.4 copy-start.6
  135.7 33.4 %all-to-all-start.3 = ((bf16[16,32,2048]{2,1,0:T(8,128)(2,1)}), bf16[16,32,2048]{2,1,0:T(8,128)(2,1)S(1)}, u32[]{:S(2)}, u32[]{:S(2)}) async-start(bf16[16,32,2048]{2,1,0:T(8,128)(2,1)} %bitcast.101), calls=%async_computation.3 | async-start | bytes 4194304 | tf_op jit(solution)/shard_map/all_to_all | solution.py:96
Sparse Core Ops, SparseCore 0:
  12.1 66.6 all-gather.1

commit v19 on v16

--- a/solution.py
+++ b/solution.py
@@ -123,7 +123,7 @@
             behind = lax.ppermute(behind, "dp", backward)
             mine = jnp.where(mine_at == step, behind, mine)
             theirs = jnp.where(theirs_at == step, behind, theirs)
-        if step == 1:
+        if step == 3:
             ahead, behind, rider = lax.optimization_barrier((ahead, behind, rider))
         mine, theirs, ahead, behind = lax.optimization_barrier((mine, theirs, ahead, behind))
     swapped = lax.ppermute(theirs, "dp", [(i, i ^ 1) for i in range(group_count)])

time: 177 us -> 185 us (1.045)
  local copies, waits for them, and re-layouts: 17.7 us -> 22 us
  other arithmetic: 16.6 us -> 19.1 us
    all_to_all x1, waiting for transfers between devices: 9.4 us -> 14.7 us  [on_device(): incoming = lax.all_to_all(outgoing, 'tensor', 0, 0, tiled=True)]
    all_to_all x1, waiting for transfers between devices: 4.03 us -> 0.01 us  [gather_rows(): received = lax.all_to_all(copies, axis, 0, 0, tiled=True)]
    ppermute x3, starting transfers between devices: 10.7 us -> 7.63 us  [fetch_slot(): behind = lax.ppermute(behind, 'dp', backward)]
    all_to_all x1, starting transfers between devices: 4.53 us -> 6.93 us  [on_device(): incoming = lax.all_to_all(outgoing, 'tensor', 0, 0, tiled=True)]
    ppermute x4, starting transfers between devices: 0.01 us -> 2.29 us  [fetch_slot(): ahead = lax.ppermute(ahead, 'dp', onward)]
    ppermute x3, waiting for transfers between devices: 4.41 us -> 2.44 us  [fetch_slot(): behind = lax.ppermute(behind, 'dp', backward)]
  transfers between devices with their start and end apart: 12 -> 12, of which waited for: 7 -> 7; matrix products, arithmetic and copies ran while one was open for 18% -> 21% of each run, Pallas kernels for 0% -> 0%
where the time goes in v19:
time: 185 us; the launch traced here: 184 us
  waiting for transfers between devices  60.2 us (33%)
  starting transfers between devices  27.8 us (15%)
  local copies, waits for them, and re-layouts  22 us (12%)
  blocking collectives  20.6 us (11%)
  other arithmetic  19.1 us (10%)
  between operations  18.6 us (10%)
  matrix products  15.8 us (9%)
    all_to_all x1, waiting for transfers between devices, sum_scatter_rows(): received = lax.all_to_all(parts, axis, 0, 0, tiled=True)  29.7 us
    all_to_all x1, blocking collectives, gather_rows(): received = lax.all_to_all(copies, axis, 0, 0, tiled=True)  20.6 us
    all_to_all x1, waiting for transfers between devices, on_device(): incoming = lax.all_to_all(outgoing, 'tensor', 0, 0, tiled=True)  14.7 us
    ppermute x4, waiting for transfers between devices, fetch_slot(): ahead = lax.ppermute(ahead, 'dp', onward)  11.8 us
    ppermute x3, starting transfers between devices, fetch_slot(): behind = lax.ppermute(behind, 'dp', backward)  7.63 us
    all_to_all x1, starting transfers between devices, gather_rows(): received = lax.all_to_all(copies, axis, 0, 0, tiled=True)  7.17 us
    all_to_all x1, starting transfers between devices, on_device(): incoming = lax.all_to_all(outgoing, 'tensor', 0, 0, tiled=True)  6.93 us
    unnamed x28, local copies, waits for them, and re-layouts  6.14 us
  transfers between devices with their start and end apart: 12, of which 7 were waited for; matrix products, arithmetic and copies ran while one was open for 21% of the time, Pallas kernels for 0%

profile of v19, /device:TPU:0, one launch (start us, length us, event | category | flops | bytes accessed | tf_op | source)
XLA Modules:
  0.0 184.2 jit_solution(1370140939018399953)
XLA Ops:
  8.5 4.1 %collective-permute-start = (bf16[4,256,128]{1,2,0:T(8,128)(2,1)}, bf16[4,256,128]{1,2,0:T(8,128)(2,1)}, u32[]{:S(2)}, u32[]{:S(2)}) collective-permute-start(bf16[4,256,128]{1,2,0:T(8,128)(2,1)} %bitcast.4), channel_id=1, source_target_pairs={{0,224},{16,240},{32,0},{48,16},{64,32},{80,48},{96,64},{112,80},{... | collective-permute-start | bytes 786440 | tf_op jit(solution)/shard_map/ppermute | solution.py:123
  12.6 2.5 %broadcast_in_dim.21 = bf16[16,32,2048]{2,1,0:T(8,128)(2,1)} broadcast(bf16[32,2048]{1,0:T(8,128)(2,1)} %param.10), dimensions={1,2} | broadcast | bytes 2228224 | tf_op jit(solution)/shard_map/broadcast_in_dim | solution.py:88
  15.1 7.2 %all-to-all-start = ((bf16[16,32,2048]{2,1,0:T(8,128)(2,1)}), bf16[16,32,2048]{2,1,0:T(8,128)(2,1)S(1)}, u32[]{:S(2)}, u32[]{:S(2)}) async-start(bf16[16,32,2048]{2,1,0:T(8,128)(2,1)} %broadcast_in_dim.21), calls=%async_computation | async-start | bytes 4194304 | tf_op jit(solution)/shard_map/all_to_all | solution.py:89
  28.8 2.0 %select_select_fusion.4 = (bf16[4,256,128]{1,2,0:T(8,128)(2,1)}, bf16[4,256,128]{1,2,0:T(8,128)(2,1)}) fusion(bf16[4,256,128]{1,2,0:T(8,128)(2,1)} %collective-permute-done, bf16[4,256,128]{1,2,0:T(8,128)(2,1)} %collective-permute-done.1, pred[]{:T(512)S(6)} %eq.70, pred[]{:T(512)S(6)} %eq.69, bf16[4,256,2,64]{1,3,2,0:T(8,128)(2,1)} %copy.21, pred[]{:T(512)S(6)} %eq.68, ...), kind=kLoop, calls=%fused_computation.53 | loop fusion | flops 524288 | bytes 1310724 | tf_op jit(solution)/shard_map/jit(_where)/select_n | solution.py:125
  30.8 3.2 %collective-permute-start.2 = (bf16[4,256,128]{1,2,0:T(8,128)(2,1)}, bf16[4,256,128]{1,2,0:T(8,128)(2,1)}, u32[]{:S(2)}, u32[]{:S(2)}) collective-permute-start(bf16[4,256,128]{1,2,0:T(8,128)(2,1)} %collective-permute-done), channel_id=1, source_target_pairs={{0,224},{16,240},{32,0},{48,16},{64,32},{80,48},{96,64},{112,80},{... | collective-permute-start | bytes 786440 | tf_op jit(solution)/shard_map/ppermute | solution.py:123
  34.0 2.6 %constant_dynamic-slice_fusion = (bf16[2048,64]{1,0:T(8,128)(2,1)}, bf16[2048,64]{1,0:T(8,128)(2,1)}) fusion(bf16[2048,256]{1,0:T(8,128)(2,1)} %param.16, s32[]{:T(128)S(6)} %select_n.187, bf16[2048,256]{1,0:T(8,128)(2,1)} %param.15), kind=kLoop, calls=%fused_computation.91 | loop fusion | bytes 1048580 | tf_op jit(solution)/shard_map/dynamic_slice | solution.py:162
  36.6 2.4 %collective-permute-done.2 = bf16[4,256,128]{1,2,0:T(8,128)(2,1)} collective-permute-done((bf16[4,256,128]{1,2,0:T(8,128)(2,1)}, bf16[4,256,128]{1,2,0:T(8,128)(2,1)}, u32[]{:S(2)}, u32[]{:S(2)}) %collective-permute-start.2) | collective-permute-done | bytes 262176 | tf_op jit(solution)/shard_map/ppermute | solution.py:123
  39.0 3.4 %collective-permute-done.3 = bf16[4,256,128]{1,2,0:T(8,128)(2,1)} collective-permute-done((bf16[4,256,128]{1,2,0:T(8,128)(2,1)}, bf16[4,256,128]{1,2,0:T(8,128)(2,1)}, u32[]{:S(2)}, u32[]{:S(2)}) %collective-permute-start.3) | collective-permute-done | bytes 262176 | tf_op jit(solution)/shard_map/ppermute | solution.py:119
  42.5 2.1 %select_select_fusion.2 = (bf16[4,256,128]{1,2,0:T(8,128)(2,1)}, bf16[4,256,128]{1,2,0:T(8,128)(2,1)}) fusion(bf16[4,256,128]{1,2,0:T(8,128)(2,1)} %collective-permute-done.2, bf16[4,256,128]{1,2,0:T(8,128)(2,1)} %collective-permute-done.3, bf16[4,256,128]{1,2,0:T(8,128)(2,1)} %get-tuple-element.23, pred[]{:T(512)S(6)} %eq.73, pred[]{:T(512)S(6)} %eq.72, ...), kind=kLoop, calls=%fused_computation.51 | loop fusion | flops 524288 | bytes 1572868 | tf_op jit(solution)/shard_map/jit(_where)/select_n | solution.py:125
  46.6 2.0 %copy.22 = bf16[2048,64]{1,0:T(8,128)(2,1)} copy(bf16[2048,64]{0,1:T(8,128)(2,1)} %param.14) | data formatting | bytes 524288 | tf_op args[4]
  48.7 3.0 %pad_maximum_fusion = bf16[2048,192]{1,0:T(8,128)(2,1)} fusion(bf16[2048,64]{1,0:T(8,128)(2,1)} %get-tuple-element.59, bf16[2048,64]{1,0:T(8,128)(2,1)} %get-tuple-element.60, bf16[2048,64]{1,0:T(8,128)(2,1)} %copy.22), kind=kLoop, calls=%fused_computation.39 | loop fusion | flops 2359296 | bytes 1572864 | tf_op jit(solution)/shard_map/concatenate | solution.py:163
  52.7 1.9 %select_select_fusion = (bf16[4,256,128]{1,2,0:T(8,128)(2,1)}, bf16[4,256,128]{1,2,0:T(8,128)(2,1)}) fusion(bf16[4,256,128]{1,2,0:T(8,128)(2,1)} %collective-permute-done.4, bf16[4,256,128]{1,2,0:T(8,128)(2,1)} %collective-permute-done.5, bf16[4,256,128]{1,2,0:T(8,128)(2,1)S(1)} %copy-done.3, pred[]{:T(512)S(6)} %eq.76, pred[]{:T(512)S(6)} %eq.75, ...), kind=kLoop, calls=%fused_computation.49 | loop fusion | flops 524288 | bytes 1572868 | tf_op jit(solution)/shard_map/jit(_where)/select_n | solution.py:125
  55.2 7.3 %collective-permute-done.6 = bf16[4,256,128]{1,2,0:T(8,128)(2,1)} collective-permute-done((bf16[4,256,128]{1,2,0:T(8,128)(2,1)}, bf16[4,256,128]{1,2,0:T(8,128)(2,1)}, u32[]{:S(2)}, u32[]{:S(2)}) %collective-permute-start.6) | collective-permute-done | bytes 262176 | tf_op jit(solution)/shard_map/ppermute | solution.py:119
  62.5 2.0 %broadcast_select_fusion = (bf16[4,256,128]{1,2,0:T(8,128)(2,1)}, bf16[4,256,128]{1,2,0:T(8,128)(2,1)}) fusion(bf16[4,256,128]{1,2,0:T(8,128)(2,1)} %collective-permute-done.6, bf16[4,256,128]{1,2,0:T(8,128)(2,1)} %get-tuple-element.31, pred[]{:T(512)S(6)} %eq.77, bf16[4,256,128]{1,2,0:T(8,128)(2,1)} %get-tuple-element.30, pred[]{:T(512)S(6)} %eq.64), kind=kLoop, calls=%fused_computation.55 | loop fusion | flops 262144 | bytes 1310722 | tf_op jit(solution)/shard_map/jit(_where)/select_n | solution.py:121
  68.2 1.8 copy.23
  70.0 2.2 %broadcast_in_dim.22 = bf16[4,4,256,128]{3,2,1,0:T(8,128)(2,1)} broadcast(bf16[4,256,128]{2,1,0:T(8,128)(2,1)} %copy.23), dimensions={0,2,3} | broadcast | bytes 1310720 | tf_op jit(solution)/shard_map/broadcast_in_dim | solution.py:173
  72.1 6.9 %all-to-all-start.1 = ((bf16[16,256,128]{2,1,0:T(8,128)(2,1)}), bf16[16,256,128]{2,1,0:T(8,128)(2,1)}, u32[]{:S(2)}, u32[]{:S(2)}) async-start(bf16[16,256,128]{2,1,0:T(8,128)(2,1)} %bitcast.106), calls=%async_computation.1 | async-start | bytes 2097152 | tf_op jit(solution)/shard_map/all_to_all | solution.py:176
  86.7 14.7 %all-to-all-done.1 = bf16[16,256,128]{2,1,0:T(8,128)(2,1)} async-done(((bf16[16,256,128]{2,1,0:T(8,128)(2,1)}), bf16[16,256,128]{2,1,0:T(8,128)(2,1)}, u32[]{:S(2)}, u32[]{:S(2)}) %all-to-all-start.1) | async-done | bytes 1048608 | tf_op jit(solution)/shard_map/all_to_all | solution.py:176
  101.5 2.1 %slice_bitcast_fusion.1 = (bf16[4096,1,64]{2,0,1:T(8,128)(2,1)S(1)}, bf16[4096,1,64]{2,0,1:T(8,128)(2,1)S(1)}) fusion(bf16[4096,128]{1,0:T(8,128)(2,1)} %bitcast.7), kind=kLoop, calls=%fused_computation.38 | loop fusion | bytes 2097152 | tf_op jit(solution)/shard_map/reshape;broadcast_in_dim;reshape | solution.py:180
  108.0 20.6 %all_to_all.20 = bf16[16,1,64,512]{3,2,1,0:T(8,128)(2,1)} all-to-all(bf16[16,1,64,512]{3,2,1,0:T(8,128)(2,1)S(1)} %broadcast_in_dim.26), channel_id=1, replica_groups=mesh['dp'=16,'tensor'=16] {'tensor'}, dimensions={0} | all-to-all | bytes 2097152 | tf_op jit(solution)/shard_map/all_to_all | solution.py:89
  128.6 5.4 %fusion.6 = (f32[512]{0:T(512)S(1)}, bf16[512,2048]{1,0:T(8,128)(2,1)S(1)}) fusion(bf16[1024,512]{1,0:T(8,128)(2,1)} %bitcast.108, bf16[1024,2048]{1,0:T(8,128)(2,1)} %all-gather.2.cloned.1.call-done, bf16[16,32,2048]{2,1,0:T(8,128)(2,1)S(1)} %all-to-all-done), kind=kOutput, calls=%fused_computation.9 | convolution fusion | flops 2153774592 | bytes 9439232 | tf_op jit(solution)/shard_map/dot_general | solution.py:224
  136.5 5.5 %convolution_convert_fusion = bf16[512,2048]{1,0:T(8,128)(2,1)} fusion(bf16[320,2048]{1,0:T(8,128)(2,1)S(1)} %copy-done, bf16[2,2048,320]{1,2,0:T(8,128)(2,1)} %param.18, bf16[512,2048]{1,0:T(8,128)(2,1)} %copy-done.9, f32[512]{0:T(512)S(1)} %add_rsqrt_fusion.1, f32[512,320]{0,1:T(8,128)S(1)} %fusion.13), kind=kOutput, calls=%fused_computation.18 | convolution fusion | flops 1347354624 | bytes 7473152 | tf_op jit(solution)/shard_map/dot_general | solution.py:231
  142.0 3.7 %all-to-all-start.3 = ((bf16[16,32,2048]{2,1,0:T(8,128)(2,1)}), bf16[16,32,2048]{2,1,0:T(8,128)(2,1)S(1)}, u32[]{:S(2)}, u32[]{:S(2)}) async-start(bf16[16,32,2048]{2,1,0:T(8,128)(2,1)} %bitcast.107), calls=%async_computation.3 | async-start | bytes 4194304 | tf_op jit(solution)/shard_map/all_to_all | solution.py:96
  145.7 29.7 %all-to-all-done.3 = bf16[16,32,2048]{2,1,0:T(8,128)(2,1)S(1)} async-done(((bf16[16,32,2048]{2,1,0:T(8,128)(2,1)}), bf16[16,32,2048]{2,1,0:T(8,128)(2,1)S(1)}, u32[]{:S(2)}, u32[]{:S(2)}) %all-to-all-start.3) | async-done | bytes 2097184 | tf_op jit(solution)/shard_map/all_to_all | solution.py:96
  (71 shorter events, 27.3 us)
Async XLA Ops:
  6.5 129.9 %copy-start = (bf16[320,2048]{1,0:T(8,128)(2,1)S(1)}, bf16[320,2048]{1,0:T(8,128)(2,1)}, u32[]{:S(2)}) copy-start(bf16[320,2048]{1,0:T(8,128)(2,1)} %param.19) | copy-start | bytes 3932164
  8.5 20.3 %collective-permute-start = (bf16[4,256,128]{1,2,0:T(8,128)(2,1)}, bf16[4,256,128]{1,2,0:T(8,128)(2,1)}, u32[]{:S(2)}, u32[]{:S(2)}) collective-permute-start(bf16[4,256,128]{1,2,0:T(8,128)(2,1)} %bitcast.4), channel_id=1, source_target_pairs={{0,224},{16,240},{32,0},{48,16},{64,32},{80,48},{96,64},{112,80},{... | collective-permute-start | bytes 786440 | tf_op jit(solution)/shard_map/ppermute | solution.py:123
  12.6 16.2 %collective-permute-start.1 = (bf16[4,256,128]{1,2,0:T(8,128)(2,1)}, bf16[4,256,128]{1,2,0:T(8,128)(2,1)}, u32[]{:S(2)}, u32[]{:S(2)}) collective-permute-start(bf16[4,256,128]{1,2,0:T(8,128)(2,1)} %bitcast.4), channel_id=1, source_target_pairs={{0,32},{16,48},{32,64},{48,80},{64,96},{80,112},{96,128},{112,144}... | collective-permute-start | bytes 786440 | tf_op jit(solution)/shard_map/ppermute | solution.py:119
  15.1 7.9 %copy-start.10 = (s32[16]{0:T(128)S(1)}, s32[16]{0:T(128)}, u32[]{:S(2)}) copy-start(s32[16]{0:T(128)} %param.12) | copy-start | bytes 196
  15.1 13.5 %copy-start.12 = (s32[1,8]{1,0:T(1,128)S(1)}, s32[1,8]{1,0:T(1,128)}, u32[]{:S(2)}) copy-start(s32[1,8]{1,0:T(1,128)} %param.11) | copy-start | bytes 100
  15.1 54.9 %all-to-all-start = ((bf16[16,32,2048]{2,1,0:T(8,128)(2,1)}), bf16[16,32,2048]{2,1,0:T(8,128)(2,1)S(1)}, u32[]{:S(2)}, u32[]{:S(2)}) async-start(bf16[16,32,2048]{2,1,0:T(8,128)(2,1)} %broadcast_in_dim.21), calls=%async_computation | async-start | bytes 4194304 | tf_op jit(solution)/shard_map/all_to_all | solution.py:89
  22.3 106.4 %all-gather.2.cloned.1.call-start = ((), (), s32[]{:S(2)}) async-start(), calls=%async_computation.4 | async-start | bytes 4456448 | tf_op jit(solution)/shard_map/all_gather | solution.py:170
  30.8 8.3 %collective-permute-start.2 = (bf16[4,256,128]{1,2,0:T(8,128)(2,1)}, bf16[4,256,128]{1,2,0:T(8,128)(2,1)}, u32[]{:S(2)}, u32[]{:S(2)}) collective-permute-start(bf16[4,256,128]{1,2,0:T(8,128)(2,1)} %collective-permute-done), channel_id=1, source_target_pairs={{0,224},{16,240},{32,0},{48,16},{64,32},{80,48},{96,64},{112,80},{... | collective-permute-start | bytes 786440 | tf_op jit(solution)/shard_map/ppermute | solution.py:123
  34.0 8.5 %collective-permute-start.3 = (bf16[4,256,128]{1,2,0:T(8,128)(2,1)}, bf16[4,256,128]{1,2,0:T(8,128)(2,1)}, u32[]{:S(2)}, u32[]{:S(2)}) collective-permute-start(bf16[4,256,128]{1,2,0:T(8,128)(2,1)} %collective-permute-done.1), channel_id=1, source_target_pairs={{0,32},{16,48},{32,64},{48,80},{64,96},{80,112},{96,128},{112,144}... | collective-permute-start | bytes 786440 | tf_op jit(solution)/shard_map/ppermute | solution.py:119
  44.5 7.1 %collective-permute-start.4 = (bf16[4,256,128]{1,2,0:T(8,128)(2,1)}, bf16[4,256,128]{1,2,0:T(8,128)(2,1)}, u32[]{:S(2)}, u32[]{:S(2)}) collective-permute-start(bf16[4,256,128]{1,2,0:T(8,128)(2,1)} %collective-permute-done.2), channel_id=1, source_target_pairs={{0,224},{16,240},{32,0},{48,16},{64,32},{80,48},{96,64},{112,80},{... | collective-permute-start | bytes 786440 | tf_op jit(solution)/shard_map/ppermute | solution.py:123
  44.8 7.9 %collective-permute-start.5 = (bf16[4,256,128]{1,2,0:T(8,128)(2,1)}, bf16[4,256,128]{1,2,0:T(8,128)(2,1)}, u32[]{:S(2)}, u32[]{:S(2)}) collective-permute-start(bf16[4,256,128]{1,2,0:T(8,128)(2,1)} %collective-permute-done.3), channel_id=1, source_target_pairs={{0,32},{16,48},{32,64},{48,80},{64,96},{80,112},{96,128},{112,144}... | collective-permute-start | bytes 786440 | tf_op jit(solution)/shard_map/ppermute | solution.py:119
  48.6 4.1 %copy-start.3 = (bf16[4,256,128]{1,2,0:T(8,128)(2,1)S(1)}, bf16[4,256,128]{1,2,0:T(8,128)(2,1)}, u32[]{:S(2)}) copy-start(bf16[4,256,128]{1,2,0:T(8,128)(2,1)} %get-tuple-element.27) | copy-start | bytes 786436
  48.7 4.1 %copy-start.4 = (bf16[4,256,128]{1,2,0:T(8,128)(2,1)S(1)}, bf16[4,256,128]{1,2,0:T(8,128)(2,1)}, u32[]{:S(2)}) copy-start(bf16[4,256,128]{1,2,0:T(8,128)(2,1)} %get-tuple-element.26) | copy-start | bytes 786436
  54.6 7.9 %collective-permute-start.6 = (bf16[4,256,128]{1,2,0:T(8,128)(2,1)}, bf16[4,256,128]{1,2,0:T(8,128)(2,1)}, u32[]{:S(2)}, u32[]{:S(2)}) collective-permute-start(bf16[4,256,128]{1,2,0:T(8,128)(2,1)} %collective-permute-done.5), channel_id=1, source_target_pairs={{0,32},{16,48},{32,64},{48,80},{64,96},{80,112},{96,128},{112,144}... | collective-permute-start | bytes 786440 | tf_op jit(solution)/shard_map/ppermute | solution.py:119
  64.5 1.9 %collective-permute-start.7 = (bf16[4,256,128]{1,2,0:T(8,128)(2,1)}, bf16[4,256,128]{1,2,0:T(8,128)(2,1)}, u32[]{:S(2)}, u32[]{:S(2)}) collective-permute-start(bf16[4,256,128]{1,2,0:T(8,128)(2,1)} %get-tuple-element.33), channel_id=1, source_target_pairs={{0,16},{16,0},{32,48},{48,32},{64,80},{80,64},{96,112},{112,96},{1... | collective-permute-start | bytes 786440 | tf_op jit(solution)/shard_map/ppermute | solution.py:129
  72.1 29.3 %all-to-all-start.1 = ((bf16[16,256,128]{2,1,0:T(8,128)(2,1)}), bf16[16,256,128]{2,1,0:T(8,128)(2,1)}, u32[]{:S(2)}, u32[]{:S(2)}) async-start(bf16[16,256,128]{2,1,0:T(8,128)(2,1)} %bitcast.106), calls=%async_computation.1 | async-start | bytes 2097152 | tf_op jit(solution)/shard_map/all_to_all | solution.py:176
  79.6 1.2 copy-start.1
  101.5 2.1 %copy-start.5 = (pred[512,512]{0,1:T(32,128)(4,1)S(1)}, pred[512,512]{0,1:T(32,128)(4,1)}, u32[]{:S(2)}) copy-start(pred[512,512]{0,1:T(32,128)(4,1)} %fusion.39) | copy-start | bytes 786436
  101.5 2.1 %copy-start.6 = (bf16[512,1,64]{2,0,1:T(8,128)(2,1)S(1)}, bf16[512,1,64]{2,0,1:T(8,128)(2,1)}, u32[]{:S(2)}) copy-start(bf16[512,1,64]{2,0,1:T(8,128)(2,1)} %copy.25) | copy-start | bytes 196612
  101.5 2.1 %copy-start.7 = (bf16[512,1,32]{0,2,1:T(8,128)(2,1)S(1)}, bf16[512,1,32]{0,2,1:T(8,128)(2,1)}, u32[]{:S(2)}) copy-start(bf16[512,1,32]{0,2,1:T(8,128)(2,1)} %get-tuple-element.47) | copy-start | bytes 98308
  101.5 2.1 %copy-start.8 = (bf16[512,1,32]{0,2,1:T(8,128)(2,1)S(1)}, bf16[512,1,32]{0,2,1:T(8,128)(2,1)}, u32[]{:S(2)}) copy-start(bf16[512,1,32]{0,2,1:T(8,128)(2,1)} %get-tuple-element.48) | copy-start | bytes 98308
  128.6 6.8 %copy-start.11 = (bf16[2,2048,320]{1,2,0:T(8,128)(2,1)S(1)}, bf16[2,2048,320]{1,2,0:T(8,128)(2,1)}, u32[]{:S(2)}) copy-start(bf16[2,2048,320]{1,2,0:T(8,128)(2,1)} %param.18) | copy-start | bytes 7864324
  134.1 1.3 copy-start.9
  142.0 33.4 %all-to-all-start.3 = ((bf16[16,32,2048]{2,1,0:T(8,128)(2,1)}), bf16[16,32,2048]{2,1,0:T(8,128)(2,1)S(1)}, u32[]{:S(2)}, u32[]{:S(2)}) async-start(bf16[16,32,2048]{2,1,0:T(8,128)(2,1)} %bitcast.107), calls=%async_computation.3 | async-start | bytes 4194304 | tf_op jit(solution)/shard_map/all_to_all | solution.py:96
  (1 other events, 0.8 us)
Sparse Core Ops, SparseCore 0:
  25.5 70.7 all-gather.1

commit v20 on v16

--- a/solution.py
+++ b/solution.py
@@ -224,8 +224,9 @@
     attn_sum = jnp.dot(every_head, out_full, preferred_element_type=jnp.float32)
     middle = (group_rows.astype(jnp.float32) + attn_sum).astype(jnp.bfloat16)
     segment = norm_rows(middle)
-    gate_value = jnp.dot(segment, gate_up_weight[0], preferred_element_type=jnp.float32)
-    upward = jnp.dot(segment, gate_up_weight[1], preferred_element_type=jnp.float32)
+    gate_value, upward = jnp.einsum(
+        "td,kdf->ktf", segment, gate_up_weight, preferred_element_type=jnp.float32
+    )
     hidden = (jax.nn.silu(gate_value) * upward).astype(jnp.bfloat16)
     ffn_sum = sum_scatter_rows(
         jnp.dot(hidden, down_weight, preferred_element_type=jnp.float32).astype(jnp.bfloat16),

time: 177 us -> 176 us (level)
  waiting for transfers between devices: 59.5 us -> 65.3 us
  local copies, waits for them, and re-layouts: 17.7 us -> 12.1 us
    all_to_all x1, waiting for transfers between devices: 4.03 us -> 12 us  [gather_rows(): received = lax.all_to_all(copies, axis, 0, 0, tiled=True)]
    select_n x3, other arithmetic: 5.01 us -> 2.14 us  [fetch_slot(): theirs = jnp.where(theirs_at == step, behind, theirs)]
    dot_general x1, matrix products: 5.51 us -> 2.68 us  [on_device(): jnp.dot(hidden, down_weight, preferred_element_type=jnp.float32)]
    another operation x2, local copies, waits for them, and re-layouts: 2.49 us -> 0.13 us  [on_device(): jnp.repeat(projected[:, query_width + kv_width:].reshape(group_tokens, lo...]
    unnamed x28 -> x20, local copies, waits for them, and re-layouts: 4.43 us -> 3.68 us
  transfers between devices with their start and end apart: 12 -> 12, of which waited for: 7 -> 7; matrix products, arithmetic and copies ran while one was open for 18% -> 16% of each run, Pallas kernels for 0% -> 0%
where the time goes in v20:
time: 176 us; the launch traced here: 175 us
  waiting for transfers between devices  65.3 us (37%)
  starting transfers between devices  27.1 us (15%)
  blocking collectives  20.6 us (12%)
  between operations  18.9 us (11%)
  other arithmetic  17.3 us (10%)
  matrix products  14.1 us (8%)
  local copies, waits for them, and re-layouts  12.1 us (7%)
    all_to_all x1, waiting for transfers between devices, sum_scatter_rows(): received = lax.all_to_all(parts, axis, 0, 0, tiled=True)  27.9 us
    all_to_all x1, blocking collectives, gather_rows(): received = lax.all_to_all(copies, axis, 0, 0, tiled=True)  20.6 us
    all_to_all x1, waiting for transfers between devices, gather_rows(): received = lax.all_to_all(copies, axis, 0, 0, tiled=True)  12 us
    ppermute x4, waiting for transfers between devices, fetch_slot(): ahead = lax.ppermute(ahead, 'dp', onward)  11.2 us
    ppermute x3, starting transfers between devices, fetch_slot(): behind = lax.ppermute(behind, 'dp', backward)  10.8 us
    all_to_all x1, waiting for transfers between devices, on_device(): incoming = lax.all_to_all(outgoing, 'tensor', 0, 0, tiled=True)  8.46 us
    all_to_all x1, starting transfers between devices, gather_rows(): received = lax.all_to_all(copies, axis, 0, 0, tiled=True)  7.22 us
    dot_general x1, matrix products, on_device(): attn_sum = jnp.dot(every_head, out_full, preferred_element_type=jnp.float32)  5.95 us
  transfers between devices with their start and end apart: 12, of which 7 were waited for; matrix products, arithmetic and copies ran while one was open for 16% of the time, Pallas kernels for 0%

profile of v20, /device:TPU:0, one launch (start us, length us, event | category | flops | bytes accessed | tf_op | source)
XLA Modules:
  0.0 175.3 jit_solution(7932820742916702769)
XLA Ops:
  7.8 4.2 %collective-permute-start = (bf16[4,256,128]{1,2,0:T(8,128)(2,1)S(1)}, bf16[4,256,128]{1,2,0:T(8,128)(2,1)}, u32[]{:S(2)}, u32[]{:S(2)}) collective-permute-start(bf16[4,256,128]{1,2,0:T(8,128)(2,1)S(1)} %bitcast.116), channel_id=1, source_target_pairs={{0,224},{16,240},{32,0},{48,16},{64,32},{80,48},{96,64},{112,80},{... | collective-permute-start | bytes 786440 | tf_op jit(solution)/shard_map/ppermute | solution.py:123
  12.1 2.3 %constant_dynamic-slice_fusion = (bf16[2048,64]{1,0:T(8,128)(2,1)S(1)}, bf16[2048,64]{1,0:T(8,128)(2,1)}) fusion(bf16[2048,256]{1,0:T(8,128)(2,1)} %param.16, s32[]{:T(128)S(6)} %select_n.173, bf16[2048,256]{1,0:T(8,128)(2,1)} %param.15), kind=kLoop, calls=%fused_computation.86 | loop fusion | bytes 1048580 | tf_op jit(solution)/shard_map/dynamic_slice | solution.py:162
  20.2 2.0 %copy.22 = bf16[2048,64]{1,0:T(8,128)(2,1)} copy(bf16[2048,64]{0,1:T(8,128)(2,1)} %param.14) | data formatting | bytes 524288 | tf_op args[4]
  22.2 2.8 %pad_maximum_fusion = bf16[2048,192]{1,0:T(8,128)(2,1)} fusion(bf16[2048,64]{1,0:T(8,128)(2,1)S(1)} %get-tuple-element.61, bf16[2048,64]{1,0:T(8,128)(2,1)} %get-tuple-element.62, bf16[2048,64]{1,0:T(8,128)(2,1)} %copy.22), kind=kLoop, calls=%fused_computation.35 | loop fusion | flops 2359296 | bytes 1572864 | tf_op jit(solution)/shard_map/concatenate | solution.py:163
  26.1 3.3 %collective-permute-start.2 = (bf16[4,256,128]{1,2,0:T(8,128)(2,1)}, bf16[4,256,128]{1,2,0:T(8,128)(2,1)S(1)}, u32[]{:S(2)}, u32[]{:S(2)}) collective-permute-start(bf16[4,256,128]{1,2,0:T(8,128)(2,1)} %collective-permute-done), channel_id=1, source_target_pairs={{0,224},{16,240},{32,0},{48,16},{64,32},{80,48},{96,64},{112,80},{... | collective-permute-start | bytes 786440 | tf_op jit(solution)/shard_map/ppermute | solution.py:123
  31.1 7.2 %all-to-all-start = ((bf16[16,32,2048]{2,1,0:T(8,128)(2,1)}), bf16[16,32,2048]{2,1,0:T(8,128)(2,1)}, u32[]{:S(2)}, u32[]{:S(2)}) async-start(bf16[16,32,2048]{2,1,0:T(8,128)(2,1)} %broadcast_in_dim.21), calls=%async_computation | async-start | bytes 4194304 | tf_op jit(solution)/shard_map/all_to_all | solution.py:89
  39.5 3.3 %collective-permute-start.4 = (bf16[4,256,128]{1,2,0:T(8,128)(2,1)S(1)}, bf16[4,256,128]{1,2,0:T(8,128)(2,1)S(1)}, u32[]{:S(2)}, u32[]{:S(2)}) collective-permute-start(bf16[4,256,128]{1,2,0:T(8,128)(2,1)S(1)} %collective-permute-done.2), channel_id=1, source_target_pairs={{0,224},{16,240},{32,0},{48,16},{64,32},{80,48},{96,64},{112,80},{... | collective-permute-start | bytes 786440 | tf_op jit(solution)/shard_map/ppermute | solution.py:123
  42.9 4.1 %collective-permute-done.4 = bf16[4,256,128]{1,2,0:T(8,128)(2,1)S(1)} collective-permute-done((bf16[4,256,128]{1,2,0:T(8,128)(2,1)S(1)}, bf16[4,256,128]{1,2,0:T(8,128)(2,1)S(1)}, u32[]{:S(2)}, u32[]{:S(2)}) %collective-permute-start.4) | collective-permute-done | bytes 262176 | tf_op jit(solution)/shard_map/ppermute | solution.py:123
  47.0 3.6 %collective-permute-done.5 = bf16[4,256,128]{1,2,0:T(8,128)(2,1)S(1)} collective-permute-done((bf16[4,256,128]{1,2,0:T(8,128)(2,1)}, bf16[4,256,128]{1,2,0:T(8,128)(2,1)S(1)}, u32[]{:S(2)}, u32[]{:S(2)}) %collective-permute-start.5) | collective-permute-done | bytes 262176 | tf_op jit(solution)/shard_map/ppermute | solution.py:119
  50.9 7.6 %collective-permute-done.6 = bf16[4,256,128]{1,2,0:T(8,128)(2,1)} collective-permute-done((bf16[4,256,128]{1,2,0:T(8,128)(2,1)S(1)}, bf16[4,256,128]{1,2,0:T(8,128)(2,1)}, u32[]{:S(2)}, u32[]{:S(2)}) %collective-permute-start.6) | collective-permute-done | bytes 262176 | tf_op jit(solution)/shard_map/ppermute | solution.py:119
  58.5 1.7 broadcast_select_fusion
  60.4 1.6 collective-permute-done.7
  62.2 12.0 %all-to-all-done = bf16[16,32,2048]{2,1,0:T(8,128)(2,1)} async-done(((bf16[16,32,2048]{2,1,0:T(8,128)(2,1)}), bf16[16,32,2048]{2,1,0:T(8,128)(2,1)}, u32[]{:S(2)}, u32[]{:S(2)}) %all-to-all-start) | async-done | bytes 2097184 | tf_op jit(solution)/shard_map/all_to_all | solution.py:89
  75.4 4.5 %all-to-all-start.1 = ((bf16[16,256,128]{2,1,0:T(8,128)(2,1)}), bf16[16,256,128]{2,1,0:T(8,128)(2,1)}, u32[]{:S(2)}, u32[]{:S(2)}) async-start(bf16[16,256,128]{2,1,0:T(8,128)(2,1)} %bitcast.114), calls=%async_computation.1 | async-start | bytes 2097152 | tf_op jit(solution)/shard_map/all_to_all | solution.py:176
  79.9 2.1 %fusion.8 = f32[16,32]{1,0:T(8,128)S(1)} fusion(bf16[16,32,2048]{2,1,0:T(8,128)(2,1)} %all-to-all-done), kind=kLoop, calls=%fused_computation.14 | loop fusion | flops 3145216 | bytes 2099200 | tf_op jit(solution)/shard_map/reduce_sum | solution.py:49
  82.1 2.1 %fusion.9 = bf16[512,2048]{1,0:T(8,128)(2,1)S(1)} fusion(bf16[16,32,2048]{2,1,0:T(8,128)(2,1)} %all-to-all-done, f32[512]{0:T(512)S(1)} %rsqrt.20), kind=kLoop, calls=%fused_computation.15 | loop fusion | flops 3145728 | bytes 4196352 | tf_op jit(solution)/shard_map/convert_element_type | solution.py:49
  86.3 8.5 %all-to-all-done.1 = bf16[16,256,128]{2,1,0:T(8,128)(2,1)} async-done(((bf16[16,256,128]{2,1,0:T(8,128)(2,1)}), bf16[16,256,128]{2,1,0:T(8,128)(2,1)}, u32[]{:S(2)}, u32[]{:S(2)}) %all-to-all-start.1) | async-done | bytes 1048608 | tf_op jit(solution)/shard_map/all_to_all | solution.py:176
  94.8 2.0 %slice_bitcast_fusion.1 = (bf16[4096,1,64]{2,0,1:T(8,128)(2,1)S(1)}, bf16[4096,1,64]{2,0,1:T(8,128)(2,1)S(1)}) fusion(bf16[4096,128]{1,0:T(8,128)(2,1)} %bitcast.7), kind=kLoop, calls=%fused_computation.34 | loop fusion | bytes 2097152 | tf_op jit(solution)/shard_map/reshape;broadcast_in_dim;reshape | solution.py:180
  101.2 20.6 %all_to_all.20 = bf16[16,1,64,512]{3,2,1,0:T(8,128)(2,1)} all-to-all(bf16[16,1,64,512]{3,2,1,0:T(8,128)(2,1)S(1)} %broadcast_in_dim.26), channel_id=1, replica_groups=mesh['dp'=16,'tensor'=16] {'tensor'}, dimensions={0} | all-to-all | bytes 2097152 | tf_op jit(solution)/shard_map/all_to_all | solution.py:89
  121.8 6.0 %fusion.6 = (f32[512]{0:T(512)S(1)}, bf16[512,2048]{1,0:T(8,128)(2,1)S(1)}) fusion(bf16[1024,512]{1,0:T(8,128)(2,1)} %bitcast.118, bf16[1024,2048]{1,0:T(8,128)(2,1)} %all-gather.2.cloned.1.call-done, bf16[16,32,2048]{2,1,0:T(8,128)(2,1)} %all-to-all-done), kind=kOutput, calls=%fused_computation.9 | convolution fusion | flops 2153774592 | bytes 9439232 | tf_op jit(solution)/shard_map/dot_general | solution.py:224
  129.9 2.7 %convolution_convert_fusion = bf16[512,2048]{1,0:T(8,128)(2,1)} fusion(bf16[320,2048]{1,0:T(8,128)(2,1)S(1)} %copy-done.7, f32[2,512,320]{1,2,0:T(8,128)S(1)} %fusion.15), kind=kOutput, calls=%fused_computation.18 | convolution fusion | flops 673120256 | bytes 4718592 | tf_op jit(solution)/shard_map/dot_general | solution.py:232
  132.6 4.4 %all-to-all-start.3 = ((bf16[16,32,2048]{2,1,0:T(8,128)(2,1)}), bf16[16,32,2048]{2,1,0:T(8,128)(2,1)}, u32[]{:S(2)}, u32[]{:S(2)}) async-start(bf16[16,32,2048]{2,1,0:T(8,128)(2,1)} %bitcast.115), calls=%async_computation.3 | async-start | bytes 4194304 | tf_op jit(solution)/shard_map/all_to_all | solution.py:96
  137.0 27.9 %all-to-all-done.3 = bf16[16,32,2048]{2,1,0:T(8,128)(2,1)} async-done(((bf16[16,32,2048]{2,1,0:T(8,128)(2,1)}), bf16[16,32,2048]{2,1,0:T(8,128)(2,1)}, u32[]{:S(2)}, u32[]{:S(2)}) %all-to-all-start.3) | async-done | bytes 2097184 | tf_op jit(solution)/shard_map/all_to_all | solution.py:96
  164.9 2.0 %convert_reduce_fusion = f32[32,2048]{1,0:T(8,128)S(1)} fusion(bf16[16,32,2048]{2,1,0:T(8,128)(2,1)} %all-to-all-done.3), kind=kLoop, calls=%fused_computation.17 | loop fusion | flops 2031616 | bytes 2359296 | tf_op jit(solution)/shard_map/reduce_sum | solution.py:97
  (63 shorter events, 18.0 us)
Async XLA Ops:
  6.5 121.3 %copy-start = (bf16[2,2048,320]{1,2,0:T(8,128)(2,1)S(1)}, bf16[2,2048,320]{1,2,0:T(8,128)(2,1)}, u32[]{:S(2)}) copy-start(bf16[2,2048,320]{1,2,0:T(8,128)(2,1)} %param.18) | copy-start | bytes 7864324
  6.5 7.9 %copy-start.6 = (s32[16]{0:T(128)S(1)}, s32[16]{0:T(128)}, u32[]{:S(2)}) copy-start(s32[16]{0:T(128)} %param.12) | copy-start | bytes 196
  6.5 115.3 %all-gather.2.cloned.1.call-start = ((), (), s32[]{:S(2)}) async-start(), calls=%async_computation.4 | async-start | bytes 4456448 | tf_op jit(solution)/shard_map/all_gather | solution.py:170
  7.8 17.2 %collective-permute-start = (bf16[4,256,128]{1,2,0:T(8,128)(2,1)S(1)}, bf16[4,256,128]{1,2,0:T(8,128)(2,1)}, u32[]{:S(2)}, u32[]{:S(2)}) collective-permute-start(bf16[4,256,128]{1,2,0:T(8,128)(2,1)S(1)} %bitcast.116), channel_id=1, source_target_pairs={{0,224},{16,240},{32,0},{48,16},{64,32},{80,48},{96,64},{112,80},{... | collective-permute-start | bytes 786440 | tf_op jit(solution)/shard_map/ppermute | solution.py:123
  12.0 13.0 %collective-permute-start.1 = (bf16[4,256,128]{1,2,0:T(8,128)(2,1)S(1)}, bf16[4,256,128]{1,2,0:T(8,128)(2,1)}, u32[]{:S(2)}, u32[]{:S(2)}) collective-permute-start(bf16[4,256,128]{1,2,0:T(8,128)(2,1)S(1)} %bitcast.117), channel_id=1, source_target_pairs={{0,32},{16,48},{32,64},{48,80},{64,96},{80,112},{96,128},{112,144}... | collective-permute-start | bytes 786440 | tf_op jit(solution)/shard_map/ppermute | solution.py:119
  20.2 9.2 %copy-start.2 = (bf16[32,2048]{1,0:T(8,128)(2,1)S(1)}, bf16[32,2048]{1,0:T(8,128)(2,1)}, u32[]{:S(2)}) copy-start(bf16[32,2048]{1,0:T(8,128)(2,1)} %param.10) | copy-start | bytes 393220
  26.1 12.4 %collective-permute-start.2 = (bf16[4,256,128]{1,2,0:T(8,128)(2,1)}, bf16[4,256,128]{1,2,0:T(8,128)(2,1)S(1)}, u32[]{:S(2)}, u32[]{:S(2)}) collective-permute-start(bf16[4,256,128]{1,2,0:T(8,128)(2,1)} %collective-permute-done), channel_id=1, source_target_pairs={{0,224},{16,240},{32,0},{48,16},{64,32},{80,48},{96,64},{112,80},{... | collective-permute-start | bytes 786440 | tf_op jit(solution)/shard_map/ppermute | solution.py:123
  29.4 9.1 %collective-permute-start.3 = (bf16[4,256,128]{1,2,0:T(8,128)(2,1)}, bf16[4,256,128]{1,2,0:T(8,128)(2,1)}, u32[]{:S(2)}, u32[]{:S(2)}) collective-permute-start(bf16[4,256,128]{1,2,0:T(8,128)(2,1)} %collective-permute-done.1), channel_id=1, source_target_pairs={{0,32},{16,48},{32,64},{48,80},{64,96},{80,112},{96,128},{112,144}... | collective-permute-start | bytes 786440 | tf_op jit(solution)/shard_map/ppermute | solution.py:119
  31.1 7.3 %copy-start.8 = (s32[1,8]{1,0:T(1,128)S(1)}, s32[1,8]{1,0:T(1,128)}, u32[]{:S(2)}) copy-start(s32[1,8]{1,0:T(1,128)} %param.11) | copy-start | bytes 100
  31.1 43.1 %all-to-all-start = ((bf16[16,32,2048]{2,1,0:T(8,128)(2,1)}), bf16[16,32,2048]{2,1,0:T(8,128)(2,1)}, u32[]{:S(2)}, u32[]{:S(2)}) async-start(bf16[16,32,2048]{2,1,0:T(8,128)(2,1)} %broadcast_in_dim.21), calls=%async_computation | async-start | bytes 4194304 | tf_op jit(solution)/shard_map/all_to_all | solution.py:89
  39.5 7.5 %collective-permute-start.4 = (bf16[4,256,128]{1,2,0:T(8,128)(2,1)S(1)}, bf16[4,256,128]{1,2,0:T(8,128)(2,1)S(1)}, u32[]{:S(2)}, u32[]{:S(2)}) collective-permute-start(bf16[4,256,128]{1,2,0:T(8,128)(2,1)S(1)} %collective-permute-done.2), channel_id=1, source_target_pairs={{0,224},{16,240},{32,0},{48,16},{64,32},{80,48},{96,64},{112,80},{... | collective-permute-start | bytes 786440 | tf_op jit(solution)/shard_map/ppermute | solution.py:123
  42.8 7.8 %collective-permute-start.5 = (bf16[4,256,128]{1,2,0:T(8,128)(2,1)}, bf16[4,256,128]{1,2,0:T(8,128)(2,1)S(1)}, u32[]{:S(2)}, u32[]{:S(2)}) collective-permute-start(bf16[4,256,128]{1,2,0:T(8,128)(2,1)} %collective-permute-done.3), channel_id=1, source_target_pairs={{0,32},{16,48},{32,64},{48,80},{64,96},{80,112},{96,128},{112,144}... | collective-permute-start | bytes 786440 | tf_op jit(solution)/shard_map/ppermute | solution.py:119
  50.7 7.8 %collective-permute-start.6 = (bf16[4,256,128]{1,2,0:T(8,128)(2,1)S(1)}, bf16[4,256,128]{1,2,0:T(8,128)(2,1)}, u32[]{:S(2)}, u32[]{:S(2)}) collective-permute-start(bf16[4,256,128]{1,2,0:T(8,128)(2,1)S(1)} %collective-permute-done.5), channel_id=1, source_target_pairs={{0,32},{16,48},{32,64},{48,80},{64,96},{80,112},{96,128},{112,144}... | collective-permute-start | bytes 786440 | tf_op jit(solution)/shard_map/ppermute | solution.py:119
  60.2 1.9 %collective-permute-start.7 = (bf16[4,256,128]{1,2,0:T(8,128)(2,1)}, bf16[4,256,128]{1,2,0:T(8,128)(2,1)}, u32[]{:S(2)}, u32[]{:S(2)}) collective-permute-start(bf16[4,256,128]{1,2,0:T(8,128)(2,1)} %get-tuple-element.35), channel_id=1, source_target_pairs={{0,16},{16,0},{32,48},{48,32},{64,80},{80,64},{96,112},{112,96},{1... | collective-permute-start | bytes 786440 | tf_op jit(solution)/shard_map/ppermute | solution.py:129
  75.4 19.4 %all-to-all-start.1 = ((bf16[16,256,128]{2,1,0:T(8,128)(2,1)}), bf16[16,256,128]{2,1,0:T(8,128)(2,1)}, u32[]{:S(2)}, u32[]{:S(2)}) async-start(bf16[16,256,128]{2,1,0:T(8,128)(2,1)} %bitcast.114), calls=%async_computation.1 | async-start | bytes 2097152 | tf_op jit(solution)/shard_map/all_to_all | solution.py:176
  82.1 2.1 %copy-start.1 = (bf16[2048,192]{1,0:T(8,128)(2,1)S(1)}, bf16[2048,192]{1,0:T(8,128)(2,1)}, u32[]{:S(2)}) copy-start(bf16[2048,192]{1,0:T(8,128)(2,1)} %pad_maximum_fusion) | copy-start | bytes 2359300
  86.0 10.7 %copy-start.3 = (bf16[512,1,32]{0,2,1:T(8,128)(2,1)S(1)}, bf16[512,1,32]{0,2,1:T(8,128)(2,1)}, u32[]{:S(2)}) copy-start(bf16[512,1,32]{0,2,1:T(8,128)(2,1)} %get-tuple-element.49) | copy-start | bytes 98308
  86.0 10.7 %copy-start.4 = (bf16[512,1,32]{0,2,1:T(8,128)(2,1)S(1)}, bf16[512,1,32]{0,2,1:T(8,128)(2,1)}, u32[]{:S(2)}) copy-start(bf16[512,1,32]{0,2,1:T(8,128)(2,1)} %get-tuple-element.50) | copy-start | bytes 98308
  127.8 1.7 copy-start.5
  127.8 2.1 %copy-start.7 = (bf16[320,2048]{1,0:T(8,128)(2,1)S(1)}, bf16[320,2048]{1,0:T(8,128)(2,1)}, u32[]{:S(2)}) copy-start(bf16[320,2048]{1,0:T(8,128)(2,1)} %param.19) | copy-start | bytes 3932164
  132.6 32.3 %all-to-all-start.3 = ((bf16[16,32,2048]{2,1,0:T(8,128)(2,1)}), bf16[16,32,2048]{2,1,0:T(8,128)(2,1)}, u32[]{:S(2)}, u32[]{:S(2)}) async-start(bf16[16,32,2048]{2,1,0:T(8,128)(2,1)} %bitcast.115), calls=%async_computation.3 | async-start | bytes 4194304 | tf_op jit(solution)/shard_map/all_to_all | solution.py:96
Sparse Core Ops, SparseCore 0:
  12.2 72.4 all-gather.1

commit v21 on v20

--- a/solution.py
+++ b/solution.py
@@ -160,7 +160,7 @@
     cos_table, sin_table = rope_tables(positions)
     key_cols = lax.dynamic_slice_in_dim(key_weight, kv_first * HD, kv_width, 1)
     value_cols = lax.dynamic_slice_in_dim(value_weight, kv_first * HD, kv_width, 1)
-    projection = jnp.concatenate([query_weight, key_cols, value_cols], axis=1)
+    projection = (query_weight, key_cols, value_cols)
 
     shard_rows = prefix_cache.shape[0]
     kv_groups = KVH // local_kv
@@ -182,7 +182,9 @@
     group_rows = gather_rows(tokens, "tensor")
     segment = norm_rows(group_rows)
     seg_rows = segment.shape[0]
-    mapped = jnp.dot(segment, projection, preferred_element_type=jnp.float32)
+    mapped = jnp.concatenate(
+        [jnp.dot(segment, part, preferred_element_type=jnp.float32) for part in projection], axis=1
+    )
     query_part = rotate(
         mapped[:, :query_width].reshape(seg_rows, local_heads, HD), cos_table, sin_table
     )

time: 176 us -> 176 us (level); the launches traced: 175 us -> 172 us
  waiting for transfers between devices: 65.3 us -> 60.4 us
  matrix products: 14.1 us -> 17.2 us
    all_to_all x1, waiting for transfers between devices: 12 us -> 7.04 us  [gather_rows(): received = lax.all_to_all(copies, axis, 0, 0, tiled=True)]
    dot_general x1 -> x3, matrix products: 0.84 us -> 3.87 us  [on_device(): jnp.dot(segment, part, preferred_element_type=jnp.float32)]
    concatenate x1 -> x0, other arithmetic: 2.8 us -> none  [on_device(): projection = jnp.concatenate([query_weight, key_cols, value_cols], axis=1)]
    unnamed x20 -> x21, local copies, waits for them, and re-layouts: 3.68 us -> 1.68 us
    select_n x3, other arithmetic: 2.14 us -> 3.94 us  [fetch_slot(): theirs = jnp.where(theirs_at == step, behind, theirs)]
  transfers between devices with their start and end apart: 12 -> 12, of which waited for: 7 -> 7; matrix products, arithmetic and copies ran while one was open for 16% -> 18% of each run, Pallas kernels for 0% -> 0%
where the time goes in v21:
time: 176 us; the launch traced here: 172 us
  waiting for transfers between devices  60.4 us (34%)
  starting transfers between devices  26.9 us (15%)
  blocking collectives  19.6 us (11%)
  between operations  19.1 us (11%)
  other arithmetic  17.3 us (10%)
  matrix products  17.2 us (10%)
  local copies, waits for them, and re-layouts  11.8 us (7%)
    all_to_all x1, waiting for transfers between devices, sum_scatter_rows(): received = lax.all_to_all(parts, axis, 0, 0, tiled=True)  27.9 us
    all_to_all x1, blocking collectives, gather_rows(): received = lax.all_to_all(copies, axis, 0, 0, tiled=True)  19.6 us
    ppermute x4, waiting for transfers between devices, fetch_slot(): ahead = lax.ppermute(ahead, 'dp', onward)  10.9 us
    ppermute x3, starting transfers between devices, fetch_slot(): behind = lax.ppermute(behind, 'dp', backward)  10.7 us
    all_to_all x1, waiting for transfers between devices, on_device(): incoming = lax.all_to_all(outgoing, 'tensor', 0, 0, tiled=True)  9.12 us
    all_to_all x1, starting transfers between devices, gather_rows(): received = lax.all_to_all(copies, axis, 0, 0, tiled=True)  7.22 us
    all_to_all x1, waiting for transfers between devices, gather_rows(): received = lax.all_to_all(copies, axis, 0, 0, tiled=True)  7.04 us
    dot_general x1, matrix products, on_device(): attn_sum = jnp.dot(every_head, out_full, preferred_element_type=jnp.float32)  5.96 us
  transfers between devices with their start and end apart: 12, of which 7 were waited for; matrix products, arithmetic and copies ran while one was open for 18% of the time, Pallas kernels for 0%

profile of v21, /device:TPU:0, one launch (start us, length us, event | category | flops | bytes accessed | tf_op | source)
XLA Modules:
  0.0 172.2 jit_solution(905038210218534730)
XLA Ops:
  7.8 4.2 %collective-permute-start = (bf16[4,256,128]{1,2,0:T(8,128)(2,1)S(1)}, bf16[4,256,128]{1,2,0:T(8,128)(2,1)}, u32[]{:S(2)}, u32[]{:S(2)}) collective-permute-start(bf16[4,256,128]{1,2,0:T(8,128)(2,1)S(1)} %bitcast.120), channel_id=1, source_target_pairs={{0,224},{16,240},{32,0},{48,16},{64,32},{80,48},{96,64},{112,80},{... | collective-permute-start | bytes 786440 | tf_op jit(solution)/shard_map/ppermute | solution.py:123
  18.9 2.4 %constant_dynamic-slice_fusion = (bf16[2048,64]{1,0:T(8,128)(2,1)S(1)}, bf16[2048,64]{1,0:T(8,128)(2,1)}) fusion(bf16[2048,256]{1,0:T(8,128)(2,1)} %param.16, s32[]{:T(128)S(6)} %select_n.173, bf16[2048,256]{1,0:T(8,128)(2,1)} %param.15), kind=kLoop, calls=%fused_computation.85 | loop fusion | bytes 1048580 | tf_op jit(solution)/shard_map/dynamic_slice | solution.py:162
  21.2 1.9 %select_select_fusion.4 = (bf16[4,256,128]{1,2,0:T(8,128)(2,1)}, bf16[4,256,128]{1,2,0:T(8,128)(2,1)}) fusion(bf16[4,256,128]{1,2,0:T(8,128)(2,1)} %collective-permute-done, bf16[4,256,128]{1,2,0:T(8,128)(2,1)} %collective-permute-done.1, pred[]{:T(512)S(6)} %eq.70, pred[]{:T(512)S(6)} %eq.69, bf16[4,256,2,64]{1,3,2,0:T(8,128)(2,1)S(1)} %copy.19, ...), kind=kLoop, calls=%fused_computation.51 | loop fusion | flops 524288 | bytes 1310724 | tf_op jit(solution)/shard_map/jit(_where)/select_n | solution.py:125
  23.1 3.2 %collective-permute-start.2 = (bf16[4,256,128]{1,2,0:T(8,128)(2,1)}, bf16[4,256,128]{1,2,0:T(8,128)(2,1)}, u32[]{:S(2)}, u32[]{:S(2)}) collective-permute-start(bf16[4,256,128]{1,2,0:T(8,128)(2,1)} %collective-permute-done), channel_id=1, source_target_pairs={{0,224},{16,240},{32,0},{48,16},{64,32},{80,48},{96,64},{112,80},{... | collective-permute-start | bytes 786440 | tf_op jit(solution)/shard_map/ppermute | solution.py:123
  27.9 7.2 %all-to-all-start = ((bf16[16,32,2048]{2,1,0:T(8,128)(2,1)}), bf16[16,32,2048]{2,1,0:T(8,128)(2,1)}, u32[]{:S(2)}, u32[]{:S(2)}) async-start(bf16[16,32,2048]{2,1,0:T(8,128)(2,1)} %broadcast_in_dim.21), calls=%async_computation | async-start | bytes 4194304 | tf_op jit(solution)/shard_map/all_to_all | solution.py:89
  36.6 3.3 %collective-permute-start.4 = (bf16[4,256,128]{1,2,0:T(8,128)(2,1)}, bf16[4,256,128]{1,2,0:T(8,128)(2,1)S(1)}, u32[]{:S(2)}, u32[]{:S(2)}) collective-permute-start(bf16[4,256,128]{1,2,0:T(8,128)(2,1)} %collective-permute-done.2), channel_id=1, source_target_pairs={{0,224},{16,240},{32,0},{48,16},{64,32},{80,48},{96,64},{112,80},{... | collective-permute-start | bytes 786440 | tf_op jit(solution)/shard_map/ppermute | solution.py:123
  40.0 4.4 %collective-permute-done.4 = bf16[4,256,128]{1,2,0:T(8,128)(2,1)S(1)} collective-permute-done((bf16[4,256,128]{1,2,0:T(8,128)(2,1)}, bf16[4,256,128]{1,2,0:T(8,128)(2,1)S(1)}, u32[]{:S(2)}, u32[]{:S(2)}) %collective-permute-start.4) | collective-permute-done | bytes 262176 | tf_op jit(solution)/shard_map/ppermute | solution.py:123
  44.4 3.3 %collective-permute-done.5 = bf16[4,256,128]{1,2,0:T(8,128)(2,1)S(1)} collective-permute-done((bf16[4,256,128]{1,2,0:T(8,128)(2,1)}, bf16[4,256,128]{1,2,0:T(8,128)(2,1)S(1)}, u32[]{:S(2)}, u32[]{:S(2)}) %collective-permute-start.5) | collective-permute-done | bytes 262176 | tf_op jit(solution)/shard_map/ppermute | solution.py:119
  48.7 7.6 %collective-permute-done.6 = bf16[4,256,128]{1,2,0:T(8,128)(2,1)} collective-permute-done((bf16[4,256,128]{1,2,0:T(8,128)(2,1)S(1)}, bf16[4,256,128]{1,2,0:T(8,128)(2,1)}, u32[]{:S(2)}, u32[]{:S(2)}) %collective-permute-start.6) | collective-permute-done | bytes 262176 | tf_op jit(solution)/shard_map/ppermute | solution.py:119
  56.3 1.9 %broadcast_select_fusion = (bf16[4,256,128]{1,2,0:T(8,128)(2,1)}, bf16[4,256,128]{1,2,0:T(8,128)(2,1)S(1)}) fusion(bf16[4,256,128]{1,2,0:T(8,128)(2,1)} %collective-permute-done.6, bf16[4,256,128]{1,2,0:T(8,128)(2,1)} %get-tuple-element.35, pred[]{:T(512)S(6)} %eq.77, bf16[4,256,128]{1,2,0:T(8,128)(2,1)} %get-tuple-element.34, pred[]{:T(512)S(6)} %eq.64), kind=kLoop, calls=%fused_computation.53 | loop fusion | flops 262144 | bytes 1310722 | tf_op jit(solution)/shard_map/jit(_where)/select_n | solution.py:121
  61.9 7.0 %all-to-all-done = bf16[16,32,2048]{2,1,0:T(8,128)(2,1)} async-done(((bf16[16,32,2048]{2,1,0:T(8,128)(2,1)}), bf16[16,32,2048]{2,1,0:T(8,128)(2,1)}, u32[]{:S(2)}, u32[]{:S(2)}) %all-to-all-start) | async-done | bytes 2097184 | tf_op jit(solution)/shard_map/all_to_all | solution.py:89
  70.1 4.5 %all-to-all-start.1 = ((bf16[16,256,128]{2,1,0:T(8,128)(2,1)}), bf16[16,256,128]{2,1,0:T(8,128)(2,1)}, u32[]{:S(2)}, u32[]{:S(2)}) async-start(bf16[16,256,128]{2,1,0:T(8,128)(2,1)} %bitcast.118), calls=%async_computation.1 | async-start | bytes 2097152 | tf_op jit(solution)/shard_map/all_to_all | solution.py:176
  74.6 2.1 %fusion.8 = f32[16,32]{1,0:T(8,128)S(1)} fusion(bf16[16,32,2048]{2,1,0:T(8,128)(2,1)} %all-to-all-done), kind=kLoop, calls=%fused_computation.14 | loop fusion | flops 3145216 | bytes 2099200 | tf_op jit(solution)/shard_map/reduce_sum | solution.py:49
  76.8 2.1 %fusion.9 = bf16[512,2048]{1,0:T(8,128)(2,1)S(1)} fusion(bf16[16,32,2048]{2,1,0:T(8,128)(2,1)} %all-to-all-done, f32[512]{0:T(512)S(1)} %rsqrt.20), kind=kLoop, calls=%fused_computation.15 | loop fusion | flops 3145728 | bytes 4196352 | tf_op jit(solution)/shard_map/convert_element_type | solution.py:49
  80.9 2.4 %fusion.25 = bf16[512,1,64]{0,2,1:T(8,128)(2,1)S(1)} fusion(bf16[512,2048]{1,0:T(8,128)(2,1)} %copy-done.1, bf16[2048,64]{1,0:T(8,128)(2,1)S(1)} %get-tuple-element.38), kind=kOutput, calls=%fused_computation.33 | convolution fusion | flops 134250496 | bytes 2424832 | tf_op jit(solution)/shard_map/dot_general | solution.py:186
  83.4 9.1 %all-to-all-done.1 = bf16[16,256,128]{2,1,0:T(8,128)(2,1)} async-done(((bf16[16,256,128]{2,1,0:T(8,128)(2,1)}), bf16[16,256,128]{2,1,0:T(8,128)(2,1)}, u32[]{:S(2)}, u32[]{:S(2)}) %all-to-all-start.1) | async-done | bytes 1048608 | tf_op jit(solution)/shard_map/all_to_all | solution.py:176
  92.5 2.1 %slice_bitcast_fusion.1 = (bf16[4096,1,64]{2,0,1:T(8,128)(2,1)S(1)}, bf16[4096,1,64]{2,0,1:T(8,128)(2,1)S(1)}) fusion(bf16[4096,128]{1,0:T(8,128)(2,1)} %bitcast.7), kind=kLoop, calls=%fused_computation.38 | loop fusion | bytes 2097152 | tf_op jit(solution)/shard_map/reshape;broadcast_in_dim;reshape | solution.py:180
  99.0 19.6 %all_to_all.20 = bf16[16,1,64,512]{3,2,1,0:T(8,128)(2,1)} all-to-all(bf16[16,1,64,512]{3,2,1,0:T(8,128)(2,1)S(1)} %broadcast_in_dim.26), channel_id=1, replica_groups=mesh['dp'=16,'tensor'=16] {'tensor'}, dimensions={0} | all-to-all | bytes 2097152 | tf_op jit(solution)/shard_map/all_to_all | solution.py:89
  118.7 6.0 %fusion.6 = (f32[512]{0:T(512)S(1)}, bf16[512,2048]{1,0:T(8,128)(2,1)S(1)}) fusion(bf16[1024,512]{1,0:T(8,128)(2,1)} %bitcast.122, bf16[1024,2048]{1,0:T(8,128)(2,1)} %all-gather.2.cloned.1.call-done, bf16[16,32,2048]{2,1,0:T(8,128)(2,1)} %all-to-all-done), kind=kOutput, calls=%fused_computation.9 | convolution fusion | flops 2153774592 | bytes 9439232 | tf_op jit(solution)/shard_map/dot_general | solution.py:226
  124.7 1.6 fusion.15
  126.7 2.7 %convolution_convert_fusion = bf16[512,2048]{1,0:T(8,128)(2,1)} fusion(bf16[320,2048]{1,0:T(8,128)(2,1)S(1)} %copy-done.8, f32[2,512,320]{1,2,0:T(8,128)S(1)} %fusion.15), kind=kOutput, calls=%fused_computation.18 | convolution fusion | flops 673120256 | bytes 4718592 | tf_op jit(solution)/shard_map/dot_general | solution.py:234
  129.4 4.4 %all-to-all-start.3 = ((bf16[16,32,2048]{2,1,0:T(8,128)(2,1)}), bf16[16,32,2048]{2,1,0:T(8,128)(2,1)}, u32[]{:S(2)}, u32[]{:S(2)}) async-start(bf16[16,32,2048]{2,1,0:T(8,128)(2,1)} %bitcast.119), calls=%async_computation.3 | async-start | bytes 4194304 | tf_op jit(solution)/shard_map/all_to_all | solution.py:96
  133.8 27.9 %all-to-all-done.3 = bf16[16,32,2048]{2,1,0:T(8,128)(2,1)} async-done(((bf16[16,32,2048]{2,1,0:T(8,128)(2,1)}), bf16[16,32,2048]{2,1,0:T(8,128)(2,1)}, u32[]{:S(2)}, u32[]{:S(2)}) %all-to-all-start.3) | async-done | bytes 2097184 | tf_op jit(solution)/shard_map/all_to_all | solution.py:96
  161.8 2.0 %convert_reduce_fusion = f32[32,2048]{1,0:T(8,128)S(1)} fusion(bf16[16,32,2048]{2,1,0:T(8,128)(2,1)} %all-to-all-done.3), kind=kLoop, calls=%fused_computation.17 | loop fusion | flops 2031616 | bytes 2359296 | tf_op jit(solution)/shard_map/reduce_sum | solution.py:97
  (63 shorter events, 20.3 us)
Async XLA Ops:
  6.5 118.1 %copy-start = (bf16[2,2048,320]{1,2,0:T(8,128)(2,1)S(1)}, bf16[2,2048,320]{1,2,0:T(8,128)(2,1)}, u32[]{:S(2)}) copy-start(bf16[2,2048,320]{1,2,0:T(8,128)(2,1)} %param.18) | copy-start | bytes 7864324
  6.5 19.8 %copy-start.6 = (bf16[32,2048]{1,0:T(8,128)(2,1)S(1)}, bf16[32,2048]{1,0:T(8,128)(2,1)}, u32[]{:S(2)}) copy-start(bf16[32,2048]{1,0:T(8,128)(2,1)} %param.10) | copy-start | bytes 393220
  6.5 112.1 %all-gather.2.cloned.1.call-start = ((), (), s32[]{:S(2)}) async-start(), calls=%async_computation.4 | async-start | bytes 4456448 | tf_op jit(solution)/shard_map/all_gather | solution.py:170
  7.8 13.4 %collective-permute-start = (bf16[4,256,128]{1,2,0:T(8,128)(2,1)S(1)}, bf16[4,256,128]{1,2,0:T(8,128)(2,1)}, u32[]{:S(2)}, u32[]{:S(2)}) collective-permute-start(bf16[4,256,128]{1,2,0:T(8,128)(2,1)S(1)} %bitcast.120), channel_id=1, source_target_pairs={{0,224},{16,240},{32,0},{48,16},{64,32},{80,48},{96,64},{112,80},{... | collective-permute-start | bytes 786440 | tf_op jit(solution)/shard_map/ppermute | solution.py:123
  12.0 9.2 %collective-permute-start.1 = (bf16[4,256,128]{1,2,0:T(8,128)(2,1)S(1)}, bf16[4,256,128]{1,2,0:T(8,128)(2,1)}, u32[]{:S(2)}, u32[]{:S(2)}) collective-permute-start(bf16[4,256,128]{1,2,0:T(8,128)(2,1)S(1)} %bitcast.121), channel_id=1, source_target_pairs={{0,32},{16,48},{32,64},{48,80},{64,96},{80,112},{96,128},{112,144}... | collective-permute-start | bytes 786440 | tf_op jit(solution)/shard_map/ppermute | solution.py:119
  23.1 12.3 %collective-permute-start.2 = (bf16[4,256,128]{1,2,0:T(8,128)(2,1)}, bf16[4,256,128]{1,2,0:T(8,128)(2,1)}, u32[]{:S(2)}, u32[]{:S(2)}) collective-permute-start(bf16[4,256,128]{1,2,0:T(8,128)(2,1)} %collective-permute-done), channel_id=1, source_target_pairs={{0,224},{16,240},{32,0},{48,16},{64,32},{80,48},{96,64},{112,80},{... | collective-permute-start | bytes 786440 | tf_op jit(solution)/shard_map/ppermute | solution.py:123
  26.3 9.1 %collective-permute-start.3 = (bf16[4,256,128]{1,2,0:T(8,128)(2,1)}, bf16[4,256,128]{1,2,0:T(8,128)(2,1)}, u32[]{:S(2)}, u32[]{:S(2)}) collective-permute-start(bf16[4,256,128]{1,2,0:T(8,128)(2,1)} %collective-permute-done.1), channel_id=1, source_target_pairs={{0,32},{16,48},{32,64},{48,80},{64,96},{80,112},{96,128},{112,144}... | collective-permute-start | bytes 786440 | tf_op jit(solution)/shard_map/ppermute | solution.py:119
  27.9 7.3 %copy-start.9 = (s32[1,8]{1,0:T(1,128)S(1)}, s32[1,8]{1,0:T(1,128)}, u32[]{:S(2)}) copy-start(s32[1,8]{1,0:T(1,128)} %param.11) | copy-start | bytes 100
  27.9 7.5 %copy-start.3 = (bf16[4,256,128]{1,2,0:T(8,128)(2,1)S(1)}, bf16[4,256,128]{1,2,0:T(8,128)(2,1)}, u32[]{:S(2)}) copy-start(bf16[4,256,128]{1,2,0:T(8,128)(2,1)} %get-tuple-element.28) | copy-start | bytes 786436
  27.9 41.0 %all-to-all-start = ((bf16[16,32,2048]{2,1,0:T(8,128)(2,1)}), bf16[16,32,2048]{2,1,0:T(8,128)(2,1)}, u32[]{:S(2)}, u32[]{:S(2)}) async-start(bf16[16,32,2048]{2,1,0:T(8,128)(2,1)} %broadcast_in_dim.21), calls=%async_computation | async-start | bytes 4194304 | tf_op jit(solution)/shard_map/all_to_all | solution.py:89
  36.6 7.8 %collective-permute-start.4 = (bf16[4,256,128]{1,2,0:T(8,128)(2,1)}, bf16[4,256,128]{1,2,0:T(8,128)(2,1)S(1)}, u32[]{:S(2)}, u32[]{:S(2)}) collective-permute-start(bf16[4,256,128]{1,2,0:T(8,128)(2,1)} %collective-permute-done.2), channel_id=1, source_target_pairs={{0,224},{16,240},{32,0},{48,16},{64,32},{80,48},{96,64},{112,80},{... | collective-permute-start | bytes 786440 | tf_op jit(solution)/shard_map/ppermute | solution.py:123
  39.9 7.8 %collective-permute-start.5 = (bf16[4,256,128]{1,2,0:T(8,128)(2,1)}, bf16[4,256,128]{1,2,0:T(8,128)(2,1)S(1)}, u32[]{:S(2)}, u32[]{:S(2)}) collective-permute-start(bf16[4,256,128]{1,2,0:T(8,128)(2,1)} %collective-permute-done.3), channel_id=1, source_target_pairs={{0,32},{16,48},{32,64},{48,80},{64,96},{80,112},{96,128},{112,144}... | collective-permute-start | bytes 786440 | tf_op jit(solution)/shard_map/ppermute | solution.py:119
  48.6 7.7 %collective-permute-start.6 = (bf16[4,256,128]{1,2,0:T(8,128)(2,1)S(1)}, bf16[4,256,128]{1,2,0:T(8,128)(2,1)}, u32[]{:S(2)}, u32[]{:S(2)}) collective-permute-start(bf16[4,256,128]{1,2,0:T(8,128)(2,1)S(1)} %collective-permute-done.5), channel_id=1, source_target_pairs={{0,32},{16,48},{32,64},{48,80},{64,96},{80,112},{96,128},{112,144}... | collective-permute-start | bytes 786440 | tf_op jit(solution)/shard_map/ppermute | solution.py:119
  58.1 1.9 %collective-permute-start.7 = (bf16[4,256,128]{1,2,0:T(8,128)(2,1)}, bf16[4,256,128]{1,2,0:T(8,128)(2,1)}, u32[]{:S(2)}, u32[]{:S(2)}) collective-permute-start(bf16[4,256,128]{1,2,0:T(8,128)(2,1)} %get-tuple-element.37), channel_id=1, source_target_pairs={{0,16},{16,0},{32,48},{48,32},{64,80},{80,64},{96,112},{112,96},{1... | collective-permute-start | bytes 786440 | tf_op jit(solution)/shard_map/ppermute | solution.py:129
  70.1 22.4 %all-to-all-start.1 = ((bf16[16,256,128]{2,1,0:T(8,128)(2,1)}), bf16[16,256,128]{2,1,0:T(8,128)(2,1)}, u32[]{:S(2)}, u32[]{:S(2)}) async-start(bf16[16,256,128]{2,1,0:T(8,128)(2,1)} %bitcast.118), calls=%async_computation.1 | async-start | bytes 2097152 | tf_op jit(solution)/shard_map/all_to_all | solution.py:176
  76.7 2.2 %copy-start.4 = (bf16[2048,64]{0,1:T(8,128)(2,1)S(1)}, bf16[2048,64]{0,1:T(8,128)(2,1)}, u32[]{:S(2)}) copy-start(bf16[2048,64]{0,1:T(8,128)(2,1)} %param.14) | copy-start | bytes 786436
  76.8 2.8 %copy-start.2 = (bf16[2048,64]{1,0:T(8,128)(2,1)S(1)}, bf16[2048,64]{1,0:T(8,128)(2,1)}, u32[]{:S(2)}) copy-start(bf16[2048,64]{1,0:T(8,128)(2,1)} %get-tuple-element.39) | copy-start | bytes 786436
  78.9 1.5 copy-start.1
  83.3 11.3 %copy-start.5 = (pred[512,512]{0,1:T(32,128)(4,1)S(1)}, pred[512,512]{0,1:T(32,128)(4,1)}, u32[]{:S(2)}) copy-start(pred[512,512]{0,1:T(32,128)(4,1)} %fusion.35) | copy-start | bytes 786436
  124.6 1.7 copy-start.7
  124.7 2.1 %copy-start.8 = (bf16[320,2048]{1,0:T(8,128)(2,1)S(1)}, bf16[320,2048]{1,0:T(8,128)(2,1)}, u32[]{:S(2)}) copy-start(bf16[320,2048]{1,0:T(8,128)(2,1)} %param.19) | copy-start | bytes 3932164
  129.4 32.4 %all-to-all-start.3 = ((bf16[16,32,2048]{2,1,0:T(8,128)(2,1)}), bf16[16,32,2048]{2,1,0:T(8,128)(2,1)}, u32[]{:S(2)}, u32[]{:S(2)}) async-start(bf16[16,32,2048]{2,1,0:T(8,128)(2,1)} %bitcast.119), calls=%async_computation.3 | async-start | bytes 4194304 | tf_op jit(solution)/shard_map/all_to_all | solution.py:96
Sparse Core Ops, SparseCore 0:
  12.2 73.2 all-gather.1
